TPU v7x, 32 devices: a whole 2x2x4 slice. The times are simulated.
32 devices in a mesh: section: 2 (over x), dp: 4 (over z), expert: 4 (over y, core).
Axes of the slice: x: 2, y: 2, z: 4, core: 2. Of those that a mesh axis runs over, the one named last changes fastest.
Arguments:
- grad_out: bfloat16 [2, 2048, 2048], P('section', ('dp', 'expert')), may hold values from -6 to 6
- routes: int32 [2, 2048, 2], P('section', ('dp', 'expert')), may hold values from 0 to 3, all different within a row; in each aligned block of 128 rows (0 to 127, 128 to 255, ..., all dimensions but the last counted through in order) at most 80 rows name the same one
- gates: float32 [2, 2048, 2], P('section', ('dp', 'expert')), may hold values from 0.2 to 1
- hidden: bfloat16 [2, 4, 4, 320, 1408], P('section', 'dp', 'expert'), may hold values from -0.09375 to 0.09375
- w_down: bfloat16 [2, 4, 1408, 2048], P('section', 'expert'), may hold values from -0.15625 to 0.15625
Outputs:
- grad_hidden: bfloat16 [2, 4, 4, 320, 1408], P('section', 'dp', 'expert')
- grad_w_down: float32 [2, 4, 1408, 2048], P('section', 'expert', 'dp')
Inputs may be any that keep to these rules, and one draw needn't show every extreme that they name: `routes`: each token names 2 different experts; among the 128 tokens of one device no expert is named more than 80 times, a bound that some block reaches.
All inputs are finite; a program needn't handle non-finite values.
Results may differ from a plain program's by a relative error of at most 0.015.
Values may be sent and summed in bfloat16 or wider, within the bound.
No kernel may reach another device: no remote copies, remote signals or barrier semaphores. Data moves between devices by JAX's collectives and lax.ppermute only.
A program may use at most 64 MiB of HBM per device.

v0:
```python
import jax
import jax.numpy as jnp
from jax import lax
from jax.sharding import PartitionSpec as P


def shifted(value, axis, steps):
    count = lax.axis_size(axis)
    pairs = [(source, (source + steps) % count) for source in range(count)]
    return lax.ppermute(value, axis, pairs)


def dispatch_block(rows, ids, weights, count, width):
    flat_ids = ids.reshape(-1)
    onehot = (flat_ids[:, None] == jnp.arange(count, dtype=jnp.int32)[None, :]).astype(jnp.int32)
    position = jnp.sum((jnp.cumsum(onehot, axis=0) - 1) * onehot, axis=1)
    target = flat_ids * width + position
    scaled = (weights[:, :, None] * rows[:, None, :].astype(jnp.float32)).astype(jnp.bfloat16)
    scaled = scaled.reshape(-1, rows.shape[1])
    buffer = jnp.zeros((count * width, rows.shape[1]), jnp.bfloat16).at[target].set(scaled)
    return buffer.reshape(count, width, rows.shape[1])


def shards(grad_out, routes, gates, hidden, w_down):
    incoming = shifted(grad_out, "section", -1)[0]
    groups = lax.axis_size("expert")
    saved = hidden[0, 0, 0]
    weight = w_down[0, 0]
    slot_count = saved.shape[0]
    width = slot_count // groups
    model_width = incoming.shape[1]
    outgoing = dispatch_block(incoming, routes[0], gates[0], groups, width)
    piece = lax.all_to_all(outgoing, "expert", split_axis=0, concat_axis=0, tiled=True)
    grad_rows_out = jnp.einsum(
        "skd,hd->skh", piece, weight, preferred_element_type=jnp.float32
    ).astype(jnp.bfloat16)
    scaled = piece.reshape(slot_count, model_width)
    full = lax.dot_general(
        saved, scaled, (((0,), (0,)), ((), ())), preferred_element_type=jnp.float32
    )
    weight_grad = lax.psum_scatter(
        full.astype(jnp.bfloat16), "dp", scatter_dimension=0, tiled=True
    ).astype(jnp.float32)
    grad_hidden = grad_rows_out.reshape(1, 1, 1, slot_count, saved.shape[1])
    return (grad_hidden, weight_grad.reshape(1, 1, weight_grad.shape[0], model_width))


def solution(mesh):
    placed = (
        P("section", ("dp", "expert"), None),
        P("section", ("dp", "expert"), None),
        P("section", ("dp", "expert"), None),
        P("section", "dp", "expert", None, None),
        P("section", "expert", None, None),
    )
    return jax.shard_map(
        shards,
        mesh=mesh,
        in_specs=placed,
        out_specs=(P("section", "dp", "expert", None, None), P("section", "expert", "dp", None)),
        check_vma=False,
    )
```

profile of v0, /device:TPU:0, one launch (start us, length us, event | category | flops | bytes accessed | tf_op | source)
XLA Modules:
  0.0 182.3 jit_solution(4368078253969527248)
XLA Ops:
  7.2 3.0 %collective-permute-start = (bf16[1,128,2048]{2,1,0:T(8,128)(2,1)}, bf16[1,128,2048]{2,1,0:T(8,128)(2,1)S(1)}, u32[]{:S(2)}, u32[]{:S(2)}) collective-permute-start(bf16[1,128,2048]{2,1,0:T(8,128)(2,1)} %param.5), channel_id=1, source_target_pairs={{0,16},{16,0},{1,17},{17,1},{2,18},{18,2},{3,19},{19,3},{4,20},{20... | collective-permute-start | bytes 1572872 | tf_op jit(solution)/shard_map/ppermute | solution.py:10
  10.3 0.7 broadcast_multiply_fusion
  10.9 0.8 copy.18
  11.7 0.1 eq.29
  11.9 0.1 eq.25
  12.0 0.1 copy.17
  12.1 0.1 mul.39
  12.3 1.2 reduce-window.6
  13.6 0.1 copy.20
  13.7 0.1 copy.21
  13.8 0.8 copy.22
  14.6 0.1 mul.41
  14.8 7.5 %collective-permute-done = bf16[1,128,2048]{2,1,0:T(8,128)(2,1)S(1)} collective-permute-done((bf16[1,128,2048]{2,1,0:T(8,128)(2,1)}, bf16[1,128,2048]{2,1,0:T(8,128)(2,1)S(1)}, u32[]{:S(2)}, u32[]{:S(2)}) %collective-permute-start) | collective-permute-done | bytes 524320 | tf_op jit(solution)/shard_map/ppermute | solution.py:10
  22.5 2.5 %mul.43 = f32[128,2,2048]{2,1,0:T(2,128)} broadcast(f32[128,2048]{1,0:T(8,128)S(1)} %bitcast_convert_fusion.1), dimensions={0,2} | broadcast | bytes 3145728 | tf_op jit(solution)/shard_map/mul | solution.py:18
  25.0 2.7 %mul.44 = f32[256,2048]{1,0:T(8,128)S(1)} reshape(f32[128,2,2048]{2,1,0:T(2,128)} %mul.43) | data formatting | bytes 4194304 | tf_op jit(solution)/shard_map/mul | solution.py:18
  27.7 3.3 %scatter_custom_fusion = bf16[320,2048]{1,0:T(8,128)(2,1)} fusion(s32[256]{0:T(256)S(1)} %bitcast.46, f32[256,2048]{1,0:T(8,128)S(1)} %mul.44, f32[256]{0:T(256)S(1)} %mul.41, bf16[]{:T(256)} %constant.5.clone.1), kind=kCustom, calls=%fused_computation.8 | custom fusion | flops 1048576 | bytes 3408898 | tf_op jit(solution)/shard_map/scatter | solution.py:20
  31.1 20.7 %all_to_all.5 = bf16[4,80,2048]{2,1,0:T(8,128)(2,1)S(1)} all-to-all(bf16[4,80,2048]{2,1,0:T(8,128)(2,1)} %bitcast.42), channel_id=1, replica_groups=mesh['section'=2,'dp'=4,'expert'=4] {'expert'}, dimensions={0} | all-to-all | bytes 2621440 | tf_op jit(solution)/shard_map/all_to_all | solution.py:33
  51.8 5.2 %fusion = bf16[1408,2048]{0,1:T(8,128)(2,1)} fusion(bf16[320,2048]{1,0:T(8,128)(2,1)S(1)} %bitcast.43, bf16[1,1,1,320,1408]{4,3,2,1,0:T(8,128)(2,1)S(1)} %copy-done), kind=kOutput, calls=%fused_computation.2 | convolution fusion | flops 1848377344 | bytes 7979008 | tf_op jit(solution)/shard_map/dot_general | solution.py:38
  57.0 8.2 %copy.24 = bf16[1408,2048]{1,0:T(8,128)(2,1)} copy(bf16[1408,2048]{0,1:T(8,128)(2,1)} %fusion) | data formatting | bytes 11534336
  65.3 5.8 %fusion.3 = bf16[4,80,1408]{2,1,0:T(8,128)(2,1)} fusion(bf16[4,80,2048]{2,1,0:T(8,128)(2,1)S(1)} %all_to_all.5, bf16[1,1,1408,2048]{3,2,1,0:T(8,128)(2,1)} %param.9), kind=kOutput, calls=%fused_computation.5 | convolution fusion | flops 1845944320 | bytes 7979008 | tf_op jit(solution)/shard_map/skd,hd->skh/dot_general | solution.py:34
  71.1 97.2 %reduce-scatter.4.cloned.1.call-done = bf16[352,2048]{1,0:T(8,128)(2,1)} async-done(((bf16[1408,2048]{1,0:T(8,128)(2,1)}), bf16[352,2048]{1,0:T(8,128)(2,1)}) %reduce-scatter.4.cloned.1.call-update) | async-done | bytes 1441808
  168.3 1.8 %copy.25 = bf16[352,2048]{0,1:T(8,128)(2,1)S(1)} copy(bf16[352,2048]{1,0:T(8,128)(2,1)} %reduce-scatter.4.cloned.1.call-done) | data formatting | bytes 2883584
  170.1 1.9 %bitcast_convert_fusion = f32[1,1,352,2048]{2,3,1,0:T(8,128)} fusion(bf16[352,2048]{0,1:T(8,128)(2,1)S(1)} %copy.25), kind=kLoop, calls=%fused_computation.7 | loop fusion | flops 720896 | bytes 4325376 | tf_op jit(solution)/shard_map/reshape | solution.py:45
  172.0 3.4 %copy.23 = f32[1,1,352,2048]{3,2,1,0:T(8,128)} copy(f32[1,1,352,2048]{2,3,1,0:T(8,128)} %bitcast_convert_fusion) | data formatting | bytes 5767168
  (12 shorter events, 0.4 us)
Async XLA Ops:
  7.2 44.6 %copy-start = (bf16[1,1,1,320,1408]{4,3,2,1,0:T(8,128)(2,1)S(1)}, bf16[1,1,1,320,1408]{4,3,2,1,0:T(8,128)(2,1)}, u32[]{:S(2)}) copy-start(bf16[1,1,1,320,1408]{4,3,2,1,0:T(8,128)(2,1)} %param.8) | copy-start | bytes 2703364
  7.2 161.1 %reduce-scatter.4.cloned.1.call-start = ((), (), s32[]{:S(2)}) async-start(), calls=%async_computation.2 | async-start | bytes 7208960
  7.2 15.2 %collective-permute-start = (bf16[1,128,2048]{2,1,0:T(8,128)(2,1)}, bf16[1,128,2048]{2,1,0:T(8,128)(2,1)S(1)}, u32[]{:S(2)}, u32[]{:S(2)}) collective-permute-start(bf16[1,128,2048]{2,1,0:T(8,128)(2,1)} %param.5), channel_id=1, source_target_pairs={{0,16},{16,0},{1,17},{17,1},{2,18},{18,2},{3,19},{19,3},{4,20},{20... | collective-permute-start | bytes 1572872 | tf_op jit(solution)/shard_map/ppermute | solution.py:10
Sparse Core Ops, SparseCore 0:
  65.4 102.8 reduce-scatter.3
where the time goes:
time: 183 us; the launch traced here: 182 us
  waiting for transfers between devices  105 us (57%)
  local copies, waits for them, and re-layouts  21.3 us (12%)
  blocking collectives  20.7 us (11%)
  between operations  14.1 us (8%)
  matrix products  11 us (6%)
  other arithmetic  7.36 us (4%)
  starting transfers between devices  3.07 us (2%)
    unnamed x2, waiting for transfers between devices  97.2 us
    all_to_all x1, blocking collectives, shards(): lax.all_to_all(outgoing, 'expert', split_axis=0, concat_axis=0, tiled=True)  20.7 us
    unnamed x7, local copies, waits for them, and re-layouts  15.1 us
    ppermute x1, waiting for transfers between devices, shifted(): return lax.ppermute(value, axis, pairs)  7.54 us
    dot_general x1, matrix products, shards(): jnp.einsum('skd,hd->skh', piece, weight, preferred_element_type=jnp.float32)  5.79 us
    mul x3, local copies, waits for them, and re-layouts, dispatch_block(): weights[:, :, None] * rows[:, None, :].astype(jnp.float32)  5.35 us
    dot_general x1, matrix products, shards(): lax.dot_general(saved, scaled, (((0,), (0,)), ((), ())), preferred_elemen...  5.24 us
  transfers between devices with their start and end apart: 2, of which 2 were waited for; matrix products, arithmetic and copies ran while one was open for 6% of the time, Pallas kernels for 0%

commit v1 on v0

--- a/solution.py
+++ b/solution.py
@@ -21,6 +21,46 @@
     return buffer.reshape(count, width, rows.shape[1])
 
 
+def line_weight_grad(saved, scaled, chunks):
+    d = lax.axis_index("dp")
+    hid = saved.shape[1]
+    blk = hid // 4
+    width = scaled.shape[1] // chunks
+    ends = [(0, 1), (3, 2)]
+    hsend = lax.dynamic_slice_in_dim(saved, jnp.where(d == 0, blk, 0), hid - blk, axis=1)
+    hrecv = lax.ppermute(hsend, "dp", ends)
+    hfull = lax.dynamic_update_slice_in_dim(
+        jnp.zeros_like(saved), hrecv, jnp.where(d == 1, blk, 0), axis=1
+    )
+    lhs = jnp.concatenate([saved, hfull], axis=0)
+    row2 = jnp.where(d == 1, 2 * blk, 0)
+    row3a = jnp.where(d == 1, 0, 3 * blk)
+    row3b = jnp.where(d == 1, 0, blk)
+    own = d * blk
+    half = jnp.where(d == 1, blk, 0)
+    edge = (d == 0) | (d == 3)
+    pieces = []
+    for c in range(chunks):
+        sc = scaled[:, c * width:(c + 1) * width]
+        srecv = lax.ppermute(sc, "dp", ends)
+        rhs = jnp.concatenate([sc, srecv], axis=0)
+        acc = lax.dot_general(
+            lhs, rhs, (((0,), (0,)), ((), ())), preferred_element_type=jnp.float32
+        )
+        s2 = lax.dynamic_slice_in_dim(acc, row2, 2 * blk, axis=0).astype(jnp.bfloat16)
+        r2 = lax.ppermute(s2, "dp", [(1, 2), (2, 1)])
+        s3 = (
+            lax.dynamic_slice_in_dim(acc, row3a, blk, axis=0)
+            + lax.dynamic_slice_in_dim(r2, row3b, blk, axis=0).astype(jnp.float32)
+        ).astype(jnp.bfloat16)
+        r3 = lax.ppermute(s3, "dp", [(1, 0), (2, 3)])
+        extra = jnp.where(edge, r3, lax.dynamic_slice_in_dim(r2, half, blk, axis=0))
+        pieces.append(
+            lax.dynamic_slice_in_dim(acc, own, blk, axis=0) + extra.astype(jnp.float32)
+        )
+    return jnp.concatenate(pieces, axis=1)
+
+
 def shards(grad_out, routes, gates, hidden, w_down):
     incoming = shifted(grad_out, "section", -1)[0]
     groups = lax.axis_size("expert")
@@ -35,12 +75,15 @@
         "skd,hd->skh", piece, weight, preferred_element_type=jnp.float32
     ).astype(jnp.bfloat16)
     scaled = piece.reshape(slot_count, model_width)
-    full = lax.dot_general(
-        saved, scaled, (((0,), (0,)), ((), ())), preferred_element_type=jnp.float32
-    )
-    weight_grad = lax.psum_scatter(
-        full.astype(jnp.bfloat16), "dp", scatter_dimension=0, tiled=True
-    ).astype(jnp.float32)
+    if lax.axis_size("dp") == 4 and saved.shape[1] % 4 == 0:
+        weight_grad = line_weight_grad(saved, scaled, 4)
+    else:
+        full = lax.dot_general(
+            saved, scaled, (((0,), (0,)), ((), ())), preferred_element_type=jnp.float32
+        )
+        weight_grad = lax.psum_scatter(
+            full.astype(jnp.bfloat16), "dp", scatter_dimension=0, tiled=True
+        ).astype(jnp.float32)
     grad_hidden = grad_rows_out.reshape(1, 1, 1, slot_count, saved.shape[1])
     return (grad_hidden, weight_grad.reshape(1, 1, weight_grad.shape[0], model_width))
 

time: 183 us -> 141 us (0.77)
  waiting for transfers between devices: 105 us -> 75.3 us
  starting transfers between devices: 3.07 us -> 28.7 us
  blocking collectives: 20.7 us -> 0 us
  between operations: 14.1 us -> 1 us
  local copies, waits for them, and re-layouts: 21.3 us -> 15.7 us
    unnamed x2 -> x0, waiting for transfers between devices: 97.2 us -> none
    ppermute x0 -> x13, waiting for transfers between devices: none -> 55.8 us  [the longest x4 48.5 us: line_weight_grad(): r3 = lax.ppermute(s3, 'dp', [(1, 0), (2, 3)])]
    ppermute x0 -> x13, starting transfers between devices: none -> 22.1 us  [the longest x4 9.89 us: line_weight_grad(): srecv = lax.ppermute(sc, 'dp', ends)]
    all_to_all x1 -> x0, blocking collectives: 20.7 us -> none  [shards(): lax.all_to_all(outgoing, 'expert', split_axis=0, concat_axis=0, tiled=True)]
    unnamed x7 -> x10, local copies, waits for them, and re-layouts: 15.1 us -> 1.6 us
    all_to_all x0 -> x1, waiting for transfers between devices: none -> 11.9 us  [shards(): lax.all_to_all(outgoing, 'expert', split_axis=0, concat_axis=0, tiled=True)]
    dynamic_update_slice x0 -> x1, local copies, waits for them, and re-layouts: none -> 5.12 us  [line_weight_grad(): lax.dynamic_update_slice_in_dim(jnp.zeros_like(saved), hrecv, jnp.where(d...]
    all_to_all x0 -> x1, starting transfers between devices: none -> 3.54 us  [shards(): lax.all_to_all(outgoing, 'expert', split_axis=0, concat_axis=0, tiled=True)]
  transfers between devices with their start and end apart: 2 -> 15, of which waited for: 2 -> 9; matrix products, arithmetic and copies ran while one was open for 6% -> 17% of each run, Pallas kernels for 0% -> 0%
where the time goes in v1:
time: 141 us; the launch traced here: 140 us
  waiting for transfers between devices  75.3 us (53%)
  starting transfers between devices  28.7 us (20%)
  local copies, waits for them, and re-layouts  15.7 us (11%)
  matrix products  11 us (8%)
  other arithmetic  8.38 us (6%)
    ppermute x4, waiting for transfers between devices, line_weight_grad(): r3 = lax.ppermute(s3, 'dp', [(1, 0), (2, 3)])  48.5 us
    all_to_all x1, waiting for transfers between devices, shards(): lax.all_to_all(outgoing, 'expert', split_axis=0, concat_axis=0, tiled=True)  11.9 us
    ppermute x4, starting transfers between devices, line_weight_grad(): srecv = lax.ppermute(sc, 'dp', ends)  9.89 us
    dot_general x4, matrix products, line_weight_grad(): lax.dot_general(lhs, rhs, (((0,), (0,)), ((), ())), preferred_element_typ...  7.78 us
    ppermute x1, waiting for transfers between devices, shifted(): return lax.ppermute(value, axis, pairs)  7.54 us
    ppermute x4, waiting for transfers between devices, line_weight_grad(): srecv = lax.ppermute(sc, 'dp', ends)  7.27 us
    mul x3, local copies, waits for them, and re-layouts, dispatch_block(): weights[:, :, None] * rows[:, None, :].astype(jnp.float32)  5.35 us
    ppermute x4, starting transfers between devices, line_weight_grad(): r3 = lax.ppermute(s3, 'dp', [(1, 0), (2, 3)])  5.17 us
  transfers between devices with their start and end apart: 15, of which 9 were waited for; matrix products, arithmetic and copies ran while one was open for 17% of the time, Pallas kernels for 0%

profile of v1, /device:TPU:0, one launch (start us, length us, event | category | flops | bytes accessed | tf_op | source)
XLA Modules:
  0.0 140.1 jit_solution(16321901420284906575)
XLA Ops:
  0.6 3.0 %collective-permute-start = (bf16[1,128,2048]{2,1,0:T(8,128)(2,1)}, bf16[1,128,2048]{2,1,0:T(8,128)(2,1)S(1)}, u32[]{:S(2)}, u32[]{:S(2)}) collective-permute-start(bf16[1,128,2048]{2,1,0:T(8,128)(2,1)} %param.5), channel_id=1, source_target_pairs={{0,16},{16,0},{1,17},{17,1},{2,18},{18,2},{3,19},{19,3},{4,20},{20... | collective-permute-start | bytes 1572872 | tf_op jit(solution)/shard_map/ppermute | solution.py:10
  8.3 7.5 %collective-permute-done = bf16[1,128,2048]{2,1,0:T(8,128)(2,1)S(1)} collective-permute-done((bf16[1,128,2048]{2,1,0:T(8,128)(2,1)}, bf16[1,128,2048]{2,1,0:T(8,128)(2,1)S(1)}, u32[]{:S(2)}, u32[]{:S(2)}) %collective-permute-start) | collective-permute-done | bytes 524320 | tf_op jit(solution)/shard_map/ppermute | solution.py:10
  15.9 2.5 %mul.46 = f32[128,2,2048]{2,1,0:T(2,128)} broadcast(f32[128,2048]{1,0:T(8,128)S(1)} %bitcast_convert_fusion), dimensions={0,2} | broadcast | bytes 3145728 | tf_op jit(solution)/shard_map/mul | solution.py:18
  18.4 2.7 %mul.47 = f32[256,2048]{1,0:T(8,128)S(1)} reshape(f32[128,2,2048]{2,1,0:T(2,128)} %mul.46) | data formatting | bytes 4194304 | tf_op jit(solution)/shard_map/mul | solution.py:18
  21.1 3.3 %scatter_custom_fusion = bf16[320,2048]{1,0:T(8,128)(2,1)} fusion(s32[256]{0:T(256)S(1)} %bitcast.43, f32[256,2048]{1,0:T(8,128)S(1)} %mul.47, f32[256]{0:T(256)S(1)} %mul.44, bf16[]{:T(256)} %constant.13.clone.1), kind=kCustom, calls=%fused_computation.11 | custom fusion | flops 1048576 | bytes 3408898 | tf_op jit(solution)/shard_map/scatter | solution.py:20
  24.5 3.5 %all-to-all-start = ((bf16[4,80,2048]{2,1,0:T(8,128)(2,1)}), bf16[4,80,2048]{2,1,0:T(8,128)(2,1)S(1)}, u32[]{:S(2)}, u32[]{:S(2)}) async-start(bf16[4,80,2048]{2,1,0:T(8,128)(2,1)} %bitcast.5), calls=%async_computation | async-start | bytes 2621440 | tf_op jit(solution)/shard_map/all_to_all | solution.py:73
  28.0 1.4 %dynamic-slice_bitcast_fusion = bf16[320,1056]{1,0:T(8,128)(2,1)S(1)} fusion(bf16[1,1,1,320,1408]{4,3,2,1,0:T(8,128)(2,1)} %param.8, s32[]{:T(128)S(6)} %select_n.72), kind=kLoop, calls=%fused_computation.13 | loop fusion | bytes 1351684 | tf_op jit(solution)/shard_map/dynamic_slice | solution.py:30
  29.5 3.8 %collective-permute-start.1 = (bf16[320,1056]{1,0:T(8,128)(2,1)S(1)}, bf16[320,1056]{1,0:T(8,128)(2,1)S(1)}, u32[]{:S(2)}, u32[]{:S(2)}) collective-permute-start(bf16[320,1056]{1,0:T(8,128)(2,1)S(1)} %dynamic-slice_bitcast_fusion), channel_id=1, source_target_pairs={{0,4},{12,8},{1,5},{13,9},{2,6},{14,10},{3,7},{15,11},{16,20},{28,... | collective-permute-start | bytes 2027528 | tf_op jit(solution)/shard_map/ppermute | solution.py:31
  33.3 11.9 %all-to-all-done = bf16[4,80,2048]{2,1,0:T(8,128)(2,1)S(1)} async-done(((bf16[4,80,2048]{2,1,0:T(8,128)(2,1)}), bf16[4,80,2048]{2,1,0:T(8,128)(2,1)S(1)}, u32[]{:S(2)}, u32[]{:S(2)}) %all-to-all-start) | async-done | bytes 1310752 | tf_op jit(solution)/shard_map/all_to_all | solution.py:73
  46.2 4.4 %collective-permute-start.11 = (bf16[320,512]{1,0:T(8,128)(2,1)}, bf16[320,512]{1,0:T(8,128)(2,1)}, u32[]{:S(2)}, u32[]{:S(2)}) collective-permute-start(bf16[320,512]{1,0:T(8,128)(2,1)} %get-tuple-element.3), channel_id=1, source_target_pairs={{0,4},{12,8},{1,5},{13,9},{2,6},{14,10},{3,7},{15,11},{16,20},{28,... | collective-permute-start | bytes 983048 | tf_op jit(solution)/shard_map/ppermute | solution.py:45
  50.6 2.0 %collective-permute-start.8 = (bf16[320,512]{1,0:T(8,128)(2,1)}, bf16[320,512]{1,0:T(8,128)(2,1)}, u32[]{:S(2)}, u32[]{:S(2)}) collective-permute-start(bf16[320,512]{1,0:T(8,128)(2,1)} %get-tuple-element.4), channel_id=1, source_target_pairs={{0,4},{12,8},{1,5},{13,9},{2,6},{14,10},{3,7},{15,11},{16,20},{28,... | collective-permute-start | bytes 983048 | tf_op jit(solution)/shard_map/ppermute | solution.py:45
  52.7 5.1 %dynamic_update_slice.3 = bf16[320,1408]{1,0:T(8,128)(2,1)S(1)} dynamic-update-slice(bf16[320,1408]{1,0:T(8,128)(2,1)S(1)} %broadcast_in_dim.9, bf16[320,1056]{1,0:T(8,128)(2,1)S(1)} %collective-permute-done.1, s32[]{:T(128)} %constant.12.clone.1, s32[]{:T(128)S(6)} %select_n.73) | dynamic-update-slice | bytes 1351684 | tf_op jit(solution)/shard_map/dynamic_update_slice | solution.py:32
  57.8 2.1 %collective-permute-start.5 = (bf16[320,512]{1,0:T(8,128)(2,1)}, bf16[320,512]{1,0:T(8,128)(2,1)S(1)}, u32[]{:S(2)}, u32[]{:S(2)}) collective-permute-start(bf16[320,512]{1,0:T(8,128)(2,1)} %get-tuple-element.5), channel_id=1, source_target_pairs={{0,4},{12,8},{1,5},{13,9},{2,6},{14,10},{3,7},{15,11},{16,20},{28,... | collective-permute-start | bytes 983048 | tf_op jit(solution)/shard_map/ppermute | solution.py:45
  61.3 2.7 %fusion.19 = f32[1408,512]{1,0:T(8,128)S(1)} fusion(bf16[320,512]{1,0:T(8,128)(2,1)} %collective-permute-done.11, bf16[320,512]{1,0:T(8,128)(2,1)} %get-tuple-element.3, bf16[320,1408]{1,0:T(8,128)(2,1)S(1)} %dynamic_update_slice.3, bf16[320,1408]{1,0:T(8,128)(2,1)} %bitcast.37), kind=kOutput, calls=%fused_computation.34 | convolution fusion | flops 927662080 | bytes 5341184 | tf_op jit(solution)/shard_map/dot_general | solution.py:47
  65.3 2.4 %fusion.15 = f32[1408,512]{1,0:T(8,128)S(1)} fusion(bf16[320,512]{1,0:T(8,128)(2,1)} %collective-permute-done.8, bf16[320,512]{1,0:T(8,128)(2,1)} %get-tuple-element.4, bf16[320,1408]{1,0:T(8,128)(2,1)S(1)} %dynamic_update_slice.3, bf16[320,1408]{1,0:T(8,128)(2,1)S(1)} %bitcast.38), kind=kOutput, calls=%fused_computation.30 | convolution fusion | flops 927662080 | bytes 5341184 | tf_op jit(solution)/shard_map/dot_general | solution.py:47
  68.6 3.8 %collective-permute-done.5 = bf16[320,512]{1,0:T(8,128)(2,1)S(1)} collective-permute-done((bf16[320,512]{1,0:T(8,128)(2,1)}, bf16[320,512]{1,0:T(8,128)(2,1)S(1)}, u32[]{:S(2)}, u32[]{:S(2)}) %collective-permute-start.5) | collective-permute-done | bytes 327712 | tf_op jit(solution)/shard_map/ppermute | solution.py:45
  74.7 3.2 %collective-permute-done.2 = bf16[320,512]{1,0:T(8,128)(2,1)S(1)} collective-permute-done((bf16[320,512]{1,0:T(8,128)(2,1)S(1)}, bf16[320,512]{1,0:T(8,128)(2,1)S(1)}, u32[]{:S(2)}, u32[]{:S(2)}) %collective-permute-start.2) | collective-permute-done | bytes 327712 | tf_op jit(solution)/shard_map/ppermute | solution.py:45
  77.8 1.3 fusion.7
  80.2 3.2 %fusion.2 = bf16[4,80,1408]{2,1,0:T(8,128)(2,1)} fusion(bf16[4,80,2048]{2,1,0:T(8,128)(2,1)S(1)} %all-to-all-done, bf16[1,1,1408,2048]{3,2,1,0:T(8,128)(2,1)S(1)} %bitcast.45), kind=kOutput, calls=%fused_computation.4 | convolution fusion | flops 1845944320 | bytes 7979008 | tf_op jit(solution)/shard_map/skd,hd->skh/dot_general | solution.py:74
  89.2 7.9 %collective-permute-done.13 = bf16[352,512]{1,0:T(8,128)(2,1)S(1)} collective-permute-done((bf16[352,512]{1,0:T(8,128)(2,1)S(1)}, bf16[352,512]{1,0:T(8,128)(2,1)S(1)}, u32[]{:S(2)}, u32[]{:S(2)}) %collective-permute-start.13) | collective-permute-done | bytes 360480 | tf_op jit(solution)/shard_map/ppermute | solution.py:56
  97.2 10.0 %collective-permute-done.10 = bf16[352,512]{1,0:T(8,128)(2,1)S(1)} collective-permute-done((bf16[352,512]{1,0:T(8,128)(2,1)S(1)}, bf16[352,512]{1,0:T(8,128)(2,1)S(1)}, u32[]{:S(2)}, u32[]{:S(2)}) %collective-permute-start.10) | collective-permute-done | bytes 360480 | tf_op jit(solution)/shard_map/ppermute | solution.py:56
  107.4 15.3 %collective-permute-done.7 = bf16[352,512]{1,0:T(8,128)(2,1)S(1)} collective-permute-done((bf16[352,512]{1,0:T(8,128)(2,1)S(1)}, bf16[352,512]{1,0:T(8,128)(2,1)S(1)}, u32[]{:S(2)}, u32[]{:S(2)}) %collective-permute-start.7) | collective-permute-done | bytes 360480 | tf_op jit(solution)/shard_map/ppermute | solution.py:56
  122.8 15.3 %collective-permute-done.4 = bf16[352,512]{1,0:T(8,128)(2,1)S(1)} collective-permute-done((bf16[352,512]{1,0:T(8,128)(2,1)S(1)}, bf16[352,512]{1,0:T(8,128)(2,1)S(1)}, u32[]{:S(2)}, u32[]{:S(2)}) %collective-permute-start.4) | collective-permute-done | bytes 360480 | tf_op jit(solution)/shard_map/ppermute | solution.py:56
  138.3 1.8 %maximum_bitcast_fusion = f32[1,1,352,2048]{3,2,1,0:T(8,128)} fusion(f32[352,512]{1,0:T(8,128)S(1)} %convert_add_fusion, f32[352,512]{1,0:T(8,128)S(1)} %convert_add_fusion.1, f32[352,512]{1,0:T(8,128)S(1)} %convert_add_fusion.2, f32[352,512]{1,0:T(8,128)S(1)} %convert_add_fusion.3), kind=kLoop, calls=%fused_computation.3 | loop fusion | flops 2162688 | bytes 5767168 | tf_op jit(solution)/shard_map/reshape | solution.py:88
  (59 shorter events, 18.6 us)
Async XLA Ops:
  0.6 15.2 %collective-permute-start = (bf16[1,128,2048]{2,1,0:T(8,128)(2,1)}, bf16[1,128,2048]{2,1,0:T(8,128)(2,1)S(1)}, u32[]{:S(2)}, u32[]{:S(2)}) collective-permute-start(bf16[1,128,2048]{2,1,0:T(8,128)(2,1)} %param.5), channel_id=1, source_target_pairs={{0,16},{16,0},{1,17},{17,1},{2,18},{18,2},{3,19},{19,3},{4,20},{20... | collective-permute-start | bytes 1572872 | tf_op jit(solution)/shard_map/ppermute | solution.py:10
  24.5 20.8 %all-to-all-start = ((bf16[4,80,2048]{2,1,0:T(8,128)(2,1)}), bf16[4,80,2048]{2,1,0:T(8,128)(2,1)S(1)}, u32[]{:S(2)}, u32[]{:S(2)}) async-start(bf16[4,80,2048]{2,1,0:T(8,128)(2,1)} %bitcast.5), calls=%async_computation | async-start | bytes 2621440 | tf_op jit(solution)/shard_map/all_to_all | solution.py:73
  29.5 23.2 %collective-permute-start.1 = (bf16[320,1056]{1,0:T(8,128)(2,1)S(1)}, bf16[320,1056]{1,0:T(8,128)(2,1)S(1)}, u32[]{:S(2)}, u32[]{:S(2)}) collective-permute-start(bf16[320,1056]{1,0:T(8,128)(2,1)S(1)} %dynamic-slice_bitcast_fusion), channel_id=1, source_target_pairs={{0,4},{12,8},{1,5},{13,9},{2,6},{14,10},{3,7},{15,11},{16,20},{28,... | collective-permute-start | bytes 2027528 | tf_op jit(solution)/shard_map/ppermute | solution.py:31
  46.2 15.1 %collective-permute-start.11 = (bf16[320,512]{1,0:T(8,128)(2,1)}, bf16[320,512]{1,0:T(8,128)(2,1)}, u32[]{:S(2)}, u32[]{:S(2)}) collective-permute-start(bf16[320,512]{1,0:T(8,128)(2,1)} %get-tuple-element.3), channel_id=1, source_target_pairs={{0,4},{12,8},{1,5},{13,9},{2,6},{14,10},{3,7},{15,11},{16,20},{28,... | collective-permute-start | bytes 983048 | tf_op jit(solution)/shard_map/ppermute | solution.py:45
  50.6 14.7 %collective-permute-start.8 = (bf16[320,512]{1,0:T(8,128)(2,1)}, bf16[320,512]{1,0:T(8,128)(2,1)}, u32[]{:S(2)}, u32[]{:S(2)}) collective-permute-start(bf16[320,512]{1,0:T(8,128)(2,1)} %get-tuple-element.4), channel_id=1, source_target_pairs={{0,4},{12,8},{1,5},{13,9},{2,6},{14,10},{3,7},{15,11},{16,20},{28,... | collective-permute-start | bytes 983048 | tf_op jit(solution)/shard_map/ppermute | solution.py:45
  57.8 14.5 %collective-permute-start.5 = (bf16[320,512]{1,0:T(8,128)(2,1)}, bf16[320,512]{1,0:T(8,128)(2,1)S(1)}, u32[]{:S(2)}, u32[]{:S(2)}) collective-permute-start(bf16[320,512]{1,0:T(8,128)(2,1)} %get-tuple-element.5), channel_id=1, source_target_pairs={{0,4},{12,8},{1,5},{13,9},{2,6},{14,10},{3,7},{15,11},{16,20},{28,... | collective-permute-start | bytes 983048 | tf_op jit(solution)/shard_map/ppermute | solution.py:45
  60.0 17.9 %collective-permute-start.2 = (bf16[320,512]{1,0:T(8,128)(2,1)S(1)}, bf16[320,512]{1,0:T(8,128)(2,1)S(1)}, u32[]{:S(2)}, u32[]{:S(2)}) collective-permute-start(bf16[320,512]{1,0:T(8,128)(2,1)S(1)} %get-tuple-element.2), channel_id=1, source_target_pairs={{0,4},{12,8},{1,5},{13,9},{2,6},{14,10},{3,7},{15,11},{16,20},{28,... | collective-permute-start | bytes 983048 | tf_op jit(solution)/shard_map/ppermute | solution.py:45
  61.3 4.0 %copy-start = (bf16[1,1,1,320,1408]{4,3,2,1,0:T(8,128)(2,1)S(1)}, bf16[1,1,1,320,1408]{4,3,2,1,0:T(8,128)(2,1)}, u32[]{:S(2)}) copy-start(bf16[1,1,1,320,1408]{4,3,2,1,0:T(8,128)(2,1)} %param.8) | copy-start | bytes 2703364
  64.2 8.2 %copy-start.1 = (bf16[320,512]{1,0:T(8,128)(2,1)S(1)}, bf16[320,512]{1,0:T(8,128)(2,1)}, u32[]{:S(2)}) copy-start(bf16[320,512]{1,0:T(8,128)(2,1)} %get-tuple-element.5) | copy-start | bytes 983044
  64.2 19.3 %collective-permute-start.12 = (bf16[704,512]{1,0:T(8,128)(2,1)S(1)}, bf16[704,512]{1,0:T(8,128)(2,1)S(1)}, u32[]{:S(2)}, u32[]{:S(2)}) collective-permute-start(bf16[704,512]{1,0:T(8,128)(2,1)S(1)} %dynamic-slice_convert_fusion), channel_id=1, source_target_pairs={{4,8},{8,4},{5,9},{9,5},{6,10},{10,6},{7,11},{11,7},{20,24},{24,20... | collective-permute-start | bytes 2162696 | tf_op jit(solution)/shard_map/ppermute | solution.py:51
  67.8 17.0 %collective-permute-start.9 = (bf16[704,512]{1,0:T(8,128)(2,1)S(1)}, bf16[704,512]{1,0:T(8,128)(2,1)S(1)}, u32[]{:S(2)}, u32[]{:S(2)}) collective-permute-start(bf16[704,512]{1,0:T(8,128)(2,1)S(1)} %dynamic-slice_convert_fusion.1), channel_id=1, source_target_pairs={{4,8},{8,4},{5,9},{9,5},{6,10},{10,6},{7,11},{11,7},{20,24},{24,20... | collective-permute-start | bytes 2162696 | tf_op jit(solution)/shard_map/ppermute | solution.py:51
  73.7 6.5 %slice-start = ((s8[5767168]{0:T(1024)(128)(4,1)}), s8[4194304]{0:T(1024)(128)(4,1)S(1)}, s32[]{:S(2)}) async-start(s8[5767168]{0:T(1024)(128)(4,1)} %bitcast.44), calls=%async_computation.1 | async-start | bytes 8388608
  73.8 6.4 %slice-start.1 = ((s8[5767168]{0:T(1024)(128)(4,1)}), s8[1572864]{0:T(1024)(128)(4,1)S(1)}, s32[]{:S(2)}) async-start(s8[5767168]{0:T(1024)(128)(4,1)} %bitcast.44), calls=%async_computation.2 | async-start | bytes 3145728
  73.8 12.5 %collective-permute-start.6 = (bf16[704,512]{1,0:T(8,128)(2,1)S(1)}, bf16[704,512]{1,0:T(8,128)(2,1)S(1)}, u32[]{:S(2)}, u32[]{:S(2)}) collective-permute-start(bf16[704,512]{1,0:T(8,128)(2,1)S(1)} %dynamic-slice_convert_fusion.2), channel_id=1, source_target_pairs={{4,8},{8,4},{5,9},{9,5},{6,10},{10,6},{7,11},{11,7},{20,24},{24,20... | collective-permute-start | bytes 2162696 | tf_op jit(solution)/shard_map/ppermute | solution.py:51
  79.3 8.5 %collective-permute-start.3 = (bf16[704,512]{1,0:T(8,128)(2,1)S(1)}, bf16[704,512]{1,0:T(8,128)(2,1)S(1)}, u32[]{:S(2)}, u32[]{:S(2)}) collective-permute-start(bf16[704,512]{1,0:T(8,128)(2,1)S(1)} %dynamic-slice_convert_fusion.3), channel_id=1, source_target_pairs={{4,8},{8,4},{5,9},{9,5},{6,10},{10,6},{7,11},{11,7},{20,24},{24,20... | collective-permute-start | bytes 2162696 | tf_op jit(solution)/shard_map/ppermute | solution.py:51
  83.6 13.5 %collective-permute-start.13 = (bf16[352,512]{1,0:T(8,128)(2,1)S(1)}, bf16[352,512]{1,0:T(8,128)(2,1)S(1)}, u32[]{:S(2)}, u32[]{:S(2)}) collective-permute-start(bf16[352,512]{1,0:T(8,128)(2,1)S(1)} %add_convert_fusion), channel_id=1, source_target_pairs={{4,0},{8,12},{5,1},{9,13},{6,2},{10,14},{7,3},{11,15},{20,16},{24,... | collective-permute-start | bytes 1081352 | tf_op jit(solution)/shard_map/ppermute | solution.py:56
  85.0 22.2 %collective-permute-start.10 = (bf16[352,512]{1,0:T(8,128)(2,1)S(1)}, bf16[352,512]{1,0:T(8,128)(2,1)S(1)}, u32[]{:S(2)}, u32[]{:S(2)}) collective-permute-start(bf16[352,512]{1,0:T(8,128)(2,1)S(1)} %add_convert_fusion.1), channel_id=1, source_target_pairs={{4,0},{8,12},{5,1},{9,13},{6,2},{10,14},{7,3},{11,15},{20,16},{24,... | collective-permute-start | bytes 1081352 | tf_op jit(solution)/shard_map/ppermute | solution.py:56
  86.4 36.2 %collective-permute-start.7 = (bf16[352,512]{1,0:T(8,128)(2,1)S(1)}, bf16[352,512]{1,0:T(8,128)(2,1)S(1)}, u32[]{:S(2)}, u32[]{:S(2)}) collective-permute-start(bf16[352,512]{1,0:T(8,128)(2,1)S(1)} %add_convert_fusion.2), channel_id=1, source_target_pairs={{4,0},{8,12},{5,1},{9,13},{6,2},{10,14},{7,3},{11,15},{20,16},{24,... | collective-permute-start | bytes 1081352 | tf_op jit(solution)/shard_map/ppermute | solution.py:56
  87.9 50.2 %collective-permute-start.4 = (bf16[352,512]{1,0:T(8,128)(2,1)S(1)}, bf16[352,512]{1,0:T(8,128)(2,1)S(1)}, u32[]{:S(2)}, u32[]{:S(2)}) collective-permute-start(bf16[352,512]{1,0:T(8,128)(2,1)S(1)} %add_convert_fusion.3), channel_id=1, source_target_pairs={{4,0},{8,12},{5,1},{9,13},{6,2},{10,14},{7,3},{11,15},{20,16},{24,... | collective-permute-start | bytes 1081352 | tf_op jit(solution)/shard_map/ppermute | solution.py:56

commit v2 on v1

--- a/solution.py
+++ b/solution.py
@@ -10,28 +10,28 @@
     return lax.ppermute(value, axis, pairs)
 
 
-def dispatch_block(rows, ids, weights, count, width):
+def dispatch_targets(ids, count, width):
     flat_ids = ids.reshape(-1)
     onehot = (flat_ids[:, None] == jnp.arange(count, dtype=jnp.int32)[None, :]).astype(jnp.int32)
     position = jnp.sum((jnp.cumsum(onehot, axis=0) - 1) * onehot, axis=1)
-    target = flat_ids * width + position
+    return flat_ids * width + position
+
+
+def dispatch_rows(rows, weights, target, count, width):
     scaled = (weights[:, :, None] * rows[:, None, :].astype(jnp.float32)).astype(jnp.bfloat16)
     scaled = scaled.reshape(-1, rows.shape[1])
     buffer = jnp.zeros((count * width, rows.shape[1]), jnp.bfloat16).at[target].set(scaled)
     return buffer.reshape(count, width, rows.shape[1])
 
 
-def line_weight_grad(saved, scaled, chunks):
+def line_weight_grad(saved, parts):
     d = lax.axis_index("dp")
     hid = saved.shape[1]
     blk = hid // 4
-    width = scaled.shape[1] // chunks
     ends = [(0, 1), (3, 2)]
-    hsend = lax.dynamic_slice_in_dim(saved, jnp.where(d == 0, blk, 0), hid - blk, axis=1)
-    hrecv = lax.ppermute(hsend, "dp", ends)
-    hfull = lax.dynamic_update_slice_in_dim(
-        jnp.zeros_like(saved), hrecv, jnp.where(d == 1, blk, 0), axis=1
-    )
+    column_block = lax.broadcasted_iota(jnp.int32, saved.shape, 1) // blk
+    hsend = jnp.where(column_block == d, jnp.zeros_like(saved), saved)
+    hfull = lax.ppermute(hsend, "dp", ends)
     lhs = jnp.concatenate([saved, hfull], axis=0)
     row2 = jnp.where(d == 1, 2 * blk, 0)
     row3a = jnp.where(d == 1, 0, 3 * blk)
@@ -40,8 +40,7 @@
     half = jnp.where(d == 1, blk, 0)
     edge = (d == 0) | (d == 3)
     pieces = []
-    for c in range(chunks):
-        sc = scaled[:, c * width:(c + 1) * width]
+    for sc in parts:
         srecv = lax.ppermute(sc, "dp", ends)
         rhs = jnp.concatenate([sc, srecv], axis=0)
         acc = lax.dot_general(
@@ -62,21 +61,27 @@
 
 
 def shards(grad_out, routes, gates, hidden, w_down):
-    incoming = shifted(grad_out, "section", -1)[0]
     groups = lax.axis_size("expert")
     saved = hidden[0, 0, 0]
     weight = w_down[0, 0]
     slot_count = saved.shape[0]
     width = slot_count // groups
-    model_width = incoming.shape[1]
-    outgoing = dispatch_block(incoming, routes[0], gates[0], groups, width)
-    piece = lax.all_to_all(outgoing, "expert", split_axis=0, concat_axis=0, tiled=True)
+    model_width = grad_out.shape[2]
+    chunks = 4 if model_width % 512 == 0 else 1
+    step = model_width // chunks
+    target = dispatch_targets(routes[0], groups, width)
+    parts = []
+    for c in range(chunks):
+        rows = shifted(grad_out[0, :, c * step:(c + 1) * step], "section", -1)
+        outgoing = dispatch_rows(rows, gates[0], target, groups, width)
+        piece = lax.all_to_all(outgoing, "expert", split_axis=0, concat_axis=0, tiled=True)
+        parts.append(piece.reshape(slot_count, step))
+    scaled = jnp.concatenate(parts, axis=1)
     grad_rows_out = jnp.einsum(
-        "skd,hd->skh", piece, weight, preferred_element_type=jnp.float32
+        "sd,hd->sh", scaled, weight, preferred_element_type=jnp.float32
     ).astype(jnp.bfloat16)
-    scaled = piece.reshape(slot_count, model_width)
     if lax.axis_size("dp") == 4 and saved.shape[1] % 4 == 0:
-        weight_grad = line_weight_grad(saved, scaled, 4)
+        weight_grad = line_weight_grad(saved, parts)
     else:
         full = lax.dot_general(
             saved, scaled, (((0,), (0,)), ((), ())), preferred_element_type=jnp.float32

time: 141 us -> 145 us (1.028)
  starting transfers between devices: 28.7 us -> 38.1 us
  local copies, waits for them, and re-layouts: 15.7 us -> 6.84 us
  other arithmetic: 8.38 us -> 14.1 us
  waiting for transfers between devices: 75.3 us -> 69.6 us
  matrix products: 11 us -> 14.2 us
    all_to_all x1 -> x4, starting transfers between devices: 3.54 us -> 14.5 us  [shards(): lax.all_to_all(outgoing, 'expert', split_axis=0, concat_axis=0, tiled=True)]
    all_to_all x1 -> x4, waiting for transfers between devices: 11.9 us -> 4.02 us  [shards(): lax.all_to_all(outgoing, 'expert', split_axis=0, concat_axis=0, tiled=True)]
    ppermute x1 -> x4, waiting for transfers between devices: 7.54 us -> 13.7 us  [shifted(): return lax.ppermute(value, axis, pairs)]
    scatter x1 -> x4, other arithmetic: 3.34 us -> 9.06 us  [dispatch_rows(): jnp.zeros((count * width, rows.shape[1]), jnp.bfloat16).at[target]]
    dynamic_update_slice x1 -> x0, local copies, waits for them, and re-layouts: 5.12 us -> none  [line_weight_grad(): lax.dynamic_update_slice_in_dim(jnp.zeros_like(saved), hrecv, jnp.where(d...]
    ppermute x4, starting transfers between devices: 9.89 us -> 5.95 us  [line_weight_grad(): srecv = lax.ppermute(sc, 'dp', ends)]
    mul x5 -> x11, local copies, waits for them, and re-layouts: 5.6 us -> 2.38 us  [the longest x9 2.13 us: dispatch_rows(): weights[:, :, None] * rows[:, None, :].astype(jnp.float32)]
    ppermute x4, waiting for transfers between devices: 7.27 us -> 4.76 us  [line_weight_grad(): srecv = lax.ppermute(sc, 'dp', ends)]
  transfers between devices with their start and end apart: 15 -> 21, of which waited for: 9 -> 10; matrix products, arithmetic and copies ran while one was open for 17% -> 20% of each run, Pallas kernels for 0% -> 0%
where the time goes in v2:
time: 145 us; the launch traced here: 144 us
  waiting for transfers between devices  69.6 us (48%)
  starting transfers between devices  38.1 us (26%)
  matrix products  14.2 us (10%)
  other arithmetic  14.1 us (10%)
  local copies, waits for them, and re-layouts  6.84 us (5%)
    ppermute x4, waiting for transfers between devices, line_weight_grad(): r3 = lax.ppermute(s3, 'dp', [(1, 0), (2, 3)])  47.1 us
    all_to_all x4, starting transfers between devices, shards(): lax.all_to_all(outgoing, 'expert', split_axis=0, concat_axis=0, tiled=True)  14.5 us
    ppermute x4, waiting for transfers between devices, shifted(): return lax.ppermute(value, axis, pairs)  13.7 us
    dot_general x4, matrix products, line_weight_grad(): lax.dot_general(lhs, rhs, (((0,), (0,)), ((), ())), preferred_element_typ...  10.1 us
    scatter x4, other arithmetic, dispatch_rows(): jnp.zeros((count * width, rows.shape[1]), jnp.bfloat16).at[target]  9.06 us
    ppermute x4, starting transfers between devices, line_weight_grad(): srecv = lax.ppermute(sc, 'dp', ends)  5.95 us
    ppermute x4, starting transfers between devices, line_weight_grad(): r3 = lax.ppermute(s3, 'dp', [(1, 0), (2, 3)])  5.17 us
    ppermute x4, starting transfers between devices, shifted(): return lax.ppermute(value, axis, pairs)  4.93 us
  transfers between devices with their start and end apart: 21, of which 10 were waited for; matrix products, arithmetic and copies ran while one was open for 20% of the time, Pallas kernels for 0%

profile of v2, /device:TPU:0, one launch (start us, length us, event | category | flops | bytes accessed | tf_op | source)
XLA Modules:
  0.0 144.0 jit_solution(16072048389574002765)
XLA Ops:
  2.6 3.0 %collective-permute-start = (bf16[128,512]{1,0:T(8,128)(2,1)S(1)}, bf16[128,512]{1,0:T(8,128)(2,1)S(1)}, u32[]{:S(2)}, u32[]{:S(2)}) collective-permute-start(bf16[128,512]{1,0:T(8,128)(2,1)S(1)} %get-tuple-element.2), channel_id=1, source_target_pairs={{0,16},{16,0},{1,17},{17,1},{2,18},{18,2},{3,19},{19,3},{4,20},{20... | collective-permute-start | bytes 393224 | tf_op jit(solution)/shard_map/ppermute | solution.py:10
  10.7 2.3 %scatter_custom_fusion = bf16[320,512]{1,0:T(8,128)(2,1)} fusion(s32[256]{0:T(256)S(1)} %bitcast.61, f32[256,512]{1,0:T(8,128)S(1)} %mul.89, f32[256]{0:T(256)S(1)} %mul.86, bf16[]{:T(256)} %constant.14.clone.1), kind=kCustom, calls=%fused_computation.51 | custom fusion | flops 262144 | bytes 852994 | tf_op jit(solution)/shard_map/scatter | solution.py:23
  12.9 3.5 %all-to-all-start = ((bf16[4,80,512]{2,1,0:T(8,128)(2,1)}), bf16[4,80,512]{2,1,0:T(8,128)(2,1)S(1)}, u32[]{:S(2)}, u32[]{:S(2)}) async-start(bf16[4,80,512]{2,1,0:T(8,128)(2,1)} %bitcast.5), calls=%async_computation | async-start | bytes 655360 | tf_op jit(solution)/shard_map/all_to_all | solution.py:77
  16.6 4.4 %collective-permute-start.4 = (bf16[320,1408]{1,0:T(8,128)(2,1)S(1)}, bf16[320,1408]{1,0:T(8,128)(2,1)}, u32[]{:S(2)}, u32[]{:S(2)}) collective-permute-start(bf16[320,1408]{1,0:T(8,128)(2,1)S(1)} %fusion.8), channel_id=1, source_target_pairs={{0,4},{12,8},{1,5},{13,9},{2,6},{14,10},{3,7},{15,11},{16,20},{28,... | collective-permute-start | bytes 2703368 | tf_op jit(solution)/shard_map/ppermute | solution.py:34
  21.6 5.0 %collective-permute-done.1 = bf16[128,512]{1,0:T(8,128)(2,1)S(1)} collective-permute-done((bf16[128,512]{1,0:T(8,128)(2,1)S(1)}, bf16[128,512]{1,0:T(8,128)(2,1)S(1)}, u32[]{:S(2)}, u32[]{:S(2)}) %collective-permute-start.1) | collective-permute-done | bytes 131104 | tf_op jit(solution)/shard_map/ppermute | solution.py:10
  27.1 2.3 %scatter_custom_fusion.1 = bf16[320,512]{1,0:T(8,128)(2,1)} fusion(s32[256]{0:T(256)S(1)} %bitcast.62, f32[256,512]{1,0:T(8,128)S(1)} %mul.92, f32[256]{0:T(256)S(1)} %mul.86, bf16[]{:T(256)} %constant.14.clone.1), kind=kCustom, calls=%fused_computation.52 | custom fusion | flops 262144 | bytes 852994 | tf_op jit(solution)/shard_map/scatter | solution.py:23
  29.3 3.5 %all-to-all-start.1 = ((bf16[4,80,512]{2,1,0:T(8,128)(2,1)}), bf16[4,80,512]{2,1,0:T(8,128)(2,1)S(1)}, u32[]{:S(2)}, u32[]{:S(2)}) async-start(bf16[4,80,512]{2,1,0:T(8,128)(2,1)} %bitcast.8), calls=%async_computation.1 | async-start | bytes 655360 | tf_op jit(solution)/shard_map/all_to_all | solution.py:77
  33.5 5.4 %collective-permute-done.2 = bf16[128,512]{1,0:T(8,128)(2,1)S(1)} collective-permute-done((bf16[128,512]{1,0:T(8,128)(2,1)}, bf16[128,512]{1,0:T(8,128)(2,1)S(1)}, u32[]{:S(2)}, u32[]{:S(2)}) %collective-permute-start.2) | collective-permute-done | bytes 131104 | tf_op jit(solution)/shard_map/ppermute | solution.py:10
  39.4 2.3 %scatter_custom_fusion.2 = bf16[320,512]{1,0:T(8,128)(2,1)} fusion(s32[256]{0:T(256)S(1)} %bitcast.63, f32[256,512]{1,0:T(8,128)S(1)} %mul.95, f32[256]{0:T(256)S(1)} %mul.86, bf16[]{:T(256)} %constant.14.clone.1), kind=kCustom, calls=%fused_computation.53 | custom fusion | flops 262144 | bytes 852994 | tf_op jit(solution)/shard_map/scatter | solution.py:23
  41.7 4.1 %all-to-all-start.2 = ((bf16[4,80,512]{2,1,0:T(8,128)(2,1)}), bf16[4,80,512]{2,1,0:T(8,128)(2,1)}, u32[]{:S(2)}, u32[]{:S(2)}) async-start(bf16[4,80,512]{2,1,0:T(8,128)(2,1)} %bitcast.11), calls=%async_computation.2 | async-start | bytes 655360 | tf_op jit(solution)/shard_map/all_to_all | solution.py:77
  48.5 3.4 %collective-permute-done.3 = bf16[128,512]{1,0:T(8,128)(2,1)S(1)} collective-permute-done((bf16[128,512]{1,0:T(8,128)(2,1)}, bf16[128,512]{1,0:T(8,128)(2,1)S(1)}, u32[]{:S(2)}, u32[]{:S(2)}) %collective-permute-start.3) | collective-permute-done | bytes 131104 | tf_op jit(solution)/shard_map/ppermute | solution.py:10
  52.4 2.3 %scatter_custom_fusion.3 = bf16[320,512]{1,0:T(8,128)(2,1)} fusion(s32[256]{0:T(256)S(1)} %bitcast.64, f32[256,512]{1,0:T(8,128)S(1)} %mul.98, f32[256]{0:T(256)S(1)} %mul.86, bf16[]{:T(256)} %constant.14.clone.1), kind=kCustom, calls=%fused_computation.54 | custom fusion | flops 262144 | bytes 852994 | tf_op jit(solution)/shard_map/scatter | solution.py:23
  54.6 3.5 %all-to-all-start.3 = ((bf16[4,80,512]{2,1,0:T(8,128)(2,1)}), bf16[4,80,512]{2,1,0:T(8,128)(2,1)S(1)}, u32[]{:S(2)}, u32[]{:S(2)}) async-start(bf16[4,80,512]{2,1,0:T(8,128)(2,1)} %bitcast.14), calls=%async_computation.3 | async-start | bytes 655360 | tf_op jit(solution)/shard_map/all_to_all | solution.py:77
  60.7 4.0 %all-to-all-done.3 = bf16[4,80,512]{2,1,0:T(8,128)(2,1)S(1)} async-done(((bf16[4,80,512]{2,1,0:T(8,128)(2,1)}), bf16[4,80,512]{2,1,0:T(8,128)(2,1)S(1)}, u32[]{:S(2)}, u32[]{:S(2)}) %all-to-all-start.3) | async-done | bytes 327712 | tf_op jit(solution)/shard_map/all_to_all | solution.py:77
  66.1 2.6 %fusion.16 = f32[1408,512]{1,0:T(8,128)S(1)} fusion(bf16[320,512]{1,0:T(8,128)(2,1)} %collective-permute-done.5, bf16[320,512]{1,0:T(8,128)(2,1)S(1)} %bitcast.51, bf16[320,1408]{1,0:T(8,128)(2,1)} %collective-permute-done.4, bf16[320,1408]{1,0:T(8,128)(2,1)S(1)} %bitcast.46), kind=kOutput, calls=%fused_computation.31 | convolution fusion | flops 927662080 | bytes 5341184 | tf_op jit(solution)/shard_map/dot_general | solution.py:46
  69.5 2.5 %fusion.20 = f32[1408,512]{1,0:T(8,128)S(1)} fusion(bf16[320,512]{1,0:T(8,128)(2,1)S(1)} %collective-permute-done.8, bf16[320,512]{1,0:T(8,128)(2,1)S(1)} %bitcast.54, bf16[320,1408]{1,0:T(8,128)(2,1)} %collective-permute-done.4, bf16[320,1408]{1,0:T(8,128)(2,1)S(1)} %bitcast.47), kind=kOutput, calls=%fused_computation.35 | convolution fusion | flops 927662080 | bytes 5341184 | tf_op jit(solution)/shard_map/dot_general | solution.py:46
  74.6 2.6 %fusion.24 = f32[1408,512]{1,0:T(8,128)S(1)} fusion(bf16[320,512]{1,0:T(8,128)(2,1)S(1)} %collective-permute-done.11, bf16[320,512]{1,0:T(8,128)(2,1)} %bitcast.12, bf16[320,1408]{1,0:T(8,128)(2,1)} %collective-permute-done.4, bf16[320,1408]{1,0:T(8,128)(2,1)S(1)} %bitcast.48), kind=kOutput, calls=%fused_computation.39 | convolution fusion | flops 927662080 | bytes 5341184 | tf_op jit(solution)/shard_map/dot_general | solution.py:46
  78.1 3.1 %collective-permute-done.14 = bf16[320,512]{1,0:T(8,128)(2,1)S(1)} collective-permute-done((bf16[320,512]{1,0:T(8,128)(2,1)S(1)}, bf16[320,512]{1,0:T(8,128)(2,1)S(1)}, u32[]{:S(2)}, u32[]{:S(2)}) %collective-permute-start.14) | collective-permute-done | bytes 327712 | tf_op jit(solution)/shard_map/ppermute | solution.py:44
  81.3 2.5 %fusion.28 = f32[1408,512]{1,0:T(8,128)S(1)} fusion(bf16[320,512]{1,0:T(8,128)(2,1)S(1)} %collective-permute-done.14, bf16[320,512]{1,0:T(8,128)(2,1)S(1)} %bitcast.57, bf16[320,1408]{1,0:T(8,128)(2,1)} %collective-permute-done.4, bf16[320,1408]{1,0:T(8,128)(2,1)S(1)} %bitcast.49), kind=kOutput, calls=%fused_computation.43 | convolution fusion | flops 927662080 | bytes 5341184 | tf_op jit(solution)/shard_map/dot_general | solution.py:46
  84.6 4.1 %fusion.5 = bf16[1,1,1,320,1408]{4,3,2,1,0:T(8,128)(2,1)} fusion(bf16[1,1,1408,2048]{3,2,1,0:T(8,128)(2,1)S(1)} %bitcast.66, bf16[320,512]{1,0:T(8,128)(2,1)S(1)} %bitcast.58, bf16[320,512]{1,0:T(8,128)(2,1)} %bitcast.12, bf16[320,512]{1,0:T(8,128)(2,1)S(1)} %bitcast.55, bf16[320,512]{1,0:T(8,128)(2,1)S(1)} %bitcast.52), kind=kOutput, calls=%fused_computation.8 | convolution fusion | flops 1851187200 | bytes 7979008 | tf_op jit(solution)/shard_map/sd,hd->sh/dot_general | solution.py:80
  94.5 9.3 %collective-permute-done.7 = bf16[352,512]{1,0:T(8,128)(2,1)S(1)} collective-permute-done((bf16[352,512]{1,0:T(8,128)(2,1)S(1)}, bf16[352,512]{1,0:T(8,128)(2,1)S(1)}, u32[]{:S(2)}, u32[]{:S(2)}) %collective-permute-start.7) | collective-permute-done | bytes 360480 | tf_op jit(solution)/shard_map/ppermute | solution.py:55
  103.9 7.4 %collective-permute-done.10 = bf16[352,512]{1,0:T(8,128)(2,1)S(1)} collective-permute-done((bf16[352,512]{1,0:T(8,128)(2,1)S(1)}, bf16[352,512]{1,0:T(8,128)(2,1)S(1)}, u32[]{:S(2)}, u32[]{:S(2)}) %collective-permute-start.10) | collective-permute-done | bytes 360480 | tf_op jit(solution)/shard_map/ppermute | solution.py:55
  111.5 15.1 %collective-permute-done.13 = bf16[352,512]{1,0:T(8,128)(2,1)S(1)} collective-permute-done((bf16[352,512]{1,0:T(8,128)(2,1)S(1)}, bf16[352,512]{1,0:T(8,128)(2,1)S(1)}, u32[]{:S(2)}, u32[]{:S(2)}) %collective-permute-start.13) | collective-permute-done | bytes 360480 | tf_op jit(solution)/shard_map/ppermute | solution.py:55
  126.7 15.3 %collective-permute-done.16 = bf16[352,512]{1,0:T(8,128)(2,1)S(1)} collective-permute-done((bf16[352,512]{1,0:T(8,128)(2,1)S(1)}, bf16[352,512]{1,0:T(8,128)(2,1)S(1)}, u32[]{:S(2)}, u32[]{:S(2)}) %collective-permute-start.16) | collective-permute-done | bytes 360480 | tf_op jit(solution)/shard_map/ppermute | solution.py:55
  (77 shorter events, 29.8 us)
Async XLA Ops:
  0.6 15.8 %copy-start = (bf16[1,1,1,320,1408]{4,3,2,1,0:T(8,128)(2,1)S(1)}, bf16[1,1,1,320,1408]{4,3,2,1,0:T(8,128)(2,1)}, u32[]{:S(2)}) copy-start(bf16[1,1,1,320,1408]{4,3,2,1,0:T(8,128)(2,1)} %param.8) | copy-start | bytes 2703364
  2.6 7.6 %collective-permute-start = (bf16[128,512]{1,0:T(8,128)(2,1)S(1)}, bf16[128,512]{1,0:T(8,128)(2,1)S(1)}, u32[]{:S(2)}, u32[]{:S(2)}) collective-permute-start(bf16[128,512]{1,0:T(8,128)(2,1)S(1)} %get-tuple-element.2), channel_id=1, source_target_pairs={{0,16},{16,0},{1,17},{17,1},{2,18},{18,2},{3,19},{19,3},{4,20},{20... | collective-permute-start | bytes 393224 | tf_op jit(solution)/shard_map/ppermute | solution.py:10
  12.9 16.4 %all-to-all-start = ((bf16[4,80,512]{2,1,0:T(8,128)(2,1)}), bf16[4,80,512]{2,1,0:T(8,128)(2,1)S(1)}, u32[]{:S(2)}, u32[]{:S(2)}) async-start(bf16[4,80,512]{2,1,0:T(8,128)(2,1)} %bitcast.5), calls=%async_computation | async-start | bytes 655360 | tf_op jit(solution)/shard_map/all_to_all | solution.py:77
  16.6 49.5 %collective-permute-start.4 = (bf16[320,1408]{1,0:T(8,128)(2,1)S(1)}, bf16[320,1408]{1,0:T(8,128)(2,1)}, u32[]{:S(2)}, u32[]{:S(2)}) collective-permute-start(bf16[320,1408]{1,0:T(8,128)(2,1)S(1)} %fusion.8), channel_id=1, source_target_pairs={{0,4},{12,8},{1,5},{13,9},{2,6},{14,10},{3,7},{15,11},{16,20},{28,... | collective-permute-start | bytes 2703368 | tf_op jit(solution)/shard_map/ppermute | solution.py:34
  21.0 5.6 %collective-permute-start.1 = (bf16[128,512]{1,0:T(8,128)(2,1)S(1)}, bf16[128,512]{1,0:T(8,128)(2,1)S(1)}, u32[]{:S(2)}, u32[]{:S(2)}) collective-permute-start(bf16[128,512]{1,0:T(8,128)(2,1)S(1)} %get-tuple-element.3), channel_id=1, source_target_pairs={{0,16},{16,0},{1,17},{17,1},{2,18},{18,2},{3,19},{19,3},{4,20},{20... | collective-permute-start | bytes 393224 | tf_op jit(solution)/shard_map/ppermute | solution.py:10
  29.3 12.3 %all-to-all-start.1 = ((bf16[4,80,512]{2,1,0:T(8,128)(2,1)}), bf16[4,80,512]{2,1,0:T(8,128)(2,1)S(1)}, u32[]{:S(2)}, u32[]{:S(2)}) async-start(bf16[4,80,512]{2,1,0:T(8,128)(2,1)} %bitcast.8), calls=%async_computation.1 | async-start | bytes 655360 | tf_op jit(solution)/shard_map/all_to_all | solution.py:77
  32.8 6.1 %collective-permute-start.2 = (bf16[128,512]{1,0:T(8,128)(2,1)}, bf16[128,512]{1,0:T(8,128)(2,1)S(1)}, u32[]{:S(2)}, u32[]{:S(2)}) collective-permute-start(bf16[128,512]{1,0:T(8,128)(2,1)} %get-tuple-element.5), channel_id=1, source_target_pairs={{0,16},{16,0},{1,17},{17,1},{2,18},{18,2},{3,19},{19,3},{4,20},{20... | collective-permute-start | bytes 393224 | tf_op jit(solution)/shard_map/ppermute | solution.py:10
  41.7 13.0 %all-to-all-start.2 = ((bf16[4,80,512]{2,1,0:T(8,128)(2,1)}), bf16[4,80,512]{2,1,0:T(8,128)(2,1)}, u32[]{:S(2)}, u32[]{:S(2)}) async-start(bf16[4,80,512]{2,1,0:T(8,128)(2,1)} %bitcast.11), calls=%async_computation.2 | async-start | bytes 655360 | tf_op jit(solution)/shard_map/all_to_all | solution.py:77
  45.8 6.1 %collective-permute-start.3 = (bf16[128,512]{1,0:T(8,128)(2,1)}, bf16[128,512]{1,0:T(8,128)(2,1)S(1)}, u32[]{:S(2)}, u32[]{:S(2)}) collective-permute-start(bf16[128,512]{1,0:T(8,128)(2,1)} %get-tuple-element.4), channel_id=1, source_target_pairs={{0,16},{16,0},{1,17},{17,1},{2,18},{18,2},{3,19},{19,3},{4,20},{20... | collective-permute-start | bytes 393224 | tf_op jit(solution)/shard_map/ppermute | solution.py:10
  46.5 19.6 %collective-permute-start.5 = (bf16[320,512]{1,0:T(8,128)(2,1)S(1)}, bf16[320,512]{1,0:T(8,128)(2,1)}, u32[]{:S(2)}, u32[]{:S(2)}) collective-permute-start(bf16[320,512]{1,0:T(8,128)(2,1)S(1)} %bitcast.50), channel_id=1, source_target_pairs={{0,4},{12,8},{1,5},{13,9},{2,6},{14,10},{3,7},{15,11},{16,20},{28,... | collective-permute-start | bytes 983048 | tf_op jit(solution)/shard_map/ppermute | solution.py:44
  54.6 10.1 %all-to-all-start.3 = ((bf16[4,80,512]{2,1,0:T(8,128)(2,1)}), bf16[4,80,512]{2,1,0:T(8,128)(2,1)S(1)}, u32[]{:S(2)}, u32[]{:S(2)}) async-start(bf16[4,80,512]{2,1,0:T(8,128)(2,1)} %bitcast.14), calls=%async_computation.3 | async-start | bytes 655360 | tf_op jit(solution)/shard_map/all_to_all | solution.py:77
  58.1 11.4 %collective-permute-start.8 = (bf16[320,512]{1,0:T(8,128)(2,1)S(1)}, bf16[320,512]{1,0:T(8,128)(2,1)S(1)}, u32[]{:S(2)}, u32[]{:S(2)}) collective-permute-start(bf16[320,512]{1,0:T(8,128)(2,1)S(1)} %bitcast.53), channel_id=1, source_target_pairs={{0,4},{12,8},{1,5},{13,9},{2,6},{14,10},{3,7},{15,11},{16,20},{28,... | collective-permute-start | bytes 983048 | tf_op jit(solution)/shard_map/ppermute | solution.py:44
  59.4 15.2 %collective-permute-start.11 = (bf16[320,512]{1,0:T(8,128)(2,1)}, bf16[320,512]{1,0:T(8,128)(2,1)S(1)}, u32[]{:S(2)}, u32[]{:S(2)}) collective-permute-start(bf16[320,512]{1,0:T(8,128)(2,1)} %bitcast.12), channel_id=1, source_target_pairs={{0,4},{12,8},{1,5},{13,9},{2,6},{14,10},{3,7},{15,11},{16,20},{28,... | collective-permute-start | bytes 983048 | tf_op jit(solution)/shard_map/ppermute | solution.py:44
  64.8 16.5 %collective-permute-start.14 = (bf16[320,512]{1,0:T(8,128)(2,1)S(1)}, bf16[320,512]{1,0:T(8,128)(2,1)S(1)}, u32[]{:S(2)}, u32[]{:S(2)}) collective-permute-start(bf16[320,512]{1,0:T(8,128)(2,1)S(1)} %bitcast.56), channel_id=1, source_target_pairs={{0,4},{12,8},{1,5},{13,9},{2,6},{14,10},{3,7},{15,11},{16,20},{28,... | collective-permute-start | bytes 983048 | tf_op jit(solution)/shard_map/ppermute | solution.py:44
  68.8 20.0 %collective-permute-start.6 = (bf16[704,512]{1,0:T(8,128)(2,1)S(1)}, bf16[704,512]{1,0:T(8,128)(2,1)S(1)}, u32[]{:S(2)}, u32[]{:S(2)}) collective-permute-start(bf16[704,512]{1,0:T(8,128)(2,1)S(1)} %dynamic-slice_convert_fusion.3), channel_id=1, source_target_pairs={{4,8},{8,4},{5,9},{9,5},{6,10},{10,6},{7,11},{11,7},{20,24},{24,20... | collective-permute-start | bytes 2162696 | tf_op jit(solution)/shard_map/ppermute | solution.py:50
  72.1 18.1 %collective-permute-start.9 = (bf16[704,512]{1,0:T(8,128)(2,1)S(1)}, bf16[704,512]{1,0:T(8,128)(2,1)S(1)}, u32[]{:S(2)}, u32[]{:S(2)}) collective-permute-start(bf16[704,512]{1,0:T(8,128)(2,1)S(1)} %dynamic-slice_convert_fusion.2), channel_id=1, source_target_pairs={{4,8},{8,4},{5,9},{9,5},{6,10},{10,6},{7,11},{11,7},{20,24},{24,20... | collective-permute-start | bytes 2162696 | tf_op jit(solution)/shard_map/ppermute | solution.py:50
  77.2 7.4 %slice-start = ((s8[5767168]{0:T(1024)(128)(4,1)}), s8[4194304]{0:T(1024)(128)(4,1)S(1)}, s32[]{:S(2)}) async-start(s8[5767168]{0:T(1024)(128)(4,1)} %bitcast.65), calls=%async_computation.4 | async-start | bytes 8388608
  77.3 7.3 %slice-start.1 = ((s8[5767168]{0:T(1024)(128)(4,1)}), s8[1572864]{0:T(1024)(128)(4,1)S(1)}, s32[]{:S(2)}) async-start(s8[5767168]{0:T(1024)(128)(4,1)} %bitcast.65), calls=%async_computation.5 | async-start | bytes 3145728
  77.3 14.3 %collective-permute-start.12 = (bf16[704,512]{1,0:T(8,128)(2,1)S(1)}, bf16[704,512]{1,0:T(8,128)(2,1)S(1)}, u32[]{:S(2)}, u32[]{:S(2)}) collective-permute-start(bf16[704,512]{1,0:T(8,128)(2,1)S(1)} %dynamic-slice_convert_fusion.1), channel_id=1, source_target_pairs={{4,8},{8,4},{5,9},{9,5},{6,10},{10,6},{7,11},{11,7},{20,24},{24,20... | collective-permute-start | bytes 2162696 | tf_op jit(solution)/shard_map/ppermute | solution.py:50
  83.9 9.2 %collective-permute-start.15 = (bf16[704,512]{1,0:T(8,128)(2,1)S(1)}, bf16[704,512]{1,0:T(8,128)(2,1)S(1)}, u32[]{:S(2)}, u32[]{:S(2)}) collective-permute-start(bf16[704,512]{1,0:T(8,128)(2,1)S(1)} %dynamic-slice_convert_fusion), channel_id=1, source_target_pairs={{4,8},{8,4},{5,9},{9,5},{6,10},{10,6},{7,11},{11,7},{20,24},{24,20... | collective-permute-start | bytes 2162696 | tf_op jit(solution)/shard_map/ppermute | solution.py:50
  88.9 14.9 %collective-permute-start.7 = (bf16[352,512]{1,0:T(8,128)(2,1)S(1)}, bf16[352,512]{1,0:T(8,128)(2,1)S(1)}, u32[]{:S(2)}, u32[]{:S(2)}) collective-permute-start(bf16[352,512]{1,0:T(8,128)(2,1)S(1)} %add_convert_fusion.3), channel_id=1, source_target_pairs={{4,0},{8,12},{5,1},{9,13},{6,2},{10,14},{7,3},{11,15},{20,16},{24,... | collective-permute-start | bytes 1081352 | tf_op jit(solution)/shard_map/ppermute | solution.py:55
  90.3 21.0 %collective-permute-start.10 = (bf16[352,512]{1,0:T(8,128)(2,1)S(1)}, bf16[352,512]{1,0:T(8,128)(2,1)S(1)}, u32[]{:S(2)}, u32[]{:S(2)}) collective-permute-start(bf16[352,512]{1,0:T(8,128)(2,1)S(1)} %add_convert_fusion.2), channel_id=1, source_target_pairs={{4,0},{8,12},{5,1},{9,13},{6,2},{10,14},{7,3},{11,15},{20,16},{24,... | collective-permute-start | bytes 1081352 | tf_op jit(solution)/shard_map/ppermute | solution.py:55
  91.7 34.8 %collective-permute-start.13 = (bf16[352,512]{1,0:T(8,128)(2,1)S(1)}, bf16[352,512]{1,0:T(8,128)(2,1)S(1)}, u32[]{:S(2)}, u32[]{:S(2)}) collective-permute-start(bf16[352,512]{1,0:T(8,128)(2,1)S(1)} %add_convert_fusion.1), channel_id=1, source_target_pairs={{4,0},{8,12},{5,1},{9,13},{6,2},{10,14},{7,3},{11,15},{20,16},{24,... | collective-permute-start | bytes 1081352 | tf_op jit(solution)/shard_map/ppermute | solution.py:55
  93.2 48.8 %collective-permute-start.16 = (bf16[352,512]{1,0:T(8,128)(2,1)S(1)}, bf16[352,512]{1,0:T(8,128)(2,1)S(1)}, u32[]{:S(2)}, u32[]{:S(2)}) collective-permute-start(bf16[352,512]{1,0:T(8,128)(2,1)S(1)} %add_convert_fusion), channel_id=1, source_target_pairs={{4,0},{8,12},{5,1},{9,13},{6,2},{10,14},{7,3},{11,15},{20,16},{24,... | collective-permute-start | bytes 1081352 | tf_op jit(solution)/shard_map/ppermute | solution.py:55

commit v3 on v2

--- a/solution.py
+++ b/solution.py
@@ -67,16 +67,14 @@
     slot_count = saved.shape[0]
     width = slot_count // groups
     model_width = grad_out.shape[2]
-    chunks = 4 if model_width % 512 == 0 else 1
+    target = dispatch_targets(routes[0], groups, width)
+    incoming = shifted(grad_out, "section", -1)[0]
+    outgoing = dispatch_rows(incoming, gates[0], target, groups, width)
+    piece = lax.all_to_all(outgoing, "expert", split_axis=0, concat_axis=0, tiled=True)
+    scaled = piece.reshape(slot_count, model_width)
+    chunks = 8 if model_width % 2048 == 0 else 1
     step = model_width // chunks
-    target = dispatch_targets(routes[0], groups, width)
-    parts = []
-    for c in range(chunks):
-        rows = shifted(grad_out[0, :, c * step:(c + 1) * step], "section", -1)
-        outgoing = dispatch_rows(rows, gates[0], target, groups, width)
-        piece = lax.all_to_all(outgoing, "expert", split_axis=0, concat_axis=0, tiled=True)
-        parts.append(piece.reshape(slot_count, step))
-    scaled = jnp.concatenate(parts, axis=1)
+    parts = [scaled[:, c * step:(c + 1) * step] for c in range(chunks)]
     grad_rows_out = jnp.einsum(
         "sd,hd->sh", scaled, weight, preferred_element_type=jnp.float32
     ).astype(jnp.bfloat16)

time: 145 us -> 154 us (1.062)
  other arithmetic: 14.1 us -> 6.64 us
  matrix products: 14.2 us -> 21.4 us
  waiting for transfers between devices: 69.6 us -> 74.2 us
  local copies, waits for them, and re-layouts: 6.84 us -> 9.75 us
  starting transfers between devices: 38.1 us -> 40.1 us
    all_to_all x4 -> x1, starting transfers between devices: 14.5 us -> 3.67 us  [shards(): lax.all_to_all(outgoing, 'expert', split_axis=0, concat_axis=0, tiled=True)]
    all_to_all x4 -> x1, waiting for transfers between devices: 4.02 us -> 12.3 us  [shards(): lax.all_to_all(outgoing, 'expert', split_axis=0, concat_axis=0, tiled=True)]
    ppermute x4 -> x8, waiting for transfers between devices: 47.1 us -> 54.2 us  [line_weight_grad(): r3 = lax.ppermute(s3, 'dp', [(1, 0), (2, 3)])]
    ppermute x4 -> x8, starting transfers between devices: 5.95 us -> 12.8 us  [line_weight_grad(): srecv = lax.ppermute(sc, 'dp', ends)]
    ppermute x4 -> x1, waiting for transfers between devices: 13.7 us -> 7.54 us  [shifted(): return lax.ppermute(value, axis, pairs)]
    scatter x4 -> x1, other arithmetic: 9.06 us -> 3.34 us  [dispatch_rows(): jnp.zeros((count * width, rows.shape[1]), jnp.bfloat16).at[target]]
    dot_general x4 -> x8, matrix products: 10.1 us -> 15.6 us  [line_weight_grad(): lax.dot_general(lhs, rhs, (((0,), (0,)), ((), ())), preferred_element_typ...]
    ppermute x4 -> x8, starting transfers between devices: 5.17 us -> 10.3 us  [line_weight_grad(): r3 = lax.ppermute(s3, 'dp', [(1, 0), (2, 3)])]
  transfers between devices with their start and end apart: 21 -> 27, of which waited for: 10 -> 10; matrix products, arithmetic and copies ran while one was open for 20% -> 18% of each run, Pallas kernels for 0% -> 0%
where the time goes in v3:
time: 154 us; the launch traced here: 153 us
  waiting for transfers between devices  74.2 us (48%)
  starting transfers between devices  40.1 us (26%)
  matrix products  21.4 us (14%)
  local copies, waits for them, and re-layouts  9.75 us (6%)
  other arithmetic  6.64 us (4%)
    ppermute x8, waiting for transfers between devices, line_weight_grad(): r3 = lax.ppermute(s3, 'dp', [(1, 0), (2, 3)])  54.2 us
    dot_general x8, matrix products, line_weight_grad(): lax.dot_general(lhs, rhs, (((0,), (0,)), ((), ())), preferred_element_typ...  15.6 us
    ppermute x8, starting transfers between devices, line_weight_grad(): srecv = lax.ppermute(sc, 'dp', ends)  12.8 us
    all_to_all x1, waiting for transfers between devices, shards(): lax.all_to_all(outgoing, 'expert', split_axis=0, concat_axis=0, tiled=True)  12.3 us
    ppermute x8, starting transfers between devices, line_weight_grad(): r3 = lax.ppermute(s3, 'dp', [(1, 0), (2, 3)])  10.3 us
    ppermute x1, waiting for transfers between devices, shifted(): return lax.ppermute(value, axis, pairs)  7.54 us
    dot_general x1, matrix products, shards(): jnp.einsum('sd,hd->sh', scaled, weight, preferred_element_type=jnp.float32)  5.78 us
    ppermute x8, starting transfers between devices, line_weight_grad(): r2 = lax.ppermute(s2, 'dp', [(1, 2), (2, 1)])  5.65 us
  transfers between devices with their start and end apart: 27, of which 10 were waited for; matrix products, arithmetic and copies ran while one was open for 18% of the time, Pallas kernels for 0%

profile of v3, /device:TPU:0, one launch (start us, length us, event | category | flops | bytes accessed | tf_op | source)
XLA Modules:
  0.0 153.3 jit_solution(1901545128824983417)
XLA Ops:
  0.6 3.0 %collective-permute-start = (bf16[1,128,2048]{2,1,0:T(8,128)(2,1)}, bf16[1,128,2048]{2,1,0:T(8,128)(2,1)S(1)}, u32[]{:S(2)}, u32[]{:S(2)}) collective-permute-start(bf16[1,128,2048]{2,1,0:T(8,128)(2,1)} %param.5), channel_id=1, source_target_pairs={{0,16},{16,0},{1,17},{17,1},{2,18},{18,2},{3,19},{19,3},{4,20},{20... | collective-permute-start | bytes 1572872 | tf_op jit(solution)/shard_map/ppermute | solution.py:10
  8.3 7.5 %collective-permute-done = bf16[1,128,2048]{2,1,0:T(8,128)(2,1)S(1)} collective-permute-done((bf16[1,128,2048]{2,1,0:T(8,128)(2,1)}, bf16[1,128,2048]{2,1,0:T(8,128)(2,1)S(1)}, u32[]{:S(2)}, u32[]{:S(2)}) %collective-permute-start) | collective-permute-done | bytes 524320 | tf_op jit(solution)/shard_map/ppermute | solution.py:10
  15.9 2.5 %mul.46 = f32[128,2,2048]{2,1,0:T(2,128)} broadcast(f32[128,2048]{1,0:T(8,128)S(1)} %bitcast_convert_fusion), dimensions={0,2} | broadcast | bytes 3145728 | tf_op jit(solution)/shard_map/mul | solution.py:21
  18.4 2.7 %mul.47 = f32[256,2048]{1,0:T(8,128)S(1)} reshape(f32[128,2,2048]{2,1,0:T(2,128)} %mul.46) | data formatting | bytes 4194304 | tf_op jit(solution)/shard_map/mul | solution.py:21
  21.1 3.3 %scatter_custom_fusion = bf16[320,2048]{1,0:T(8,128)(2,1)} fusion(s32[256]{0:T(256)S(1)} %bitcast.48, f32[256,2048]{1,0:T(8,128)S(1)} %mul.47, f32[256]{0:T(256)S(1)} %mul.44, bf16[]{:T(256)} %constant.14.clone.1), kind=kCustom, calls=%fused_computation.9 | custom fusion | flops 1048576 | bytes 3408898 | tf_op jit(solution)/shard_map/scatter | solution.py:23
  24.5 3.7 %all-to-all-start = ((bf16[4,80,2048]{2,1,0:T(8,128)(2,1)}), bf16[4,80,2048]{2,1,0:T(8,128)(2,1)S(1)}, u32[]{:S(2)}, u32[]{:S(2)}) async-start(bf16[4,80,2048]{2,1,0:T(8,128)(2,1)} %bitcast.5), calls=%async_computation | async-start | bytes 2621440 | tf_op jit(solution)/shard_map/all_to_all | solution.py:73
  28.3 4.7 %collective-permute-start.1 = (bf16[320,1408]{1,0:T(8,128)(2,1)S(1)}, bf16[320,1408]{1,0:T(8,128)(2,1)}, u32[]{:S(2)}, u32[]{:S(2)}) collective-permute-start(bf16[320,1408]{1,0:T(8,128)(2,1)S(1)} %fusion.8), channel_id=1, source_target_pairs={{0,4},{12,8},{1,5},{13,9},{2,6},{14,10},{3,7},{15,11},{16,20},{28,... | collective-permute-start | bytes 2703368 | tf_op jit(solution)/shard_map/ppermute | solution.py:34
  33.0 12.3 %all-to-all-done = bf16[4,80,2048]{2,1,0:T(8,128)(2,1)S(1)} async-done(((bf16[4,80,2048]{2,1,0:T(8,128)(2,1)}), bf16[4,80,2048]{2,1,0:T(8,128)(2,1)S(1)}, u32[]{:S(2)}, u32[]{:S(2)}) %all-to-all-start) | async-done | bytes 1310752 | tf_op jit(solution)/shard_map/all_to_all | solution.py:73
  45.4 3.7 %collective-permute-start.2 = (bf16[320,256]{1,0:T(8,128)(2,1)S(1)}, bf16[320,256]{1,0:T(8,128)(2,1)S(1)}, u32[]{:S(2)}, u32[]{:S(2)}) collective-permute-start(bf16[320,256]{1,0:T(8,128)(2,1)S(1)} %get-tuple-element.9), channel_id=1, source_target_pairs={{0,4},{12,8},{1,5},{13,9},{2,6},{14,10},{3,7},{15,11},{16,20},{28,... | collective-permute-start | bytes 491528 | tf_op jit(solution)/shard_map/ppermute | solution.py:44
  50.5 5.8 %fusion.5 = bf16[1,1,1,320,1408]{4,3,2,1,0:T(8,128)(2,1)} fusion(bf16[320,2048]{1,0:T(8,128)(2,1)S(1)} %bitcast.36, bf16[1,1,1408,2048]{3,2,1,0:T(8,128)(2,1)} %param.9), kind=kOutput, calls=%fused_computation.4 | convolution fusion | flops 1845944320 | bytes 7979008 | tf_op jit(solution)/shard_map/sd,hd->sh/dot_general | solution.py:78
  61.5 1.9 %fusion.12 = f32[1408,256]{1,0:T(8,128)S(1)} fusion(bf16[320,256]{1,0:T(8,128)(2,1)S(1)} %collective-permute-done.2, bf16[320,256]{1,0:T(8,128)(2,1)S(1)} %get-tuple-element.9, bf16[320,1408]{1,0:T(8,128)(2,1)} %collective-permute-done.1, bf16[320,1408]{1,0:T(8,128)(2,1)S(1)} %bitcast.37), kind=kOutput, calls=%fused_computation.37 | convolution fusion | flops 465633280 | bytes 3571712 | tf_op jit(solution)/shard_map/dot_general | solution.py:46
  64.8 1.9 %fusion.16 = f32[1408,256]{1,0:T(8,128)S(1)} fusion(bf16[320,256]{1,0:T(8,128)(2,1)S(1)} %collective-permute-done.5, bf16[320,256]{1,0:T(8,128)(2,1)S(1)} %get-tuple-element.8, bf16[320,1408]{1,0:T(8,128)(2,1)} %collective-permute-done.1, bf16[320,1408]{1,0:T(8,128)(2,1)S(1)} %bitcast.38), kind=kOutput, calls=%fused_computation.41 | convolution fusion | flops 465633280 | bytes 3571712 | tf_op jit(solution)/shard_map/dot_general | solution.py:46
  68.1 2.0 %fusion.20 = f32[1408,256]{1,0:T(8,128)S(1)} fusion(bf16[320,256]{1,0:T(8,128)(2,1)S(1)} %collective-permute-done.8, bf16[320,256]{1,0:T(8,128)(2,1)S(1)} %get-tuple-element.7, bf16[320,1408]{1,0:T(8,128)(2,1)} %collective-permute-done.1, bf16[320,1408]{1,0:T(8,128)(2,1)S(1)} %bitcast.39), kind=kOutput, calls=%fused_computation.45 | convolution fusion | flops 465633280 | bytes 3571712 | tf_op jit(solution)/shard_map/dot_general | solution.py:46
  70.8 2.0 %fusion.24 = f32[1408,256]{1,0:T(8,128)S(1)} fusion(bf16[320,256]{1,0:T(8,128)(2,1)S(1)} %collective-permute-done.11, bf16[320,256]{1,0:T(8,128)(2,1)S(1)} %get-tuple-element.6, bf16[320,1408]{1,0:T(8,128)(2,1)} %collective-permute-done.1, bf16[320,1408]{1,0:T(8,128)(2,1)S(1)} %bitcast.40), kind=kOutput, calls=%fused_computation.49 | convolution fusion | flops 465633280 | bytes 3571712 | tf_op jit(solution)/shard_map/dot_general | solution.py:46
  73.7 2.0 %fusion.28 = f32[1408,256]{1,0:T(8,128)S(1)} fusion(bf16[320,256]{1,0:T(8,128)(2,1)S(1)} %collective-permute-done.14, bf16[320,256]{1,0:T(8,128)(2,1)S(1)} %get-tuple-element.5, bf16[320,1408]{1,0:T(8,128)(2,1)} %collective-permute-done.1, bf16[320,1408]{1,0:T(8,128)(2,1)S(1)} %bitcast.41), kind=kOutput, calls=%fused_computation.53 | convolution fusion | flops 465633280 | bytes 3571712 | tf_op jit(solution)/shard_map/dot_general | solution.py:46
  76.4 2.0 %fusion.32 = f32[1408,256]{1,0:T(8,128)S(1)} fusion(bf16[320,256]{1,0:T(8,128)(2,1)S(1)} %collective-permute-done.17, bf16[320,256]{1,0:T(8,128)(2,1)S(1)} %get-tuple-element.4, bf16[320,1408]{1,0:T(8,128)(2,1)} %collective-permute-done.1, bf16[320,1408]{1,0:T(8,128)(2,1)S(1)} %bitcast.42), kind=kOutput, calls=%fused_computation.57 | convolution fusion | flops 465633280 | bytes 3571712 | tf_op jit(solution)/shard_map/dot_general | solution.py:46
  79.2 1.9 %fusion.36 = f32[1408,256]{1,0:T(8,128)S(1)} fusion(bf16[320,256]{1,0:T(8,128)(2,1)S(1)} %collective-permute-done.20, bf16[320,256]{1,0:T(8,128)(2,1)S(1)} %get-tuple-element.3, bf16[320,1408]{1,0:T(8,128)(2,1)} %collective-permute-done.1, bf16[320,1408]{1,0:T(8,128)(2,1)S(1)} %bitcast.43), kind=kOutput, calls=%fused_computation.61 | convolution fusion | flops 465633280 | bytes 3571712 | tf_op jit(solution)/shard_map/dot_general | solution.py:46
  93.1 17.4 %collective-permute-done.4 = bf16[352,256]{1,0:T(8,128)(2,1)S(1)} collective-permute-done((bf16[352,256]{1,0:T(8,128)(2,1)S(1)}, bf16[352,256]{1,0:T(8,128)(2,1)S(1)}, u32[]{:S(2)}, u32[]{:S(2)}) %collective-permute-start.4) | collective-permute-done | bytes 180256 | tf_op jit(solution)/shard_map/ppermute | solution.py:55
  111.9 6.4 %collective-permute-done.7 = bf16[352,256]{1,0:T(8,128)(2,1)S(1)} collective-permute-done((bf16[352,256]{1,0:T(8,128)(2,1)S(1)}, bf16[352,256]{1,0:T(8,128)(2,1)S(1)}, u32[]{:S(2)}, u32[]{:S(2)}) %collective-permute-start.7) | collective-permute-done | bytes 180256 | tf_op jit(solution)/shard_map/ppermute | solution.py:55
  119.6 6.4 %collective-permute-done.10 = bf16[352,256]{1,0:T(8,128)(2,1)S(1)} collective-permute-done((bf16[352,256]{1,0:T(8,128)(2,1)S(1)}, bf16[352,256]{1,0:T(8,128)(2,1)S(1)}, u32[]{:S(2)}, u32[]{:S(2)}) %collective-permute-start.10) | collective-permute-done | bytes 180256 | tf_op jit(solution)/shard_map/ppermute | solution.py:55
  127.3 6.4 %collective-permute-done.13 = bf16[352,256]{1,0:T(8,128)(2,1)S(1)} collective-permute-done((bf16[352,256]{1,0:T(8,128)(2,1)S(1)}, bf16[352,256]{1,0:T(8,128)(2,1)S(1)}, u32[]{:S(2)}, u32[]{:S(2)}) %collective-permute-start.13) | collective-permute-done | bytes 180256 | tf_op jit(solution)/shard_map/ppermute | solution.py:55
  133.7 8.3 %collective-permute-done.16 = bf16[352,256]{1,0:T(8,128)(2,1)S(1)} collective-permute-done((bf16[352,256]{1,0:T(8,128)(2,1)S(1)}, bf16[352,256]{1,0:T(8,128)(2,1)S(1)}, u32[]{:S(2)}, u32[]{:S(2)}) %collective-permute-start.16) | collective-permute-done | bytes 180256 | tf_op jit(solution)/shard_map/ppermute | solution.py:55
  142.1 3.8 %collective-permute-done.19 = bf16[352,256]{1,0:T(8,128)(2,1)S(1)} collective-permute-done((bf16[352,256]{1,0:T(8,128)(2,1)S(1)}, bf16[352,256]{1,0:T(8,128)(2,1)S(1)}, u32[]{:S(2)}, u32[]{:S(2)}) %collective-permute-start.19) | collective-permute-done | bytes 180256 | tf_op jit(solution)/shard_map/ppermute | solution.py:55
  145.9 3.8 %collective-permute-done.22 = bf16[352,256]{1,0:T(8,128)(2,1)S(1)} collective-permute-done((bf16[352,256]{1,0:T(8,128)(2,1)S(1)}, bf16[352,256]{1,0:T(8,128)(2,1)S(1)}, u32[]{:S(2)}, u32[]{:S(2)}) %collective-permute-start.22) | collective-permute-done | bytes 180256 | tf_op jit(solution)/shard_map/ppermute | solution.py:55
  (93 shorter events, 36.8 us)
Async XLA Ops:
  0.6 15.2 %collective-permute-start = (bf16[1,128,2048]{2,1,0:T(8,128)(2,1)}, bf16[1,128,2048]{2,1,0:T(8,128)(2,1)S(1)}, u32[]{:S(2)}, u32[]{:S(2)}) collective-permute-start(bf16[1,128,2048]{2,1,0:T(8,128)(2,1)} %param.5), channel_id=1, source_target_pairs={{0,16},{16,0},{1,17},{17,1},{2,18},{18,2},{3,19},{19,3},{4,20},{20... | collective-permute-start | bytes 1572872 | tf_op jit(solution)/shard_map/ppermute | solution.py:10
  24.5 20.9 %all-to-all-start = ((bf16[4,80,2048]{2,1,0:T(8,128)(2,1)}), bf16[4,80,2048]{2,1,0:T(8,128)(2,1)S(1)}, u32[]{:S(2)}, u32[]{:S(2)}) async-start(bf16[4,80,2048]{2,1,0:T(8,128)(2,1)} %bitcast.5), calls=%async_computation | async-start | bytes 2621440 | tf_op jit(solution)/shard_map/all_to_all | solution.py:73
  28.3 30.5 %collective-permute-start.1 = (bf16[320,1408]{1,0:T(8,128)(2,1)S(1)}, bf16[320,1408]{1,0:T(8,128)(2,1)}, u32[]{:S(2)}, u32[]{:S(2)}) collective-permute-start(bf16[320,1408]{1,0:T(8,128)(2,1)S(1)} %fusion.8), channel_id=1, source_target_pairs={{0,4},{12,8},{1,5},{13,9},{2,6},{14,10},{3,7},{15,11},{16,20},{28,... | collective-permute-start | bytes 2703368 | tf_op jit(solution)/shard_map/ppermute | solution.py:34
  45.4 14.8 %collective-permute-start.2 = (bf16[320,256]{1,0:T(8,128)(2,1)S(1)}, bf16[320,256]{1,0:T(8,128)(2,1)S(1)}, u32[]{:S(2)}, u32[]{:S(2)}) collective-permute-start(bf16[320,256]{1,0:T(8,128)(2,1)S(1)} %get-tuple-element.9), channel_id=1, source_target_pairs={{0,4},{12,8},{1,5},{13,9},{2,6},{14,10},{3,7},{15,11},{16,20},{28,... | collective-permute-start | bytes 491528 | tf_op jit(solution)/shard_map/ppermute | solution.py:44
  49.2 14.3 %collective-permute-start.5 = (bf16[320,256]{1,0:T(8,128)(2,1)S(1)}, bf16[320,256]{1,0:T(8,128)(2,1)S(1)}, u32[]{:S(2)}, u32[]{:S(2)}) collective-permute-start(bf16[320,256]{1,0:T(8,128)(2,1)S(1)} %get-tuple-element.8), channel_id=1, source_target_pairs={{0,4},{12,8},{1,5},{13,9},{2,6},{14,10},{3,7},{15,11},{16,20},{28,... | collective-permute-start | bytes 491528 | tf_op jit(solution)/shard_map/ppermute | solution.py:44
  56.3 10.5 %collective-permute-start.8 = (bf16[320,256]{1,0:T(8,128)(2,1)S(1)}, bf16[320,256]{1,0:T(8,128)(2,1)S(1)}, u32[]{:S(2)}, u32[]{:S(2)}) collective-permute-start(bf16[320,256]{1,0:T(8,128)(2,1)S(1)} %get-tuple-element.7), channel_id=1, source_target_pairs={{0,4},{12,8},{1,5},{13,9},{2,6},{14,10},{3,7},{15,11},{16,20},{28,... | collective-permute-start | bytes 491528 | tf_op jit(solution)/shard_map/ppermute | solution.py:44
  57.6 12.5 %collective-permute-start.11 = (bf16[320,256]{1,0:T(8,128)(2,1)S(1)}, bf16[320,256]{1,0:T(8,128)(2,1)S(1)}, u32[]{:S(2)}, u32[]{:S(2)}) collective-permute-start(bf16[320,256]{1,0:T(8,128)(2,1)S(1)} %get-tuple-element.6), channel_id=1, source_target_pairs={{0,4},{12,8},{1,5},{13,9},{2,6},{14,10},{3,7},{15,11},{16,20},{28,... | collective-permute-start | bytes 491528 | tf_op jit(solution)/shard_map/ppermute | solution.py:44
  58.9 14.0 %collective-permute-start.14 = (bf16[320,256]{1,0:T(8,128)(2,1)S(1)}, bf16[320,256]{1,0:T(8,128)(2,1)S(1)}, u32[]{:S(2)}, u32[]{:S(2)}) collective-permute-start(bf16[320,256]{1,0:T(8,128)(2,1)S(1)} %get-tuple-element.5), channel_id=1, source_target_pairs={{0,4},{12,8},{1,5},{13,9},{2,6},{14,10},{3,7},{15,11},{16,20},{28,... | collective-permute-start | bytes 491528 | tf_op jit(solution)/shard_map/ppermute | solution.py:44
  60.2 15.5 %collective-permute-start.17 = (bf16[320,256]{1,0:T(8,128)(2,1)S(1)}, bf16[320,256]{1,0:T(8,128)(2,1)S(1)}, u32[]{:S(2)}, u32[]{:S(2)}) collective-permute-start(bf16[320,256]{1,0:T(8,128)(2,1)S(1)} %get-tuple-element.4), channel_id=1, source_target_pairs={{0,4},{12,8},{1,5},{13,9},{2,6},{14,10},{3,7},{15,11},{16,20},{28,... | collective-permute-start | bytes 491528 | tf_op jit(solution)/shard_map/ppermute | solution.py:44
  63.5 15.0 %collective-permute-start.20 = (bf16[320,256]{1,0:T(8,128)(2,1)S(1)}, bf16[320,256]{1,0:T(8,128)(2,1)S(1)}, u32[]{:S(2)}, u32[]{:S(2)}) collective-permute-start(bf16[320,256]{1,0:T(8,128)(2,1)S(1)} %get-tuple-element.3), channel_id=1, source_target_pairs={{0,4},{12,8},{1,5},{13,9},{2,6},{14,10},{3,7},{15,11},{16,20},{28,... | collective-permute-start | bytes 491528 | tf_op jit(solution)/shard_map/ppermute | solution.py:44
  66.8 14.3 %collective-permute-start.23 = (bf16[320,256]{1,0:T(8,128)(2,1)S(1)}, bf16[320,256]{1,0:T(8,128)(2,1)S(1)}, u32[]{:S(2)}, u32[]{:S(2)}) collective-permute-start(bf16[320,256]{1,0:T(8,128)(2,1)S(1)} %get-tuple-element.2), channel_id=1, source_target_pairs={{0,4},{12,8},{1,5},{13,9},{2,6},{14,10},{3,7},{15,11},{16,20},{28,... | collective-permute-start | bytes 491528 | tf_op jit(solution)/shard_map/ppermute | solution.py:44
  70.1 13.9 %collective-permute-start.3 = (bf16[704,256]{1,0:T(8,128)(2,1)S(1)}, bf16[704,256]{1,0:T(8,128)(2,1)S(1)}, u32[]{:S(2)}, u32[]{:S(2)}) collective-permute-start(bf16[704,256]{1,0:T(8,128)(2,1)S(1)} %dynamic-slice_convert_fusion.7), channel_id=1, source_target_pairs={{4,8},{8,4},{5,9},{9,5},{6,10},{10,6},{7,11},{11,7},{20,24},{24,20... | collective-permute-start | bytes 1081352 | tf_op jit(solution)/shard_map/ppermute | solution.py:50
  72.9 11.8 %collective-permute-start.6 = (bf16[704,256]{1,0:T(8,128)(2,1)S(1)}, bf16[704,256]{1,0:T(8,128)(2,1)S(1)}, u32[]{:S(2)}, u32[]{:S(2)}) collective-permute-start(bf16[704,256]{1,0:T(8,128)(2,1)S(1)} %dynamic-slice_convert_fusion.6), channel_id=1, source_target_pairs={{4,8},{8,4},{5,9},{9,5},{6,10},{10,6},{7,11},{11,7},{20,24},{24,20... | collective-permute-start | bytes 1081352 | tf_op jit(solution)/shard_map/ppermute | solution.py:50
  75.7 9.8 %collective-permute-start.9 = (bf16[704,256]{1,0:T(8,128)(2,1)S(1)}, bf16[704,256]{1,0:T(8,128)(2,1)S(1)}, u32[]{:S(2)}, u32[]{:S(2)}) collective-permute-start(bf16[704,256]{1,0:T(8,128)(2,1)S(1)} %dynamic-slice_convert_fusion.5), channel_id=1, source_target_pairs={{4,8},{8,4},{5,9},{9,5},{6,10},{10,6},{7,11},{11,7},{20,24},{24,20... | collective-permute-start | bytes 1081352 | tf_op jit(solution)/shard_map/ppermute | solution.py:50
  78.5 7.8 %collective-permute-start.12 = (bf16[704,256]{1,0:T(8,128)(2,1)S(1)}, bf16[704,256]{1,0:T(8,128)(2,1)S(1)}, u32[]{:S(2)}, u32[]{:S(2)}) collective-permute-start(bf16[704,256]{1,0:T(8,128)(2,1)S(1)} %dynamic-slice_convert_fusion.4), channel_id=1, source_target_pairs={{4,8},{8,4},{5,9},{9,5},{6,10},{10,6},{7,11},{11,7},{20,24},{24,20... | collective-permute-start | bytes 1081352 | tf_op jit(solution)/shard_map/ppermute | solution.py:50
  81.1 6.5 %collective-permute-start.15 = (bf16[704,256]{1,0:T(8,128)(2,1)S(1)}, bf16[704,256]{1,0:T(8,128)(2,1)S(1)}, u32[]{:S(2)}, u32[]{:S(2)}) collective-permute-start(bf16[704,256]{1,0:T(8,128)(2,1)S(1)} %dynamic-slice_convert_fusion.3), channel_id=1, source_target_pairs={{4,8},{8,4},{5,9},{9,5},{6,10},{10,6},{7,11},{11,7},{20,24},{24,20... | collective-permute-start | bytes 1081352 | tf_op jit(solution)/shard_map/ppermute | solution.py:50
  86.2 24.3 %collective-permute-start.4 = (bf16[352,256]{1,0:T(8,128)(2,1)S(1)}, bf16[352,256]{1,0:T(8,128)(2,1)S(1)}, u32[]{:S(2)}, u32[]{:S(2)}) collective-permute-start(bf16[352,256]{1,0:T(8,128)(2,1)S(1)} %add_convert_fusion.7), channel_id=1, source_target_pairs={{4,0},{8,12},{5,1},{9,13},{6,2},{10,14},{7,3},{11,15},{20,16},{24,... | collective-permute-start | bytes 540680 | tf_op jit(solution)/shard_map/ppermute | solution.py:55
  87.6 30.6 %collective-permute-start.7 = (bf16[352,256]{1,0:T(8,128)(2,1)S(1)}, bf16[352,256]{1,0:T(8,128)(2,1)S(1)}, u32[]{:S(2)}, u32[]{:S(2)}) collective-permute-start(bf16[352,256]{1,0:T(8,128)(2,1)S(1)} %add_convert_fusion.6), channel_id=1, source_target_pairs={{4,0},{8,12},{5,1},{9,13},{6,2},{10,14},{7,3},{11,15},{20,16},{24,... | collective-permute-start | bytes 540680 | tf_op jit(solution)/shard_map/ppermute | solution.py:55
  89.0 37.0 %collective-permute-start.10 = (bf16[352,256]{1,0:T(8,128)(2,1)S(1)}, bf16[352,256]{1,0:T(8,128)(2,1)S(1)}, u32[]{:S(2)}, u32[]{:S(2)}) collective-permute-start(bf16[352,256]{1,0:T(8,128)(2,1)S(1)} %add_convert_fusion.5), channel_id=1, source_target_pairs={{4,0},{8,12},{5,1},{9,13},{6,2},{10,14},{7,3},{11,15},{20,16},{24,... | collective-permute-start | bytes 540680 | tf_op jit(solution)/shard_map/ppermute | solution.py:55
  90.3 43.3 %collective-permute-start.13 = (bf16[352,256]{1,0:T(8,128)(2,1)S(1)}, bf16[352,256]{1,0:T(8,128)(2,1)S(1)}, u32[]{:S(2)}, u32[]{:S(2)}) collective-permute-start(bf16[352,256]{1,0:T(8,128)(2,1)S(1)} %add_convert_fusion.4), channel_id=1, source_target_pairs={{4,0},{8,12},{5,1},{9,13},{6,2},{10,14},{7,3},{11,15},{20,16},{24,... | collective-permute-start | bytes 540680 | tf_op jit(solution)/shard_map/ppermute | solution.py:55
  91.7 50.3 %collective-permute-start.16 = (bf16[352,256]{1,0:T(8,128)(2,1)S(1)}, bf16[352,256]{1,0:T(8,128)(2,1)S(1)}, u32[]{:S(2)}, u32[]{:S(2)}) collective-permute-start(bf16[352,256]{1,0:T(8,128)(2,1)S(1)} %add_convert_fusion.3), channel_id=1, source_target_pairs={{4,0},{8,12},{5,1},{9,13},{6,2},{10,14},{7,3},{11,15},{20,16},{24,... | collective-permute-start | bytes 540680 | tf_op jit(solution)/shard_map/ppermute | solution.py:55
  110.5 35.4 %collective-permute-start.19 = (bf16[352,256]{1,0:T(8,128)(2,1)S(1)}, bf16[352,256]{1,0:T(8,128)(2,1)S(1)}, u32[]{:S(2)}, u32[]{:S(2)}) collective-permute-start(bf16[352,256]{1,0:T(8,128)(2,1)S(1)} %add_convert_fusion.2), channel_id=1, source_target_pairs={{4,0},{8,12},{5,1},{9,13},{6,2},{10,14},{7,3},{11,15},{20,16},{24,... | collective-permute-start | bytes 540680 | tf_op jit(solution)/shard_map/ppermute | solution.py:55
  118.2 31.5 %collective-permute-start.22 = (bf16[352,256]{1,0:T(8,128)(2,1)S(1)}, bf16[352,256]{1,0:T(8,128)(2,1)S(1)}, u32[]{:S(2)}, u32[]{:S(2)}) collective-permute-start(bf16[352,256]{1,0:T(8,128)(2,1)S(1)} %add_convert_fusion.1), channel_id=1, source_target_pairs={{4,0},{8,12},{5,1},{9,13},{6,2},{10,14},{7,3},{11,15},{20,16},{24,... | collective-permute-start | bytes 540680 | tf_op jit(solution)/shard_map/ppermute | solution.py:55
  126.0 25.7 %collective-permute-start.25 = (bf16[352,256]{1,0:T(8,128)(2,1)S(1)}, bf16[352,256]{1,0:T(8,128)(2,1)S(1)}, u32[]{:S(2)}, u32[]{:S(2)}) collective-permute-start(bf16[352,256]{1,0:T(8,128)(2,1)S(1)} %add_convert_fusion), channel_id=1, source_target_pairs={{4,0},{8,12},{5,1},{9,13},{6,2},{10,14},{7,3},{11,15},{20,16},{24,... | collective-permute-start | bytes 540680 | tf_op jit(solution)/shard_map/ppermute | solution.py:55
  (5 other events, 22.2 us)

commit v4 on v1

--- a/solution.py
+++ b/solution.py
@@ -10,28 +10,38 @@
     return lax.ppermute(value, axis, pairs)
 
 
-def dispatch_block(rows, ids, weights, count, width):
+def dispatch_targets(ids, count, width):
     flat_ids = ids.reshape(-1)
     onehot = (flat_ids[:, None] == jnp.arange(count, dtype=jnp.int32)[None, :]).astype(jnp.int32)
     position = jnp.sum((jnp.cumsum(onehot, axis=0) - 1) * onehot, axis=1)
-    target = flat_ids * width + position
-    scaled = (weights[:, :, None] * rows[:, None, :].astype(jnp.float32)).astype(jnp.bfloat16)
-    scaled = scaled.reshape(-1, rows.shape[1])
-    buffer = jnp.zeros((count * width, rows.shape[1]), jnp.bfloat16).at[target].set(scaled)
-    return buffer.reshape(count, width, rows.shape[1])
+    return (flat_ids * width + position).reshape(ids.shape)
 
 
-def line_weight_grad(saved, scaled, chunks):
+def dispatch_rows(rows, weights, target, count, width):
+    slots = count * width
+    total = None
+    for k in range(target.shape[1]):
+        scaled = (weights[:, k:k + 1] * rows.astype(jnp.float32)).astype(jnp.bfloat16)
+        onehot = lax.broadcasted_iota(jnp.int32, (slots, rows.shape[0]), 0) == target[None, :, k]
+        term = jnp.dot(onehot.astype(jnp.bfloat16), scaled, preferred_element_type=jnp.float32)
+        total = term if total is None else total + term
+    return total.astype(jnp.bfloat16).reshape(count, width, rows.shape[1])
+
+
+def send_hidden(saved):
+    d = lax.axis_index("dp")
+    blk = saved.shape[1] // 4
+    column_block = lax.broadcasted_iota(jnp.int32, saved.shape, 1) // blk
+    hsend = jnp.where(column_block == d, jnp.zeros_like(saved), saved)
+    return lax.ppermute(hsend, "dp", [(0, 1), (3, 2)])
+
+
+def line_weight_grad(saved, hfull, scaled, chunks):
     d = lax.axis_index("dp")
     hid = saved.shape[1]
     blk = hid // 4
     width = scaled.shape[1] // chunks
     ends = [(0, 1), (3, 2)]
-    hsend = lax.dynamic_slice_in_dim(saved, jnp.where(d == 0, blk, 0), hid - blk, axis=1)
-    hrecv = lax.ppermute(hsend, "dp", ends)
-    hfull = lax.dynamic_update_slice_in_dim(
-        jnp.zeros_like(saved), hrecv, jnp.where(d == 1, blk, 0), axis=1
-    )
     lhs = jnp.concatenate([saved, hfull], axis=0)
     row2 = jnp.where(d == 1, 2 * blk, 0)
     row3a = jnp.where(d == 1, 0, 3 * blk)
@@ -58,7 +68,7 @@
         pieces.append(
             lax.dynamic_slice_in_dim(acc, own, blk, axis=0) + extra.astype(jnp.float32)
         )
-    return jnp.concatenate(pieces, axis=1)
+    return jnp.concatenate(pieces, axis=1), s2
 
 
 def shards(grad_out, routes, gates, hidden, w_down):
@@ -69,14 +79,17 @@
     slot_count = saved.shape[0]
     width = slot_count // groups
     model_width = incoming.shape[1]
-    outgoing = dispatch_block(incoming, routes[0], gates[0], groups, width)
+    target = dispatch_targets(routes[0], groups, width)
+    outgoing = dispatch_rows(incoming, gates[0], target, groups, width)
+    line = lax.axis_size("dp") == 4 and saved.shape[1] % 4 == 0
+    if line:
+        hfull = send_hidden(saved)
+        outgoing, hfull = lax.optimization_barrier((outgoing, hfull))
     piece = lax.all_to_all(outgoing, "expert", split_axis=0, concat_axis=0, tiled=True)
-    grad_rows_out = jnp.einsum(
-        "skd,hd->skh", piece, weight, preferred_element_type=jnp.float32
-    ).astype(jnp.bfloat16)
     scaled = piece.reshape(slot_count, model_width)
-    if lax.axis_size("dp") == 4 and saved.shape[1] % 4 == 0:
-        weight_grad = line_weight_grad(saved, scaled, 4)
+    if line:
+        weight_grad, anchor = line_weight_grad(saved, hfull, scaled, 4)
+        late, _ = lax.optimization_barrier((scaled, anchor))
     else:
         full = lax.dot_general(
             saved, scaled, (((0,), (0,)), ((), ())), preferred_element_type=jnp.float32
@@ -84,6 +97,10 @@
         weight_grad = lax.psum_scatter(
             full.astype(jnp.bfloat16), "dp", scatter_dimension=0, tiled=True
         ).astype(jnp.float32)
+        late = scaled
+    grad_rows_out = jnp.einsum(
+        "sd,hd->sh", late, weight, preferred_element_type=jnp.float32
+    ).astype(jnp.bfloat16)
     grad_hidden = grad_rows_out.reshape(1, 1, 1, slot_count, saved.shape[1])
     return (grad_hidden, weight_grad.reshape(1, 1, weight_grad.shape[0], model_width))
 

time: 141 us -> 139 us (0.986)
  blocking collectives: 0 us -> 19.9 us
  local copies, waits for them, and re-layouts: 15.7 us -> 3.88 us
  starting transfers between devices: 28.7 us -> 24.4 us
  waiting for transfers between devices: 75.3 us -> 71.7 us
  other arithmetic: 8.38 us -> 5.61 us
    all_to_all x0 -> x1, blocking collectives: none -> 19.9 us  [shards(): lax.all_to_all(outgoing, 'expert', split_axis=0, concat_axis=0, tiled=True)]
    all_to_all x1 -> x0, waiting for transfers between devices: 11.9 us -> none  [shards(): lax.all_to_all(outgoing, 'expert', split_axis=0, concat_axis=0, tiled=True)]
    ppermute x1, waiting for transfers between devices: 0.01 us -> 10.5 us  [send_hidden(): return lax.ppermute(hsend, 'dp', [(0, 1), (3, 2)])]
    ppermute x4, waiting for transfers between devices: 7.27 us -> 13.4 us  [line_weight_grad(): srecv = lax.ppermute(sc, 'dp', ends)]
    dynamic_update_slice x1 -> x0, local copies, waits for them, and re-layouts: 5.12 us -> none  [line_weight_grad(): lax.dynamic_update_slice_in_dim(jnp.zeros_like(saved), hrecv, jnp.where(d...]
    mul x5 -> x1, local copies, waits for them, and re-layouts: 5.6 us -> 0.77 us  [dispatch_rows(): weights[:, k:k + 1] * rows.astype(jnp.float32)]
    ppermute x1, waiting for transfers between devices: 7.54 us -> 3.4 us  [shifted(): return lax.ppermute(value, axis, pairs)]
    ppermute x4, waiting for transfers between devices: 48.5 us -> 44.4 us  [line_weight_grad(): r3 = lax.ppermute(s3, 'dp', [(1, 0), (2, 3)])]
  transfers between devices with their start and end apart: 15 -> 14, of which waited for: 9 -> 10; matrix products, arithmetic and copies ran while one was open for 17% -> 13% of each run, Pallas kernels for 0% -> 0%
where the time goes in v4:
time: 139 us; the launch traced here: 138 us
  waiting for transfers between devices  71.7 us (52%)
  starting transfers between devices  24.4 us (18%)
  blocking collectives  19.9 us (14%)
  matrix products  12 us (9%)
  other arithmetic  5.61 us (4%)
  local copies, waits for them, and re-layouts  3.88 us (3%)
    ppermute x4, waiting for transfers between devices, line_weight_grad(): r3 = lax.ppermute(s3, 'dp', [(1, 0), (2, 3)])  44.4 us
    all_to_all x1, blocking collectives, shards(): lax.all_to_all(outgoing, 'expert', split_axis=0, concat_axis=0, tiled=True)  19.9 us
    ppermute x4, waiting for transfers between devices, line_weight_grad(): srecv = lax.ppermute(sc, 'dp', ends)  13.4 us
    ppermute x1, waiting for transfers between devices, send_hidden(): return lax.ppermute(hsend, 'dp', [(0, 1), (3, 2)])  10.5 us
    ppermute x4, starting transfers between devices, line_weight_grad(): srecv = lax.ppermute(sc, 'dp', ends)  9.74 us
    dot_general x4, matrix products, line_weight_grad(): lax.dot_general(lhs, rhs, (((0,), (0,)), ((), ())), preferred_element_typ...  7.55 us
    ppermute x4, starting transfers between devices, line_weight_grad(): r3 = lax.ppermute(s3, 'dp', [(1, 0), (2, 3)])  5.17 us
    ppermute x1, starting transfers between devices, send_hidden(): return lax.ppermute(hsend, 'dp', [(0, 1), (3, 2)])  3.54 us
  transfers between devices with their start and end apart: 14, of which 10 were waited for; matrix products, arithmetic and copies ran while one was open for 13% of the time, Pallas kernels for 0%

profile of v4, /device:TPU:0, one launch (start us, length us, event | category | flops | bytes accessed | tf_op | source)
XLA Modules:
  0.0 138.5 jit_solution(3023919356687036452)
XLA Ops:
  0.6 3.0 %collective-permute-start = (bf16[1,128,2048]{2,1,0:T(8,128)(2,1)}, bf16[1,128,2048]{2,1,0:T(8,128)(2,1)S(1)}, u32[]{:S(2)}, u32[]{:S(2)}) collective-permute-start(bf16[1,128,2048]{2,1,0:T(8,128)(2,1)} %param.5), channel_id=1, source_target_pairs={{0,16},{16,0},{1,17},{17,1},{2,18},{18,2},{3,19},{19,3},{4,20},{20... | collective-permute-start | bytes 1572872 | tf_op jit(solution)/shard_map/ppermute | solution.py:10
  3.7 1.3 fusion.9
  5.0 3.5 %collective-permute-start.1 = (bf16[320,1408]{1,0:T(8,128)(2,1)S(1)}, bf16[320,1408]{1,0:T(8,128)(2,1)S(1)}, u32[]{:S(2)}, u32[]{:S(2)}) collective-permute-start(bf16[320,1408]{1,0:T(8,128)(2,1)S(1)} %fusion.9), channel_id=1, source_target_pairs={{0,4},{12,8},{1,5},{13,9},{2,6},{14,10},{3,7},{15,11},{16,20},{28,... | collective-permute-start | bytes 2703368 | tf_op jit(solution)/shard_map/ppermute | solution.py:36
  12.4 3.4 %collective-permute-done = bf16[1,128,2048]{2,1,0:T(8,128)(2,1)S(1)} collective-permute-done((bf16[1,128,2048]{2,1,0:T(8,128)(2,1)}, bf16[1,128,2048]{2,1,0:T(8,128)(2,1)S(1)}, u32[]{:S(2)}, u32[]{:S(2)}) %collective-permute-start) | collective-permute-done | bytes 524320 | tf_op jit(solution)/shard_map/ppermute | solution.py:10
  17.0 10.5 %collective-permute-done.1 = bf16[320,1408]{1,0:T(8,128)(2,1)S(1)} collective-permute-done((bf16[320,1408]{1,0:T(8,128)(2,1)S(1)}, bf16[320,1408]{1,0:T(8,128)(2,1)S(1)}, u32[]{:S(2)}, u32[]{:S(2)}) %collective-permute-start.1) | collective-permute-done | bytes 901152 | tf_op jit(solution)/shard_map/ppermute | solution.py:36
  28.4 19.9 %all_to_all.5 = bf16[4,80,2048]{2,1,0:T(8,128)(2,1)S(1)} all-to-all(bf16[4,80,2048]{2,1,0:T(8,128)(2,1)S(1)} %bitcast.48), channel_id=1, replica_groups=mesh['section'=2,'dp'=4,'expert'=4] {'expert'}, dimensions={0} | all-to-all | bytes 2621440 | tf_op jit(solution)/shard_map/all_to_all | solution.py:88
  48.5 5.1 %collective-permute-start.2 = (bf16[320,512]{1,0:T(8,128)(2,1)S(1)}, bf16[320,512]{1,0:T(8,128)(2,1)}, u32[]{:S(2)}, u32[]{:S(2)}) collective-permute-start(bf16[320,512]{1,0:T(8,128)(2,1)S(1)} %get-tuple-element.13), channel_id=1, source_target_pairs={{0,4},{12,8},{1,5},{13,9},{2,6},{14,10},{3,7},{15,11},{16,20},{28,... | collective-permute-start | bytes 983048 | tf_op jit(solution)/shard_map/ppermute | solution.py:55
  53.6 2.0 %collective-permute-start.9 = (bf16[320,512]{1,0:T(8,128)(2,1)S(1)}, bf16[320,512]{1,0:T(8,128)(2,1)}, u32[]{:S(2)}, u32[]{:S(2)}) collective-permute-start(bf16[320,512]{1,0:T(8,128)(2,1)S(1)} %get-tuple-element.11), channel_id=1, source_target_pairs={{0,4},{12,8},{1,5},{13,9},{2,6},{14,10},{3,7},{15,11},{16,20},{28,... | collective-permute-start | bytes 983048 | tf_op jit(solution)/shard_map/ppermute | solution.py:55
  55.6 1.3 collective-permute-start.6
  56.9 1.3 collective-permute-start.3
  58.2 2.7 %collective-permute-done.2 = bf16[320,512]{1,0:T(8,128)(2,1)} collective-permute-done((bf16[320,512]{1,0:T(8,128)(2,1)S(1)}, bf16[320,512]{1,0:T(8,128)(2,1)}, u32[]{:S(2)}, u32[]{:S(2)}) %collective-permute-start.2) | collective-permute-done | bytes 327712 | tf_op jit(solution)/shard_map/ppermute | solution.py:55
  60.9 2.6 %fusion.12 = f32[1408,512]{1,0:T(8,128)S(1)} fusion(bf16[320,512]{1,0:T(8,128)(2,1)} %collective-permute-done.2, bf16[320,512]{1,0:T(8,128)(2,1)S(1)} %get-tuple-element.13, bf16[320,1408]{1,0:T(8,128)(2,1)} %copy-done.1, bf16[320,1408]{1,0:T(8,128)(2,1)S(1)} %bitcast.51), kind=kOutput, calls=%fused_computation.26 | convolution fusion | flops 927662080 | bytes 5341184 | tf_op jit(solution)/shard_map/dot_general | solution.py:57
  64.4 3.5 %collective-permute-done.9 = bf16[320,512]{1,0:T(8,128)(2,1)} collective-permute-done((bf16[320,512]{1,0:T(8,128)(2,1)S(1)}, bf16[320,512]{1,0:T(8,128)(2,1)}, u32[]{:S(2)}, u32[]{:S(2)}) %collective-permute-start.9) | collective-permute-done | bytes 327712 | tf_op jit(solution)/shard_map/ppermute | solution.py:55
  68.0 2.3 %fusion.24 = f32[1408,512]{1,0:T(8,128)S(1)} fusion(bf16[320,512]{1,0:T(8,128)(2,1)} %collective-permute-done.9, bf16[320,512]{1,0:T(8,128)(2,1)S(1)} %get-tuple-element.11, bf16[320,1408]{1,0:T(8,128)(2,1)S(1)} %copy-done.2, bf16[320,1408]{1,0:T(8,128)(2,1)S(1)} %bitcast.52), kind=kOutput, calls=%fused_computation.38 | convolution fusion | flops 927662080 | bytes 5341184 | tf_op jit(solution)/shard_map/dot_general | solution.py:57
  71.1 3.9 %collective-permute-done.6 = bf16[320,512]{1,0:T(8,128)(2,1)S(1)} collective-permute-done((bf16[320,512]{1,0:T(8,128)(2,1)S(1)}, bf16[320,512]{1,0:T(8,128)(2,1)S(1)}, u32[]{:S(2)}, u32[]{:S(2)}) %collective-permute-start.6) | collective-permute-done | bytes 327712 | tf_op jit(solution)/shard_map/ppermute | solution.py:55
  75.0 1.3 fusion.20
  77.3 3.2 %collective-permute-done.3 = bf16[320,512]{1,0:T(8,128)(2,1)S(1)} collective-permute-done((bf16[320,512]{1,0:T(8,128)(2,1)S(1)}, bf16[320,512]{1,0:T(8,128)(2,1)S(1)}, u32[]{:S(2)}, u32[]{:S(2)}) %collective-permute-start.3) | collective-permute-done | bytes 327712 | tf_op jit(solution)/shard_map/ppermute | solution.py:55
  80.5 1.3 fusion.16
  82.7 3.2 %fusion.6 = bf16[1,1,1,320,1408]{4,3,2,1,0:T(8,128)(2,1)} fusion(bf16[320,2048]{1,0:T(8,128)(2,1)S(1)} %bitcast.50, bf16[1,1,1408,2048]{3,2,1,0:T(8,128)(2,1)S(1)} %bitcast.58), kind=kOutput, calls=%fused_computation.6 | convolution fusion | flops 1845944320 | bytes 7979008 | tf_op jit(solution)/shard_map/sd,hd->sh/dot_general | solution.py:101
  91.6 10.0 %collective-permute-done.13 = bf16[352,512]{1,0:T(8,128)(2,1)S(1)} collective-permute-done((bf16[352,512]{1,0:T(8,128)(2,1)S(1)}, bf16[352,512]{1,0:T(8,128)(2,1)S(1)}, u32[]{:S(2)}, u32[]{:S(2)}) %collective-permute-start.13) | collective-permute-done | bytes 360480 | tf_op jit(solution)/shard_map/ppermute | solution.py:66
  101.8 7.6 %collective-permute-done.11 = bf16[352,512]{1,0:T(8,128)(2,1)S(1)} collective-permute-done((bf16[352,512]{1,0:T(8,128)(2,1)S(1)}, bf16[352,512]{1,0:T(8,128)(2,1)S(1)}, u32[]{:S(2)}, u32[]{:S(2)}) %collective-permute-start.11) | collective-permute-done | bytes 360480 | tf_op jit(solution)/shard_map/ppermute | solution.py:66
  109.6 15.3 %collective-permute-done.8 = bf16[352,512]{1,0:T(8,128)(2,1)S(1)} collective-permute-done((bf16[352,512]{1,0:T(8,128)(2,1)S(1)}, bf16[352,512]{1,0:T(8,128)(2,1)S(1)}, u32[]{:S(2)}, u32[]{:S(2)}) %collective-permute-start.8) | collective-permute-done | bytes 360480 | tf_op jit(solution)/shard_map/ppermute | solution.py:66
  125.0 11.5 %collective-permute-done.5 = bf16[352,512]{1,0:T(8,128)(2,1)S(1)} collective-permute-done((bf16[352,512]{1,0:T(8,128)(2,1)S(1)}, bf16[352,512]{1,0:T(8,128)(2,1)S(1)}, u32[]{:S(2)}, u32[]{:S(2)}) %collective-permute-start.5) | collective-permute-done | bytes 360480 | tf_op jit(solution)/shard_map/ppermute | solution.py:66
  136.6 1.8 %maximum_bitcast_fusion = f32[1,1,352,2048]{3,2,1,0:T(8,128)} fusion(f32[352,512]{1,0:T(8,128)S(1)} %convert_add_fusion, f32[352,512]{1,0:T(8,128)S(1)} %convert_add_fusion.1, f32[352,512]{1,0:T(8,128)S(1)} %convert_add_fusion.2, f32[352,512]{1,0:T(8,128)S(1)} %convert_add_fusion.3), kind=kLoop, calls=%fused_computation.2 | loop fusion | flops 2162688 | bytes 5767168 | tf_op jit(solution)/shard_map/reshape | solution.py:105
  (56 shorter events, 15.6 us)
Async XLA Ops:
  0.6 15.2 %collective-permute-start = (bf16[1,128,2048]{2,1,0:T(8,128)(2,1)}, bf16[1,128,2048]{2,1,0:T(8,128)(2,1)S(1)}, u32[]{:S(2)}, u32[]{:S(2)}) collective-permute-start(bf16[1,128,2048]{2,1,0:T(8,128)(2,1)} %param.5), channel_id=1, source_target_pairs={{0,16},{16,0},{1,17},{17,1},{2,18},{18,2},{3,19},{19,3},{4,20},{20... | collective-permute-start | bytes 1572872 | tf_op jit(solution)/shard_map/ppermute | solution.py:10
  5.0 22.4 %collective-permute-start.1 = (bf16[320,1408]{1,0:T(8,128)(2,1)S(1)}, bf16[320,1408]{1,0:T(8,128)(2,1)S(1)}, u32[]{:S(2)}, u32[]{:S(2)}) collective-permute-start(bf16[320,1408]{1,0:T(8,128)(2,1)S(1)} %fusion.9), channel_id=1, source_target_pairs={{0,4},{12,8},{1,5},{13,9},{2,6},{14,10},{3,7},{15,11},{16,20},{28,... | collective-permute-start | bytes 2703368 | tf_op jit(solution)/shard_map/ppermute | solution.py:36
  27.5 0.9 copy-start.1
  28.4 32.6 %copy-start = (bf16[1,1,1,320,1408]{4,3,2,1,0:T(8,128)(2,1)S(1)}, bf16[1,1,1,320,1408]{4,3,2,1,0:T(8,128)(2,1)}, u32[]{:S(2)}) copy-start(bf16[1,1,1,320,1408]{4,3,2,1,0:T(8,128)(2,1)} %param.8) | copy-start | bytes 2703364
  48.5 12.5 %collective-permute-start.2 = (bf16[320,512]{1,0:T(8,128)(2,1)S(1)}, bf16[320,512]{1,0:T(8,128)(2,1)}, u32[]{:S(2)}, u32[]{:S(2)}) collective-permute-start(bf16[320,512]{1,0:T(8,128)(2,1)S(1)} %get-tuple-element.13), channel_id=1, source_target_pairs={{0,4},{12,8},{1,5},{13,9},{2,6},{14,10},{3,7},{15,11},{16,20},{28,... | collective-permute-start | bytes 983048 | tf_op jit(solution)/shard_map/ppermute | solution.py:55
  53.6 14.4 %collective-permute-start.9 = (bf16[320,512]{1,0:T(8,128)(2,1)S(1)}, bf16[320,512]{1,0:T(8,128)(2,1)}, u32[]{:S(2)}, u32[]{:S(2)}) collective-permute-start(bf16[320,512]{1,0:T(8,128)(2,1)S(1)} %get-tuple-element.11), channel_id=1, source_target_pairs={{0,4},{12,8},{1,5},{13,9},{2,6},{14,10},{3,7},{15,11},{16,20},{28,... | collective-permute-start | bytes 983048 | tf_op jit(solution)/shard_map/ppermute | solution.py:55
  55.6 19.4 %collective-permute-start.6 = (bf16[320,512]{1,0:T(8,128)(2,1)S(1)}, bf16[320,512]{1,0:T(8,128)(2,1)S(1)}, u32[]{:S(2)}, u32[]{:S(2)}) collective-permute-start(bf16[320,512]{1,0:T(8,128)(2,1)S(1)} %get-tuple-element.12), channel_id=1, source_target_pairs={{0,4},{12,8},{1,5},{13,9},{2,6},{14,10},{3,7},{15,11},{16,20},{28,... | collective-permute-start | bytes 983048 | tf_op jit(solution)/shard_map/ppermute | solution.py:55
  56.9 23.6 %collective-permute-start.3 = (bf16[320,512]{1,0:T(8,128)(2,1)S(1)}, bf16[320,512]{1,0:T(8,128)(2,1)S(1)}, u32[]{:S(2)}, u32[]{:S(2)}) collective-permute-start(bf16[320,512]{1,0:T(8,128)(2,1)S(1)} %get-tuple-element.10), channel_id=1, source_target_pairs={{0,4},{12,8},{1,5},{13,9},{2,6},{14,10},{3,7},{15,11},{16,20},{28,... | collective-permute-start | bytes 983048 | tf_op jit(solution)/shard_map/ppermute | solution.py:55
  60.9 7.0 %copy-start.2 = (bf16[320,1408]{1,0:T(8,128)(2,1)S(1)}, bf16[320,1408]{1,0:T(8,128)(2,1)}, u32[]{:S(2)}) copy-start(bf16[320,1408]{1,0:T(8,128)(2,1)} %copy-done.1) | copy-start | bytes 2703364
  63.7 22.2 %collective-permute-start.12 = (bf16[704,512]{1,0:T(8,128)(2,1)S(1)}, bf16[704,512]{1,0:T(8,128)(2,1)S(1)}, u32[]{:S(2)}, u32[]{:S(2)}) collective-permute-start(bf16[704,512]{1,0:T(8,128)(2,1)S(1)} %dynamic-slice_convert_fusion.3), channel_id=1, source_target_pairs={{4,8},{8,4},{5,9},{9,5},{6,10},{10,6},{7,11},{11,7},{20,24},{24,20... | collective-permute-start | bytes 2162696 | tf_op jit(solution)/shard_map/ppermute | solution.py:61
  70.4 17.0 %collective-permute-start.10 = (bf16[704,512]{1,0:T(8,128)(2,1)S(1)}, bf16[704,512]{1,0:T(8,128)(2,1)S(1)}, u32[]{:S(2)}, u32[]{:S(2)}) collective-permute-start(bf16[704,512]{1,0:T(8,128)(2,1)S(1)} %dynamic-slice_convert_fusion), channel_id=1, source_target_pairs={{4,8},{8,4},{5,9},{9,5},{6,10},{10,6},{7,11},{11,7},{20,24},{24,20... | collective-permute-start | bytes 2162696 | tf_op jit(solution)/shard_map/ppermute | solution.py:61
  76.3 6.3 %slice-start = ((s8[5767168]{0:T(1024)(128)(4,1)}), s8[4194304]{0:T(1024)(128)(4,1)S(1)}, s32[]{:S(2)}) async-start(s8[5767168]{0:T(1024)(128)(4,1)} %bitcast.57), calls=%async_computation.1 | async-start | bytes 8388608
  76.4 6.2 %slice-start.1 = ((s8[5767168]{0:T(1024)(128)(4,1)}), s8[1572864]{0:T(1024)(128)(4,1)S(1)}, s32[]{:S(2)}) async-start(s8[5767168]{0:T(1024)(128)(4,1)} %bitcast.57), calls=%async_computation.2 | async-start | bytes 3145728
  76.4 12.3 %collective-permute-start.7 = (bf16[704,512]{1,0:T(8,128)(2,1)S(1)}, bf16[704,512]{1,0:T(8,128)(2,1)S(1)}, u32[]{:S(2)}, u32[]{:S(2)}) collective-permute-start(bf16[704,512]{1,0:T(8,128)(2,1)S(1)} %dynamic-slice_convert_fusion.1), channel_id=1, source_target_pairs={{4,8},{8,4},{5,9},{9,5},{6,10},{10,6},{7,11},{11,7},{20,24},{24,20... | collective-permute-start | bytes 2162696 | tf_op jit(solution)/shard_map/ppermute | solution.py:61
  81.9 8.3 %collective-permute-start.4 = (bf16[704,512]{1,0:T(8,128)(2,1)S(1)}, bf16[704,512]{1,0:T(8,128)(2,1)S(1)}, u32[]{:S(2)}, u32[]{:S(2)}) collective-permute-start(bf16[704,512]{1,0:T(8,128)(2,1)S(1)} %dynamic-slice_convert_fusion.2), channel_id=1, source_target_pairs={{4,8},{8,4},{5,9},{9,5},{6,10},{10,6},{7,11},{11,7},{20,24},{24,20... | collective-permute-start | bytes 2162696 | tf_op jit(solution)/shard_map/ppermute | solution.py:61
  86.0 15.6 %collective-permute-start.13 = (bf16[352,512]{1,0:T(8,128)(2,1)S(1)}, bf16[352,512]{1,0:T(8,128)(2,1)S(1)}, u32[]{:S(2)}, u32[]{:S(2)}) collective-permute-start(bf16[352,512]{1,0:T(8,128)(2,1)S(1)} %add_convert_fusion), channel_id=1, source_target_pairs={{4,0},{8,12},{5,1},{9,13},{6,2},{10,14},{7,3},{11,15},{20,16},{24,... | collective-permute-start | bytes 1081352 | tf_op jit(solution)/shard_map/ppermute | solution.py:66
  87.5 22.0 %collective-permute-start.11 = (bf16[352,512]{1,0:T(8,128)(2,1)S(1)}, bf16[352,512]{1,0:T(8,128)(2,1)S(1)}, u32[]{:S(2)}, u32[]{:S(2)}) collective-permute-start(bf16[352,512]{1,0:T(8,128)(2,1)S(1)} %add_convert_fusion.1), channel_id=1, source_target_pairs={{4,0},{8,12},{5,1},{9,13},{6,2},{10,14},{7,3},{11,15},{20,16},{24,... | collective-permute-start | bytes 1081352 | tf_op jit(solution)/shard_map/ppermute | solution.py:66
  88.9 36.0 %collective-permute-start.8 = (bf16[352,512]{1,0:T(8,128)(2,1)S(1)}, bf16[352,512]{1,0:T(8,128)(2,1)S(1)}, u32[]{:S(2)}, u32[]{:S(2)}) collective-permute-start(bf16[352,512]{1,0:T(8,128)(2,1)S(1)} %add_convert_fusion.2), channel_id=1, source_target_pairs={{4,0},{8,12},{5,1},{9,13},{6,2},{10,14},{7,3},{11,15},{20,16},{24,... | collective-permute-start | bytes 1081352 | tf_op jit(solution)/shard_map/ppermute | solution.py:66
  90.3 46.1 %collective-permute-start.5 = (bf16[352,512]{1,0:T(8,128)(2,1)S(1)}, bf16[352,512]{1,0:T(8,128)(2,1)S(1)}, u32[]{:S(2)}, u32[]{:S(2)}) collective-permute-start(bf16[352,512]{1,0:T(8,128)(2,1)S(1)} %add_convert_fusion.3), channel_id=1, source_target_pairs={{4,0},{8,12},{5,1},{9,13},{6,2},{10,14},{7,3},{11,15},{20,16},{24,... | collective-permute-start | bytes 1081352 | tf_op jit(solution)/shard_map/ppermute | solution.py:66

commit v5 on v4

--- a/solution.py
+++ b/solution.py
@@ -36,11 +36,16 @@
     return lax.ppermute(hsend, "dp", [(0, 1), (3, 2)])
 
 
-def line_weight_grad(saved, hfull, scaled, chunks):
+def line_weight_grad(saved, hfull, scaled):
     d = lax.axis_index("dp")
     hid = saved.shape[1]
     blk = hid // 4
-    width = scaled.shape[1] // chunks
+    model_width = scaled.shape[1]
+    if model_width % 2048 == 0:
+        unit = model_width // 8
+        widths = [unit, 3 * unit, 3 * unit, unit]
+    else:
+        widths = [model_width]
     ends = [(0, 1), (3, 2)]
     lhs = jnp.concatenate([saved, hfull], axis=0)
     row2 = jnp.where(d == 1, 2 * blk, 0)
@@ -50,15 +55,25 @@
     half = jnp.where(d == 1, blk, 0)
     edge = (d == 0) | (d == 3)
     pieces = []
-    for c in range(chunks):
-        sc = scaled[:, c * width:(c + 1) * width]
-        srecv = lax.ppermute(sc, "dp", ends)
+    srecv = None
+    landed = []
+    begin = 0
+    for width in widths:
+        sc = scaled[:, begin:begin + width]
+        begin += width
+        sent = sc
+        if srecv is not None:
+            sent, _ = lax.optimization_barrier((sc, srecv))
+        srecv = lax.ppermute(sent, "dp", ends)
         rhs = jnp.concatenate([sc, srecv], axis=0)
         acc = lax.dot_general(
             lhs, rhs, (((0,), (0,)), ((), ())), preferred_element_type=jnp.float32
         )
         s2 = lax.dynamic_slice_in_dim(acc, row2, 2 * blk, axis=0).astype(jnp.bfloat16)
+        if len(landed) >= 2:
+            s2, _ = lax.optimization_barrier((s2, landed[-2]))
         r2 = lax.ppermute(s2, "dp", [(1, 2), (2, 1)])
+        landed.append(r2)
         s3 = (
             lax.dynamic_slice_in_dim(acc, row3a, blk, axis=0)
             + lax.dynamic_slice_in_dim(r2, row3b, blk, axis=0).astype(jnp.float32)
@@ -84,11 +99,12 @@
     line = lax.axis_size("dp") == 4 and saved.shape[1] % 4 == 0
     if line:
         hfull = send_hidden(saved)
-        outgoing, hfull = lax.optimization_barrier((outgoing, hfull))
     piece = lax.all_to_all(outgoing, "expert", split_axis=0, concat_axis=0, tiled=True)
     scaled = piece.reshape(slot_count, model_width)
     if line:
-        weight_grad, anchor = line_weight_grad(saved, hfull, scaled, 4)
+        scaled, hfull = lax.optimization_barrier((scaled, hfull))
+    if line:
+        weight_grad, anchor = line_weight_grad(saved, hfull, scaled)
         late, _ = lax.optimization_barrier((scaled, anchor))
     else:
         full = lax.dot_general(

time: 139 us -> 159 us (1.14)
  starting transfers between devices: 24.4 us -> 62.2 us
  blocking collectives: 19.9 us -> 0 us
  waiting for transfers between devices: 71.7 us -> 61.9 us
  matrix products: 12 us -> 18.8 us
  local copies, waits for them, and re-layouts: 3.88 us -> 8.43 us
    ppermute x4, starting transfers between devices: 9.74 us -> 42.4 us  [line_weight_grad(): srecv = lax.ppermute(sent, 'dp', ends)]
    ppermute x4, waiting for transfers between devices: 44.4 us -> 22.9 us  [line_weight_grad(): r3 = lax.ppermute(s3, 'dp', [(1, 0), (2, 3)])]
    all_to_all x1 -> x0, blocking collectives: 19.9 us -> none  [shards(): lax.all_to_all(outgoing, 'expert', split_axis=0, concat_axis=0, tiled=True)]
    ppermute x1, waiting for transfers between devices: 10.5 us -> 18.9 us  [send_hidden(): return lax.ppermute(hsend, 'dp', [(0, 1), (3, 2)])]
    ppermute x1, waiting for transfers between devices: 3.4 us -> 8.28 us  [shifted(): return lax.ppermute(value, axis, pairs)]
    all_to_all x0 -> x1, starting transfers between devices: none -> 3.67 us  [shards(): lax.all_to_all(outgoing, 'expert', split_axis=0, concat_axis=0, tiled=True)]
    dot_general x4, matrix products: 7.55 us -> 10.8 us  [line_weight_grad(): lax.dot_general(lhs, rhs, (((0,), (0,)), ((), ())), preferred_element_typ...]
    dot_general x1, matrix products: 3.23 us -> 5.79 us  [shards(): jnp.einsum('sd,hd->sh', late, weight, preferred_element_type=jnp.float32)]
  transfers between devices with their start and end apart: 14 -> 15, of which waited for: 10 -> 8; matrix products, arithmetic and copies ran while one was open for 13% -> 17% of each run, Pallas kernels for 0% -> 0%
where the time goes in v5:
time: 159 us
  starting transfers between devices  62.2 us (39%)
  waiting for transfers between devices  61.9 us (39%)
  matrix products  18.8 us (12%)
  local copies, waits for them, and re-layouts  8.43 us (5%)
  other arithmetic  6.37 us (4%)
    ppermute x4, starting transfers between devices, line_weight_grad(): srecv = lax.ppermute(sent, 'dp', ends)  42.4 us
    ppermute x4, waiting for transfers between devices, line_weight_grad(): r3 = lax.ppermute(s3, 'dp', [(1, 0), (2, 3)])  22.9 us
    ppermute x1, waiting for transfers between devices, send_hidden(): return lax.ppermute(hsend, 'dp', [(0, 1), (3, 2)])  18.9 us
    ppermute x4, waiting for transfers between devices, line_weight_grad(): srecv = lax.ppermute(sent, 'dp', ends)  11.8 us
    dot_general x4, matrix products, line_weight_grad(): lax.dot_general(lhs, rhs, (((0,), (0,)), ((), ())), preferred_element_typ...  10.8 us
    ppermute x1, waiting for transfers between devices, shifted(): return lax.ppermute(value, axis, pairs)  8.28 us
    dot_general x1, matrix products, shards(): jnp.einsum('sd,hd->sh', late, weight, preferred_element_type=jnp.float32)  5.79 us
    ppermute x4, starting transfers between devices, line_weight_grad(): r3 = lax.ppermute(s3, 'dp', [(1, 0), (2, 3)])  5.48 us
  transfers between devices with their start and end apart: 15, of which 8 were waited for; matrix products, arithmetic and copies ran while one was open for 17% of the time, Pallas kernels for 0%

profile of v5, /device:TPU:0, one launch (start us, length us, event | category | flops | bytes accessed | tf_op | source)
XLA Modules:
  0.0 158.7 jit_solution(2832768854301213752)
XLA Ops:
  0.6 3.0 %collective-permute-start = (bf16[1,128,2048]{2,1,0:T(8,128)(2,1)}, bf16[1,128,2048]{2,1,0:T(8,128)(2,1)S(1)}, u32[]{:S(2)}, u32[]{:S(2)}) collective-permute-start(bf16[1,128,2048]{2,1,0:T(8,128)(2,1)} %param.5), channel_id=1, source_target_pairs={{0,16},{16,0},{1,17},{17,1},{2,18},{18,2},{3,19},{19,3},{4,20},{20... | collective-permute-start | bytes 1572872 | tf_op jit(solution)/shard_map/ppermute | solution.py:10
  7.5 8.3 %collective-permute-done = bf16[1,128,2048]{2,1,0:T(8,128)(2,1)S(1)} collective-permute-done((bf16[1,128,2048]{2,1,0:T(8,128)(2,1)}, bf16[1,128,2048]{2,1,0:T(8,128)(2,1)S(1)}, u32[]{:S(2)}, u32[]{:S(2)}) %collective-permute-start) | collective-permute-done | bytes 524320 | tf_op jit(solution)/shard_map/ppermute | solution.py:10
  16.4 1.7 %fusion.5 = bf16[320,2048]{1,0:T(8,128)(2,1)} fusion(f32[320,2048]{1,0:T(8,128)S(1)} %fusion.20, bf16[1,128,2048]{2,1,0:T(8,128)(2,1)S(1)} %collective-permute-done, f32[128]{0:T(128)S(1)} %get-tuple-element.24, s32[128]{0:T(128)S(1)} %get-tuple-element.18), kind=kOutput, calls=%fused_computation.5 | convolution fusion | flops 169910272 | bytes 4457472 | tf_op jit(solution)/shard_map/dot_general | solution.py:26
  18.0 3.7 %all-to-all-start = ((bf16[4,80,2048]{2,1,0:T(8,128)(2,1)}), bf16[4,80,2048]{2,1,0:T(8,128)(2,1)S(1)}, u32[]{:S(2)}, u32[]{:S(2)}) async-start(bf16[4,80,2048]{2,1,0:T(8,128)(2,1)} %bitcast.8), calls=%async_computation | async-start | bytes 2621440 | tf_op jit(solution)/shard_map/all_to_all | solution.py:102
  21.9 4.7 %collective-permute-start.1 = (bf16[320,1408]{1,0:T(8,128)(2,1)S(1)}, bf16[320,1408]{1,0:T(8,128)(2,1)}, u32[]{:S(2)}, u32[]{:S(2)}) collective-permute-start(bf16[320,1408]{1,0:T(8,128)(2,1)S(1)} %fusion.9), channel_id=1, source_target_pairs={{0,4},{12,8},{1,5},{13,9},{2,6},{14,10},{3,7},{15,11},{16,20},{28,... | collective-permute-start | bytes 2703368 | tf_op jit(solution)/shard_map/ppermute | solution.py:36
  26.6 18.9 %collective-permute-done.1 = bf16[320,1408]{1,0:T(8,128)(2,1)} collective-permute-done((bf16[320,1408]{1,0:T(8,128)(2,1)S(1)}, bf16[320,1408]{1,0:T(8,128)(2,1)}, u32[]{:S(2)}, u32[]{:S(2)}) %collective-permute-start.1) | collective-permute-done | bytes 901152 | tf_op jit(solution)/shard_map/ppermute | solution.py:36
  46.2 4.5 %collective-permute-start.2 = (bf16[320,256]{1,0:T(8,128)(2,1)S(1)}, bf16[320,256]{1,0:T(8,128)(2,1)S(1)}, u32[]{:S(2)}, u32[]{:S(2)}) collective-permute-start(bf16[320,256]{1,0:T(8,128)(2,1)S(1)} %get-tuple-element.20), channel_id=1, source_target_pairs={{0,4},{12,8},{1,5},{13,9},{2,6},{14,10},{3,7},{15,11},{16,20},{28,... | collective-permute-start | bytes 491528 | tf_op jit(solution)/shard_map/ppermute | solution.py:67
  51.5 2.3 %collective-permute-done.2 = bf16[320,256]{1,0:T(8,128)(2,1)S(1)} collective-permute-done((bf16[320,256]{1,0:T(8,128)(2,1)S(1)}, bf16[320,256]{1,0:T(8,128)(2,1)S(1)}, u32[]{:S(2)}, u32[]{:S(2)}) %collective-permute-start.2) | collective-permute-done | bytes 163872 | tf_op jit(solution)/shard_map/ppermute | solution.py:67
  53.9 5.2 %collective-permute-start.3 = (bf16[320,768]{1,0:T(8,128)(2,1)S(1)}, bf16[320,768]{1,0:T(8,128)(2,1)}, u32[]{:S(2)}, u32[]{:S(2)}) collective-permute-start(bf16[320,768]{1,0:T(8,128)(2,1)S(1)} %get-tuple-element.12), channel_id=1, source_target_pairs={{0,4},{12,8},{1,5},{13,9},{2,6},{14,10},{3,7},{15,11},{16,20},{28,... | collective-permute-start | bytes 1474568 | tf_op jit(solution)/shard_map/ppermute | solution.py:67
  59.0 1.9 %fusion.31 = f32[1408,256]{1,0:T(8,128)S(1)} fusion(bf16[320,256]{1,0:T(8,128)(2,1)S(1)} %collective-permute-done.2, bf16[320,256]{1,0:T(8,128)(2,1)S(1)} %get-tuple-element.20, bf16[320,1408]{1,0:T(8,128)(2,1)} %collective-permute-done.1, bf16[320,1408]{1,0:T(8,128)(2,1)S(1)} %bitcast.52), kind=kOutput, calls=%fused_computation.43 | convolution fusion | flops 465633280 | bytes 3571712 | tf_op jit(solution)/shard_map/dot_general | solution.py:69
  61.0 6.6 %collective-permute-done.3 = bf16[320,768]{1,0:T(8,128)(2,1)} collective-permute-done((bf16[320,768]{1,0:T(8,128)(2,1)S(1)}, bf16[320,768]{1,0:T(8,128)(2,1)}, u32[]{:S(2)}, u32[]{:S(2)}) %collective-permute-start.3) | collective-permute-done | bytes 491552 | tf_op jit(solution)/shard_map/ppermute | solution.py:67
  67.6 4.5 %collective-permute-start.4 = (bf16[320,768]{1,0:T(8,128)(2,1)}, bf16[320,768]{1,0:T(8,128)(2,1)S(1)}, u32[]{:S(2)}, u32[]{:S(2)}) collective-permute-start(bf16[320,768]{1,0:T(8,128)(2,1)} %get-tuple-element.13), channel_id=1, source_target_pairs={{0,4},{12,8},{1,5},{13,9},{2,6},{14,10},{3,7},{15,11},{16,20},{28,... | collective-permute-start | bytes 1474568 | tf_op jit(solution)/shard_map/ppermute | solution.py:67
  72.1 3.2 %fusion.12 = f32[1408,768]{1,0:T(8,128)S(1)} fusion(bf16[320,768]{1,0:T(8,128)(2,1)} %collective-permute-done.3, bf16[320,768]{1,0:T(8,128)(2,1)S(1)} %get-tuple-element.12, bf16[320,1408]{1,0:T(8,128)(2,1)} %collective-permute-done.1, bf16[320,1408]{1,0:T(8,128)(2,1)S(1)} %bitcast.53), kind=kOutput, calls=%fused_computation.20 | convolution fusion | flops 1389690880 | bytes 7110656 | tf_op jit(solution)/shard_map/dot_general | solution.py:69
  78.1 2.8 %collective-permute-done.4 = bf16[320,768]{1,0:T(8,128)(2,1)S(1)} collective-permute-done((bf16[320,768]{1,0:T(8,128)(2,1)}, bf16[320,768]{1,0:T(8,128)(2,1)S(1)}, u32[]{:S(2)}, u32[]{:S(2)}) %collective-permute-start.4) | collective-permute-done | bytes 491552 | tf_op jit(solution)/shard_map/ppermute | solution.py:67
  80.9 3.2 %fusion.16 = f32[1408,768]{1,0:T(8,128)S(1)} fusion(bf16[320,768]{1,0:T(8,128)(2,1)S(1)} %collective-permute-done.4, bf16[320,768]{1,0:T(8,128)(2,1)} %get-tuple-element.13, bf16[320,1408]{1,0:T(8,128)(2,1)} %collective-permute-done.1, bf16[320,1408]{1,0:T(8,128)(2,1)S(1)} %bitcast.54), kind=kOutput, calls=%fused_computation.24 | convolution fusion | flops 1389690880 | bytes 7110656 | tf_op jit(solution)/shard_map/dot_general | solution.py:69
  88.0 28.2 %collective-permute-start.5 = (bf16[320,256]{1,0:T(8,128)(2,1)}, bf16[320,256]{1,0:T(8,128)(2,1)}, u32[]{:S(2)}, u32[]{:S(2)}) collective-permute-start(bf16[320,256]{1,0:T(8,128)(2,1)} %get-tuple-element.14), channel_id=1, source_target_pairs={{0,4},{12,8},{1,5},{13,9},{2,6},{14,10},{3,7},{15,11},{16,20},{28,... | collective-permute-start | bytes 491528 | tf_op jit(solution)/shard_map/ppermute | solution.py:67
  117.3 1.4 collective-permute-start.8
  118.8 2.4 %fusion.27 = f32[1408,256]{1,0:T(8,128)S(1)} fusion(bf16[320,256]{1,0:T(8,128)(2,1)} %collective-permute-done.5, bf16[320,256]{1,0:T(8,128)(2,1)} %get-tuple-element.14, bf16[320,1408]{1,0:T(8,128)(2,1)} %collective-permute-done.1, bf16[320,1408]{1,0:T(8,128)(2,1)} %bitcast.51), kind=kOutput, calls=%fused_computation.39 | convolution fusion | flops 465633280 | bytes 3571712 | tf_op jit(solution)/shard_map/dot_general | solution.py:69
  122.1 2.7 %collective-permute-done.8 = bf16[352,256]{1,0:T(8,128)(2,1)S(1)} collective-permute-done((bf16[352,256]{1,0:T(8,128)(2,1)S(1)}, bf16[352,256]{1,0:T(8,128)(2,1)S(1)}, u32[]{:S(2)}, u32[]{:S(2)}) %collective-permute-start.8) | collective-permute-done | bytes 180256 | tf_op jit(solution)/shard_map/ppermute | solution.py:81
  128.9 1.5 collective-permute-start.11
  130.4 5.8 %fusion.6 = bf16[1,1,1,320,1408]{4,3,2,1,0:T(8,128)(2,1)} fusion(bf16[320,2048]{1,0:T(8,128)(2,1)S(1)} %bitcast.50, bf16[1,1,1408,2048]{3,2,1,0:T(8,128)(2,1)} %param.9), kind=kOutput, calls=%fused_computation.6 | convolution fusion | flops 1845944320 | bytes 7979008 | tf_op jit(solution)/shard_map/sd,hd->sh/dot_general | solution.py:117
  136.2 13.4 %collective-permute-done.13 = bf16[352,256]{1,0:T(8,128)(2,1)S(1)} collective-permute-done((bf16[352,256]{1,0:T(8,128)(2,1)S(1)}, bf16[352,256]{1,0:T(8,128)(2,1)S(1)}, u32[]{:S(2)}, u32[]{:S(2)}) %collective-permute-start.13) | collective-permute-done | bytes 180256 | tf_op jit(solution)/shard_map/ppermute | solution.py:81
  149.8 6.8 %collective-permute-done.11 = bf16[352,768]{1,0:T(8,128)(2,1)S(1)} collective-permute-done((bf16[352,768]{1,0:T(8,128)(2,1)S(1)}, bf16[352,768]{1,0:T(8,128)(2,1)S(1)}, u32[]{:S(2)}, u32[]{:S(2)}) %collective-permute-start.11) | collective-permute-done | bytes 540704 | tf_op jit(solution)/shard_map/ppermute | solution.py:81
  156.8 1.9 %maximum_bitcast_fusion = f32[1,1,352,2048]{3,2,1,0:T(8,128)} fusion(f32[352,256]{1,0:T(8,128)S(1)} %convert_add_fusion.2, f32[352,768]{1,0:T(8,128)S(1)} %convert_add_fusion, f32[352,768]{1,0:T(8,128)S(1)} %convert_add_fusion.1, f32[352,256]{1,0:T(8,128)S(1)} %convert_add_fusion.3), kind=kLoop, calls=%fused_computation.2 | loop fusion | flops 2162688 | bytes 5767168 | tf_op jit(solution)/shard_map/reshape | solution.py:121
  (63 shorter events, 19.0 us)
Async XLA Ops:
  0.6 15.2 %collective-permute-start = (bf16[1,128,2048]{2,1,0:T(8,128)(2,1)}, bf16[1,128,2048]{2,1,0:T(8,128)(2,1)S(1)}, u32[]{:S(2)}, u32[]{:S(2)}) collective-permute-start(bf16[1,128,2048]{2,1,0:T(8,128)(2,1)} %param.5), channel_id=1, source_target_pairs={{0,16},{16,0},{1,17},{17,1},{2,18},{18,2},{3,19},{19,3},{4,20},{20... | collective-permute-start | bytes 1572872 | tf_op jit(solution)/shard_map/ppermute | solution.py:10
  18.0 3.7 %copy-start.4 = (bf16[1,1,1,320,1408]{4,3,2,1,0:T(8,128)(2,1)S(1)}, bf16[1,1,1,320,1408]{4,3,2,1,0:T(8,128)(2,1)}, u32[]{:S(2)}) copy-start(bf16[1,1,1,320,1408]{4,3,2,1,0:T(8,128)(2,1)} %param.8) | copy-start | bytes 2703364
  18.0 27.5 %all-to-all-start = ((bf16[4,80,2048]{2,1,0:T(8,128)(2,1)}), bf16[4,80,2048]{2,1,0:T(8,128)(2,1)S(1)}, u32[]{:S(2)}, u32[]{:S(2)}) async-start(bf16[4,80,2048]{2,1,0:T(8,128)(2,1)} %bitcast.8), calls=%async_computation | async-start | bytes 2621440 | tf_op jit(solution)/shard_map/all_to_all | solution.py:102
  21.9 23.6 %collective-permute-start.1 = (bf16[320,1408]{1,0:T(8,128)(2,1)S(1)}, bf16[320,1408]{1,0:T(8,128)(2,1)}, u32[]{:S(2)}, u32[]{:S(2)}) collective-permute-start(bf16[320,1408]{1,0:T(8,128)(2,1)S(1)} %fusion.9), channel_id=1, source_target_pairs={{0,4},{12,8},{1,5},{13,9},{2,6},{14,10},{3,7},{15,11},{16,20},{28,... | collective-permute-start | bytes 2703368 | tf_op jit(solution)/shard_map/ppermute | solution.py:36
  46.2 7.7 %collective-permute-start.2 = (bf16[320,256]{1,0:T(8,128)(2,1)S(1)}, bf16[320,256]{1,0:T(8,128)(2,1)S(1)}, u32[]{:S(2)}, u32[]{:S(2)}) collective-permute-start(bf16[320,256]{1,0:T(8,128)(2,1)S(1)} %get-tuple-element.20), channel_id=1, source_target_pairs={{0,4},{12,8},{1,5},{13,9},{2,6},{14,10},{3,7},{15,11},{16,20},{28,... | collective-permute-start | bytes 491528 | tf_op jit(solution)/shard_map/ppermute | solution.py:67
  53.9 13.8 %collective-permute-start.3 = (bf16[320,768]{1,0:T(8,128)(2,1)S(1)}, bf16[320,768]{1,0:T(8,128)(2,1)}, u32[]{:S(2)}, u32[]{:S(2)}) collective-permute-start(bf16[320,768]{1,0:T(8,128)(2,1)S(1)} %get-tuple-element.12), channel_id=1, source_target_pairs={{0,4},{12,8},{1,5},{13,9},{2,6},{14,10},{3,7},{15,11},{16,20},{28,... | collective-permute-start | bytes 1474568 | tf_op jit(solution)/shard_map/ppermute | solution.py:67
  61.0 16.4 %copy-start.5 = (f32[1408,256]{1,0:T(8,128)}, f32[1408,256]{1,0:T(8,128)S(1)}, u32[]{:S(2)}) copy-start(f32[1408,256]{1,0:T(8,128)S(1)} %fusion.31) | copy-start | bytes 4325380
  67.6 13.3 %collective-permute-start.4 = (bf16[320,768]{1,0:T(8,128)(2,1)}, bf16[320,768]{1,0:T(8,128)(2,1)S(1)}, u32[]{:S(2)}, u32[]{:S(2)}) collective-permute-start(bf16[320,768]{1,0:T(8,128)(2,1)} %get-tuple-element.13), channel_id=1, source_target_pairs={{0,4},{12,8},{1,5},{13,9},{2,6},{14,10},{3,7},{15,11},{16,20},{28,... | collective-permute-start | bytes 1474568 | tf_op jit(solution)/shard_map/ppermute | solution.py:67
  75.4 8.8 %copy-start = (f32[1408,768]{1,0:T(8,128)}, f32[1408,768]{1,0:T(8,128)S(1)}, u32[]{:S(2)}) copy-start(f32[1408,768]{1,0:T(8,128)S(1)} %fusion.12) | copy-start | bytes 12976132
  76.6 44.7 %collective-permute-start.6 = (bf16[704,768]{1,0:T(8,128)(2,1)}, bf16[704,768]{1,0:T(8,128)(2,1)S(1)}, u32[]{:S(2)}, u32[]{:S(2)}) collective-permute-start(bf16[704,768]{1,0:T(8,128)(2,1)} %dynamic-slice_convert_fusion.1), channel_id=1, source_target_pairs={{4,8},{8,4},{5,9},{9,5},{6,10},{10,6},{7,11},{11,7},{20,24},{24,20... | collective-permute-start | bytes 3244040 | tf_op jit(solution)/shard_map/ppermute | solution.py:75
  77.4 9.1 %collective-permute-start.7 = (bf16[704,256]{1,0:T(8,128)(2,1)S(1)}, bf16[704,256]{1,0:T(8,128)(2,1)S(1)}, u32[]{:S(2)}, u32[]{:S(2)}) collective-permute-start(bf16[704,256]{1,0:T(8,128)(2,1)S(1)} %dynamic-slice_convert_fusion.2), channel_id=1, source_target_pairs={{4,8},{8,4},{5,9},{9,5},{6,10},{10,6},{7,11},{11,7},{20,24},{24,20... | collective-permute-start | bytes 1081352 | tf_op jit(solution)/shard_map/ppermute | solution.py:75
  84.2 2.4 %copy-start.2 = (f32[1408,768]{1,0:T(8,128)}, f32[1408,768]{1,0:T(8,128)S(1)}, u32[]{:S(2)}) copy-start(f32[1408,768]{1,0:T(8,128)S(1)} %fusion.16) | copy-start | bytes 12976132
  86.5 0.7 copy-start.6
  87.3 41.4 %collective-permute-start.10 = (bf16[704,768]{1,0:T(8,128)(2,1)}, bf16[704,768]{1,0:T(8,128)(2,1)S(1)}, u32[]{:S(2)}, u32[]{:S(2)}) collective-permute-start(bf16[704,768]{1,0:T(8,128)(2,1)} %dynamic-slice_convert_fusion), channel_id=1, source_target_pairs={{4,8},{8,4},{5,9},{9,5},{6,10},{10,6},{7,11},{11,7},{20,24},{24,20... | collective-permute-start | bytes 3244040 | tf_op jit(solution)/shard_map/ppermute | solution.py:75
  88.0 30.8 %collective-permute-start.5 = (bf16[320,256]{1,0:T(8,128)(2,1)}, bf16[320,256]{1,0:T(8,128)(2,1)}, u32[]{:S(2)}, u32[]{:S(2)}) collective-permute-start(bf16[320,256]{1,0:T(8,128)(2,1)} %get-tuple-element.14), channel_id=1, source_target_pairs={{0,4},{12,8},{1,5},{13,9},{2,6},{14,10},{3,7},{15,11},{16,20},{28,... | collective-permute-start | bytes 491528 | tf_op jit(solution)/shard_map/ppermute | solution.py:67
  117.3 7.5 %copy-start.7 = (bf16[704,256]{1,0:T(8,128)(2,1)S(1)}, bf16[704,256]{1,0:T(8,128)(2,1)}, u32[]{:S(2)}) copy-start(bf16[704,256]{1,0:T(8,128)(2,1)} %copy-done.6) | copy-start | bytes 1081348
  117.3 7.5 %collective-permute-start.8 = (bf16[352,256]{1,0:T(8,128)(2,1)S(1)}, bf16[352,256]{1,0:T(8,128)(2,1)S(1)}, u32[]{:S(2)}, u32[]{:S(2)}) collective-permute-start(bf16[352,256]{1,0:T(8,128)(2,1)S(1)} %add_convert_fusion.3), channel_id=1, source_target_pairs={{4,0},{8,12},{5,1},{9,13},{6,2},{10,14},{7,3},{11,15},{20,16},{24,... | collective-permute-start | bytes 540680 | tf_op jit(solution)/shard_map/ppermute | solution.py:81
  118.8 7.1 %copy-start.1 = (f32[1408,768]{1,0:T(8,128)S(1)}, f32[1408,768]{1,0:T(8,128)}, u32[]{:S(2)}) copy-start(f32[1408,768]{1,0:T(8,128)} %copy-done) | copy-start | bytes 12976132
  121.2 7.5 %copy-start.3 = (f32[1408,768]{1,0:T(8,128)S(1)}, f32[1408,768]{1,0:T(8,128)}, u32[]{:S(2)}) copy-start(f32[1408,768]{1,0:T(8,128)} %copy-done.2) | copy-start | bytes 12976132
  121.3 6.1 %collective-permute-start.12 = (bf16[704,256]{1,0:T(8,128)(2,1)S(1)}, bf16[704,256]{1,0:T(8,128)(2,1)S(1)}, u32[]{:S(2)}, u32[]{:S(2)}) collective-permute-start(bf16[704,256]{1,0:T(8,128)(2,1)S(1)} %dynamic-slice_convert_fusion.3), channel_id=1, source_target_pairs={{4,8},{8,4},{5,9},{9,5},{6,10},{10,6},{7,11},{11,7},{20,24},{24,20... | collective-permute-start | bytes 1081352 | tf_op jit(solution)/shard_map/ppermute | solution.py:75
  126.1 23.5 %collective-permute-start.9 = (bf16[352,768]{1,0:T(8,128)(2,1)S(1)}, bf16[352,768]{1,0:T(8,128)(2,1)S(1)}, u32[]{:S(2)}, u32[]{:S(2)}) collective-permute-start(bf16[352,768]{1,0:T(8,128)(2,1)S(1)} %add_convert_fusion.1), channel_id=1, source_target_pairs={{4,0},{8,12},{5,1},{9,13},{6,2},{10,14},{7,3},{11,15},{20,16},{24,... | collective-permute-start | bytes 1622024 | tf_op jit(solution)/shard_map/ppermute | solution.py:81
  127.4 22.1 %collective-permute-start.13 = (bf16[352,256]{1,0:T(8,128)(2,1)S(1)}, bf16[352,256]{1,0:T(8,128)(2,1)S(1)}, u32[]{:S(2)}, u32[]{:S(2)}) collective-permute-start(bf16[352,256]{1,0:T(8,128)(2,1)S(1)} %add_convert_fusion.2), channel_id=1, source_target_pairs={{4,0},{8,12},{5,1},{9,13},{6,2},{10,14},{7,3},{11,15},{20,16},{24,... | collective-permute-start | bytes 540680 | tf_op jit(solution)/shard_map/ppermute | solution.py:81
  128.9 27.7 %collective-permute-start.11 = (bf16[352,768]{1,0:T(8,128)(2,1)S(1)}, bf16[352,768]{1,0:T(8,128)(2,1)S(1)}, u32[]{:S(2)}, u32[]{:S(2)}) collective-permute-start(bf16[352,768]{1,0:T(8,128)(2,1)S(1)} %add_convert_fusion), channel_id=1, source_target_pairs={{4,0},{8,12},{5,1},{9,13},{6,2},{10,14},{7,3},{11,15},{20,16},{24,... | collective-permute-start | bytes 1622024 | tf_op jit(solution)/shard_map/ppermute | solution.py:81

commit v6 on v4

--- a/solution.py
+++ b/solution.py
@@ -84,7 +84,6 @@
     line = lax.axis_size("dp") == 4 and saved.shape[1] % 4 == 0
     if line:
         hfull = send_hidden(saved)
-        outgoing, hfull = lax.optimization_barrier((outgoing, hfull))
     piece = lax.all_to_all(outgoing, "expert", split_axis=0, concat_axis=0, tiled=True)
     scaled = piece.reshape(slot_count, model_width)
     if line:

time: 139 us -> 135 us (0.971)
  blocking collectives: 19.9 us -> 0 us
  waiting for transfers between devices: 71.7 us -> 80.4 us
  starting transfers between devices: 24.4 us -> 28.6 us
  matrix products: 12 us -> 15.8 us
    all_to_all x1 -> x0, blocking collectives: 19.9 us -> none  [shards(): lax.all_to_all(outgoing, 'expert', split_axis=0, concat_axis=0, tiled=True)]
    all_to_all x0 -> x1, waiting for transfers between devices: none -> 12.3 us  [shards(): lax.all_to_all(outgoing, 'expert', split_axis=0, concat_axis=0, tiled=True)]
    ppermute x1, waiting for transfers between devices: 10.5 us -> 0.01 us  [send_hidden(): return lax.ppermute(hsend, 'dp', [(0, 1), (3, 2)])]
    ppermute x1, waiting for transfers between devices: 3.4 us -> 8.3 us  [shifted(): return lax.ppermute(value, axis, pairs)]
    all_to_all x0 -> x1, starting transfers between devices: none -> 3.54 us  [shards(): lax.all_to_all(outgoing, 'expert', split_axis=0, concat_axis=0, tiled=True)]
    dot_general x4, matrix products: 7.55 us -> 10.3 us  [line_weight_grad(): lax.dot_general(lhs, rhs, (((0,), (0,)), ((), ())), preferred_element_typ...]
  transfers between devices with their start and end apart: 14 -> 15, of which waited for: 10 -> 10; matrix products, arithmetic and copies ran while one was open for 13% -> 15% of each run, Pallas kernels for 0% -> 0%
where the time goes in v6:
time: 135 us; the launch traced here: 134 us
  waiting for transfers between devices  80.4 us (60%)
  starting transfers between devices  28.6 us (21%)
  matrix products  15.8 us (12%)
  other arithmetic  4.44 us (3%)
  local copies, waits for them, and re-layouts  3.81 us (3%)
    ppermute x4, waiting for transfers between devices, line_weight_grad(): r3 = lax.ppermute(s3, 'dp', [(1, 0), (2, 3)])  45.8 us
    ppermute x4, waiting for transfers between devices, line_weight_grad(): srecv = lax.ppermute(sc, 'dp', ends)  14 us
    all_to_all x1, waiting for transfers between devices, shards(): lax.all_to_all(outgoing, 'expert', split_axis=0, concat_axis=0, tiled=True)  12.3 us
    dot_general x4, matrix products, line_weight_grad(): lax.dot_general(lhs, rhs, (((0,), (0,)), ((), ())), preferred_element_typ...  10.3 us
    ppermute x4, starting transfers between devices, line_weight_grad(): srecv = lax.ppermute(sc, 'dp', ends)  9.1 us
    ppermute x1, waiting for transfers between devices, shifted(): return lax.ppermute(value, axis, pairs)  8.3 us
    ppermute x4, starting transfers between devices, line_weight_grad(): r3 = lax.ppermute(s3, 'dp', [(1, 0), (2, 3)])  5.17 us
    ppermute x1, starting transfers between devices, send_hidden(): return lax.ppermute(hsend, 'dp', [(0, 1), (3, 2)])  4.67 us
  transfers between devices with their start and end apart: 15, of which 10 were waited for; matrix products, arithmetic and copies ran while one was open for 15% of the time, Pallas kernels for 0%

profile of v6, /device:TPU:0, one launch (start us, length us, event | category | flops | bytes accessed | tf_op | source)
XLA Modules:
  0.0 134.0 jit_solution(17821156181286770699)
XLA Ops:
  0.6 3.0 %collective-permute-start = (bf16[1,128,2048]{2,1,0:T(8,128)(2,1)}, bf16[1,128,2048]{2,1,0:T(8,128)(2,1)S(1)}, u32[]{:S(2)}, u32[]{:S(2)}) collective-permute-start(bf16[1,128,2048]{2,1,0:T(8,128)(2,1)} %param.5), channel_id=1, source_target_pairs={{0,16},{16,0},{1,17},{17,1},{2,18},{18,2},{3,19},{19,3},{4,20},{20... | collective-permute-start | bytes 1572872 | tf_op jit(solution)/shard_map/ppermute | solution.py:10
  7.5 8.3 %collective-permute-done = bf16[1,128,2048]{2,1,0:T(8,128)(2,1)S(1)} collective-permute-done((bf16[1,128,2048]{2,1,0:T(8,128)(2,1)}, bf16[1,128,2048]{2,1,0:T(8,128)(2,1)S(1)}, u32[]{:S(2)}, u32[]{:S(2)}) %collective-permute-start) | collective-permute-done | bytes 524320 | tf_op jit(solution)/shard_map/ppermute | solution.py:10
  16.4 1.7 %fusion.5 = bf16[320,2048]{1,0:T(8,128)(2,1)} fusion(f32[320,2048]{1,0:T(8,128)S(1)} %fusion.28, bf16[1,128,2048]{2,1,0:T(8,128)(2,1)S(1)} %collective-permute-done, f32[128]{0:T(128)S(1)} %get-tuple-element.10, s32[128]{0:T(128)S(1)} %get-tuple-element.4), kind=kOutput, calls=%fused_computation.5 | convolution fusion | flops 169910272 | bytes 4457472 | tf_op jit(solution)/shard_map/dot_general | solution.py:26
  18.0 3.5 %all-to-all-start = ((bf16[4,80,2048]{2,1,0:T(8,128)(2,1)}), bf16[4,80,2048]{2,1,0:T(8,128)(2,1)S(1)}, u32[]{:S(2)}, u32[]{:S(2)}) async-start(bf16[4,80,2048]{2,1,0:T(8,128)(2,1)} %bitcast.8), calls=%async_computation | async-start | bytes 2621440 | tf_op jit(solution)/shard_map/all_to_all | solution.py:87
  21.8 4.7 %collective-permute-start.1 = (bf16[320,1408]{1,0:T(8,128)(2,1)S(1)}, bf16[320,1408]{1,0:T(8,128)(2,1)}, u32[]{:S(2)}, u32[]{:S(2)}) collective-permute-start(bf16[320,1408]{1,0:T(8,128)(2,1)S(1)} %fusion.9), channel_id=1, source_target_pairs={{0,4},{12,8},{1,5},{13,9},{2,6},{14,10},{3,7},{15,11},{16,20},{28,... | collective-permute-start | bytes 2703368 | tf_op jit(solution)/shard_map/ppermute | solution.py:36
  26.5 12.3 %all-to-all-done = bf16[4,80,2048]{2,1,0:T(8,128)(2,1)S(1)} async-done(((bf16[4,80,2048]{2,1,0:T(8,128)(2,1)}), bf16[4,80,2048]{2,1,0:T(8,128)(2,1)S(1)}, u32[]{:S(2)}, u32[]{:S(2)}) %all-to-all-start) | async-done | bytes 1310752 | tf_op jit(solution)/shard_map/all_to_all | solution.py:87
  39.8 4.5 %collective-permute-start.2 = (bf16[320,512]{1,0:T(8,128)(2,1)}, bf16[320,512]{1,0:T(8,128)(2,1)}, u32[]{:S(2)}, u32[]{:S(2)}) collective-permute-start(bf16[320,512]{1,0:T(8,128)(2,1)} %get-tuple-element.9), channel_id=1, source_target_pairs={{0,4},{12,8},{1,5},{13,9},{2,6},{14,10},{3,7},{15,11},{16,20},{28,... | collective-permute-start | bytes 983048 | tf_op jit(solution)/shard_map/ppermute | solution.py:55
  44.2 2.0 %collective-permute-start.9 = (bf16[320,512]{1,0:T(8,128)(2,1)}, bf16[320,512]{1,0:T(8,128)(2,1)}, u32[]{:S(2)}, u32[]{:S(2)}) collective-permute-start(bf16[320,512]{1,0:T(8,128)(2,1)} %get-tuple-element.7), channel_id=1, source_target_pairs={{0,4},{12,8},{1,5},{13,9},{2,6},{14,10},{3,7},{15,11},{16,20},{28,... | collective-permute-start | bytes 983048 | tf_op jit(solution)/shard_map/ppermute | solution.py:55
  46.3 1.3 collective-permute-start.6
  47.6 1.3 collective-permute-start.3
  48.9 4.2 %collective-permute-done.2 = bf16[320,512]{1,0:T(8,128)(2,1)} collective-permute-done((bf16[320,512]{1,0:T(8,128)(2,1)}, bf16[320,512]{1,0:T(8,128)(2,1)}, u32[]{:S(2)}, u32[]{:S(2)}) %collective-permute-start.2) | collective-permute-done | bytes 327712 | tf_op jit(solution)/shard_map/ppermute | solution.py:55
  53.0 2.7 %fusion.12 = f32[1408,512]{1,0:T(8,128)S(1)} fusion(bf16[320,512]{1,0:T(8,128)(2,1)} %collective-permute-done.2, bf16[320,512]{1,0:T(8,128)(2,1)} %get-tuple-element.9, bf16[320,1408]{1,0:T(8,128)(2,1)} %collective-permute-done.1, bf16[320,1408]{1,0:T(8,128)(2,1)S(1)} %bitcast.50), kind=kOutput, calls=%fused_computation.26 | convolution fusion | flops 927662080 | bytes 5341184 | tf_op jit(solution)/shard_map/dot_general | solution.py:57
  56.7 3.4 %collective-permute-done.9 = bf16[320,512]{1,0:T(8,128)(2,1)} collective-permute-done((bf16[320,512]{1,0:T(8,128)(2,1)}, bf16[320,512]{1,0:T(8,128)(2,1)}, u32[]{:S(2)}, u32[]{:S(2)}) %collective-permute-start.9) | collective-permute-done | bytes 327712 | tf_op jit(solution)/shard_map/ppermute | solution.py:55
  60.1 2.7 %fusion.24 = f32[1408,512]{1,0:T(8,128)S(1)} fusion(bf16[320,512]{1,0:T(8,128)(2,1)} %collective-permute-done.9, bf16[320,512]{1,0:T(8,128)(2,1)} %get-tuple-element.7, bf16[320,1408]{1,0:T(8,128)(2,1)} %collective-permute-done.1, bf16[320,1408]{1,0:T(8,128)(2,1)S(1)} %bitcast.51), kind=kOutput, calls=%fused_computation.38 | convolution fusion | flops 927662080 | bytes 5341184 | tf_op jit(solution)/shard_map/dot_general | solution.py:57
  63.6 3.5 %collective-permute-done.6 = bf16[320,512]{1,0:T(8,128)(2,1)S(1)} collective-permute-done((bf16[320,512]{1,0:T(8,128)(2,1)}, bf16[320,512]{1,0:T(8,128)(2,1)S(1)}, u32[]{:S(2)}, u32[]{:S(2)}) %collective-permute-start.6) | collective-permute-done | bytes 327712 | tf_op jit(solution)/shard_map/ppermute | solution.py:55
  67.1 2.5 %fusion.20 = f32[1408,512]{1,0:T(8,128)S(1)} fusion(bf16[320,512]{1,0:T(8,128)(2,1)S(1)} %collective-permute-done.6, bf16[320,512]{1,0:T(8,128)(2,1)S(1)} %copy-done.1, bf16[320,1408]{1,0:T(8,128)(2,1)} %collective-permute-done.1, bf16[320,1408]{1,0:T(8,128)(2,1)S(1)} %bitcast.52), kind=kOutput, calls=%fused_computation.34 | convolution fusion | flops 927662080 | bytes 5341184 | tf_op jit(solution)/shard_map/dot_general | solution.py:57
  70.6 2.9 %collective-permute-done.3 = bf16[320,512]{1,0:T(8,128)(2,1)S(1)} collective-permute-done((bf16[320,512]{1,0:T(8,128)(2,1)S(1)}, bf16[320,512]{1,0:T(8,128)(2,1)S(1)}, u32[]{:S(2)}, u32[]{:S(2)}) %collective-permute-start.3) | collective-permute-done | bytes 327712 | tf_op jit(solution)/shard_map/ppermute | solution.py:55
  73.5 2.5 %fusion.16 = f32[1408,512]{1,0:T(8,128)S(1)} fusion(bf16[320,512]{1,0:T(8,128)(2,1)S(1)} %collective-permute-done.3, bf16[320,512]{1,0:T(8,128)(2,1)S(1)} %get-tuple-element.6, bf16[320,1408]{1,0:T(8,128)(2,1)} %collective-permute-done.1, bf16[320,1408]{1,0:T(8,128)(2,1)S(1)} %bitcast.53), kind=kOutput, calls=%fused_computation.30 | convolution fusion | flops 927662080 | bytes 5341184 | tf_op jit(solution)/shard_map/dot_general | solution.py:57
  76.9 3.2 %fusion.6 = bf16[1,1,1,320,1408]{4,3,2,1,0:T(8,128)(2,1)} fusion(bf16[320,2048]{1,0:T(8,128)(2,1)S(1)} %bitcast.49, bf16[1,1,1408,2048]{3,2,1,0:T(8,128)(2,1)S(1)} %bitcast.57), kind=kOutput, calls=%fused_computation.6 | convolution fusion | flops 1845944320 | bytes 7979008 | tf_op jit(solution)/shard_map/sd,hd->sh/dot_general | solution.py:100
  85.8 10.0 %collective-permute-done.13 = bf16[352,512]{1,0:T(8,128)(2,1)S(1)} collective-permute-done((bf16[352,512]{1,0:T(8,128)(2,1)S(1)}, bf16[352,512]{1,0:T(8,128)(2,1)S(1)}, u32[]{:S(2)}, u32[]{:S(2)}) %collective-permute-start.13) | collective-permute-done | bytes 360480 | tf_op jit(solution)/shard_map/ppermute | solution.py:66
  96.0 6.4 %collective-permute-done.11 = bf16[352,512]{1,0:T(8,128)(2,1)S(1)} collective-permute-done((bf16[352,512]{1,0:T(8,128)(2,1)S(1)}, bf16[352,512]{1,0:T(8,128)(2,1)S(1)}, u32[]{:S(2)}, u32[]{:S(2)}) %collective-permute-start.11) | collective-permute-done | bytes 360480 | tf_op jit(solution)/shard_map/ppermute | solution.py:66
  102.5 14.5 %collective-permute-done.8 = bf16[352,512]{1,0:T(8,128)(2,1)S(1)} collective-permute-done((bf16[352,512]{1,0:T(8,128)(2,1)S(1)}, bf16[352,512]{1,0:T(8,128)(2,1)S(1)}, u32[]{:S(2)}, u32[]{:S(2)}) %collective-permute-start.8) | collective-permute-done | bytes 360480 | tf_op jit(solution)/shard_map/ppermute | solution.py:66
  117.2 14.9 %collective-permute-done.5 = bf16[352,512]{1,0:T(8,128)(2,1)S(1)} collective-permute-done((bf16[352,512]{1,0:T(8,128)(2,1)S(1)}, bf16[352,512]{1,0:T(8,128)(2,1)S(1)}, u32[]{:S(2)}, u32[]{:S(2)}) %collective-permute-start.5) | collective-permute-done | bytes 360480 | tf_op jit(solution)/shard_map/ppermute | solution.py:66
  132.2 1.8 %maximum_bitcast_fusion = f32[1,1,352,2048]{3,2,1,0:T(8,128)} fusion(f32[352,512]{1,0:T(8,128)S(1)} %convert_add_fusion, f32[352,512]{1,0:T(8,128)S(1)} %convert_add_fusion.1, f32[352,512]{1,0:T(8,128)S(1)} %convert_add_fusion.2, f32[352,512]{1,0:T(8,128)S(1)} %convert_add_fusion.3), kind=kLoop, calls=%fused_computation.2 | loop fusion | flops 2162688 | bytes 5767168 | tf_op jit(solution)/shard_map/reshape | solution.py:104
  (55 shorter events, 15.3 us)
Async XLA Ops:
  0.6 15.2 %collective-permute-start = (bf16[1,128,2048]{2,1,0:T(8,128)(2,1)}, bf16[1,128,2048]{2,1,0:T(8,128)(2,1)S(1)}, u32[]{:S(2)}, u32[]{:S(2)}) collective-permute-start(bf16[1,128,2048]{2,1,0:T(8,128)(2,1)} %param.5), channel_id=1, source_target_pairs={{0,16},{16,0},{1,17},{17,1},{2,18},{18,2},{3,19},{19,3},{4,20},{20... | collective-permute-start | bytes 1572872 | tf_op jit(solution)/shard_map/ppermute | solution.py:10
  16.4 5.3 %copy-start = (bf16[1,1,1,320,1408]{4,3,2,1,0:T(8,128)(2,1)S(1)}, bf16[1,1,1,320,1408]{4,3,2,1,0:T(8,128)(2,1)}, u32[]{:S(2)}) copy-start(bf16[1,1,1,320,1408]{4,3,2,1,0:T(8,128)(2,1)} %param.8) | copy-start | bytes 2703364
  18.0 20.8 %all-to-all-start = ((bf16[4,80,2048]{2,1,0:T(8,128)(2,1)}), bf16[4,80,2048]{2,1,0:T(8,128)(2,1)S(1)}, u32[]{:S(2)}, u32[]{:S(2)}) async-start(bf16[4,80,2048]{2,1,0:T(8,128)(2,1)} %bitcast.8), calls=%async_computation | async-start | bytes 2621440 | tf_op jit(solution)/shard_map/all_to_all | solution.py:87
  21.8 27.1 %collective-permute-start.1 = (bf16[320,1408]{1,0:T(8,128)(2,1)S(1)}, bf16[320,1408]{1,0:T(8,128)(2,1)}, u32[]{:S(2)}, u32[]{:S(2)}) collective-permute-start(bf16[320,1408]{1,0:T(8,128)(2,1)S(1)} %fusion.9), channel_id=1, source_target_pairs={{0,4},{12,8},{1,5},{13,9},{2,6},{14,10},{3,7},{15,11},{16,20},{28,... | collective-permute-start | bytes 2703368 | tf_op jit(solution)/shard_map/ppermute | solution.py:36
  39.8 13.3 %collective-permute-start.2 = (bf16[320,512]{1,0:T(8,128)(2,1)}, bf16[320,512]{1,0:T(8,128)(2,1)}, u32[]{:S(2)}, u32[]{:S(2)}) collective-permute-start(bf16[320,512]{1,0:T(8,128)(2,1)} %get-tuple-element.9), channel_id=1, source_target_pairs={{0,4},{12,8},{1,5},{13,9},{2,6},{14,10},{3,7},{15,11},{16,20},{28,... | collective-permute-start | bytes 983048 | tf_op jit(solution)/shard_map/ppermute | solution.py:55
  44.2 15.8 %collective-permute-start.9 = (bf16[320,512]{1,0:T(8,128)(2,1)}, bf16[320,512]{1,0:T(8,128)(2,1)}, u32[]{:S(2)}, u32[]{:S(2)}) collective-permute-start(bf16[320,512]{1,0:T(8,128)(2,1)} %get-tuple-element.7), channel_id=1, source_target_pairs={{0,4},{12,8},{1,5},{13,9},{2,6},{14,10},{3,7},{15,11},{16,20},{28,... | collective-permute-start | bytes 983048 | tf_op jit(solution)/shard_map/ppermute | solution.py:55
  46.3 20.8 %collective-permute-start.6 = (bf16[320,512]{1,0:T(8,128)(2,1)}, bf16[320,512]{1,0:T(8,128)(2,1)S(1)}, u32[]{:S(2)}, u32[]{:S(2)}) collective-permute-start(bf16[320,512]{1,0:T(8,128)(2,1)} %get-tuple-element.8), channel_id=1, source_target_pairs={{0,4},{12,8},{1,5},{13,9},{2,6},{14,10},{3,7},{15,11},{16,20},{28,... | collective-permute-start | bytes 983048 | tf_op jit(solution)/shard_map/ppermute | solution.py:55
  47.6 25.9 %collective-permute-start.3 = (bf16[320,512]{1,0:T(8,128)(2,1)S(1)}, bf16[320,512]{1,0:T(8,128)(2,1)S(1)}, u32[]{:S(2)}, u32[]{:S(2)}) collective-permute-start(bf16[320,512]{1,0:T(8,128)(2,1)S(1)} %get-tuple-element.6), channel_id=1, source_target_pairs={{0,4},{12,8},{1,5},{13,9},{2,6},{14,10},{3,7},{15,11},{16,20},{28,... | collective-permute-start | bytes 983048 | tf_op jit(solution)/shard_map/ppermute | solution.py:55
  55.8 11.3 %copy-start.1 = (bf16[320,512]{1,0:T(8,128)(2,1)S(1)}, bf16[320,512]{1,0:T(8,128)(2,1)}, u32[]{:S(2)}) copy-start(bf16[320,512]{1,0:T(8,128)(2,1)} %get-tuple-element.8) | copy-start | bytes 983044
  55.8 24.3 %collective-permute-start.12 = (bf16[704,512]{1,0:T(8,128)(2,1)S(1)}, bf16[704,512]{1,0:T(8,128)(2,1)S(1)}, u32[]{:S(2)}, u32[]{:S(2)}) collective-permute-start(bf16[704,512]{1,0:T(8,128)(2,1)S(1)} %dynamic-slice_convert_fusion.3), channel_id=1, source_target_pairs={{4,8},{8,4},{5,9},{9,5},{6,10},{10,6},{7,11},{11,7},{20,24},{24,20... | collective-permute-start | bytes 2162696 | tf_op jit(solution)/shard_map/ppermute | solution.py:61
  62.8 18.7 %collective-permute-start.10 = (bf16[704,512]{1,0:T(8,128)(2,1)S(1)}, bf16[704,512]{1,0:T(8,128)(2,1)S(1)}, u32[]{:S(2)}, u32[]{:S(2)}) collective-permute-start(bf16[704,512]{1,0:T(8,128)(2,1)S(1)} %dynamic-slice_convert_fusion), channel_id=1, source_target_pairs={{4,8},{8,4},{5,9},{9,5},{6,10},{10,6},{7,11},{11,7},{20,24},{24,20... | collective-permute-start | bytes 2162696 | tf_op jit(solution)/shard_map/ppermute | solution.py:61
  69.6 7.2 %slice-start = ((s8[5767168]{0:T(1024)(128)(4,1)}), s8[4194304]{0:T(1024)(128)(4,1)S(1)}, s32[]{:S(2)}) async-start(s8[5767168]{0:T(1024)(128)(4,1)} %bitcast.56), calls=%async_computation.1 | async-start | bytes 8388608
  69.7 7.1 %slice-start.1 = ((s8[5767168]{0:T(1024)(128)(4,1)}), s8[1572864]{0:T(1024)(128)(4,1)S(1)}, s32[]{:S(2)}) async-start(s8[5767168]{0:T(1024)(128)(4,1)} %bitcast.56), calls=%async_computation.2 | async-start | bytes 3145728
  69.7 13.2 %collective-permute-start.7 = (bf16[704,512]{1,0:T(8,128)(2,1)S(1)}, bf16[704,512]{1,0:T(8,128)(2,1)S(1)}, u32[]{:S(2)}, u32[]{:S(2)}) collective-permute-start(bf16[704,512]{1,0:T(8,128)(2,1)S(1)} %dynamic-slice_convert_fusion.1), channel_id=1, source_target_pairs={{4,8},{8,4},{5,9},{9,5},{6,10},{10,6},{7,11},{11,7},{20,24},{24,20... | collective-permute-start | bytes 2162696 | tf_op jit(solution)/shard_map/ppermute | solution.py:61
  76.1 8.3 %collective-permute-start.4 = (bf16[704,512]{1,0:T(8,128)(2,1)S(1)}, bf16[704,512]{1,0:T(8,128)(2,1)S(1)}, u32[]{:S(2)}, u32[]{:S(2)}) collective-permute-start(bf16[704,512]{1,0:T(8,128)(2,1)S(1)} %dynamic-slice_convert_fusion.2), channel_id=1, source_target_pairs={{4,8},{8,4},{5,9},{9,5},{6,10},{10,6},{7,11},{11,7},{20,24},{24,20... | collective-permute-start | bytes 2162696 | tf_op jit(solution)/shard_map/ppermute | solution.py:61
  80.2 15.6 %collective-permute-start.13 = (bf16[352,512]{1,0:T(8,128)(2,1)S(1)}, bf16[352,512]{1,0:T(8,128)(2,1)S(1)}, u32[]{:S(2)}, u32[]{:S(2)}) collective-permute-start(bf16[352,512]{1,0:T(8,128)(2,1)S(1)} %add_convert_fusion), channel_id=1, source_target_pairs={{4,0},{8,12},{5,1},{9,13},{6,2},{10,14},{7,3},{11,15},{20,16},{24,... | collective-permute-start | bytes 1081352 | tf_op jit(solution)/shard_map/ppermute | solution.py:66
  81.7 20.7 %collective-permute-start.11 = (bf16[352,512]{1,0:T(8,128)(2,1)S(1)}, bf16[352,512]{1,0:T(8,128)(2,1)S(1)}, u32[]{:S(2)}, u32[]{:S(2)}) collective-permute-start(bf16[352,512]{1,0:T(8,128)(2,1)S(1)} %add_convert_fusion.1), channel_id=1, source_target_pairs={{4,0},{8,12},{5,1},{9,13},{6,2},{10,14},{7,3},{11,15},{20,16},{24,... | collective-permute-start | bytes 1081352 | tf_op jit(solution)/shard_map/ppermute | solution.py:66
  83.1 34.0 %collective-permute-start.8 = (bf16[352,512]{1,0:T(8,128)(2,1)S(1)}, bf16[352,512]{1,0:T(8,128)(2,1)S(1)}, u32[]{:S(2)}, u32[]{:S(2)}) collective-permute-start(bf16[352,512]{1,0:T(8,128)(2,1)S(1)} %add_convert_fusion.2), channel_id=1, source_target_pairs={{4,0},{8,12},{5,1},{9,13},{6,2},{10,14},{7,3},{11,15},{20,16},{24,... | collective-permute-start | bytes 1081352 | tf_op jit(solution)/shard_map/ppermute | solution.py:66
  84.5 47.5 %collective-permute-start.5 = (bf16[352,512]{1,0:T(8,128)(2,1)S(1)}, bf16[352,512]{1,0:T(8,128)(2,1)S(1)}, u32[]{:S(2)}, u32[]{:S(2)}) collective-permute-start(bf16[352,512]{1,0:T(8,128)(2,1)S(1)} %add_convert_fusion.3), channel_id=1, source_target_pairs={{4,0},{8,12},{5,1},{9,13},{6,2},{10,14},{7,3},{11,15},{20,16},{24,... | collective-permute-start | bytes 1081352 | tf_op jit(solution)/shard_map/ppermute | solution.py:66

commit v7 on v6

--- a/solution.py
+++ b/solution.py
@@ -49,25 +49,38 @@
     own = d * blk
     half = jnp.where(d == 1, blk, 0)
     edge = (d == 0) | (d == 3)
+
+    def finish(acc, r2, after):
+        part = (
+            lax.dynamic_slice_in_dim(acc, row3a, blk, axis=0)
+            + lax.dynamic_slice_in_dim(r2, row3b, blk, axis=0).astype(jnp.float32)
+        )
+        if after is not None:
+            part, _ = lax.optimization_barrier((part, after))
+        r3 = lax.ppermute(part.astype(jnp.bfloat16), "dp", [(1, 0), (2, 3)])
+        extra = jnp.where(edge, r3, lax.dynamic_slice_in_dim(r2, half, blk, axis=0))
+        return lax.dynamic_slice_in_dim(acc, own, blk, axis=0) + extra.astype(jnp.float32)
+
+    first = lax.ppermute(scaled[:, :width], "dp", ends)
+    second, _ = lax.optimization_barrier((scaled[:, width:2 * width], first))
+    second = lax.ppermute(second, "dp", ends)
+    rest, _ = lax.optimization_barrier((scaled[:, 2 * width:], second))
+    rest = lax.ppermute(rest, "dp", ends)
+    received = [first, second] + [rest[:, c * width:(c + 1) * width] for c in range(chunks - 2)]
     pieces = []
+    held = None
     for c in range(chunks):
         sc = scaled[:, c * width:(c + 1) * width]
-        srecv = lax.ppermute(sc, "dp", ends)
-        rhs = jnp.concatenate([sc, srecv], axis=0)
+        rhs = jnp.concatenate([sc, received[c]], axis=0)
         acc = lax.dot_general(
             lhs, rhs, (((0,), (0,)), ((), ())), preferred_element_type=jnp.float32
         )
         s2 = lax.dynamic_slice_in_dim(acc, row2, 2 * blk, axis=0).astype(jnp.bfloat16)
         r2 = lax.ppermute(s2, "dp", [(1, 2), (2, 1)])
-        s3 = (
-            lax.dynamic_slice_in_dim(acc, row3a, blk, axis=0)
-            + lax.dynamic_slice_in_dim(r2, row3b, blk, axis=0).astype(jnp.float32)
-        ).astype(jnp.bfloat16)
-        r3 = lax.ppermute(s3, "dp", [(1, 0), (2, 3)])
-        extra = jnp.where(edge, r3, lax.dynamic_slice_in_dim(r2, half, blk, axis=0))
-        pieces.append(
-            lax.dynamic_slice_in_dim(acc, own, blk, axis=0) + extra.astype(jnp.float32)
-        )
+        if held is not None:
+            pieces.append(finish(*held, s2))
+        held = (acc, r2)
+    pieces.append(finish(*held, None))
     return jnp.concatenate(pieces, axis=1), s2
 
 

time: 135 us -> 139 us (1.030)
  waiting for transfers between devices: 80.4 us -> 74.7 us
  starting transfers between devices: 28.6 us -> 33.6 us
  local copies, waits for them, and re-layouts: 3.81 us -> 8.27 us
    ppermute x8 -> x7, waiting for transfers between devices: 59.8 us -> 54 us  [the longest x4 38.4 us: finish(): r3 = lax.ppermute(part.astype(jnp.bfloat16), 'dp', [(1, 0), (2, 3)])]
    ppermute x8 -> x7, starting transfers between devices: 14.3 us -> 19.5 us  [the longest x4 5.17 us: finish(): r3 = lax.ppermute(part.astype(jnp.bfloat16), 'dp', [(1, 0), (2, 3)])]
    slice x2 -> x4, local copies, waits for them, and re-layouts: 0.18 us -> 2.21 us  [the longest x1 1.11 us: line_weight_grad(): rest[:, c * width:(c + 1) * width]]
    unnamed x9 -> x13, local copies, waits for them, and re-layouts: 0.81 us -> 2.39 us
  transfers between devices with their start and end apart: 15 -> 14, of which waited for: 10 -> 7; matrix products, arithmetic and copies ran while one was open for 15% -> 17% of each run, Pallas kernels for 0% -> 0%
where the time goes in v7:
time: 139 us; the launch traced here: 138 us
  waiting for transfers between devices  74.7 us (54%)
  starting transfers between devices  33.6 us (24%)
  matrix products  16.2 us (12%)
  local copies, waits for them, and re-layouts  8.27 us (6%)
  other arithmetic  4.47 us (3%)
    ppermute x4, waiting for transfers between devices, finish(): r3 = lax.ppermute(part.astype(jnp.bfloat16), 'dp', [(1, 0), (2, 3)])  38.4 us
    all_to_all x1, waiting for transfers between devices, shards(): lax.all_to_all(outgoing, 'expert', split_axis=0, concat_axis=0, tiled=True)  12.3 us
    dot_general x4, matrix products, line_weight_grad(): lax.dot_general(lhs, rhs, (((0,), (0,)), ((), ())), preferred_element_typ...  10.8 us
    ppermute x1, waiting for transfers between devices, line_weight_grad(): first = lax.ppermute(scaled[:, :width], 'dp', ends)  8.31 us
    ppermute x1, waiting for transfers between devices, shifted(): return lax.ppermute(value, axis, pairs)  8.3 us
    ppermute x1, waiting for transfers between devices, line_weight_grad(): rest = lax.ppermute(rest, 'dp', ends)  7.28 us
    ppermute x4, starting transfers between devices, finish(): r3 = lax.ppermute(part.astype(jnp.bfloat16), 'dp', [(1, 0), (2, 3)])  5.17 us
    ppermute x1, starting transfers between devices, line_weight_grad(): second = lax.ppermute(second, 'dp', ends)  5.14 us
  transfers between devices with their start and end apart: 14, of which 7 were waited for; matrix products, arithmetic and copies ran while one was open for 17% of the time, Pallas kernels for 0%

profile of v7, /device:TPU:0, one launch (start us, length us, event | category | flops | bytes accessed | tf_op | source)
XLA Modules:
  0.0 138.3 jit_solution(12394502772692586729)
XLA Ops:
  0.6 3.0 %collective-permute-start = (bf16[1,128,2048]{2,1,0:T(8,128)(2,1)}, bf16[1,128,2048]{2,1,0:T(8,128)(2,1)S(1)}, u32[]{:S(2)}, u32[]{:S(2)}) collective-permute-start(bf16[1,128,2048]{2,1,0:T(8,128)(2,1)} %param.5), channel_id=1, source_target_pairs={{0,16},{16,0},{1,17},{17,1},{2,18},{18,2},{3,19},{19,3},{4,20},{20... | collective-permute-start | bytes 1572872 | tf_op jit(solution)/shard_map/ppermute | solution.py:10
  7.5 8.3 %collective-permute-done = bf16[1,128,2048]{2,1,0:T(8,128)(2,1)S(1)} collective-permute-done((bf16[1,128,2048]{2,1,0:T(8,128)(2,1)}, bf16[1,128,2048]{2,1,0:T(8,128)(2,1)S(1)}, u32[]{:S(2)}, u32[]{:S(2)}) %collective-permute-start) | collective-permute-done | bytes 524320 | tf_op jit(solution)/shard_map/ppermute | solution.py:10
  16.4 1.7 %fusion.5 = bf16[320,2048]{1,0:T(8,128)(2,1)} fusion(f32[320,2048]{1,0:T(8,128)S(1)} %fusion.28, bf16[1,128,2048]{2,1,0:T(8,128)(2,1)S(1)} %collective-permute-done, f32[128]{0:T(128)S(1)} %get-tuple-element.22, s32[128]{0:T(128)S(1)} %get-tuple-element.14), kind=kOutput, calls=%fused_computation.5 | convolution fusion | flops 169910272 | bytes 4457472 | tf_op jit(solution)/shard_map/dot_general | solution.py:26
  18.0 3.5 %all-to-all-start = ((bf16[4,80,2048]{2,1,0:T(8,128)(2,1)}), bf16[4,80,2048]{2,1,0:T(8,128)(2,1)S(1)}, u32[]{:S(2)}, u32[]{:S(2)}) async-start(bf16[4,80,2048]{2,1,0:T(8,128)(2,1)} %bitcast.8), calls=%async_computation | async-start | bytes 2621440 | tf_op jit(solution)/shard_map/all_to_all | solution.py:100
  21.8 4.7 %collective-permute-start.1 = (bf16[320,1408]{1,0:T(8,128)(2,1)S(1)}, bf16[320,1408]{1,0:T(8,128)(2,1)}, u32[]{:S(2)}, u32[]{:S(2)}) collective-permute-start(bf16[320,1408]{1,0:T(8,128)(2,1)S(1)} %fusion.9), channel_id=1, source_target_pairs={{0,4},{12,8},{1,5},{13,9},{2,6},{14,10},{3,7},{15,11},{16,20},{28,... | collective-permute-start | bytes 2703368 | tf_op jit(solution)/shard_map/ppermute | solution.py:36
  26.5 12.3 %all-to-all-done = bf16[4,80,2048]{2,1,0:T(8,128)(2,1)S(1)} async-done(((bf16[4,80,2048]{2,1,0:T(8,128)(2,1)}), bf16[4,80,2048]{2,1,0:T(8,128)(2,1)S(1)}, u32[]{:S(2)}, u32[]{:S(2)}) %all-to-all-start) | async-done | bytes 1310752 | tf_op jit(solution)/shard_map/all_to_all | solution.py:100
  39.8 4.5 %collective-permute-start.2 = (bf16[320,512]{1,0:T(8,128)(2,1)}, bf16[320,512]{1,0:T(8,128)(2,1)}, u32[]{:S(2)}, u32[]{:S(2)}) collective-permute-start(bf16[320,512]{1,0:T(8,128)(2,1)} %get-tuple-element.17), channel_id=1, source_target_pairs={{0,4},{12,8},{1,5},{13,9},{2,6},{14,10},{3,7},{15,11},{16,20},{28,... | collective-permute-start | bytes 983048 | tf_op jit(solution)/shard_map/ppermute | solution.py:64
  44.2 8.3 %collective-permute-done.2 = bf16[320,512]{1,0:T(8,128)(2,1)} collective-permute-done((bf16[320,512]{1,0:T(8,128)(2,1)}, bf16[320,512]{1,0:T(8,128)(2,1)}, u32[]{:S(2)}, u32[]{:S(2)}) %collective-permute-start.2) | collective-permute-done | bytes 327712 | tf_op jit(solution)/shard_map/ppermute | solution.py:64
  52.5 5.1 %collective-permute-start.3 = (bf16[320,512]{1,0:T(8,128)(2,1)}, bf16[320,512]{1,0:T(8,128)(2,1)}, u32[]{:S(2)}, u32[]{:S(2)}) collective-permute-start(bf16[320,512]{1,0:T(8,128)(2,1)} %get-tuple-element.8), channel_id=1, source_target_pairs={{0,4},{12,8},{1,5},{13,9},{2,6},{14,10},{3,7},{15,11},{16,20},{28,... | collective-permute-start | bytes 983048 | tf_op jit(solution)/shard_map/ppermute | solution.py:66
  57.7 2.7 %fusion.16 = f32[1408,512]{1,0:T(8,128)S(1)} fusion(bf16[320,512]{1,0:T(8,128)(2,1)} %collective-permute-done.2, bf16[320,512]{1,0:T(8,128)(2,1)} %get-tuple-element.17, bf16[320,1408]{1,0:T(8,128)(2,1)} %collective-permute-done.1, bf16[320,1408]{1,0:T(8,128)(2,1)S(1)} %bitcast.51), kind=kOutput, calls=%fused_computation.30 | convolution fusion | flops 927662080 | bytes 5341184 | tf_op jit(solution)/shard_map/dot_general | solution.py:75
  60.4 1.6 %copy-done = f32[1408,512]{1,0:T(8,128)} copy-done((f32[1408,512]{1,0:T(8,128)}, f32[1408,512]{1,0:T(8,128)S(1)}, u32[]{:S(2)}) %copy-start) | copy-done | bytes 2883608
  64.5 4.7 %collective-permute-start.4 = (bf16[320,1024]{1,0:T(8,128)(2,1)}, bf16[320,1024]{1,0:T(8,128)(2,1)}, u32[]{:S(2)}, u32[]{:S(2)}) collective-permute-start(bf16[320,1024]{1,0:T(8,128)(2,1)} %slice.58), channel_id=1, source_target_pairs={{0,4},{12,8},{1,5},{13,9},{2,6},{14,10},{3,7},{15,11},{16,20},{28,... | collective-permute-start | bytes 1966088 | tf_op jit(solution)/shard_map/ppermute | solution.py:68
  69.2 2.8 %fusion.20 = f32[1408,512]{1,0:T(8,128)S(1)} fusion(bf16[320,512]{1,0:T(8,128)(2,1)} %collective-permute-done.3, bf16[320,512]{1,0:T(8,128)(2,1)} %get-tuple-element.8, bf16[320,1408]{1,0:T(8,128)(2,1)} %collective-permute-done.1, bf16[320,1408]{1,0:T(8,128)(2,1)S(1)} %bitcast.52), kind=kOutput, calls=%fused_computation.34 | convolution fusion | flops 927662080 | bytes 5341184 | tf_op jit(solution)/shard_map/dot_general | solution.py:75
  73.0 1.3 collective-permute-start.6
  74.3 7.3 %collective-permute-done.4 = bf16[320,1024]{1,0:T(8,128)(2,1)} collective-permute-done((bf16[320,1024]{1,0:T(8,128)(2,1)}, bf16[320,1024]{1,0:T(8,128)(2,1)}, u32[]{:S(2)}, u32[]{:S(2)}) %collective-permute-start.4) | collective-permute-done | bytes 655392 | tf_op jit(solution)/shard_map/ppermute | solution.py:68
  82.7 2.5 %fusion.12 = f32[1408,512]{1,0:T(8,128)S(1)} fusion(bf16[320,512]{1,0:T(8,128)(2,1)S(1)} %get-tuple-element.21, bf16[320,512]{1,0:T(8,128)(2,1)S(1)} %copy-done.3, bf16[320,1408]{1,0:T(8,128)(2,1)} %collective-permute-done.1, bf16[320,1408]{1,0:T(8,128)(2,1)S(1)} %bitcast.53), kind=kOutput, calls=%fused_computation.26 | convolution fusion | flops 927662080 | bytes 5341184 | tf_op jit(solution)/shard_map/dot_general | solution.py:75
  86.2 2.8 %fusion.24 = f32[1408,512]{1,0:T(8,128)S(1)} fusion(bf16[320,512]{1,0:T(8,128)(2,1)S(1)} %get-tuple-element.20, bf16[320,512]{1,0:T(8,128)(2,1)S(1)} %get-tuple-element.16, bf16[320,1408]{1,0:T(8,128)(2,1)} %collective-permute-done.1, bf16[320,1408]{1,0:T(8,128)(2,1)S(1)} %bitcast.54), kind=kOutput, calls=%fused_computation.38 | convolution fusion | flops 927662080 | bytes 5341184 | tf_op jit(solution)/shard_map/dot_general | solution.py:75
  89.9 3.2 %fusion.6 = bf16[1,1,1,320,1408]{4,3,2,1,0:T(8,128)(2,1)} fusion(bf16[320,2048]{1,0:T(8,128)(2,1)S(1)} %bitcast.50, bf16[1,1,1408,2048]{3,2,1,0:T(8,128)(2,1)S(1)} %bitcast.58), kind=kOutput, calls=%fused_computation.6 | convolution fusion | flops 1845944320 | bytes 7979008 | tf_op jit(solution)/shard_map/sd,hd->sh/dot_general | solution.py:113
  93.2 1.3 collective-permute-start.8
  94.8 1.3 collective-permute-start.12
  97.6 9.7 %collective-permute-done.8 = bf16[352,512]{1,0:T(8,128)(2,1)S(1)} collective-permute-done((bf16[352,512]{1,0:T(8,128)(2,1)S(1)}, bf16[352,512]{1,0:T(8,128)(2,1)S(1)}, u32[]{:S(2)}, u32[]{:S(2)}) %collective-permute-start.8) | collective-permute-done | bytes 360480 | tf_op jit(solution)/shard_map/ppermute | solution.py:60
  107.5 13.4 %collective-permute-done.12 = bf16[352,512]{1,0:T(8,128)(2,1)S(1)} collective-permute-done((bf16[352,512]{1,0:T(8,128)(2,1)S(1)}, bf16[352,512]{1,0:T(8,128)(2,1)S(1)}, u32[]{:S(2)}, u32[]{:S(2)}) %collective-permute-start.12) | collective-permute-done | bytes 360480 | tf_op jit(solution)/shard_map/ppermute | solution.py:60
  121.0 15.3 %collective-permute-done.10 = bf16[352,512]{1,0:T(8,128)(2,1)S(1)} collective-permute-done((bf16[352,512]{1,0:T(8,128)(2,1)S(1)}, bf16[352,512]{1,0:T(8,128)(2,1)S(1)}, u32[]{:S(2)}, u32[]{:S(2)}) %collective-permute-start.10) | collective-permute-done | bytes 360480 | tf_op jit(solution)/shard_map/ppermute | solution.py:60
  136.5 1.8 %maximum_bitcast_fusion = f32[1,1,352,2048]{3,2,1,0:T(8,128)} fusion(f32[352,512]{1,0:T(8,128)S(1)} %convert_add_fusion, f32[352,512]{1,0:T(8,128)S(1)} %convert_add_fusion.1, f32[352,512]{1,0:T(8,128)S(1)} %convert_add_fusion.3, f32[352,512]{1,0:T(8,128)S(1)} %convert_add_fusion.5), kind=kLoop, calls=%fused_computation.2 | loop fusion | flops 2162688 | bytes 5767168 | tf_op jit(solution)/shard_map/reshape | solution.py:117
  (59 shorter events, 14.2 us)
Async XLA Ops:
  0.6 15.2 %collective-permute-start = (bf16[1,128,2048]{2,1,0:T(8,128)(2,1)}, bf16[1,128,2048]{2,1,0:T(8,128)(2,1)S(1)}, u32[]{:S(2)}, u32[]{:S(2)}) collective-permute-start(bf16[1,128,2048]{2,1,0:T(8,128)(2,1)} %param.5), channel_id=1, source_target_pairs={{0,16},{16,0},{1,17},{17,1},{2,18},{18,2},{3,19},{19,3},{4,20},{20... | collective-permute-start | bytes 1572872 | tf_op jit(solution)/shard_map/ppermute | solution.py:10
  16.4 5.3 %copy-start.2 = (bf16[1,1,1,320,1408]{4,3,2,1,0:T(8,128)(2,1)S(1)}, bf16[1,1,1,320,1408]{4,3,2,1,0:T(8,128)(2,1)}, u32[]{:S(2)}) copy-start(bf16[1,1,1,320,1408]{4,3,2,1,0:T(8,128)(2,1)} %param.8) | copy-start | bytes 2703364
  18.0 20.8 %all-to-all-start = ((bf16[4,80,2048]{2,1,0:T(8,128)(2,1)}), bf16[4,80,2048]{2,1,0:T(8,128)(2,1)S(1)}, u32[]{:S(2)}, u32[]{:S(2)}) async-start(bf16[4,80,2048]{2,1,0:T(8,128)(2,1)} %bitcast.8), calls=%async_computation | async-start | bytes 2621440 | tf_op jit(solution)/shard_map/all_to_all | solution.py:100
  21.8 35.9 %collective-permute-start.1 = (bf16[320,1408]{1,0:T(8,128)(2,1)S(1)}, bf16[320,1408]{1,0:T(8,128)(2,1)}, u32[]{:S(2)}, u32[]{:S(2)}) collective-permute-start(bf16[320,1408]{1,0:T(8,128)(2,1)S(1)} %fusion.9), channel_id=1, source_target_pairs={{0,4},{12,8},{1,5},{13,9},{2,6},{14,10},{3,7},{15,11},{16,20},{28,... | collective-permute-start | bytes 2703368 | tf_op jit(solution)/shard_map/ppermute | solution.py:36
  39.8 12.8 %collective-permute-start.2 = (bf16[320,512]{1,0:T(8,128)(2,1)}, bf16[320,512]{1,0:T(8,128)(2,1)}, u32[]{:S(2)}, u32[]{:S(2)}) collective-permute-start(bf16[320,512]{1,0:T(8,128)(2,1)} %get-tuple-element.17), channel_id=1, source_target_pairs={{0,4},{12,8},{1,5},{13,9},{2,6},{14,10},{3,7},{15,11},{16,20},{28,... | collective-permute-start | bytes 983048 | tf_op jit(solution)/shard_map/ppermute | solution.py:64
  52.5 12.0 %collective-permute-start.3 = (bf16[320,512]{1,0:T(8,128)(2,1)}, bf16[320,512]{1,0:T(8,128)(2,1)}, u32[]{:S(2)}, u32[]{:S(2)}) collective-permute-start(bf16[320,512]{1,0:T(8,128)(2,1)} %get-tuple-element.8), channel_id=1, source_target_pairs={{0,4},{12,8},{1,5},{13,9},{2,6},{14,10},{3,7},{15,11},{16,20},{28,... | collective-permute-start | bytes 983048 | tf_op jit(solution)/shard_map/ppermute | solution.py:66
  60.3 1.6 %copy-start = (f32[1408,512]{1,0:T(8,128)}, f32[1408,512]{1,0:T(8,128)S(1)}, u32[]{:S(2)}) copy-start(f32[1408,512]{1,0:T(8,128)S(1)} %fusion.16) | copy-start | bytes 8650756
  62.9 10.0 %collective-permute-start.5 = (bf16[704,512]{1,0:T(8,128)(2,1)}, bf16[704,512]{1,0:T(8,128)(2,1)S(1)}, u32[]{:S(2)}, u32[]{:S(2)}) collective-permute-start(bf16[704,512]{1,0:T(8,128)(2,1)} %dynamic-slice_convert_fusion.2), channel_id=1, source_target_pairs={{4,8},{8,4},{5,9},{9,5},{6,10},{10,6},{7,11},{11,7},{20,24},{24,20... | collective-permute-start | bytes 2162696 | tf_op jit(solution)/shard_map/ppermute | solution.py:79
  64.5 17.1 %collective-permute-start.4 = (bf16[320,1024]{1,0:T(8,128)(2,1)}, bf16[320,1024]{1,0:T(8,128)(2,1)}, u32[]{:S(2)}, u32[]{:S(2)}) collective-permute-start(bf16[320,1024]{1,0:T(8,128)(2,1)} %slice.58), channel_id=1, source_target_pairs={{0,4},{12,8},{1,5},{13,9},{2,6},{14,10},{3,7},{15,11},{16,20},{28,... | collective-permute-start | bytes 1966088 | tf_op jit(solution)/shard_map/ppermute | solution.py:68
  69.2 3.7 %copy-start.1 = (f32[1408,512]{1,0:T(8,128)S(1)}, f32[1408,512]{1,0:T(8,128)}, u32[]{:S(2)}) copy-start(f32[1408,512]{1,0:T(8,128)} %copy-done) | copy-start | bytes 8650756
  72.0 10.7 %copy-start.3 = (bf16[320,512]{1,0:T(8,128)(2,1)S(1)}, bf16[320,512]{1,0:T(8,128)(2,1)}, u32[]{:S(2)}) copy-start(bf16[320,512]{1,0:T(8,128)(2,1)} %get-tuple-element.19) | copy-start | bytes 983044
  72.1 21.0 %collective-permute-start.7 = (bf16[704,512]{1,0:T(8,128)(2,1)S(1)}, bf16[704,512]{1,0:T(8,128)(2,1)S(1)}, u32[]{:S(2)}, u32[]{:S(2)}) collective-permute-start(bf16[704,512]{1,0:T(8,128)(2,1)S(1)} %dynamic-slice_convert_fusion.1), channel_id=1, source_target_pairs={{4,8},{8,4},{5,9},{9,5},{6,10},{10,6},{7,11},{11,7},{20,24},{24,20... | collective-permute-start | bytes 2162696 | tf_op jit(solution)/shard_map/ppermute | solution.py:79
  73.0 21.5 %collective-permute-start.6 = (bf16[352,512]{1,0:T(8,128)(2,1)S(1)}, bf16[352,512]{1,0:T(8,128)(2,1)S(1)}, u32[]{:S(2)}, u32[]{:S(2)}) collective-permute-start(bf16[352,512]{1,0:T(8,128)(2,1)S(1)} %convert_add_fusion.6), channel_id=1, source_target_pairs={{4,0},{8,12},{5,1},{9,13},{6,2},{10,14},{7,3},{11,15},{20,16},{24,... | collective-permute-start | bytes 1081352 | tf_op jit(solution)/shard_map/ppermute | solution.py:60
  85.2 4.6 %slice-start = ((s8[5767168]{0:T(1024)(128)(4,1)}), s8[4194304]{0:T(1024)(128)(4,1)S(1)}, s32[]{:S(2)}) async-start(s8[5767168]{0:T(1024)(128)(4,1)} %bitcast.57), calls=%async_computation.1 | async-start | bytes 8388608
  85.4 9.3 %collective-permute-start.11 = (bf16[704,512]{1,0:T(8,128)(2,1)S(1)}, bf16[704,512]{1,0:T(8,128)(2,1)S(1)}, u32[]{:S(2)}, u32[]{:S(2)}) collective-permute-start(bf16[704,512]{1,0:T(8,128)(2,1)S(1)} %dynamic-slice_convert_fusion.3), channel_id=1, source_target_pairs={{4,8},{8,4},{5,9},{9,5},{6,10},{10,6},{7,11},{11,7},{20,24},{24,20... | collective-permute-start | bytes 2162696 | tf_op jit(solution)/shard_map/ppermute | solution.py:79
  86.2 3.6 %slice-start.1 = ((s8[5767168]{0:T(1024)(128)(4,1)}), s8[1572864]{0:T(1024)(128)(4,1)S(1)}, s32[]{:S(2)}) async-start(s8[5767168]{0:T(1024)(128)(4,1)} %bitcast.57), calls=%async_computation.2 | async-start | bytes 3145728
  89.1 7.0 %collective-permute-start.9 = (bf16[704,512]{1,0:T(8,128)(2,1)S(1)}, bf16[704,512]{1,0:T(8,128)(2,1)S(1)}, u32[]{:S(2)}, u32[]{:S(2)}) collective-permute-start(bf16[704,512]{1,0:T(8,128)(2,1)S(1)} %dynamic-slice_convert_fusion), channel_id=1, source_target_pairs={{4,8},{8,4},{5,9},{9,5},{6,10},{10,6},{7,11},{11,7},{20,24},{24,20... | collective-permute-start | bytes 2162696 | tf_op jit(solution)/shard_map/ppermute | solution.py:79
  93.2 14.1 %collective-permute-start.8 = (bf16[352,512]{1,0:T(8,128)(2,1)S(1)}, bf16[352,512]{1,0:T(8,128)(2,1)S(1)}, u32[]{:S(2)}, u32[]{:S(2)}) collective-permute-start(bf16[352,512]{1,0:T(8,128)(2,1)S(1)} %convert_add_fusion.4), channel_id=1, source_target_pairs={{4,0},{8,12},{5,1},{9,13},{6,2},{10,14},{7,3},{11,15},{20,16},{24,... | collective-permute-start | bytes 1081352 | tf_op jit(solution)/shard_map/ppermute | solution.py:60
  94.8 26.0 %collective-permute-start.12 = (bf16[352,512]{1,0:T(8,128)(2,1)S(1)}, bf16[352,512]{1,0:T(8,128)(2,1)S(1)}, u32[]{:S(2)}, u32[]{:S(2)}) collective-permute-start(bf16[352,512]{1,0:T(8,128)(2,1)S(1)} %add_convert_fusion), channel_id=1, source_target_pairs={{4,0},{8,12},{5,1},{9,13},{6,2},{10,14},{7,3},{11,15},{20,16},{24,... | collective-permute-start | bytes 1081352 | tf_op jit(solution)/shard_map/ppermute | solution.py:60
  96.3 40.0 %collective-permute-start.10 = (bf16[352,512]{1,0:T(8,128)(2,1)S(1)}, bf16[352,512]{1,0:T(8,128)(2,1)S(1)}, u32[]{:S(2)}, u32[]{:S(2)}) collective-permute-start(bf16[352,512]{1,0:T(8,128)(2,1)S(1)} %convert_add_fusion.2), channel_id=1, source_target_pairs={{4,0},{8,12},{5,1},{9,13},{6,2},{10,14},{7,3},{11,15},{20,16},{24,... | collective-permute-start | bytes 1081352 | tf_op jit(solution)/shard_map/ppermute | solution.py:60

commit v8 on v6

--- a/solution.py
+++ b/solution.py
@@ -28,47 +28,45 @@
     return total.astype(jnp.bfloat16).reshape(count, width, rows.shape[1])
 
 
-def send_hidden(saved):
+def cols(array, start, size):
+    return lax.dynamic_slice_in_dim(array, start, size, axis=1)
+
+
+def line_weight_grad(saved, scaled, chunks):
     d = lax.axis_index("dp")
     blk = saved.shape[1] // 4
-    column_block = lax.broadcasted_iota(jnp.int32, saved.shape, 1) // blk
-    hsend = jnp.where(column_block == d, jnp.zeros_like(saved), saved)
-    return lax.ppermute(hsend, "dp", [(0, 1), (3, 2)])
-
-
-def line_weight_grad(saved, hfull, scaled, chunks):
-    d = lax.axis_index("dp")
-    hid = saved.shape[1]
-    blk = hid // 4
+    inner = [(0, 1), (3, 2)]
+    across = [(1, 2), (2, 1)]
+    far = [(0, 2), (3, 1)]
+    back = [(1, 0), (2, 3)]
+    h_near = lax.ppermute(cols(saved, jnp.where(d == 0, blk, 2 * blk), blk), "dp", inner)
+    h_far = lax.ppermute(cols(saved, jnp.where(d == 0, 2 * blk, 0), 2 * blk), "dp", far)
+    h_mid = lax.ppermute(cols(saved, jnp.where(d == 1, 2 * blk, 0), 2 * blk), "dp", across)
+    own_at = jnp.where(d == 1, blk, 0)
+    end_at = jnp.where(d == 1, 0, blk)
+    own_block = jnp.concatenate(
+        [cols(saved, d * blk, blk), h_near, cols(h_mid, own_at, blk), cols(h_far, own_at, blk)], axis=0
+    )
+    end_block = jnp.concatenate(
+        [cols(saved, jnp.where(d == 1, 0, 3 * blk), blk), jnp.zeros_like(h_near),
+         cols(h_mid, end_at, blk), cols(h_far, end_at, blk)], axis=0
+    )
+    lhs = jnp.concatenate([own_block, end_block], axis=1)
+    edge = (d == 0) | (d == 3)
     width = scaled.shape[1] // chunks
-    ends = [(0, 1), (3, 2)]
-    lhs = jnp.concatenate([saved, hfull], axis=0)
-    row2 = jnp.where(d == 1, 2 * blk, 0)
-    row3a = jnp.where(d == 1, 0, 3 * blk)
-    row3b = jnp.where(d == 1, 0, blk)
-    own = d * blk
-    half = jnp.where(d == 1, blk, 0)
-    edge = (d == 0) | (d == 3)
     pieces = []
     for c in range(chunks):
         sc = scaled[:, c * width:(c + 1) * width]
-        srecv = lax.ppermute(sc, "dp", ends)
-        rhs = jnp.concatenate([sc, srecv], axis=0)
+        rhs = jnp.concatenate(
+            [sc, lax.ppermute(sc, "dp", inner), lax.ppermute(sc, "dp", across),
+             lax.ppermute(sc, "dp", far)], axis=0
+        )
         acc = lax.dot_general(
             lhs, rhs, (((0,), (0,)), ((), ())), preferred_element_type=jnp.float32
         )
-        s2 = lax.dynamic_slice_in_dim(acc, row2, 2 * blk, axis=0).astype(jnp.bfloat16)
-        r2 = lax.ppermute(s2, "dp", [(1, 2), (2, 1)])
-        s3 = (
-            lax.dynamic_slice_in_dim(acc, row3a, blk, axis=0)
-            + lax.dynamic_slice_in_dim(r2, row3b, blk, axis=0).astype(jnp.float32)
-        ).astype(jnp.bfloat16)
-        r3 = lax.ppermute(s3, "dp", [(1, 0), (2, 3)])
-        extra = jnp.where(edge, r3, lax.dynamic_slice_in_dim(r2, half, blk, axis=0))
-        pieces.append(
-            lax.dynamic_slice_in_dim(acc, own, blk, axis=0) + extra.astype(jnp.float32)
-        )
-    return jnp.concatenate(pieces, axis=1), s2
+        tail = lax.ppermute(acc[blk:].astype(jnp.bfloat16), "dp", back)
+        pieces.append(acc[:blk] + jnp.where(edge, tail.astype(jnp.float32), 0.0))
+    return jnp.concatenate(pieces, axis=1), tail
 
 
 def shards(grad_out, routes, gates, hidden, w_down):
@@ -82,12 +80,10 @@
     target = dispatch_targets(routes[0], groups, width)
     outgoing = dispatch_rows(incoming, gates[0], target, groups, width)
     line = lax.axis_size("dp") == 4 and saved.shape[1] % 4 == 0
-    if line:
-        hfull = send_hidden(saved)
     piece = lax.all_to_all(outgoing, "expert", split_axis=0, concat_axis=0, tiled=True)
     scaled = piece.reshape(slot_count, model_width)
     if line:
-        weight_grad, anchor = line_weight_grad(saved, hfull, scaled, 4)
+        weight_grad, anchor = line_weight_grad(saved, scaled, 4)
         late, _ = lax.optimization_barrier((scaled, anchor))
     else:
         full = lax.dot_general(

time: 135 us -> 140 us (1.037)
  waiting for transfers between devices: 80.4 us -> 41.7 us
  starting transfers between devices: 28.6 us -> 64.7 us
  other arithmetic: 4.44 us -> 15.5 us
  matrix products: 15.8 us -> 9.96 us
  local copies, waits for them, and re-layouts: 3.81 us -> 6.74 us
    ppermute x13 -> x19, starting transfers between devices: 22 us -> 58 us  [the longest x4 24.5 us: line_weight_grad(): lax.ppermute(sc, 'dp', far)]
    ppermute x13 -> x19, waiting for transfers between devices: 59.8 us -> 33.4 us  [the longest x4 17.1 us: line_weight_grad(): tail = lax.ppermute(acc[blk:].astype(jnp.bfloat16), 'dp', back)]
    all_to_all x1, waiting for transfers between devices: 12.3 us -> 0.01 us  [shards(): lax.all_to_all(outgoing, 'expert', split_axis=0, concat_axis=0, tiled=True)]
    concatenate x0 -> x1, other arithmetic: none -> 11.8 us  [line_weight_grad(): lhs = jnp.concatenate([own_block, end_block], axis=1)]
    dot_general x4, matrix products: 10.3 us -> 4.5 us  [line_weight_grad(): lax.dot_general(lhs, rhs, (((0,), (0,)), ((), ())), preferred_element_typ...]
    dynamic_slice x0 -> x4, local copies, waits for them, and re-layouts: none -> 4 us  [cols(): return lax.dynamic_slice_in_dim(array, start, size, axis=1)]
  transfers between devices with their start and end apart: 15 -> 21, of which waited for: 10 -> 9; matrix products, arithmetic and copies ran while one was open for 15% -> 20% of each run, Pallas kernels for 0% -> 0%
where the time goes in v8:
time: 140 us
  starting transfers between devices  64.7 us (46%)
  waiting for transfers between devices  41.7 us (30%)
  other arithmetic  15.5 us (11%)
  matrix products  9.96 us (7%)
  local copies, waits for them, and re-layouts  6.74 us (5%)
    ppermute x4, starting transfers between devices, line_weight_grad(): lax.ppermute(sc, 'dp', far)  24.5 us
    ppermute x4, waiting for transfers between devices, line_weight_grad(): tail = lax.ppermute(acc[blk:].astype(jnp.bfloat16), 'dp', back)  17.1 us
    ppermute x4, starting transfers between devices, line_weight_grad(): lax.ppermute(sc, 'dp', inner)  16.2 us
    concatenate x1, other arithmetic, line_weight_grad(): lhs = jnp.concatenate([own_block, end_block], axis=1)  11.8 us
    ppermute x1, waiting for transfers between devices, shifted(): return lax.ppermute(value, axis, pairs)  8.3 us
    ppermute x1, waiting for transfers between devices, line_weight_grad(): lax.ppermute(cols(saved, jnp.where(d == 0, 2 * blk, 0), 2 * blk), 'dp', far)  6.45 us
    ppermute x1, starting transfers between devices, line_weight_grad(): lax.ppermute(cols(saved, jnp.where(d == 0, 2 * blk, 0), 2 * blk), 'dp', far)  5.52 us
    ppermute x4, starting transfers between devices, line_weight_grad(): tail = lax.ppermute(acc[blk:].astype(jnp.bfloat16), 'dp', back)  5.14 us
  transfers between devices with their start and end apart: 21, of which 9 were waited for; matrix products, arithmetic and copies ran while one was open for 20% of the time, Pallas kernels for 0%

profile of v8, /device:TPU:0, one launch (start us, length us, event | category | flops | bytes accessed | tf_op | source)
XLA Modules:
  0.0 139.6 jit_solution(8577631127995089446)
XLA Ops:
  0.6 3.0 %collective-permute-start = (bf16[1,128,2048]{2,1,0:T(8,128)(2,1)}, bf16[1,128,2048]{2,1,0:T(8,128)(2,1)S(1)}, u32[]{:S(2)}, u32[]{:S(2)}) collective-permute-start(bf16[1,128,2048]{2,1,0:T(8,128)(2,1)} %param.5), channel_id=1, source_target_pairs={{0,16},{16,0},{1,17},{17,1},{2,18},{18,2},{3,19},{19,3},{4,20},{20... | collective-permute-start | bytes 1572872 | tf_op jit(solution)/shard_map/ppermute | solution.py:10
  7.5 8.3 %collective-permute-done = bf16[1,128,2048]{2,1,0:T(8,128)(2,1)S(1)} collective-permute-done((bf16[1,128,2048]{2,1,0:T(8,128)(2,1)}, bf16[1,128,2048]{2,1,0:T(8,128)(2,1)S(1)}, u32[]{:S(2)}, u32[]{:S(2)}) %collective-permute-start) | collective-permute-done | bytes 524320 | tf_op jit(solution)/shard_map/ppermute | solution.py:10
  16.4 1.7 %fusion.5 = bf16[320,2048]{1,0:T(8,128)(2,1)} fusion(f32[320,2048]{1,0:T(8,128)S(1)} %fusion.43, bf16[1,128,2048]{2,1,0:T(8,128)(2,1)S(1)} %collective-permute-done, f32[128]{0:T(128)S(1)} %get-tuple-element.19, s32[128]{0:T(128)S(1)} %get-tuple-element.4), kind=kOutput, calls=%fused_computation.5 | convolution fusion | flops 169910272 | bytes 4457472 | tf_op jit(solution)/shard_map/dot_general | solution.py:26
  18.0 3.7 %all-to-all-start = ((bf16[4,80,2048]{2,1,0:T(8,128)(2,1)}), bf16[4,80,2048]{2,1,0:T(8,128)(2,1)S(1)}, u32[]{:S(2)}, u32[]{:S(2)}) async-start(bf16[4,80,2048]{2,1,0:T(8,128)(2,1)} %bitcast.8), calls=%async_computation | async-start | bytes 2621440 | tf_op jit(solution)/shard_map/all_to_all | solution.py:83
  21.7 1.4 %dynamic-slice_bitcast_fusion.1 = (bf16[320,704]{1,0:T(8,128)(2,1)}, bf16[320,704]{1,0:T(8,128)(2,1)}) fusion(bf16[1,1,1,320,1408]{4,3,2,1,0:T(8,128)(2,1)S(1)} %copy-done, s32[]{:T(128)S(6)} %select_n.52, s32[]{:T(128)S(6)} %select_n.54), kind=kLoop, calls=%fused_computation.58 | loop fusion | bytes 1802248 | tf_op jit(solution)/shard_map/dynamic_slice | solution.py:32
  23.2 5.5 %collective-permute-start.3 = (bf16[320,704]{1,0:T(8,128)(2,1)}, bf16[320,704]{1,0:T(8,128)(2,1)}, u32[]{:S(2)}, u32[]{:S(2)}) collective-permute-start(bf16[320,704]{1,0:T(8,128)(2,1)} %get-tuple-element.14), channel_id=1, source_target_pairs={{0,8},{12,4},{1,9},{13,5},{2,10},{14,6},{3,11},{15,7},{16,24},{28,... | collective-permute-start | bytes 1351688 | tf_op jit(solution)/shard_map/ppermute | solution.py:43
  30.4 3.0 %collective-permute-start.1 = (bf16[320,352]{1,0:T(8,128)(2,1)}, bf16[320,352]{1,0:T(8,128)(2,1)}, u32[]{:S(2)}, u32[]{:S(2)}) collective-permute-start(bf16[320,352]{1,0:T(8,128)(2,1)} %get-tuple-element.11), channel_id=1, source_target_pairs={{0,4},{12,8},{1,5},{13,9},{2,6},{14,10},{3,7},{15,11},{16,20},{28,... | collective-permute-start | bytes 675848 | tf_op jit(solution)/shard_map/ppermute | solution.py:42
  33.4 6.4 %collective-permute-done.3 = bf16[320,704]{1,0:T(8,128)(2,1)} collective-permute-done((bf16[320,704]{1,0:T(8,128)(2,1)}, bf16[320,704]{1,0:T(8,128)(2,1)}, u32[]{:S(2)}, u32[]{:S(2)}) %collective-permute-start.3) | collective-permute-done | bytes 450592 | tf_op jit(solution)/shard_map/ppermute | solution.py:43
  41.5 13.8 %collective-permute-start.6 = (bf16[320,512]{1,0:T(8,128)(2,1)S(1)}, bf16[320,512]{1,0:T(8,128)(2,1)S(1)}, u32[]{:S(2)}, u32[]{:S(2)}) collective-permute-start(bf16[320,512]{1,0:T(8,128)(2,1)S(1)} %get-tuple-element.9), channel_id=1, source_target_pairs={{0,8},{12,4},{1,9},{13,5},{2,10},{14,6},{3,11},{15,7},{16,24},{28,... | collective-permute-start | bytes 983048 | tf_op jit(solution)/shard_map/ppermute | solution.py:62
  56.1 3.1 %collective-permute-start.4 = (bf16[320,512]{1,0:T(8,128)(2,1)S(1)}, bf16[320,512]{1,0:T(8,128)(2,1)S(1)}, u32[]{:S(2)}, u32[]{:S(2)}) collective-permute-start(bf16[320,512]{1,0:T(8,128)(2,1)S(1)} %get-tuple-element.9), channel_id=1, source_target_pairs={{0,4},{12,8},{1,5},{13,9},{2,6},{14,10},{3,7},{15,11},{16,20},{28,... | collective-permute-start | bytes 983048 | tf_op jit(solution)/shard_map/ppermute | solution.py:61
  59.2 11.8 %maximum_maximum_fusion = bf16[1280,704]{1,0:T(8,128)(2,1)S(1)} fusion(bf16[320,352]{1,0:T(8,128)(2,1)S(1)} %get-tuple-element.18, bf16[320,352]{1,0:T(8,128)(2,1)S(1)} %get-tuple-element.16, bf16[320,352]{1,0:T(8,128)(2,1)S(1)} %broadcast_in_dim.11, bf16[320,352]{1,0:T(8,128)(2,1)S(1)} %get-tuple-element.12, bf16[320,352]{1,0:T(8,128)(2,1)S(1)} %get-tuple-element.17, ...), kind=kLoop, calls=%fused_computation.7 | loop fusion | flops 14417920 | bytes 3604480 | tf_op jit(solution)/shard_map/concatenate | solution.py:54
  71.0 1.3 collective-permute-start.18
  73.0 3.0 %collective-permute-start.16 = (bf16[320,512]{1,0:T(8,128)(2,1)S(1)}, bf16[320,512]{1,0:T(8,128)(2,1)S(1)}, u32[]{:S(2)}, u32[]{:S(2)}) collective-permute-start(bf16[320,512]{1,0:T(8,128)(2,1)S(1)} %get-tuple-element.7), channel_id=1, source_target_pairs={{0,4},{12,8},{1,5},{13,9},{2,6},{14,10},{3,7},{15,11},{16,20},{28,... | collective-permute-start | bytes 983048 | tf_op jit(solution)/shard_map/ppermute | solution.py:61
  76.0 2.3 %collective-permute-start.14 = (bf16[320,512]{1,0:T(8,128)(2,1)S(1)}, bf16[320,512]{1,0:T(8,128)(2,1)S(1)}, u32[]{:S(2)}, u32[]{:S(2)}) collective-permute-start(bf16[320,512]{1,0:T(8,128)(2,1)S(1)} %get-tuple-element.8), channel_id=1, source_target_pairs={{0,8},{12,4},{1,9},{13,5},{2,10},{14,6},{3,11},{15,7},{16,24},{28,... | collective-permute-start | bytes 983048 | tf_op jit(solution)/shard_map/ppermute | solution.py:62
  80.5 5.3 %collective-permute-start.12 = (bf16[320,512]{1,0:T(8,128)(2,1)S(1)}, bf16[320,512]{1,0:T(8,128)(2,1)S(1)}, u32[]{:S(2)}, u32[]{:S(2)}) collective-permute-start(bf16[320,512]{1,0:T(8,128)(2,1)S(1)} %get-tuple-element.8), channel_id=1, source_target_pairs={{0,4},{12,8},{1,5},{13,9},{2,6},{14,10},{3,7},{15,11},{16,20},{28,... | collective-permute-start | bytes 983048 | tf_op jit(solution)/shard_map/ppermute | solution.py:61
  85.7 7.1 %collective-permute-start.10 = (bf16[320,512]{1,0:T(8,128)(2,1)S(1)}, bf16[320,512]{1,0:T(8,128)(2,1)S(1)}, u32[]{:S(2)}, u32[]{:S(2)}) collective-permute-start(bf16[320,512]{1,0:T(8,128)(2,1)S(1)} %get-tuple-element.6), channel_id=1, source_target_pairs={{0,8},{12,4},{1,9},{13,5},{2,10},{14,6},{3,11},{15,7},{16,24},{28,... | collective-permute-start | bytes 983048 | tf_op jit(solution)/shard_map/ppermute | solution.py:62
  94.9 4.9 %collective-permute-start.8 = (bf16[320,512]{1,0:T(8,128)(2,1)S(1)}, bf16[320,512]{1,0:T(8,128)(2,1)S(1)}, u32[]{:S(2)}, u32[]{:S(2)}) collective-permute-start(bf16[320,512]{1,0:T(8,128)(2,1)S(1)} %get-tuple-element.6), channel_id=1, source_target_pairs={{0,4},{12,8},{1,5},{13,9},{2,6},{14,10},{3,7},{15,11},{16,20},{28,... | collective-permute-start | bytes 983048 | tf_op jit(solution)/shard_map/ppermute | solution.py:61
  104.1 4.6 %collective-permute-done.10 = bf16[320,512]{1,0:T(8,128)(2,1)S(1)} collective-permute-done((bf16[320,512]{1,0:T(8,128)(2,1)S(1)}, bf16[320,512]{1,0:T(8,128)(2,1)S(1)}, u32[]{:S(2)}, u32[]{:S(2)}) %collective-permute-start.10) | collective-permute-done | bytes 327712 | tf_op jit(solution)/shard_map/ppermute | solution.py:62
  109.9 4.5 %collective-permute-done.8 = bf16[320,512]{1,0:T(8,128)(2,1)S(1)} collective-permute-done((bf16[320,512]{1,0:T(8,128)(2,1)S(1)}, bf16[320,512]{1,0:T(8,128)(2,1)S(1)}, u32[]{:S(2)}, u32[]{:S(2)}) %collective-permute-start.8) | collective-permute-done | bytes 327712 | tf_op jit(solution)/shard_map/ppermute | solution.py:61
  117.0 3.2 %fusion.6 = bf16[1,1,1,320,1408]{4,3,2,1,0:T(8,128)(2,1)} fusion(bf16[320,2048]{1,0:T(8,128)(2,1)S(1)} %bitcast.61, bf16[1,1,1408,2048]{3,2,1,0:T(8,128)(2,1)S(1)} %bitcast.65), kind=kOutput, calls=%fused_computation.6 | convolution fusion | flops 1845944320 | bytes 7979008 | tf_op jit(solution)/shard_map/sd,hd->sh/dot_general | solution.py:96
  120.3 2.9 %collective-permute-done.19 = bf16[352,512]{1,0:T(8,128)(2,1)S(1)} collective-permute-done((bf16[352,512]{1,0:T(8,128)(2,1)S(1)}, bf16[352,512]{1,0:T(8,128)(2,1)S(1)}, u32[]{:S(2)}, u32[]{:S(2)}) %collective-permute-start.19) | collective-permute-done | bytes 360480 | tf_op jit(solution)/shard_map/ppermute | solution.py:67
  123.3 7.6 %collective-permute-done.15 = bf16[352,512]{1,0:T(8,128)(2,1)S(1)} collective-permute-done((bf16[352,512]{1,0:T(8,128)(2,1)S(1)}, bf16[352,512]{1,0:T(8,128)(2,1)S(1)}, u32[]{:S(2)}, u32[]{:S(2)}) %collective-permute-start.15) | collective-permute-done | bytes 360480 | tf_op jit(solution)/shard_map/ppermute | solution.py:67
  131.0 6.6 %collective-permute-done.11 = bf16[352,512]{1,0:T(8,128)(2,1)S(1)} collective-permute-done((bf16[352,512]{1,0:T(8,128)(2,1)S(1)}, bf16[352,512]{1,0:T(8,128)(2,1)S(1)}, u32[]{:S(2)}, u32[]{:S(2)}) %collective-permute-start.11) | collective-permute-done | bytes 360480 | tf_op jit(solution)/shard_map/ppermute | solution.py:67
  137.8 1.8 %maximum_bitcast_fusion = f32[1,1,352,2048]{3,2,1,0:T(8,128)} fusion(f32[352,512]{1,0:T(8,128)S(1)} %slice_add_fusion, f32[352,512]{1,0:T(8,128)S(1)} %slice_add_fusion.1, f32[352,512]{1,0:T(8,128)S(1)} %slice_add_fusion.2, f32[352,512]{1,0:T(8,128)S(1)} %slice_add_fusion.3), kind=kLoop, calls=%fused_computation.2 | loop fusion | flops 2162688 | bytes 5767168 | tf_op jit(solution)/shard_map/reshape | solution.py:100
  (64 shorter events, 21.7 us)
Async XLA Ops:
  0.6 15.2 %collective-permute-start = (bf16[1,128,2048]{2,1,0:T(8,128)(2,1)}, bf16[1,128,2048]{2,1,0:T(8,128)(2,1)S(1)}, u32[]{:S(2)}, u32[]{:S(2)}) collective-permute-start(bf16[1,128,2048]{2,1,0:T(8,128)(2,1)} %param.5), channel_id=1, source_target_pairs={{0,16},{16,0},{1,17},{17,1},{2,18},{18,2},{3,19},{19,3},{4,20},{20... | collective-permute-start | bytes 1572872 | tf_op jit(solution)/shard_map/ppermute | solution.py:10
  18.0 3.7 %copy-start = (bf16[1,1,1,320,1408]{4,3,2,1,0:T(8,128)(2,1)S(1)}, bf16[1,1,1,320,1408]{4,3,2,1,0:T(8,128)(2,1)}, u32[]{:S(2)}) copy-start(bf16[1,1,1,320,1408]{4,3,2,1,0:T(8,128)(2,1)} %param.8) | copy-start | bytes 2703364
  18.0 23.4 %all-to-all-start = ((bf16[4,80,2048]{2,1,0:T(8,128)(2,1)}), bf16[4,80,2048]{2,1,0:T(8,128)(2,1)S(1)}, u32[]{:S(2)}, u32[]{:S(2)}) async-start(bf16[4,80,2048]{2,1,0:T(8,128)(2,1)} %bitcast.8), calls=%async_computation | async-start | bytes 2621440 | tf_op jit(solution)/shard_map/all_to_all | solution.py:83
  23.2 16.7 %collective-permute-start.3 = (bf16[320,704]{1,0:T(8,128)(2,1)}, bf16[320,704]{1,0:T(8,128)(2,1)}, u32[]{:S(2)}, u32[]{:S(2)}) collective-permute-start(bf16[320,704]{1,0:T(8,128)(2,1)} %get-tuple-element.14), channel_id=1, source_target_pairs={{0,8},{12,4},{1,9},{13,5},{2,10},{14,6},{3,11},{15,7},{16,24},{28,... | collective-permute-start | bytes 1351688 | tf_op jit(solution)/shard_map/ppermute | solution.py:43
  28.7 12.5 %collective-permute-start.2 = (bf16[320,704]{1,0:T(8,128)(2,1)}, bf16[320,704]{1,0:T(8,128)(2,1)S(1)}, u32[]{:S(2)}, u32[]{:S(2)}) collective-permute-start(bf16[320,704]{1,0:T(8,128)(2,1)} %get-tuple-element.13), channel_id=1, source_target_pairs={{4,8},{8,4},{5,9},{9,5},{6,10},{10,6},{7,11},{11,7},{20,24},{24,20... | collective-permute-start | bytes 1351688 | tf_op jit(solution)/shard_map/ppermute | solution.py:44
  30.4 28.8 %collective-permute-start.1 = (bf16[320,352]{1,0:T(8,128)(2,1)}, bf16[320,352]{1,0:T(8,128)(2,1)}, u32[]{:S(2)}, u32[]{:S(2)}) collective-permute-start(bf16[320,352]{1,0:T(8,128)(2,1)} %get-tuple-element.11), channel_id=1, source_target_pairs={{0,4},{12,8},{1,5},{13,9},{2,6},{14,10},{3,7},{15,11},{16,20},{28,... | collective-permute-start | bytes 675848 | tf_op jit(solution)/shard_map/ppermute | solution.py:42
  41.5 31.5 %collective-permute-start.6 = (bf16[320,512]{1,0:T(8,128)(2,1)S(1)}, bf16[320,512]{1,0:T(8,128)(2,1)S(1)}, u32[]{:S(2)}, u32[]{:S(2)}) collective-permute-start(bf16[320,512]{1,0:T(8,128)(2,1)S(1)} %get-tuple-element.9), channel_id=1, source_target_pairs={{0,8},{12,4},{1,9},{13,5},{2,10},{14,6},{3,11},{15,7},{16,24},{28,... | collective-permute-start | bytes 983048 | tf_op jit(solution)/shard_map/ppermute | solution.py:62
  55.4 20.6 %collective-permute-start.5 = (bf16[320,512]{1,0:T(8,128)(2,1)S(1)}, bf16[320,512]{1,0:T(8,128)(2,1)S(1)}, u32[]{:S(2)}, u32[]{:S(2)}) collective-permute-start(bf16[320,512]{1,0:T(8,128)(2,1)S(1)} %get-tuple-element.9), channel_id=1, source_target_pairs={{4,8},{8,4},{5,9},{9,5},{6,10},{10,6},{7,11},{11,7},{20,24},{24,20... | collective-permute-start | bytes 983048 | tf_op jit(solution)/shard_map/ppermute | solution.py:61
  56.1 22.3 %collective-permute-start.4 = (bf16[320,512]{1,0:T(8,128)(2,1)S(1)}, bf16[320,512]{1,0:T(8,128)(2,1)S(1)}, u32[]{:S(2)}, u32[]{:S(2)}) collective-permute-start(bf16[320,512]{1,0:T(8,128)(2,1)S(1)} %get-tuple-element.9), channel_id=1, source_target_pairs={{0,4},{12,8},{1,5},{13,9},{2,6},{14,10},{3,7},{15,11},{16,20},{28,... | collective-permute-start | bytes 983048 | tf_op jit(solution)/shard_map/ppermute | solution.py:61
  71.0 9.4 %collective-permute-start.18 = (bf16[320,512]{1,0:T(8,128)(2,1)S(1)}, bf16[320,512]{1,0:T(8,128)(2,1)S(1)}, u32[]{:S(2)}, u32[]{:S(2)}) collective-permute-start(bf16[320,512]{1,0:T(8,128)(2,1)S(1)} %get-tuple-element.7), channel_id=1, source_target_pairs={{0,8},{12,4},{1,9},{13,5},{2,10},{14,6},{3,11},{15,7},{16,24},{28,... | collective-permute-start | bytes 983048 | tf_op jit(solution)/shard_map/ppermute | solution.py:62
  72.3 13.4 %collective-permute-start.17 = (bf16[320,512]{1,0:T(8,128)(2,1)S(1)}, bf16[320,512]{1,0:T(8,128)(2,1)S(1)}, u32[]{:S(2)}, u32[]{:S(2)}) collective-permute-start(bf16[320,512]{1,0:T(8,128)(2,1)S(1)} %get-tuple-element.7), channel_id=1, source_target_pairs={{4,8},{8,4},{5,9},{9,5},{6,10},{10,6},{7,11},{11,7},{20,24},{24,20... | collective-permute-start | bytes 983048 | tf_op jit(solution)/shard_map/ppermute | solution.py:61
  73.0 19.8 %collective-permute-start.16 = (bf16[320,512]{1,0:T(8,128)(2,1)S(1)}, bf16[320,512]{1,0:T(8,128)(2,1)S(1)}, u32[]{:S(2)}, u32[]{:S(2)}) collective-permute-start(bf16[320,512]{1,0:T(8,128)(2,1)S(1)} %get-tuple-element.7), channel_id=1, source_target_pairs={{0,4},{12,8},{1,5},{13,9},{2,6},{14,10},{3,7},{15,11},{16,20},{28,... | collective-permute-start | bytes 983048 | tf_op jit(solution)/shard_map/ppermute | solution.py:61
  76.0 18.9 %collective-permute-start.14 = (bf16[320,512]{1,0:T(8,128)(2,1)S(1)}, bf16[320,512]{1,0:T(8,128)(2,1)S(1)}, u32[]{:S(2)}, u32[]{:S(2)}) collective-permute-start(bf16[320,512]{1,0:T(8,128)(2,1)S(1)} %get-tuple-element.8), channel_id=1, source_target_pairs={{0,8},{12,4},{1,9},{13,5},{2,10},{14,6},{3,11},{15,7},{16,24},{28,... | collective-permute-start | bytes 983048 | tf_op jit(solution)/shard_map/ppermute | solution.py:62
  78.3 21.5 %collective-permute-start.13 = (bf16[320,512]{1,0:T(8,128)(2,1)S(1)}, bf16[320,512]{1,0:T(8,128)(2,1)S(1)}, u32[]{:S(2)}, u32[]{:S(2)}) collective-permute-start(bf16[320,512]{1,0:T(8,128)(2,1)S(1)} %get-tuple-element.8), channel_id=1, source_target_pairs={{4,8},{8,4},{5,9},{9,5},{6,10},{10,6},{7,11},{11,7},{20,24},{24,20... | collective-permute-start | bytes 983048 | tf_op jit(solution)/shard_map/ppermute | solution.py:61
  80.5 21.1 %collective-permute-start.12 = (bf16[320,512]{1,0:T(8,128)(2,1)S(1)}, bf16[320,512]{1,0:T(8,128)(2,1)S(1)}, u32[]{:S(2)}, u32[]{:S(2)}) collective-permute-start(bf16[320,512]{1,0:T(8,128)(2,1)S(1)} %get-tuple-element.8), channel_id=1, source_target_pairs={{0,4},{12,8},{1,5},{13,9},{2,6},{14,10},{3,7},{15,11},{16,20},{28,... | collective-permute-start | bytes 983048 | tf_op jit(solution)/shard_map/ppermute | solution.py:61
  85.7 22.9 %collective-permute-start.10 = (bf16[320,512]{1,0:T(8,128)(2,1)S(1)}, bf16[320,512]{1,0:T(8,128)(2,1)S(1)}, u32[]{:S(2)}, u32[]{:S(2)}) collective-permute-start(bf16[320,512]{1,0:T(8,128)(2,1)S(1)} %get-tuple-element.6), channel_id=1, source_target_pairs={{0,8},{12,4},{1,9},{13,5},{2,10},{14,6},{3,11},{15,7},{16,24},{28,... | collective-permute-start | bytes 983048 | tf_op jit(solution)/shard_map/ppermute | solution.py:62
  92.8 17.1 %collective-permute-start.9 = (bf16[320,512]{1,0:T(8,128)(2,1)S(1)}, bf16[320,512]{1,0:T(8,128)(2,1)S(1)}, u32[]{:S(2)}, u32[]{:S(2)}) collective-permute-start(bf16[320,512]{1,0:T(8,128)(2,1)S(1)} %get-tuple-element.6), channel_id=1, source_target_pairs={{4,8},{8,4},{5,9},{9,5},{6,10},{10,6},{7,11},{11,7},{20,24},{24,20... | collective-permute-start | bytes 983048 | tf_op jit(solution)/shard_map/ppermute | solution.py:61
  94.9 19.6 %collective-permute-start.8 = (bf16[320,512]{1,0:T(8,128)(2,1)S(1)}, bf16[320,512]{1,0:T(8,128)(2,1)S(1)}, u32[]{:S(2)}, u32[]{:S(2)}) collective-permute-start(bf16[320,512]{1,0:T(8,128)(2,1)S(1)} %get-tuple-element.6), channel_id=1, source_target_pairs={{0,4},{12,8},{1,5},{13,9},{2,6},{14,10},{3,7},{15,11},{16,20},{28,... | collective-permute-start | bytes 983048 | tf_op jit(solution)/shard_map/ppermute | solution.py:61
  99.8 17.1 %collective-permute-start.7 = (bf16[352,512]{1,0:T(8,128)(2,1)S(1)}, bf16[352,512]{1,0:T(8,128)(2,1)S(1)}, u32[]{:S(2)}, u32[]{:S(2)}) collective-permute-start(bf16[352,512]{1,0:T(8,128)(2,1)S(1)} %slice.106), channel_id=1, source_target_pairs={{4,0},{8,12},{5,1},{9,13},{6,2},{10,14},{7,3},{11,15},{20,16},{24,... | collective-permute-start | bytes 1081352 | tf_op jit(solution)/shard_map/ppermute | solution.py:67
  101.6 21.6 %collective-permute-start.19 = (bf16[352,512]{1,0:T(8,128)(2,1)S(1)}, bf16[352,512]{1,0:T(8,128)(2,1)S(1)}, u32[]{:S(2)}, u32[]{:S(2)}) collective-permute-start(bf16[352,512]{1,0:T(8,128)(2,1)S(1)} %slice.103), channel_id=1, source_target_pairs={{4,0},{8,12},{5,1},{9,13},{6,2},{10,14},{7,3},{11,15},{20,16},{24,... | collective-permute-start | bytes 1081352 | tf_op jit(solution)/shard_map/ppermute | solution.py:67
  104.0 13.0 %slice-start = ((s8[5767168]{0:T(1024)(128)(4,1)}), s8[4194304]{0:T(1024)(128)(4,1)S(1)}, s32[]{:S(2)}) async-start(s8[5767168]{0:T(1024)(128)(4,1)} %bitcast.64), calls=%async_computation.1 | async-start | bytes 8388608
  104.0 12.9 %slice-start.1 = ((s8[5767168]{0:T(1024)(128)(4,1)}), s8[1572864]{0:T(1024)(128)(4,1)S(1)}, s32[]{:S(2)}) async-start(s8[5767168]{0:T(1024)(128)(4,1)} %bitcast.64), calls=%async_computation.2 | async-start | bytes 3145728
  108.6 22.3 %collective-permute-start.15 = (bf16[352,512]{1,0:T(8,128)(2,1)S(1)}, bf16[352,512]{1,0:T(8,128)(2,1)S(1)}, u32[]{:S(2)}, u32[]{:S(2)}) collective-permute-start(bf16[352,512]{1,0:T(8,128)(2,1)S(1)} %slice.104), channel_id=1, source_target_pairs={{4,0},{8,12},{5,1},{9,13},{6,2},{10,14},{7,3},{11,15},{20,16},{24,... | collective-permute-start | bytes 1081352 | tf_op jit(solution)/shard_map/ppermute | solution.py:67
  115.7 22.0 %collective-permute-start.11 = (bf16[352,512]{1,0:T(8,128)(2,1)S(1)}, bf16[352,512]{1,0:T(8,128)(2,1)S(1)}, u32[]{:S(2)}, u32[]{:S(2)}) collective-permute-start(bf16[352,512]{1,0:T(8,128)(2,1)S(1)} %slice.105), channel_id=1, source_target_pairs={{4,0},{8,12},{5,1},{9,13},{6,2},{10,14},{7,3},{11,15},{20,16},{24,... | collective-permute-start | bytes 1081352 | tf_op jit(solution)/shard_map/ppermute | solution.py:67

commit v9 on v8

--- a/solution.py
+++ b/solution.py
@@ -28,44 +28,46 @@
     return total.astype(jnp.bfloat16).reshape(count, width, rows.shape[1])
 
 
-def cols(array, start, size):
-    return lax.dynamic_slice_in_dim(array, start, size, axis=1)
+def rows(array, start, size):
+    return lax.dynamic_slice_in_dim(array, start, size, axis=0)
 
 
-def line_weight_grad(saved, scaled, chunks):
+def hidden_blocks(saved):
     d = lax.axis_index("dp")
     blk = saved.shape[1] // 4
-    inner = [(0, 1), (3, 2)]
-    across = [(1, 2), (2, 1)]
-    far = [(0, 2), (3, 1)]
-    back = [(1, 0), (2, 3)]
-    h_near = lax.ppermute(cols(saved, jnp.where(d == 0, blk, 2 * blk), blk), "dp", inner)
-    h_far = lax.ppermute(cols(saved, jnp.where(d == 0, 2 * blk, 0), 2 * blk), "dp", far)
-    h_mid = lax.ppermute(cols(saved, jnp.where(d == 1, 2 * blk, 0), 2 * blk), "dp", across)
+    flipped = saved.T
+    near = lax.ppermute(rows(flipped, jnp.where(d == 0, blk, 2 * blk), blk), "dp", [(0, 1), (3, 2)])
+    far = lax.ppermute(rows(flipped, jnp.where(d == 0, 2 * blk, 0), 2 * blk), "dp", [(0, 2), (3, 1)])
+    mid = lax.ppermute(rows(flipped, jnp.where(d == 1, 2 * blk, 0), 2 * blk), "dp", [(1, 2), (2, 1)])
+    return flipped, near, far, mid
+
+
+def line_weight_grad(blocks, scaled, chunks):
+    flipped, near, far, mid = blocks
+    d = lax.axis_index("dp")
+    blk = flipped.shape[0] // 4
     own_at = jnp.where(d == 1, blk, 0)
     end_at = jnp.where(d == 1, 0, blk)
-    own_block = jnp.concatenate(
-        [cols(saved, d * blk, blk), h_near, cols(h_mid, own_at, blk), cols(h_far, own_at, blk)], axis=0
-    )
-    end_block = jnp.concatenate(
-        [cols(saved, jnp.where(d == 1, 0, 3 * blk), blk), jnp.zeros_like(h_near),
-         cols(h_mid, end_at, blk), cols(h_far, end_at, blk)], axis=0
-    )
-    lhs = jnp.concatenate([own_block, end_block], axis=1)
+    own = [rows(flipped, d * blk, blk), near, rows(mid, own_at, blk), rows(far, own_at, blk)]
+    end = [rows(flipped, jnp.where(d == 1, 0, 3 * blk), blk), rows(mid, end_at, blk), rows(far, end_at, blk)]
     edge = (d == 0) | (d == 3)
     width = scaled.shape[1] // chunks
     pieces = []
     for c in range(chunks):
         sc = scaled[:, c * width:(c + 1) * width]
-        rhs = jnp.concatenate(
-            [sc, lax.ppermute(sc, "dp", inner), lax.ppermute(sc, "dp", across),
-             lax.ppermute(sc, "dp", far)], axis=0
+        inner = lax.ppermute(sc, "dp", [(0, 1), (3, 2)])
+        across = lax.ppermute(sc, "dp", [(1, 2), (2, 1)])
+        beyond = lax.ppermute(sc, "dp", [(0, 2), (3, 1)])
+        mine = sum(
+            jnp.dot(h, s, preferred_element_type=jnp.float32)
+            for h, s in zip(own, [sc, inner, across, beyond])
         )
-        acc = lax.dot_general(
-            lhs, rhs, (((0,), (0,)), ((), ())), preferred_element_type=jnp.float32
+        theirs = sum(
+            jnp.dot(h, s, preferred_element_type=jnp.float32)
+            for h, s in zip(end, [sc, across, beyond])
         )
-        tail = lax.ppermute(acc[blk:].astype(jnp.bfloat16), "dp", back)
-        pieces.append(acc[:blk] + jnp.where(edge, tail.astype(jnp.float32), 0.0))
+        tail = lax.ppermute(theirs.astype(jnp.bfloat16), "dp", [(1, 0), (2, 3)])
+        pieces.append(mine + jnp.where(edge, tail.astype(jnp.float32), 0.0))
     return jnp.concatenate(pieces, axis=1), tail
 
 
@@ -80,10 +82,13 @@
     target = dispatch_targets(routes[0], groups, width)
     outgoing = dispatch_rows(incoming, gates[0], target, groups, width)
     line = lax.axis_size("dp") == 4 and saved.shape[1] % 4 == 0
+    if line:
+        blocks = hidden_blocks(saved)
+        outgoing, blocks = lax.optimization_barrier((outgoing, blocks))
     piece = lax.all_to_all(outgoing, "expert", split_axis=0, concat_axis=0, tiled=True)
     scaled = piece.reshape(slot_count, model_width)
     if line:
-        weight_grad, anchor = line_weight_grad(saved, scaled, 4)
+        weight_grad, anchor = line_weight_grad(blocks, scaled, 4)
         late, _ = lax.optimization_barrier((scaled, anchor))
     else:
         full = lax.dot_general(

time: 140 us -> 150 us (1.071)
  blocking collectives: 0 us -> 19.8 us
  other arithmetic: 15.5 us -> 3.21 us
  matrix products: 9.96 us -> 20.6 us
  waiting for transfers between devices: 41.7 us -> 35 us
    all_to_all x0 -> x1, blocking collectives: none -> 19.8 us  [shards(): lax.all_to_all(outgoing, 'expert', split_axis=0, concat_axis=0, tiled=True)]
    concatenate x1 -> x0, other arithmetic: 11.8 us -> none  [line_weight_grad(): lhs = jnp.concatenate([own_block, end_block], axis=1)]
    dot_general x4 -> x28, matrix products: 4.5 us -> 16.2 us  [line_weight_grad(): jnp.dot(h, s, preferred_element_type=jnp.float32)]
    ppermute x1, waiting for transfers between devices: 8.3 us -> 0.01 us  [shifted(): return lax.ppermute(value, axis, pairs)]
    all_to_all x1 -> x0, starting transfers between devices: 3.67 us -> none  [shards(): lax.all_to_all(outgoing, 'expert', split_axis=0, concat_axis=0, tiled=True)]
    ppermute x19, starting transfers between devices: 58 us -> 61 us  [the longest x4 29.3 us: line_weight_grad(): beyond = lax.ppermute(sc, 'dp', [(0, 2), (3, 1)])]
    ppermute x19, waiting for transfers between devices: 33.4 us -> 35 us  [the longest x4 14.1 us: line_weight_grad(): tail = lax.ppermute(theirs.astype(jnp.bfloat16), 'dp', [(1, 0), (2, 3)])]
    dynamic_slice x4 -> x2, local copies, waits for them, and re-layouts: 4 us -> 3.29 us  [rows(): return lax.dynamic_slice_in_dim(array, start, size, axis=0)]
  transfers between devices with their start and end apart: 21 -> 20, of which waited for: 9 -> 3; matrix products, arithmetic and copies ran while one was open for 20% -> 17% of each run, Pallas kernels for 0% -> 0%
where the time goes in v9:
time: 150 us
  starting transfers between devices  64.1 us (43%)
  waiting for transfers between devices  35 us (23%)
  matrix products  20.6 us (14%)
  blocking collectives  19.8 us (13%)
  local copies, waits for them, and re-layouts  5.8 us (4%)
  other arithmetic  3.21 us (2%)
    ppermute x4, starting transfers between devices, line_weight_grad(): beyond = lax.ppermute(sc, 'dp', [(0, 2), (3, 1)])  29.3 us
    all_to_all x1, blocking collectives, shards(): lax.all_to_all(outgoing, 'expert', split_axis=0, concat_axis=0, tiled=True)  19.8 us
    dot_general x28, matrix products, line_weight_grad(): jnp.dot(h, s, preferred_element_type=jnp.float32)  16.2 us
    ppermute x4, starting transfers between devices, line_weight_grad(): inner = lax.ppermute(sc, 'dp', [(0, 1), (3, 2)])  14.5 us
    ppermute x4, waiting for transfers between devices, line_weight_grad(): tail = lax.ppermute(theirs.astype(jnp.bfloat16), 'dp', [(1, 0), (2, 3)])  14.1 us
    ppermute x4, waiting for transfers between devices, line_weight_grad(): beyond = lax.ppermute(sc, 'dp', [(0, 2), (3, 1)])  13.4 us
    ppermute x1, waiting for transfers between devices, hidden_blocks(): lax.ppermute(rows(flipped, jnp.where(d == 0, blk, 2 * blk), blk), 'dp', [...  7.56 us
    ppermute x4, starting transfers between devices, line_weight_grad(): tail = lax.ppermute(theirs.astype(jnp.bfloat16), 'dp', [(1, 0), (2, 3)])  5.34 us
  transfers between devices with their start and end apart: 20, of which 3 were waited for; matrix products, arithmetic and copies ran while one was open for 17% of the time, Pallas kernels for 0%

profile of v9, /device:TPU:0, one launch (start us, length us, event | category | flops | bytes accessed | tf_op | source)
XLA Modules:
  0.0 149.7 jit_solution(15646349148185206646)
XLA Ops:
  0.7 3.0 %collective-permute-start = (bf16[1,128,2048]{2,1,0:T(8,128)(2,1)}, bf16[1,128,2048]{2,1,0:T(8,128)(2,1)S(1)}, u32[]{:S(2)}, u32[]{:S(2)}) collective-permute-start(bf16[1,128,2048]{2,1,0:T(8,128)(2,1)} %param.5), channel_id=1, source_target_pairs={{0,16},{16,0},{1,17},{17,1},{2,18},{18,2},{3,19},{19,3},{4,20},{20... | collective-permute-start | bytes 1572872 | tf_op jit(solution)/shard_map/ppermute | solution.py:10
  3.7 2.5 %dynamic-slice_bitcast_fusion = (bf16[704,320]{0,1:T(8,128)(2,1)S(1)}, bf16[704,320]{0,1:T(8,128)(2,1)}) fusion(bf16[1,1,1,320,1408]{4,3,2,1,0:T(8,128)(2,1)} %param.8, s32[]{:T(128)S(6)} %select_n.52, s32[]{:T(128)S(6)} %select_n.51), kind=kLoop, calls=%fused_computation.44 | loop fusion | bytes 1802248 | tf_op jit(solution)/shard_map/dynamic_slice | solution.py:32
  6.1 4.6 %collective-permute-start.2 = (bf16[704,320]{0,1:T(8,128)(2,1)}, bf16[704,320]{0,1:T(8,128)(2,1)S(1)}, u32[]{:S(2)}, u32[]{:S(2)}) collective-permute-start(bf16[704,320]{0,1:T(8,128)(2,1)} %get-tuple-element.21), channel_id=1, source_target_pairs={{0,8},{12,4},{1,9},{13,5},{2,10},{14,6},{3,11},{15,7},{16,24},{28,... | collective-permute-start | bytes 1351688 | tf_op jit(solution)/shard_map/ppermute | solution.py:40
  12.3 3.0 %collective-permute-start.1 = (bf16[352,320]{0,1:T(8,128)(2,1)}, bf16[352,320]{0,1:T(8,128)(2,1)S(1)}, u32[]{:S(2)}, u32[]{:S(2)}) collective-permute-start(bf16[352,320]{0,1:T(8,128)(2,1)} %dynamic-slice_bitcast_fusion.2), channel_id=1, source_target_pairs={{0,4},{12,8},{1,5},{13,9},{2,6},{14,10},{3,7},{15,11},{16,20},{28,... | collective-permute-start | bytes 675848 | tf_op jit(solution)/shard_map/ppermute | solution.py:39
  19.0 7.6 %collective-permute-done.1 = bf16[352,320]{0,1:T(8,128)(2,1)S(1)} collective-permute-done((bf16[352,320]{0,1:T(8,128)(2,1)}, bf16[352,320]{0,1:T(8,128)(2,1)S(1)}, u32[]{:S(2)}, u32[]{:S(2)}) %collective-permute-start.1) | collective-permute-done | bytes 225312 | tf_op jit(solution)/shard_map/ppermute | solution.py:39
  26.6 19.8 %all_to_all.5 = bf16[4,80,2048]{2,1,0:T(8,128)(2,1)S(1)} all-to-all(bf16[4,80,2048]{2,1,0:T(8,128)(2,1)S(1)} %bitcast.103), channel_id=1, replica_groups=mesh['section'=2,'dp'=4,'expert'=4] {'expert'}, dimensions={0} | all-to-all | bytes 2621440 | tf_op jit(solution)/shard_map/all_to_all | solution.py:88
  47.4 1.4 collective-permute-start.8
  48.8 11.3 %collective-permute-start.9 = (bf16[320,512]{1,0:T(8,128)(2,1)}, bf16[320,512]{1,0:T(8,128)(2,1)S(1)}, u32[]{:S(2)}, u32[]{:S(2)}) collective-permute-start(bf16[320,512]{1,0:T(8,128)(2,1)} %get-tuple-element.16), channel_id=1, source_target_pairs={{0,8},{12,4},{1,9},{13,5},{2,10},{14,6},{3,11},{15,7},{16,24},{28,... | collective-permute-start | bytes 983048 | tf_op jit(solution)/shard_map/ppermute | solution.py:60
  60.1 1.5 %collective-permute-start.7 = (bf16[320,512]{1,0:T(8,128)(2,1)}, bf16[320,512]{1,0:T(8,128)(2,1)S(1)}, u32[]{:S(2)}, u32[]{:S(2)}) collective-permute-start(bf16[320,512]{1,0:T(8,128)(2,1)} %get-tuple-element.16), channel_id=1, source_target_pairs={{0,4},{12,8},{1,5},{13,9},{2,6},{14,10},{3,7},{15,11},{16,20},{28,... | collective-permute-start | bytes 983048 | tf_op jit(solution)/shard_map/ppermute | solution.py:58
  62.4 4.0 %collective-permute-start.13 = (bf16[320,512]{1,0:T(8,128)(2,1)}, bf16[320,512]{1,0:T(8,128)(2,1)S(1)}, u32[]{:S(2)}, u32[]{:S(2)}) collective-permute-start(bf16[320,512]{1,0:T(8,128)(2,1)} %get-tuple-element.18), channel_id=1, source_target_pairs={{0,8},{12,4},{1,9},{13,5},{2,10},{14,6},{3,11},{15,7},{16,24},{28,... | collective-permute-start | bytes 983048 | tf_op jit(solution)/shard_map/ppermute | solution.py:60
  66.4 10.2 %collective-permute-start.11 = (bf16[320,512]{1,0:T(8,128)(2,1)}, bf16[320,512]{1,0:T(8,128)(2,1)S(1)}, u32[]{:S(2)}, u32[]{:S(2)}) collective-permute-start(bf16[320,512]{1,0:T(8,128)(2,1)} %get-tuple-element.18), channel_id=1, source_target_pairs={{0,4},{12,8},{1,5},{13,9},{2,6},{14,10},{3,7},{15,11},{16,20},{28,... | collective-permute-start | bytes 983048 | tf_op jit(solution)/shard_map/ppermute | solution.py:58
  76.5 1.5 %fusion.54 = f32[352,512]{1,0:T(8,128)S(1)} fusion(bf16[320,512]{1,0:T(8,128)(2,1)} %collective-permute-done.8, bf16[704,320]{0,1:T(8,128)(2,1)S(1)} %collective-permute-done.3, s32[]{:T(128)S(6)} %select_n.54), kind=kOutput, calls=%fused_computation.73 | convolution fusion | flops 115343360 | bytes 1294340 | tf_op jit(solution)/shard_map/dot_general | solution.py:66
  80.8 12.8 %collective-permute-start.17 = (bf16[320,512]{1,0:T(8,128)(2,1)S(1)}, bf16[320,512]{1,0:T(8,128)(2,1)S(1)}, u32[]{:S(2)}, u32[]{:S(2)}) collective-permute-start(bf16[320,512]{1,0:T(8,128)(2,1)S(1)} %copy-done.2), channel_id=1, source_target_pairs={{0,8},{12,4},{1,9},{13,5},{2,10},{14,6},{3,11},{15,7},{16,24},{28,... | collective-permute-start | bytes 983048 | tf_op jit(solution)/shard_map/ppermute | solution.py:60
  94.1 1.5 %collective-permute-start.15 = (bf16[320,512]{1,0:T(8,128)(2,1)S(1)}, bf16[320,512]{1,0:T(8,128)(2,1)S(1)}, u32[]{:S(2)}, u32[]{:S(2)}) collective-permute-start(bf16[320,512]{1,0:T(8,128)(2,1)S(1)} %copy-done.2), channel_id=1, source_target_pairs={{0,4},{12,8},{1,5},{13,9},{2,6},{14,10},{3,7},{15,11},{16,20},{28,... | collective-permute-start | bytes 983048 | tf_op jit(solution)/shard_map/ppermute | solution.py:58
  96.1 1.3 collective-permute-start.19
  97.8 1.3 collective-permute-start.5
  101.4 1.3 collective-permute-start.10
  103.8 1.3 collective-permute-start.14
  106.7 13.4 %collective-permute-done.5 = bf16[320,512]{1,0:T(8,128)(2,1)S(1)} collective-permute-done((bf16[320,512]{1,0:T(8,128)(2,1)S(1)}, bf16[320,512]{1,0:T(8,128)(2,1)S(1)}, u32[]{:S(2)}, u32[]{:S(2)}) %collective-permute-start.5) | collective-permute-done | bytes 327712 | tf_op jit(solution)/shard_map/ppermute | solution.py:60
  123.0 1.5 collective-permute-start.6
  127.4 14.1 %collective-permute-done.6 = bf16[352,512]{1,0:T(8,128)(2,1)S(1)} collective-permute-done((bf16[352,512]{1,0:T(8,128)(2,1)S(1)}, bf16[352,512]{1,0:T(8,128)(2,1)S(1)}, u32[]{:S(2)}, u32[]{:S(2)}) %collective-permute-start.6) | collective-permute-done | bytes 360480 | tf_op jit(solution)/shard_map/ppermute | solution.py:69
  141.4 3.2 %fusion.6 = bf16[1,1,1,320,1408]{4,3,2,1,0:T(8,128)(2,1)} fusion(bf16[320,2048]{1,0:T(8,128)(2,1)S(1)} %bitcast.94, bf16[1,1,1408,2048]{3,2,1,0:T(8,128)(2,1)S(1)} %bitcast.107), kind=kOutput, calls=%fused_computation.6 | convolution fusion | flops 1845944320 | bytes 7979008 | tf_op jit(solution)/shard_map/sd,hd->sh/dot_general | solution.py:101
  145.2 1.5 %fusion.16 = f32[352,512]{1,0:T(8,128)S(1)} fusion(f32[352,512]{1,0:T(8,128)S(1)} %fusion.36, f32[352,512]{1,0:T(8,128)S(1)} %convolution_add_fusion.14, bf16[320,512]{1,0:T(8,128)(2,1)} %collective-permute-done.8, bf16[352,512]{1,0:T(8,128)(2,1)S(1)} %collective-permute-done.10, pred[]{:T(512)S(6)} %or.3, bf16[704,320]{0,1:T(8,128)(2,1)S(1)} %collective-permute-done.3, ...), kind=kOutput, calls=%fused_computation.29 | convolution fusion | flops 116244480 | bytes 3096581 | tf_op jit(solution)/shard_map/dot_general | solution.py:62
  147.9 1.8 %maximum_bitcast_fusion = f32[1,1,352,2048]{3,2,1,0:T(8,128)} fusion(f32[352,512]{1,0:T(8,128)S(1)} %fusion.10, f32[352,512]{1,0:T(8,128)S(1)} %fusion.12, f32[352,512]{1,0:T(8,128)S(1)} %fusion.14, f32[352,512]{1,0:T(8,128)S(1)} %fusion.16), kind=kLoop, calls=%fused_computation.2 | loop fusion | flops 2162688 | bytes 5767168 | tf_op jit(solution)/shard_map/reshape | solution.py:105
  (83 shorter events, 23.1 us)
Async XLA Ops:
  0.6 14.7 %copy-start.3 = (s32[1,128,2]{1,2,0:T(2,128)S(1)}, s32[1,128,2]{1,2,0:T(2,128)}, u32[]{:S(2)}) copy-start(s32[1,128,2]{1,2,0:T(2,128)} %param.6) | copy-start | bytes 3076
  0.7 17.2 %collective-permute-start = (bf16[1,128,2048]{2,1,0:T(8,128)(2,1)}, bf16[1,128,2048]{2,1,0:T(8,128)(2,1)S(1)}, u32[]{:S(2)}, u32[]{:S(2)}) collective-permute-start(bf16[1,128,2048]{2,1,0:T(8,128)(2,1)} %param.5), channel_id=1, source_target_pairs={{0,16},{16,0},{1,17},{17,1},{2,18},{18,2},{3,19},{19,3},{4,20},{20... | collective-permute-start | bytes 1572872 | tf_op jit(solution)/shard_map/ppermute | solution.py:10
  6.1 20.4 %collective-permute-start.2 = (bf16[704,320]{0,1:T(8,128)(2,1)}, bf16[704,320]{0,1:T(8,128)(2,1)S(1)}, u32[]{:S(2)}, u32[]{:S(2)}) collective-permute-start(bf16[704,320]{0,1:T(8,128)(2,1)} %get-tuple-element.21), channel_id=1, source_target_pairs={{0,8},{12,4},{1,9},{13,5},{2,10},{14,6},{3,11},{15,7},{16,24},{28,... | collective-permute-start | bytes 1351688 | tf_op jit(solution)/shard_map/ppermute | solution.py:40
  10.8 15.8 %collective-permute-start.3 = (bf16[704,320]{0,1:T(8,128)(2,1)S(1)}, bf16[704,320]{0,1:T(8,128)(2,1)S(1)}, u32[]{:S(2)}, u32[]{:S(2)}) collective-permute-start(bf16[704,320]{0,1:T(8,128)(2,1)S(1)} %get-tuple-element.20), channel_id=1, source_target_pairs={{4,8},{8,4},{5,9},{9,5},{6,10},{10,6},{7,11},{11,7},{20,24},{24,20... | collective-permute-start | bytes 1351688 | tf_op jit(solution)/shard_map/ppermute | solution.py:41
  12.3 14.2 %collective-permute-start.1 = (bf16[352,320]{0,1:T(8,128)(2,1)}, bf16[352,320]{0,1:T(8,128)(2,1)S(1)}, u32[]{:S(2)}, u32[]{:S(2)}) collective-permute-start(bf16[352,320]{0,1:T(8,128)(2,1)} %dynamic-slice_bitcast_fusion.2), channel_id=1, source_target_pairs={{0,4},{12,8},{1,5},{13,9},{2,6},{14,10},{3,7},{15,11},{16,20},{28,... | collective-permute-start | bytes 675848 | tf_op jit(solution)/shard_map/ppermute | solution.py:39
  47.4 18.9 %collective-permute-start.8 = (bf16[320,512]{1,0:T(8,128)(2,1)}, bf16[320,512]{1,0:T(8,128)(2,1)}, u32[]{:S(2)}, u32[]{:S(2)}) collective-permute-start(bf16[320,512]{1,0:T(8,128)(2,1)} %get-tuple-element.16), channel_id=1, source_target_pairs={{4,8},{8,4},{5,9},{9,5},{6,10},{10,6},{7,11},{11,7},{20,24},{24,20... | collective-permute-start | bytes 983048 | tf_op jit(solution)/shard_map/ppermute | solution.py:59
  48.8 31.9 %collective-permute-start.9 = (bf16[320,512]{1,0:T(8,128)(2,1)}, bf16[320,512]{1,0:T(8,128)(2,1)S(1)}, u32[]{:S(2)}, u32[]{:S(2)}) collective-permute-start(bf16[320,512]{1,0:T(8,128)(2,1)} %get-tuple-element.16), channel_id=1, source_target_pairs={{0,8},{12,4},{1,9},{13,5},{2,10},{14,6},{3,11},{15,7},{16,24},{28,... | collective-permute-start | bytes 983048 | tf_op jit(solution)/shard_map/ppermute | solution.py:60
  60.1 34.0 %collective-permute-start.7 = (bf16[320,512]{1,0:T(8,128)(2,1)}, bf16[320,512]{1,0:T(8,128)(2,1)S(1)}, u32[]{:S(2)}, u32[]{:S(2)}) collective-permute-start(bf16[320,512]{1,0:T(8,128)(2,1)} %get-tuple-element.16), channel_id=1, source_target_pairs={{0,4},{12,8},{1,5},{13,9},{2,6},{14,10},{3,7},{15,11},{16,20},{28,... | collective-permute-start | bytes 983048 | tf_op jit(solution)/shard_map/ppermute | solution.py:58
  61.7 16.9 %collective-permute-start.12 = (bf16[320,512]{1,0:T(8,128)(2,1)}, bf16[320,512]{1,0:T(8,128)(2,1)S(1)}, u32[]{:S(2)}, u32[]{:S(2)}) collective-permute-start(bf16[320,512]{1,0:T(8,128)(2,1)} %get-tuple-element.18), channel_id=1, source_target_pairs={{4,8},{8,4},{5,9},{9,5},{6,10},{10,6},{7,11},{11,7},{20,24},{24,20... | collective-permute-start | bytes 983048 | tf_op jit(solution)/shard_map/ppermute | solution.py:59
  62.4 35.4 %collective-permute-start.13 = (bf16[320,512]{1,0:T(8,128)(2,1)}, bf16[320,512]{1,0:T(8,128)(2,1)S(1)}, u32[]{:S(2)}, u32[]{:S(2)}) collective-permute-start(bf16[320,512]{1,0:T(8,128)(2,1)} %get-tuple-element.18), channel_id=1, source_target_pairs={{0,8},{12,4},{1,9},{13,5},{2,10},{14,6},{3,11},{15,7},{16,24},{28,... | collective-permute-start | bytes 983048 | tf_op jit(solution)/shard_map/ppermute | solution.py:60
  66.4 29.7 %collective-permute-start.11 = (bf16[320,512]{1,0:T(8,128)(2,1)}, bf16[320,512]{1,0:T(8,128)(2,1)S(1)}, u32[]{:S(2)}, u32[]{:S(2)}) collective-permute-start(bf16[320,512]{1,0:T(8,128)(2,1)} %get-tuple-element.18), channel_id=1, source_target_pairs={{0,4},{12,8},{1,5},{13,9},{2,6},{14,10},{3,7},{15,11},{16,20},{28,... | collective-permute-start | bytes 983048 | tf_op jit(solution)/shard_map/ppermute | solution.py:58
  79.0 20.6 %collective-permute-start.16 = (bf16[320,512]{1,0:T(8,128)(2,1)S(1)}, bf16[320,512]{1,0:T(8,128)(2,1)S(1)}, u32[]{:S(2)}, u32[]{:S(2)}) collective-permute-start(bf16[320,512]{1,0:T(8,128)(2,1)S(1)} %copy-done.2), channel_id=1, source_target_pairs={{4,8},{8,4},{5,9},{9,5},{6,10},{10,6},{7,11},{11,7},{20,24},{24,20... | collective-permute-start | bytes 983048 | tf_op jit(solution)/shard_map/ppermute | solution.py:59
  80.8 15.3 %copy-start.1 = (bf16[320,512]{1,0:T(8,128)(2,1)S(1)}, bf16[320,512]{1,0:T(8,128)(2,1)}, u32[]{:S(2)}) copy-start(bf16[320,512]{1,0:T(8,128)(2,1)} %get-tuple-element.19) | copy-start | bytes 983044
  80.8 23.0 %collective-permute-start.17 = (bf16[320,512]{1,0:T(8,128)(2,1)S(1)}, bf16[320,512]{1,0:T(8,128)(2,1)S(1)}, u32[]{:S(2)}, u32[]{:S(2)}) collective-permute-start(bf16[320,512]{1,0:T(8,128)(2,1)S(1)} %copy-done.2), channel_id=1, source_target_pairs={{0,8},{12,4},{1,9},{13,5},{2,10},{14,6},{3,11},{15,7},{16,24},{28,... | collective-permute-start | bytes 983048 | tf_op jit(solution)/shard_map/ppermute | solution.py:60
  94.1 28.8 %collective-permute-start.15 = (bf16[320,512]{1,0:T(8,128)(2,1)S(1)}, bf16[320,512]{1,0:T(8,128)(2,1)S(1)}, u32[]{:S(2)}, u32[]{:S(2)}) collective-permute-start(bf16[320,512]{1,0:T(8,128)(2,1)S(1)} %copy-done.2), channel_id=1, source_target_pairs={{0,4},{12,8},{1,5},{13,9},{2,6},{14,10},{3,7},{15,11},{16,20},{28,... | collective-permute-start | bytes 983048 | tf_op jit(solution)/shard_map/ppermute | solution.py:58
  96.1 29.9 %collective-permute-start.19 = (bf16[320,512]{1,0:T(8,128)(2,1)S(1)}, bf16[320,512]{1,0:T(8,128)(2,1)S(1)}, u32[]{:S(2)}, u32[]{:S(2)}) collective-permute-start(bf16[320,512]{1,0:T(8,128)(2,1)S(1)} %copy-done.1), channel_id=1, source_target_pairs={{0,4},{12,8},{1,5},{13,9},{2,6},{14,10},{3,7},{15,11},{16,20},{28,... | collective-permute-start | bytes 983048 | tf_op jit(solution)/shard_map/ppermute | solution.py:58
  97.8 22.3 %collective-permute-start.5 = (bf16[320,512]{1,0:T(8,128)(2,1)S(1)}, bf16[320,512]{1,0:T(8,128)(2,1)S(1)}, u32[]{:S(2)}, u32[]{:S(2)}) collective-permute-start(bf16[320,512]{1,0:T(8,128)(2,1)S(1)} %copy-done.1), channel_id=1, source_target_pairs={{0,8},{12,4},{1,9},{13,5},{2,10},{14,6},{3,11},{15,7},{16,24},{28,... | collective-permute-start | bytes 983048 | tf_op jit(solution)/shard_map/ppermute | solution.py:60
  99.6 1.7 %collective-permute-start.4 = (bf16[320,512]{1,0:T(8,128)(2,1)S(1)}, bf16[320,512]{1,0:T(8,128)(2,1)S(1)}, u32[]{:S(2)}, u32[]{:S(2)}) collective-permute-start(bf16[320,512]{1,0:T(8,128)(2,1)S(1)} %copy-done.1), channel_id=1, source_target_pairs={{4,8},{8,4},{5,9},{9,5},{6,10},{10,6},{7,11},{11,7},{20,24},{24,20... | collective-permute-start | bytes 983048 | tf_op jit(solution)/shard_map/ppermute | solution.py:59
  101.4 43.8 %collective-permute-start.10 = (bf16[352,512]{1,0:T(8,128)(2,1)S(1)}, bf16[352,512]{1,0:T(8,128)(2,1)S(1)}, u32[]{:S(2)}, u32[]{:S(2)}) collective-permute-start(bf16[352,512]{1,0:T(8,128)(2,1)S(1)} %fusion.18), channel_id=1, source_target_pairs={{4,0},{8,12},{5,1},{9,13},{6,2},{10,14},{7,3},{11,15},{20,16},{24,... | collective-permute-start | bytes 1081352 | tf_op jit(solution)/shard_map/ppermute | solution.py:69
  103.8 43.0 %collective-permute-start.14 = (bf16[352,512]{1,0:T(8,128)(2,1)S(1)}, bf16[352,512]{1,0:T(8,128)(2,1)S(1)}, u32[]{:S(2)}, u32[]{:S(2)}) collective-permute-start(bf16[352,512]{1,0:T(8,128)(2,1)S(1)} %fusion.19), channel_id=1, source_target_pairs={{4,0},{8,12},{5,1},{9,13},{6,2},{10,14},{7,3},{11,15},{20,16},{24,... | collective-permute-start | bytes 1081352 | tf_op jit(solution)/shard_map/ppermute | solution.py:69
  120.1 27.2 %collective-permute-start.18 = (bf16[352,512]{1,0:T(8,128)(2,1)S(1)}, bf16[352,512]{1,0:T(8,128)(2,1)S(1)}, u32[]{:S(2)}, u32[]{:S(2)}) collective-permute-start(bf16[352,512]{1,0:T(8,128)(2,1)S(1)} %fusion.20), channel_id=1, source_target_pairs={{4,0},{8,12},{5,1},{9,13},{6,2},{10,14},{7,3},{11,15},{20,16},{24,... | collective-permute-start | bytes 1081352 | tf_op jit(solution)/shard_map/ppermute | solution.py:69
  121.4 20.1 %slice-start = ((s8[5767168]{0:T(1024)(128)(4,1)}), s8[4194304]{0:T(1024)(128)(4,1)S(1)}, s32[]{:S(2)}) async-start(s8[5767168]{0:T(1024)(128)(4,1)} %bitcast.106), calls=%async_computation.1 | async-start | bytes 8388608
  123.0 18.5 %collective-permute-start.6 = (bf16[352,512]{1,0:T(8,128)(2,1)S(1)}, bf16[352,512]{1,0:T(8,128)(2,1)S(1)}, u32[]{:S(2)}, u32[]{:S(2)}) collective-permute-start(bf16[352,512]{1,0:T(8,128)(2,1)S(1)} %fusion.17), channel_id=1, source_target_pairs={{4,0},{8,12},{5,1},{9,13},{6,2},{10,14},{7,3},{11,15},{20,16},{24,... | collective-permute-start | bytes 1081352 | tf_op jit(solution)/shard_map/ppermute | solution.py:69
  124.8 16.6 %slice-start.1 = ((s8[5767168]{0:T(1024)(128)(4,1)}), s8[1572864]{0:T(1024)(128)(4,1)S(1)}, s32[]{:S(2)}) async-start(s8[5767168]{0:T(1024)(128)(4,1)} %bitcast.106), calls=%async_computation.2 | async-start | bytes 3145728
  (3 other events, 25.9 us)

commit v10 on v6

--- a/solution.py
+++ b/solution.py
@@ -40,7 +40,9 @@
     d = lax.axis_index("dp")
     hid = saved.shape[1]
     blk = hid // 4
-    width = scaled.shape[1] // chunks
+    model_width = scaled.shape[1]
+    unit = model_width // (2 * chunks)
+    widths = [unit, 3 * unit, 3 * unit, model_width - 7 * unit] if chunks == 4 else [model_width]
     ends = [(0, 1), (3, 2)]
     lhs = jnp.concatenate([saved, hfull], axis=0)
     row2 = jnp.where(d == 1, 2 * blk, 0)
@@ -50,8 +52,10 @@
     half = jnp.where(d == 1, blk, 0)
     edge = (d == 0) | (d == 3)
     pieces = []
-    for c in range(chunks):
-        sc = scaled[:, c * width:(c + 1) * width]
+    begin = 0
+    for width in widths:
+        sc = scaled[:, begin:begin + width]
+        begin += width
         srecv = lax.ppermute(sc, "dp", ends)
         rhs = jnp.concatenate([sc, srecv], axis=0)
         acc = lax.dot_general(

time: 135 us -> 171 us (1.27)
  waiting for transfers between devices: 80.4 us -> 116 us
    ppermute x4, waiting for transfers between devices: 45.8 us -> 73.9 us  [line_weight_grad(): r3 = lax.ppermute(s3, 'dp', [(1, 0), (2, 3)])]
    ppermute x4, waiting for transfers between devices: 14 us -> 21.8 us  [line_weight_grad(): srecv = lax.ppermute(sc, 'dp', ends)]
  transfers between devices with their start and end apart: 15 -> 15, of which waited for: 10 -> 8; matrix products, arithmetic and copies ran while one was open for 15% -> 12% of each run, Pallas kernels for 0% -> 0%
where the time goes in v10:
time: 171 us; the launch traced here: 170 us
  waiting for transfers between devices  116 us (68%)
  starting transfers between devices  28.6 us (17%)
  matrix products  16.3 us (10%)
  other arithmetic  4.24 us (2%)
  local copies, waits for them, and re-layouts  3.81 us (2%)
    ppermute x4, waiting for transfers between devices, line_weight_grad(): r3 = lax.ppermute(s3, 'dp', [(1, 0), (2, 3)])  73.9 us
    ppermute x4, waiting for transfers between devices, line_weight_grad(): srecv = lax.ppermute(sc, 'dp', ends)  21.8 us
    all_to_all x1, waiting for transfers between devices, shards(): lax.all_to_all(outgoing, 'expert', split_axis=0, concat_axis=0, tiled=True)  12.3 us
    dot_general x4, matrix products, line_weight_grad(): lax.dot_general(lhs, rhs, (((0,), (0,)), ((), ())), preferred_element_typ...  10.9 us
    ppermute x4, starting transfers between devices, line_weight_grad(): srecv = lax.ppermute(sc, 'dp', ends)  9.08 us
    ppermute x1, waiting for transfers between devices, shifted(): return lax.ppermute(value, axis, pairs)  8.3 us
    ppermute x4, starting transfers between devices, line_weight_grad(): r3 = lax.ppermute(s3, 'dp', [(1, 0), (2, 3)])  5.17 us
    ppermute x1, starting transfers between devices, send_hidden(): return lax.ppermute(hsend, 'dp', [(0, 1), (3, 2)])  4.66 us
  transfers between devices with their start and end apart: 15, of which 8 were waited for; matrix products, arithmetic and copies ran while one was open for 12% of the time, Pallas kernels for 0%

profile of v10, /device:TPU:0, one launch (start us, length us, event | category | flops | bytes accessed | tf_op | source)
XLA Modules:
  0.0 170.3 jit_solution(8905295745621567147)
XLA Ops:
  0.6 3.0 %collective-permute-start = (bf16[1,128,2048]{2,1,0:T(8,128)(2,1)}, bf16[1,128,2048]{2,1,0:T(8,128)(2,1)S(1)}, u32[]{:S(2)}, u32[]{:S(2)}) collective-permute-start(bf16[1,128,2048]{2,1,0:T(8,128)(2,1)} %param.5), channel_id=1, source_target_pairs={{0,16},{16,0},{1,17},{17,1},{2,18},{18,2},{3,19},{19,3},{4,20},{20... | collective-permute-start | bytes 1572872 | tf_op jit(solution)/shard_map/ppermute | solution.py:10
  7.5 8.3 %collective-permute-done = bf16[1,128,2048]{2,1,0:T(8,128)(2,1)S(1)} collective-permute-done((bf16[1,128,2048]{2,1,0:T(8,128)(2,1)}, bf16[1,128,2048]{2,1,0:T(8,128)(2,1)S(1)}, u32[]{:S(2)}, u32[]{:S(2)}) %collective-permute-start) | collective-permute-done | bytes 524320 | tf_op jit(solution)/shard_map/ppermute | solution.py:10
  16.4 1.7 fusion.5
  18.0 3.7 %all-to-all-start = ((bf16[4,80,2048]{2,1,0:T(8,128)(2,1)}), bf16[4,80,2048]{2,1,0:T(8,128)(2,1)S(1)}, u32[]{:S(2)}, u32[]{:S(2)}) async-start(bf16[4,80,2048]{2,1,0:T(8,128)(2,1)} %bitcast.8), calls=%async_computation | async-start | bytes 2621440 | tf_op jit(solution)/shard_map/all_to_all | solution.py:91
  21.9 4.7 %collective-permute-start.1 = (bf16[320,1408]{1,0:T(8,128)(2,1)S(1)}, bf16[320,1408]{1,0:T(8,128)(2,1)}, u32[]{:S(2)}, u32[]{:S(2)}) collective-permute-start(bf16[320,1408]{1,0:T(8,128)(2,1)S(1)} %fusion.9), channel_id=1, source_target_pairs={{0,4},{12,8},{1,5},{13,9},{2,6},{14,10},{3,7},{15,11},{16,20},{28,... | collective-permute-start | bytes 2703368 | tf_op jit(solution)/shard_map/ppermute | solution.py:36
  26.6 12.3 %all-to-all-done = bf16[4,80,2048]{2,1,0:T(8,128)(2,1)S(1)} async-done(((bf16[4,80,2048]{2,1,0:T(8,128)(2,1)}), bf16[4,80,2048]{2,1,0:T(8,128)(2,1)S(1)}, u32[]{:S(2)}, u32[]{:S(2)}) %all-to-all-start) | async-done | bytes 1310752 | tf_op jit(solution)/shard_map/all_to_all | solution.py:91
  38.9 4.4 %collective-permute-start.2 = (bf16[320,256]{1,0:T(8,128)(2,1)S(1)}, bf16[320,256]{1,0:T(8,128)(2,1)}, u32[]{:S(2)}, u32[]{:S(2)}) collective-permute-start(bf16[320,256]{1,0:T(8,128)(2,1)S(1)} %get-tuple-element.7), channel_id=1, source_target_pairs={{0,4},{12,8},{1,5},{13,9},{2,6},{14,10},{3,7},{15,11},{16,20},{28,... | collective-permute-start | bytes 491528 | tf_op jit(solution)/shard_map/ppermute | solution.py:59
  44.4 2.1 %collective-permute-start.9 = (bf16[320,768]{1,0:T(8,128)(2,1)}, bf16[320,768]{1,0:T(8,128)(2,1)}, u32[]{:S(2)}, u32[]{:S(2)}) collective-permute-start(bf16[320,768]{1,0:T(8,128)(2,1)} %get-tuple-element.9), channel_id=1, source_target_pairs={{0,4},{12,8},{1,5},{13,9},{2,6},{14,10},{3,7},{15,11},{16,20},{28,... | collective-permute-start | bytes 1474568 | tf_op jit(solution)/shard_map/ppermute | solution.py:59
  46.4 1.3 collective-permute-start.6
  47.8 1.3 collective-permute-start.3
  49.5 2.0 %fusion.27 = f32[1408,256]{1,0:T(8,128)S(1)} fusion(bf16[320,256]{1,0:T(8,128)(2,1)} %collective-permute-done.2, bf16[320,256]{1,0:T(8,128)(2,1)S(1)} %get-tuple-element.7, bf16[320,1408]{1,0:T(8,128)(2,1)} %collective-permute-done.1, bf16[320,1408]{1,0:T(8,128)(2,1)S(1)} %bitcast.51), kind=kOutput, calls=%fused_computation.39 | convolution fusion | flops 465633280 | bytes 3571712 | tf_op jit(solution)/shard_map/dot_general | solution.py:61
  52.3 21.4 %collective-permute-done.3 = bf16[320,256]{1,0:T(8,128)(2,1)S(1)} collective-permute-done((bf16[320,256]{1,0:T(8,128)(2,1)S(1)}, bf16[320,256]{1,0:T(8,128)(2,1)S(1)}, u32[]{:S(2)}, u32[]{:S(2)}) %collective-permute-start.3) | collective-permute-done | bytes 163872 | tf_op jit(solution)/shard_map/ppermute | solution.py:59
  73.6 1.9 %fusion.31 = f32[1408,256]{1,0:T(8,128)S(1)} fusion(bf16[320,256]{1,0:T(8,128)(2,1)S(1)} %collective-permute-done.3, bf16[320,256]{1,0:T(8,128)(2,1)S(1)} %get-tuple-element.6, bf16[320,1408]{1,0:T(8,128)(2,1)} %collective-permute-done.1, bf16[320,1408]{1,0:T(8,128)(2,1)S(1)} %bitcast.52), kind=kOutput, calls=%fused_computation.43 | convolution fusion | flops 465633280 | bytes 3571712 | tf_op jit(solution)/shard_map/dot_general | solution.py:61
  75.6 3.4 %fusion.16 = f32[1408,768]{1,0:T(8,128)S(1)} fusion(bf16[320,768]{1,0:T(8,128)(2,1)} %collective-permute-done.9, bf16[320,768]{1,0:T(8,128)(2,1)} %get-tuple-element.9, bf16[320,1408]{1,0:T(8,128)(2,1)} %collective-permute-done.1, bf16[320,1408]{1,0:T(8,128)(2,1)S(1)} %bitcast.53), kind=kOutput, calls=%fused_computation.24 | convolution fusion | flops 1389690880 | bytes 7110656 | tf_op jit(solution)/shard_map/dot_general | solution.py:61
  80.0 3.6 %fusion.12 = f32[1408,768]{1,0:T(8,128)S(1)} fusion(bf16[320,768]{1,0:T(8,128)(2,1)S(1)} %collective-permute-done.6, bf16[320,768]{1,0:T(8,128)(2,1)S(1)} %copy-done.1, bf16[320,1408]{1,0:T(8,128)(2,1)} %collective-permute-done.1, bf16[320,1408]{1,0:T(8,128)(2,1)S(1)} %bitcast.54), kind=kOutput, calls=%fused_computation.20 | convolution fusion | flops 1389690880 | bytes 7110656 | tf_op jit(solution)/shard_map/dot_general | solution.py:61
  85.2 3.2 %fusion.6 = bf16[1,1,1,320,1408]{4,3,2,1,0:T(8,128)(2,1)} fusion(bf16[320,2048]{1,0:T(8,128)(2,1)S(1)} %bitcast.50, bf16[1,1,1408,2048]{3,2,1,0:T(8,128)(2,1)S(1)} %bitcast.58), kind=kOutput, calls=%fused_computation.6 | convolution fusion | flops 1845944320 | bytes 7979008 | tf_op jit(solution)/shard_map/sd,hd->sh/dot_general | solution.py:104
  88.5 1.3 collective-permute-start.13
  89.9 1.3 collective-permute-start.5
  91.3 1.3 collective-permute-start.11
  94.1 8.5 %collective-permute-done.13 = bf16[352,256]{1,0:T(8,128)(2,1)S(1)} collective-permute-done((bf16[352,256]{1,0:T(8,128)(2,1)S(1)}, bf16[352,256]{1,0:T(8,128)(2,1)S(1)}, u32[]{:S(2)}, u32[]{:S(2)}) %collective-permute-start.13) | collective-permute-done | bytes 180256 | tf_op jit(solution)/shard_map/ppermute | solution.py:70
  102.6 44.2 %collective-permute-done.5 = bf16[352,256]{1,0:T(8,128)(2,1)S(1)} collective-permute-done((bf16[352,256]{1,0:T(8,128)(2,1)S(1)}, bf16[352,256]{1,0:T(8,128)(2,1)S(1)}, u32[]{:S(2)}, u32[]{:S(2)}) %collective-permute-start.5) | collective-permute-done | bytes 180256 | tf_op jit(solution)/shard_map/ppermute | solution.py:70
  146.9 11.5 %collective-permute-done.11 = bf16[352,768]{1,0:T(8,128)(2,1)S(1)} collective-permute-done((bf16[352,768]{1,0:T(8,128)(2,1)S(1)}, bf16[352,768]{1,0:T(8,128)(2,1)S(1)}, u32[]{:S(2)}, u32[]{:S(2)}) %collective-permute-start.11) | collective-permute-done | bytes 540704 | tf_op jit(solution)/shard_map/ppermute | solution.py:70
  158.6 9.6 %collective-permute-done.8 = bf16[352,768]{1,0:T(8,128)(2,1)S(1)} collective-permute-done((bf16[352,768]{1,0:T(8,128)(2,1)S(1)}, bf16[352,768]{1,0:T(8,128)(2,1)S(1)}, u32[]{:S(2)}, u32[]{:S(2)}) %collective-permute-start.8) | collective-permute-done | bytes 540704 | tf_op jit(solution)/shard_map/ppermute | solution.py:70
  168.4 1.9 %maximum_bitcast_fusion = f32[1,1,352,2048]{3,2,1,0:T(8,128)} fusion(f32[352,256]{1,0:T(8,128)S(1)} %convert_add_fusion.2, f32[352,768]{1,0:T(8,128)S(1)} %convert_add_fusion, f32[352,768]{1,0:T(8,128)S(1)} %convert_add_fusion.1, f32[352,256]{1,0:T(8,128)S(1)} %convert_add_fusion.3), kind=kLoop, calls=%fused_computation.2 | loop fusion | flops 2162688 | bytes 5767168 | tf_op jit(solution)/shard_map/reshape | solution.py:108
  (56 shorter events, 11.4 us)
Async XLA Ops:
  0.6 15.2 %collective-permute-start = (bf16[1,128,2048]{2,1,0:T(8,128)(2,1)}, bf16[1,128,2048]{2,1,0:T(8,128)(2,1)S(1)}, u32[]{:S(2)}, u32[]{:S(2)}) collective-permute-start(bf16[1,128,2048]{2,1,0:T(8,128)(2,1)} %param.5), channel_id=1, source_target_pairs={{0,16},{16,0},{1,17},{17,1},{2,18},{18,2},{3,19},{19,3},{4,20},{20... | collective-permute-start | bytes 1572872 | tf_op jit(solution)/shard_map/ppermute | solution.py:10
  18.0 3.7 %copy-start = (bf16[1,1,1,320,1408]{4,3,2,1,0:T(8,128)(2,1)S(1)}, bf16[1,1,1,320,1408]{4,3,2,1,0:T(8,128)(2,1)}, u32[]{:S(2)}) copy-start(bf16[1,1,1,320,1408]{4,3,2,1,0:T(8,128)(2,1)} %param.8) | copy-start | bytes 2703364
  18.0 20.9 %all-to-all-start = ((bf16[4,80,2048]{2,1,0:T(8,128)(2,1)}), bf16[4,80,2048]{2,1,0:T(8,128)(2,1)S(1)}, u32[]{:S(2)}, u32[]{:S(2)}) async-start(bf16[4,80,2048]{2,1,0:T(8,128)(2,1)} %bitcast.8), calls=%async_computation | async-start | bytes 2621440 | tf_op jit(solution)/shard_map/all_to_all | solution.py:91
  21.9 27.1 %collective-permute-start.1 = (bf16[320,1408]{1,0:T(8,128)(2,1)S(1)}, bf16[320,1408]{1,0:T(8,128)(2,1)}, u32[]{:S(2)}, u32[]{:S(2)}) collective-permute-start(bf16[320,1408]{1,0:T(8,128)(2,1)S(1)} %fusion.9), channel_id=1, source_target_pairs={{0,4},{12,8},{1,5},{13,9},{2,6},{14,10},{3,7},{15,11},{16,20},{28,... | collective-permute-start | bytes 2703368 | tf_op jit(solution)/shard_map/ppermute | solution.py:36
  38.9 10.6 %collective-permute-start.2 = (bf16[320,256]{1,0:T(8,128)(2,1)S(1)}, bf16[320,256]{1,0:T(8,128)(2,1)}, u32[]{:S(2)}, u32[]{:S(2)}) collective-permute-start(bf16[320,256]{1,0:T(8,128)(2,1)S(1)} %get-tuple-element.7), channel_id=1, source_target_pairs={{0,4},{12,8},{1,5},{13,9},{2,6},{14,10},{3,7},{15,11},{16,20},{28,... | collective-permute-start | bytes 491528 | tf_op jit(solution)/shard_map/ppermute | solution.py:59
  44.4 31.2 %collective-permute-start.9 = (bf16[320,768]{1,0:T(8,128)(2,1)}, bf16[320,768]{1,0:T(8,128)(2,1)}, u32[]{:S(2)}, u32[]{:S(2)}) collective-permute-start(bf16[320,768]{1,0:T(8,128)(2,1)} %get-tuple-element.9), channel_id=1, source_target_pairs={{0,4},{12,8},{1,5},{13,9},{2,6},{14,10},{3,7},{15,11},{16,20},{28,... | collective-permute-start | bytes 1474568 | tf_op jit(solution)/shard_map/ppermute | solution.py:59
  46.4 33.5 %collective-permute-start.6 = (bf16[320,768]{1,0:T(8,128)(2,1)}, bf16[320,768]{1,0:T(8,128)(2,1)S(1)}, u32[]{:S(2)}, u32[]{:S(2)}) collective-permute-start(bf16[320,768]{1,0:T(8,128)(2,1)} %get-tuple-element.8), channel_id=1, source_target_pairs={{0,4},{12,8},{1,5},{13,9},{2,6},{14,10},{3,7},{15,11},{16,20},{28,... | collective-permute-start | bytes 1474568 | tf_op jit(solution)/shard_map/ppermute | solution.py:59
  47.8 25.9 %collective-permute-start.3 = (bf16[320,256]{1,0:T(8,128)(2,1)S(1)}, bf16[320,256]{1,0:T(8,128)(2,1)S(1)}, u32[]{:S(2)}, u32[]{:S(2)}) collective-permute-start(bf16[320,256]{1,0:T(8,128)(2,1)S(1)} %get-tuple-element.6), channel_id=1, source_target_pairs={{0,4},{12,8},{1,5},{13,9},{2,6},{14,10},{3,7},{15,11},{16,20},{28,... | collective-permute-start | bytes 491528 | tf_op jit(solution)/shard_map/ppermute | solution.py:59
  51.6 36.9 %collective-permute-start.12 = (bf16[704,256]{1,0:T(8,128)(2,1)S(1)}, bf16[704,256]{1,0:T(8,128)(2,1)S(1)}, u32[]{:S(2)}, u32[]{:S(2)}) collective-permute-start(bf16[704,256]{1,0:T(8,128)(2,1)S(1)} %dynamic-slice_convert_fusion.3), channel_id=1, source_target_pairs={{4,8},{8,4},{5,9},{9,5},{6,10},{10,6},{7,11},{11,7},{20,24},{24,20... | collective-permute-start | bytes 1081352 | tf_op jit(solution)/shard_map/ppermute | solution.py:65
  78.9 1.0 copy-start.1
  79.0 6.3 %slice-start = ((s8[5767168]{0:T(1024)(128)(4,1)}), s8[4194304]{0:T(1024)(128)(4,1)S(1)}, s32[]{:S(2)}) async-start(s8[5767168]{0:T(1024)(128)(4,1)} %bitcast.57), calls=%async_computation.1 | async-start | bytes 8388608
  79.1 6.1 %slice-start.1 = ((s8[5767168]{0:T(1024)(128)(4,1)}), s8[1572864]{0:T(1024)(128)(4,1)S(1)}, s32[]{:S(2)}) async-start(s8[5767168]{0:T(1024)(128)(4,1)} %bitcast.57), calls=%async_computation.2 | async-start | bytes 3145728
  79.1 12.1 %collective-permute-start.10 = (bf16[704,768]{1,0:T(8,128)(2,1)S(1)}, bf16[704,768]{1,0:T(8,128)(2,1)S(1)}, u32[]{:S(2)}, u32[]{:S(2)}) collective-permute-start(bf16[704,768]{1,0:T(8,128)(2,1)S(1)} %dynamic-slice_convert_fusion), channel_id=1, source_target_pairs={{4,8},{8,4},{5,9},{9,5},{6,10},{10,6},{7,11},{11,7},{20,24},{24,20... | collective-permute-start | bytes 3244040 | tf_op jit(solution)/shard_map/ppermute | solution.py:65
  83.7 8.9 %collective-permute-start.7 = (bf16[704,768]{1,0:T(8,128)(2,1)S(1)}, bf16[704,768]{1,0:T(8,128)(2,1)S(1)}, u32[]{:S(2)}, u32[]{:S(2)}) collective-permute-start(bf16[704,768]{1,0:T(8,128)(2,1)S(1)} %dynamic-slice_convert_fusion.1), channel_id=1, source_target_pairs={{4,8},{8,4},{5,9},{9,5},{6,10},{10,6},{7,11},{11,7},{20,24},{24,20... | collective-permute-start | bytes 3244040 | tf_op jit(solution)/shard_map/ppermute | solution.py:65
  84.5 5.3 %collective-permute-start.4 = (bf16[704,256]{1,0:T(8,128)(2,1)S(1)}, bf16[704,256]{1,0:T(8,128)(2,1)S(1)}, u32[]{:S(2)}, u32[]{:S(2)}) collective-permute-start(bf16[704,256]{1,0:T(8,128)(2,1)S(1)} %dynamic-slice_convert_fusion.2), channel_id=1, source_target_pairs={{4,8},{8,4},{5,9},{9,5},{6,10},{10,6},{7,11},{11,7},{20,24},{24,20... | collective-permute-start | bytes 1081352 | tf_op jit(solution)/shard_map/ppermute | solution.py:65
  88.5 14.1 %collective-permute-start.13 = (bf16[352,256]{1,0:T(8,128)(2,1)S(1)}, bf16[352,256]{1,0:T(8,128)(2,1)S(1)}, u32[]{:S(2)}, u32[]{:S(2)}) collective-permute-start(bf16[352,256]{1,0:T(8,128)(2,1)S(1)} %add_convert_fusion.2), channel_id=1, source_target_pairs={{4,0},{8,12},{5,1},{9,13},{6,2},{10,14},{7,3},{11,15},{20,16},{24,... | collective-permute-start | bytes 540680 | tf_op jit(solution)/shard_map/ppermute | solution.py:70
  89.9 57.0 %collective-permute-start.5 = (bf16[352,256]{1,0:T(8,128)(2,1)S(1)}, bf16[352,256]{1,0:T(8,128)(2,1)S(1)}, u32[]{:S(2)}, u32[]{:S(2)}) collective-permute-start(bf16[352,256]{1,0:T(8,128)(2,1)S(1)} %add_convert_fusion.3), channel_id=1, source_target_pairs={{4,0},{8,12},{5,1},{9,13},{6,2},{10,14},{7,3},{11,15},{20,16},{24,... | collective-permute-start | bytes 540680 | tf_op jit(solution)/shard_map/ppermute | solution.py:70
  91.3 67.1 %collective-permute-start.11 = (bf16[352,768]{1,0:T(8,128)(2,1)S(1)}, bf16[352,768]{1,0:T(8,128)(2,1)S(1)}, u32[]{:S(2)}, u32[]{:S(2)}) collective-permute-start(bf16[352,768]{1,0:T(8,128)(2,1)S(1)} %add_convert_fusion), channel_id=1, source_target_pairs={{4,0},{8,12},{5,1},{9,13},{6,2},{10,14},{7,3},{11,15},{20,16},{24,... | collective-permute-start | bytes 1622024 | tf_op jit(solution)/shard_map/ppermute | solution.py:70
  92.8 75.4 %collective-permute-start.8 = (bf16[352,768]{1,0:T(8,128)(2,1)S(1)}, bf16[352,768]{1,0:T(8,128)(2,1)S(1)}, u32[]{:S(2)}, u32[]{:S(2)}) collective-permute-start(bf16[352,768]{1,0:T(8,128)(2,1)S(1)} %add_convert_fusion.1), channel_id=1, source_target_pairs={{4,0},{8,12},{5,1},{9,13},{6,2},{10,14},{7,3},{11,15},{20,16},{24,... | collective-permute-start | bytes 1622024 | tf_op jit(solution)/shard_map/ppermute | solution.py:70

commit v11 on v6

--- a/solution.py
+++ b/solution.py
@@ -31,9 +31,8 @@
 def send_hidden(saved):
     d = lax.axis_index("dp")
     blk = saved.shape[1] // 4
-    column_block = lax.broadcasted_iota(jnp.int32, saved.shape, 1) // blk
-    hsend = jnp.where(column_block == d, jnp.zeros_like(saved), saved)
-    return lax.ppermute(hsend, "dp", [(0, 1), (3, 2)])
+    part = lax.dynamic_slice_in_dim(saved.T, jnp.where(d == 0, blk, 0), 3 * blk, axis=0)
+    return lax.ppermute(part, "dp", [(0, 1), (3, 2)])
 
 
 def line_weight_grad(saved, hfull, scaled, chunks):
@@ -42,7 +41,7 @@
     blk = hid // 4
     width = scaled.shape[1] // chunks
     ends = [(0, 1), (3, 2)]
-    lhs = jnp.concatenate([saved, hfull], axis=0)
+    place = jnp.where(d == 1, blk, 0)
     row2 = jnp.where(d == 1, 2 * blk, 0)
     row3a = jnp.where(d == 1, 0, 3 * blk)
     row3b = jnp.where(d == 1, 0, blk)
@@ -53,10 +52,11 @@
     for c in range(chunks):
         sc = scaled[:, c * width:(c + 1) * width]
         srecv = lax.ppermute(sc, "dp", ends)
-        rhs = jnp.concatenate([sc, srecv], axis=0)
         acc = lax.dot_general(
-            lhs, rhs, (((0,), (0,)), ((), ())), preferred_element_type=jnp.float32
+            saved, sc, (((0,), (0,)), ((), ())), preferred_element_type=jnp.float32
         )
+        near = jnp.dot(hfull, srecv, preferred_element_type=jnp.float32)
+        acc = acc + lax.dynamic_update_slice_in_dim(jnp.zeros_like(acc), near, place, axis=0)
         s2 = lax.dynamic_slice_in_dim(acc, row2, 2 * blk, axis=0).astype(jnp.bfloat16)
         r2 = lax.ppermute(s2, "dp", [(1, 2), (2, 1)])
         s3 = (

time: 135 us -> 159 us (1.18)
  waiting for transfers between devices: 80.4 us -> 109 us
  matrix products: 15.8 us -> 12.3 us
  starting transfers between devices: 28.6 us -> 26.5 us
    ppermute x4, waiting for transfers between devices: 45.8 us -> 67.5 us  [line_weight_grad(): r3 = lax.ppermute(s3, 'dp', [(1, 0), (2, 3)])]
    ppermute x4, waiting for transfers between devices: 14 us -> 20.7 us  [line_weight_grad(): srecv = lax.ppermute(sc, 'dp', ends)]
    dot_general x4 -> x8, matrix products: 10.3 us -> 6.89 us  [the longest x4 3.84 us: line_weight_grad(): lax.dot_general(saved, sc, (((0,), (0,)), ((), ())), preferred_element_ty...]
  transfers between devices with their start and end apart: 15 -> 15, of which waited for: 10 -> 7; matrix products, arithmetic and copies ran while one was open for 15% -> 11% of each run, Pallas kernels for 0% -> 0%
where the time goes in v11:
time: 159 us; the launch traced here: 158 us
  waiting for transfers between devices  109 us (69%)
  starting transfers between devices  26.5 us (17%)
  matrix products  12.3 us (8%)
  local copies, waits for them, and re-layouts  5.24 us (3%)
  other arithmetic  4.3 us (3%)
    ppermute x4, waiting for transfers between devices, line_weight_grad(): r3 = lax.ppermute(s3, 'dp', [(1, 0), (2, 3)])  67.5 us
    ppermute x4, waiting for transfers between devices, line_weight_grad(): srecv = lax.ppermute(sc, 'dp', ends)  20.7 us
    all_to_all x1, waiting for transfers between devices, shards(): lax.all_to_all(outgoing, 'expert', split_axis=0, concat_axis=0, tiled=True)  12.2 us
    ppermute x1, waiting for transfers between devices, shifted(): return lax.ppermute(value, axis, pairs)  8.3 us
    ppermute x4, starting transfers between devices, line_weight_grad(): srecv = lax.ppermute(sc, 'dp', ends)  7.68 us
    ppermute x4, starting transfers between devices, line_weight_grad(): r3 = lax.ppermute(s3, 'dp', [(1, 0), (2, 3)])  5.17 us
    dot_general x4, matrix products, line_weight_grad(): lax.dot_general(saved, sc, (((0,), (0,)), ((), ())), preferred_element_ty...  3.84 us
    ppermute x1, starting transfers between devices, send_hidden(): return lax.ppermute(part, 'dp', [(0, 1), (3, 2)])  3.77 us
  transfers between devices with their start and end apart: 15, of which 7 were waited for; matrix products, arithmetic and copies ran while one was open for 11% of the time, Pallas kernels for 0%

profile of v11, /device:TPU:0, one launch (start us, length us, event | category | flops | bytes accessed | tf_op | source)
XLA Modules:
  0.0 158.1 jit_solution(3798986369882488246)
XLA Ops:
  0.6 3.0 %collective-permute-start = (bf16[1,128,2048]{2,1,0:T(8,128)(2,1)}, bf16[1,128,2048]{2,1,0:T(8,128)(2,1)S(1)}, u32[]{:S(2)}, u32[]{:S(2)}) collective-permute-start(bf16[1,128,2048]{2,1,0:T(8,128)(2,1)} %param.5), channel_id=1, source_target_pairs={{0,16},{16,0},{1,17},{17,1},{2,18},{18,2},{3,19},{19,3},{4,20},{20... | collective-permute-start | bytes 1572872 | tf_op jit(solution)/shard_map/ppermute | solution.py:10
  4.8 1.2 reduce-window.6
  7.5 8.3 %collective-permute-done = bf16[1,128,2048]{2,1,0:T(8,128)(2,1)S(1)} collective-permute-done((bf16[1,128,2048]{2,1,0:T(8,128)(2,1)}, bf16[1,128,2048]{2,1,0:T(8,128)(2,1)S(1)}, u32[]{:S(2)}, u32[]{:S(2)}) %collective-permute-start) | collective-permute-done | bytes 524320 | tf_op jit(solution)/shard_map/ppermute | solution.py:10
  16.4 1.7 %fusion.9 = bf16[320,2048]{1,0:T(8,128)(2,1)} fusion(f32[320,2048]{1,0:T(8,128)S(1)} %fusion.23, bf16[1,128,2048]{2,1,0:T(8,128)(2,1)S(1)} %collective-permute-done, f32[128]{0:T(128)S(1)} %get-tuple-element.18, s32[128]{0:T(128)S(1)} %get-tuple-element.12), kind=kOutput, calls=%fused_computation.13 | convolution fusion | flops 169910272 | bytes 4457472 | tf_op jit(solution)/shard_map/dot_general | solution.py:26
  18.0 3.5 %all-to-all-start = ((bf16[4,80,2048]{2,1,0:T(8,128)(2,1)}), bf16[4,80,2048]{2,1,0:T(8,128)(2,1)S(1)}, u32[]{:S(2)}, u32[]{:S(2)}) async-start(bf16[4,80,2048]{2,1,0:T(8,128)(2,1)} %bitcast.8), calls=%async_computation | async-start | bytes 2621440 | tf_op jit(solution)/shard_map/all_to_all | solution.py:87
  21.6 1.2 dynamic-slice_bitcast_fusion
  22.8 3.8 %collective-permute-start.1 = (bf16[1056,320]{0,1:T(8,128)(2,1)}, bf16[1056,320]{0,1:T(8,128)(2,1)S(1)}, u32[]{:S(2)}, u32[]{:S(2)}) collective-permute-start(bf16[1056,320]{0,1:T(8,128)(2,1)} %dynamic-slice_bitcast_fusion), channel_id=1, source_target_pairs={{0,4},{12,8},{1,5},{13,9},{2,6},{14,10},{3,7},{15,11},{16,20},{28,... | collective-permute-start | bytes 2027528 | tf_op jit(solution)/shard_map/ppermute | solution.py:35
  26.6 12.2 %all-to-all-done = bf16[4,80,2048]{2,1,0:T(8,128)(2,1)S(1)} async-done(((bf16[4,80,2048]{2,1,0:T(8,128)(2,1)}), bf16[4,80,2048]{2,1,0:T(8,128)(2,1)S(1)}, u32[]{:S(2)}, u32[]{:S(2)}) %all-to-all-start) | async-done | bytes 1310752 | tf_op jit(solution)/shard_map/all_to_all | solution.py:87
  39.8 1.0 fusion.17
  40.9 3.8 %collective-permute-start.3 = (bf16[320,512]{1,0:T(8,128)(2,1)S(1)}, bf16[320,512]{1,0:T(8,128)(2,1)S(1)}, u32[]{:S(2)}, u32[]{:S(2)}) collective-permute-start(bf16[320,512]{1,0:T(8,128)(2,1)S(1)} %get-tuple-element.14), channel_id=1, source_target_pairs={{0,4},{12,8},{1,5},{13,9},{2,6},{14,10},{3,7},{15,11},{16,20},{28,... | collective-permute-start | bytes 983048 | tf_op jit(solution)/shard_map/ppermute | solution.py:54
  44.9 1.3 collective-permute-start.6
  46.5 1.3 collective-permute-start.9
  49.1 1.3 collective-permute-start.2
  51.6 20.7 %collective-permute-done.2 = bf16[320,512]{1,0:T(8,128)(2,1)S(1)} collective-permute-done((bf16[320,512]{1,0:T(8,128)(2,1)S(1)}, bf16[320,512]{1,0:T(8,128)(2,1)S(1)}, u32[]{:S(2)}, u32[]{:S(2)}) %collective-permute-start.2) | collective-permute-done | bytes 327712 | tf_op jit(solution)/shard_map/ppermute | solution.py:54
  79.2 3.2 %fusion.10 = bf16[1,1,1,320,1408]{4,3,2,1,0:T(8,128)(2,1)} fusion(bf16[320,2048]{1,0:T(8,128)(2,1)S(1)} %bitcast.88, bf16[1,1,1408,2048]{3,2,1,0:T(8,128)(2,1)S(1)} %bitcast.92), kind=kOutput, calls=%fused_computation.14 | convolution fusion | flops 1845944320 | bytes 7979008 | tf_op jit(solution)/shard_map/sd,hd->sh/dot_general | solution.py:100
  82.5 1.3 collective-permute-start.5
  84.0 1.3 collective-permute-start.8
  85.4 1.3 collective-permute-start.11
  86.8 1.3 collective-permute-start.13
  88.1 30.7 %collective-permute-done.5 = bf16[352,512]{1,0:T(8,128)(2,1)S(1)} collective-permute-done((bf16[352,512]{1,0:T(8,128)(2,1)S(1)}, bf16[352,512]{1,0:T(8,128)(2,1)S(1)}, u32[]{:S(2)}, u32[]{:S(2)}) %collective-permute-start.5) | collective-permute-done | bytes 360480 | tf_op jit(solution)/shard_map/ppermute | solution.py:66
  119.0 15.3 %collective-permute-done.8 = bf16[352,512]{1,0:T(8,128)(2,1)S(1)} collective-permute-done((bf16[352,512]{1,0:T(8,128)(2,1)S(1)}, bf16[352,512]{1,0:T(8,128)(2,1)S(1)}, u32[]{:S(2)}, u32[]{:S(2)}) %collective-permute-start.8) | collective-permute-done | bytes 360480 | tf_op jit(solution)/shard_map/ppermute | solution.py:66
  134.4 16.9 %collective-permute-done.11 = bf16[352,512]{1,0:T(8,128)(2,1)S(1)} collective-permute-done((bf16[352,512]{1,0:T(8,128)(2,1)S(1)}, bf16[352,512]{1,0:T(8,128)(2,1)S(1)}, u32[]{:S(2)}, u32[]{:S(2)}) %collective-permute-start.11) | collective-permute-done | bytes 360480 | tf_op jit(solution)/shard_map/ppermute | solution.py:66
  151.4 4.7 %collective-permute-done.13 = bf16[352,512]{1,0:T(8,128)(2,1)S(1)} collective-permute-done((bf16[352,512]{1,0:T(8,128)(2,1)S(1)}, bf16[352,512]{1,0:T(8,128)(2,1)S(1)}, u32[]{:S(2)}, u32[]{:S(2)}) %collective-permute-start.13) | collective-permute-done | bytes 360480 | tf_op jit(solution)/shard_map/ppermute | solution.py:66
  156.3 1.8 %maximum_bitcast_fusion = f32[1,1,352,2048]{3,2,1,0:T(8,128)} fusion(f32[352,512]{1,0:T(8,128)S(1)} %convert_add_fusion, f32[352,512]{1,0:T(8,128)S(1)} %convert_add_fusion.1, f32[352,512]{1,0:T(8,128)S(1)} %convert_add_fusion.2, f32[352,512]{1,0:T(8,128)S(1)} %convert_add_fusion.3), kind=kLoop, calls=%fused_computation.10 | loop fusion | flops 2162688 | bytes 5767168 | tf_op jit(solution)/shard_map/reshape | solution.py:104
  (59 shorter events, 15.1 us)
Async XLA Ops:
  0.6 21.0 %copy-start = (bf16[1,1,1,320,1408]{4,3,2,1,0:T(8,128)(2,1)S(1)}, bf16[1,1,1,320,1408]{4,3,2,1,0:T(8,128)(2,1)}, u32[]{:S(2)}) copy-start(bf16[1,1,1,320,1408]{4,3,2,1,0:T(8,128)(2,1)} %param.8) | copy-start | bytes 2703364
  0.6 15.2 %collective-permute-start = (bf16[1,128,2048]{2,1,0:T(8,128)(2,1)}, bf16[1,128,2048]{2,1,0:T(8,128)(2,1)S(1)}, u32[]{:S(2)}, u32[]{:S(2)}) collective-permute-start(bf16[1,128,2048]{2,1,0:T(8,128)(2,1)} %param.5), channel_id=1, source_target_pairs={{0,16},{16,0},{1,17},{17,1},{2,18},{18,2},{3,19},{19,3},{4,20},{20... | collective-permute-start | bytes 1572872 | tf_op jit(solution)/shard_map/ppermute | solution.py:10
  18.0 20.8 %all-to-all-start = ((bf16[4,80,2048]{2,1,0:T(8,128)(2,1)}), bf16[4,80,2048]{2,1,0:T(8,128)(2,1)S(1)}, u32[]{:S(2)}, u32[]{:S(2)}) async-start(bf16[4,80,2048]{2,1,0:T(8,128)(2,1)} %bitcast.8), calls=%async_computation | async-start | bytes 2621440 | tf_op jit(solution)/shard_map/all_to_all | solution.py:87
  22.8 28.8 %collective-permute-start.1 = (bf16[1056,320]{0,1:T(8,128)(2,1)}, bf16[1056,320]{0,1:T(8,128)(2,1)S(1)}, u32[]{:S(2)}, u32[]{:S(2)}) collective-permute-start(bf16[1056,320]{0,1:T(8,128)(2,1)} %dynamic-slice_bitcast_fusion), channel_id=1, source_target_pairs={{0,4},{12,8},{1,5},{13,9},{2,6},{14,10},{3,7},{15,11},{16,20},{28,... | collective-permute-start | bytes 2027528 | tf_op jit(solution)/shard_map/ppermute | solution.py:35
  40.9 33.1 %collective-permute-start.3 = (bf16[320,512]{1,0:T(8,128)(2,1)S(1)}, bf16[320,512]{1,0:T(8,128)(2,1)S(1)}, u32[]{:S(2)}, u32[]{:S(2)}) collective-permute-start(bf16[320,512]{1,0:T(8,128)(2,1)S(1)} %get-tuple-element.14), channel_id=1, source_target_pairs={{0,4},{12,8},{1,5},{13,9},{2,6},{14,10},{3,7},{15,11},{16,20},{28,... | collective-permute-start | bytes 983048 | tf_op jit(solution)/shard_map/ppermute | solution.py:54
  44.9 30.8 %collective-permute-start.6 = (bf16[320,512]{1,0:T(8,128)(2,1)S(1)}, bf16[320,512]{1,0:T(8,128)(2,1)S(1)}, u32[]{:S(2)}, u32[]{:S(2)}) collective-permute-start(bf16[320,512]{1,0:T(8,128)(2,1)S(1)} %get-tuple-element.16), channel_id=1, source_target_pairs={{0,4},{12,8},{1,5},{13,9},{2,6},{14,10},{3,7},{15,11},{16,20},{28,... | collective-permute-start | bytes 983048 | tf_op jit(solution)/shard_map/ppermute | solution.py:54
  46.5 30.9 %collective-permute-start.9 = (bf16[320,512]{1,0:T(8,128)(2,1)S(1)}, bf16[320,512]{1,0:T(8,128)(2,1)S(1)}, u32[]{:S(2)}, u32[]{:S(2)}) collective-permute-start(bf16[320,512]{1,0:T(8,128)(2,1)S(1)} %get-tuple-element.15), channel_id=1, source_target_pairs={{0,4},{12,8},{1,5},{13,9},{2,6},{14,10},{3,7},{15,11},{16,20},{28,... | collective-permute-start | bytes 983048 | tf_op jit(solution)/shard_map/ppermute | solution.py:54
  49.1 23.3 %collective-permute-start.2 = (bf16[320,512]{1,0:T(8,128)(2,1)S(1)}, bf16[320,512]{1,0:T(8,128)(2,1)S(1)}, u32[]{:S(2)}, u32[]{:S(2)}) collective-permute-start(bf16[320,512]{1,0:T(8,128)(2,1)S(1)} %get-tuple-element.17), channel_id=1, source_target_pairs={{0,4},{12,8},{1,5},{13,9},{2,6},{14,10},{3,7},{15,11},{16,20},{28,... | collective-permute-start | bytes 983048 | tf_op jit(solution)/shard_map/ppermute | solution.py:54
  73.2 13.5 %collective-permute-start.12 = (bf16[704,512]{1,0:T(8,128)(2,1)S(1)}, bf16[704,512]{1,0:T(8,128)(2,1)S(1)}, u32[]{:S(2)}, u32[]{:S(2)}) collective-permute-start(bf16[704,512]{1,0:T(8,128)(2,1)S(1)} %dynamic-slice_convert_fusion.3), channel_id=1, source_target_pairs={{4,8},{8,4},{5,9},{9,5},{6,10},{10,6},{7,11},{11,7},{20,24},{24,20... | collective-permute-start | bytes 2162696 | tf_op jit(solution)/shard_map/ppermute | solution.py:61
  74.7 4.5 %slice-start = ((s8[5767168]{0:T(1024)(128)(4,1)}), s8[4194304]{0:T(1024)(128)(4,1)S(1)}, s32[]{:S(2)}) async-start(s8[5767168]{0:T(1024)(128)(4,1)} %bitcast.91), calls=%async_computation.1 | async-start | bytes 8388608
  74.8 7.6 %collective-permute-start.4 = (bf16[704,512]{1,0:T(8,128)(2,1)S(1)}, bf16[704,512]{1,0:T(8,128)(2,1)S(1)}, u32[]{:S(2)}, u32[]{:S(2)}) collective-permute-start(bf16[704,512]{1,0:T(8,128)(2,1)S(1)} %dynamic-slice_convert_fusion.2), channel_id=1, source_target_pairs={{4,8},{8,4},{5,9},{9,5},{6,10},{10,6},{7,11},{11,7},{20,24},{24,20... | collective-permute-start | bytes 2162696 | tf_op jit(solution)/shard_map/ppermute | solution.py:61
  76.4 2.8 %slice-start.1 = ((s8[5767168]{0:T(1024)(128)(4,1)}), s8[1572864]{0:T(1024)(128)(4,1)S(1)}, s32[]{:S(2)}) async-start(s8[5767168]{0:T(1024)(128)(4,1)} %bitcast.91), calls=%async_computation.2 | async-start | bytes 3145728
  76.6 7.3 %collective-permute-start.7 = (bf16[704,512]{1,0:T(8,128)(2,1)S(1)}, bf16[704,512]{1,0:T(8,128)(2,1)S(1)}, u32[]{:S(2)}, u32[]{:S(2)}) collective-permute-start(bf16[704,512]{1,0:T(8,128)(2,1)S(1)} %dynamic-slice_convert_fusion.1), channel_id=1, source_target_pairs={{4,8},{8,4},{5,9},{9,5},{6,10},{10,6},{7,11},{11,7},{20,24},{24,20... | collective-permute-start | bytes 2162696 | tf_op jit(solution)/shard_map/ppermute | solution.py:61
  78.3 7.0 %collective-permute-start.10 = (bf16[704,512]{1,0:T(8,128)(2,1)S(1)}, bf16[704,512]{1,0:T(8,128)(2,1)S(1)}, u32[]{:S(2)}, u32[]{:S(2)}) collective-permute-start(bf16[704,512]{1,0:T(8,128)(2,1)S(1)} %dynamic-slice_convert_fusion), channel_id=1, source_target_pairs={{4,8},{8,4},{5,9},{9,5},{6,10},{10,6},{7,11},{11,7},{20,24},{24,20... | collective-permute-start | bytes 2162696 | tf_op jit(solution)/shard_map/ppermute | solution.py:61
  82.5 36.3 %collective-permute-start.5 = (bf16[352,512]{1,0:T(8,128)(2,1)S(1)}, bf16[352,512]{1,0:T(8,128)(2,1)S(1)}, u32[]{:S(2)}, u32[]{:S(2)}) collective-permute-start(bf16[352,512]{1,0:T(8,128)(2,1)S(1)} %add_convert_fusion.3), channel_id=1, source_target_pairs={{4,0},{8,12},{5,1},{9,13},{6,2},{10,14},{7,3},{11,15},{20,16},{24,... | collective-permute-start | bytes 1081352 | tf_op jit(solution)/shard_map/ppermute | solution.py:66
  84.0 50.3 %collective-permute-start.8 = (bf16[352,512]{1,0:T(8,128)(2,1)S(1)}, bf16[352,512]{1,0:T(8,128)(2,1)S(1)}, u32[]{:S(2)}, u32[]{:S(2)}) collective-permute-start(bf16[352,512]{1,0:T(8,128)(2,1)S(1)} %add_convert_fusion.2), channel_id=1, source_target_pairs={{4,0},{8,12},{5,1},{9,13},{6,2},{10,14},{7,3},{11,15},{20,16},{24,... | collective-permute-start | bytes 1081352 | tf_op jit(solution)/shard_map/ppermute | solution.py:66
  85.4 65.9 %collective-permute-start.11 = (bf16[352,512]{1,0:T(8,128)(2,1)S(1)}, bf16[352,512]{1,0:T(8,128)(2,1)S(1)}, u32[]{:S(2)}, u32[]{:S(2)}) collective-permute-start(bf16[352,512]{1,0:T(8,128)(2,1)S(1)} %add_convert_fusion.1), channel_id=1, source_target_pairs={{4,0},{8,12},{5,1},{9,13},{6,2},{10,14},{7,3},{11,15},{20,16},{24,... | collective-permute-start | bytes 1081352 | tf_op jit(solution)/shard_map/ppermute | solution.py:66
  86.8 69.3 %collective-permute-start.13 = (bf16[352,512]{1,0:T(8,128)(2,1)S(1)}, bf16[352,512]{1,0:T(8,128)(2,1)S(1)}, u32[]{:S(2)}, u32[]{:S(2)}) collective-permute-start(bf16[352,512]{1,0:T(8,128)(2,1)S(1)} %add_convert_fusion), channel_id=1, source_target_pairs={{4,0},{8,12},{5,1},{9,13},{6,2},{10,14},{7,3},{11,15},{20,16},{24,... | collective-permute-start | bytes 1081352 | tf_op jit(solution)/shard_map/ppermute | solution.py:66

commit v12 on v6

--- a/solution.py
+++ b/solution.py
@@ -72,20 +72,25 @@
 
 
 def shards(grad_out, routes, gates, hidden, w_down):
-    incoming = shifted(grad_out, "section", -1)[0]
     groups = lax.axis_size("expert")
     saved = hidden[0, 0, 0]
     weight = w_down[0, 0]
     slot_count = saved.shape[0]
     width = slot_count // groups
-    model_width = incoming.shape[1]
+    model_width = grad_out.shape[2]
     target = dispatch_targets(routes[0], groups, width)
-    outgoing = dispatch_rows(incoming, gates[0], target, groups, width)
     line = lax.axis_size("dp") == 4 and saved.shape[1] % 4 == 0
     if line:
         hfull = send_hidden(saved)
-    piece = lax.all_to_all(outgoing, "expert", split_axis=0, concat_axis=0, tiled=True)
-    scaled = piece.reshape(slot_count, model_width)
+    halves = 2 if model_width % 256 == 0 else 1
+    step = model_width // halves
+    parts = []
+    for h in range(halves):
+        rows = shifted(grad_out[0, :, h * step:(h + 1) * step], "section", -1)
+        outgoing = dispatch_rows(rows, gates[0], target, groups, width)
+        piece = lax.all_to_all(outgoing, "expert", split_axis=0, concat_axis=0, tiled=True)
+        parts.append(piece.reshape(slot_count, step))
+    scaled = jnp.concatenate(parts, axis=1)
     if line:
         weight_grad, anchor = line_weight_grad(saved, hfull, scaled, 4)
         late, _ = lax.optimization_barrier((scaled, anchor))

time: 135 us -> 144 us (1.067)
  waiting for transfers between devices: 80.4 us -> 84.5 us
  starting transfers between devices: 28.6 us -> 31.8 us
    ppermute x1, waiting for transfers between devices: 0.01 us -> 7.55 us  [send_hidden(): return lax.ppermute(hsend, 'dp', [(0, 1), (3, 2)])]
    ppermute x1 -> x2, waiting for transfers between devices: 8.3 us -> 3.22 us  [shifted(): return lax.ppermute(value, axis, pairs)]
    all_to_all x1 -> x2, starting transfers between devices: 3.54 us -> 6.97 us  [shards(): lax.all_to_all(outgoing, 'expert', split_axis=0, concat_axis=0, tiled=True)]
    ppermute x4, waiting for transfers between devices: 14 us -> 17.3 us  [line_weight_grad(): srecv = lax.ppermute(sc, 'dp', ends)]
    all_to_all x1 -> x2, waiting for transfers between devices: 12.3 us -> 10.8 us  [shards(): lax.all_to_all(outgoing, 'expert', split_axis=0, concat_axis=0, tiled=True)]
    dot_general x2 -> x4, matrix products: 2.23 us -> 3.3 us  [dispatch_rows(): jnp.dot(onehot.astype(jnp.bfloat16), scaled, preferred_element_type=jnp.f...]
    ppermute x1 -> x2, starting transfers between devices: 3.03 us -> 3.11 us  [shifted(): return lax.ppermute(value, axis, pairs)]
  transfers between devices with their start and end apart: 15 -> 17, of which waited for: 10 -> 12; matrix products, arithmetic and copies ran while one was open for 15% -> 16% of each run, Pallas kernels for 0% -> 0%
where the time goes in v12:
time: 144 us; the launch traced here: 143 us
  waiting for transfers between devices  84.5 us (59%)
  starting transfers between devices  31.8 us (22%)
  matrix products  16.6 us (12%)
  local copies, waits for them, and re-layouts  4.72 us (3%)
  other arithmetic  4.54 us (3%)
    ppermute x4, waiting for transfers between devices, line_weight_grad(): r3 = lax.ppermute(s3, 'dp', [(1, 0), (2, 3)])  45.7 us
    ppermute x4, waiting for transfers between devices, line_weight_grad(): srecv = lax.ppermute(sc, 'dp', ends)  17.3 us
    all_to_all x2, waiting for transfers between devices, shards(): lax.all_to_all(outgoing, 'expert', split_axis=0, concat_axis=0, tiled=True)  10.8 us
    dot_general x4, matrix products, line_weight_grad(): lax.dot_general(lhs, rhs, (((0,), (0,)), ((), ())), preferred_element_typ...  10.2 us
    ppermute x4, starting transfers between devices, line_weight_grad(): srecv = lax.ppermute(sc, 'dp', ends)  8.67 us
    ppermute x1, waiting for transfers between devices, send_hidden(): return lax.ppermute(hsend, 'dp', [(0, 1), (3, 2)])  7.55 us
    all_to_all x2, starting transfers between devices, shards(): lax.all_to_all(outgoing, 'expert', split_axis=0, concat_axis=0, tiled=True)  6.97 us
    ppermute x4, starting transfers between devices, line_weight_grad(): r3 = lax.ppermute(s3, 'dp', [(1, 0), (2, 3)])  5.17 us
  transfers between devices with their start and end apart: 17, of which 12 were waited for; matrix products, arithmetic and copies ran while one was open for 16% of the time, Pallas kernels for 0%

profile of v12, /device:TPU:0, one launch (start us, length us, event | category | flops | bytes accessed | tf_op | source)
XLA Modules:
  0.0 143.2 jit_solution(16203507970114639090)
XLA Ops:
  1.7 3.0 %collective-permute-start.1 = (bf16[128,1024]{1,0:T(8,128)(2,1)S(1)}, bf16[128,1024]{1,0:T(8,128)(2,1)S(1)}, u32[]{:S(2)}, u32[]{:S(2)}) collective-permute-start(bf16[128,1024]{1,0:T(8,128)(2,1)S(1)} %get-tuple-element.11), channel_id=1, source_target_pairs={{0,16},{16,0},{1,17},{17,1},{2,18},{18,2},{3,19},{19,3},{4,20},{20... | collective-permute-start | bytes 786440 | tf_op jit(solution)/shard_map/ppermute | solution.py:10
  8.7 3.2 %collective-permute-done.1 = bf16[128,1024]{1,0:T(8,128)(2,1)S(1)} collective-permute-done((bf16[128,1024]{1,0:T(8,128)(2,1)S(1)}, bf16[128,1024]{1,0:T(8,128)(2,1)S(1)}, u32[]{:S(2)}, u32[]{:S(2)}) %collective-permute-start.1) | collective-permute-done | bytes 262176 | tf_op jit(solution)/shard_map/ppermute | solution.py:10
  13.5 3.5 %all-to-all-start.1 = ((bf16[4,80,1024]{2,1,0:T(8,128)(2,1)}), bf16[4,80,1024]{2,1,0:T(8,128)(2,1)S(1)}, u32[]{:S(2)}, u32[]{:S(2)}) async-start(bf16[4,80,1024]{2,1,0:T(8,128)(2,1)} %bitcast.10), calls=%async_computation.1 | async-start | bytes 1310720 | tf_op jit(solution)/shard_map/all_to_all | solution.py:91
  18.7 8.5 %all-to-all-done.1 = bf16[4,80,1024]{2,1,0:T(8,128)(2,1)S(1)} async-done(((bf16[4,80,1024]{2,1,0:T(8,128)(2,1)}), bf16[4,80,1024]{2,1,0:T(8,128)(2,1)S(1)}, u32[]{:S(2)}, u32[]{:S(2)}) %all-to-all-start.1) | async-done | bytes 655392 | tf_op jit(solution)/shard_map/all_to_all | solution.py:91
  27.2 3.5 %all-to-all-start = ((bf16[4,80,1024]{2,1,0:T(8,128)(2,1)}), bf16[4,80,1024]{2,1,0:T(8,128)(2,1)S(1)}, u32[]{:S(2)}, u32[]{:S(2)}) async-start(bf16[4,80,1024]{2,1,0:T(8,128)(2,1)} %bitcast.7), calls=%async_computation | async-start | bytes 1310720 | tf_op jit(solution)/shard_map/all_to_all | solution.py:91
  30.9 4.9 %collective-permute-start.2 = (bf16[320,1408]{1,0:T(8,128)(2,1)S(1)}, bf16[320,1408]{1,0:T(8,128)(2,1)}, u32[]{:S(2)}, u32[]{:S(2)}) collective-permute-start(bf16[320,1408]{1,0:T(8,128)(2,1)S(1)} %fusion.8), channel_id=1, source_target_pairs={{0,4},{12,8},{1,5},{13,9},{2,6},{14,10},{3,7},{15,11},{16,20},{28,... | collective-permute-start | bytes 2703368 | tf_op jit(solution)/shard_map/ppermute | solution.py:36
  36.6 2.0 %collective-permute-start.3 = (bf16[320,512]{1,0:T(8,128)(2,1)}, bf16[320,512]{1,0:T(8,128)(2,1)}, u32[]{:S(2)}, u32[]{:S(2)}) collective-permute-start(bf16[320,512]{1,0:T(8,128)(2,1)} %get-tuple-element.9), channel_id=1, source_target_pairs={{0,4},{12,8},{1,5},{13,9},{2,6},{14,10},{3,7},{15,11},{16,20},{28,... | collective-permute-start | bytes 983048 | tf_op jit(solution)/shard_map/ppermute | solution.py:55
  38.6 2.3 %all-to-all-done = bf16[4,80,1024]{2,1,0:T(8,128)(2,1)S(1)} async-done(((bf16[4,80,1024]{2,1,0:T(8,128)(2,1)}), bf16[4,80,1024]{2,1,0:T(8,128)(2,1)S(1)}, u32[]{:S(2)}, u32[]{:S(2)}) %all-to-all-start) | async-done | bytes 655392 | tf_op jit(solution)/shard_map/all_to_all | solution.py:91
  41.0 4.0 %collective-permute-start.10 = (bf16[320,512]{1,0:T(8,128)(2,1)S(1)}, bf16[320,512]{1,0:T(8,128)(2,1)S(1)}, u32[]{:S(2)}, u32[]{:S(2)}) collective-permute-start(bf16[320,512]{1,0:T(8,128)(2,1)S(1)} %get-tuple-element.8), channel_id=1, source_target_pairs={{0,4},{12,8},{1,5},{13,9},{2,6},{14,10},{3,7},{15,11},{16,20},{28,... | collective-permute-start | bytes 983048 | tf_op jit(solution)/shard_map/ppermute | solution.py:55
  47.7 7.5 %collective-permute-done.2 = bf16[320,1408]{1,0:T(8,128)(2,1)} collective-permute-done((bf16[320,1408]{1,0:T(8,128)(2,1)S(1)}, bf16[320,1408]{1,0:T(8,128)(2,1)}, u32[]{:S(2)}, u32[]{:S(2)}) %collective-permute-start.2) | collective-permute-done | bytes 901152 | tf_op jit(solution)/shard_map/ppermute | solution.py:36
  55.3 7.1 %collective-permute-done.3 = bf16[320,512]{1,0:T(8,128)(2,1)} collective-permute-done((bf16[320,512]{1,0:T(8,128)(2,1)}, bf16[320,512]{1,0:T(8,128)(2,1)}, u32[]{:S(2)}, u32[]{:S(2)}) %collective-permute-start.3) | collective-permute-done | bytes 327712 | tf_op jit(solution)/shard_map/ppermute | solution.py:55
  62.4 2.7 %fusion.11 = f32[1408,512]{1,0:T(8,128)S(1)} fusion(bf16[320,512]{1,0:T(8,128)(2,1)} %collective-permute-done.3, bf16[320,512]{1,0:T(8,128)(2,1)} %get-tuple-element.9, bf16[320,1408]{1,0:T(8,128)(2,1)} %collective-permute-done.2, bf16[320,1408]{1,0:T(8,128)(2,1)S(1)} %bitcast.48), kind=kOutput, calls=%fused_computation.29 | convolution fusion | flops 927662080 | bytes 5341184 | tf_op jit(solution)/shard_map/dot_general | solution.py:57
  65.9 3.4 %collective-permute-done.10 = bf16[320,512]{1,0:T(8,128)(2,1)S(1)} collective-permute-done((bf16[320,512]{1,0:T(8,128)(2,1)S(1)}, bf16[320,512]{1,0:T(8,128)(2,1)S(1)}, u32[]{:S(2)}, u32[]{:S(2)}) %collective-permute-start.10) | collective-permute-done | bytes 327712 | tf_op jit(solution)/shard_map/ppermute | solution.py:55
  69.3 2.5 %fusion.23 = f32[1408,512]{1,0:T(8,128)S(1)} fusion(bf16[320,512]{1,0:T(8,128)(2,1)S(1)} %collective-permute-done.10, bf16[320,512]{1,0:T(8,128)(2,1)S(1)} %get-tuple-element.8, bf16[320,1408]{1,0:T(8,128)(2,1)} %collective-permute-done.2, bf16[320,1408]{1,0:T(8,128)(2,1)S(1)} %bitcast.49), kind=kOutput, calls=%fused_computation.41 | convolution fusion | flops 927662080 | bytes 5341184 | tf_op jit(solution)/shard_map/dot_general | solution.py:57
  72.6 3.7 %collective-permute-done.7 = bf16[320,512]{1,0:T(8,128)(2,1)S(1)} collective-permute-done((bf16[320,512]{1,0:T(8,128)(2,1)S(1)}, bf16[320,512]{1,0:T(8,128)(2,1)S(1)}, u32[]{:S(2)}, u32[]{:S(2)}) %collective-permute-start.7) | collective-permute-done | bytes 327712 | tf_op jit(solution)/shard_map/ppermute | solution.py:55
  76.3 2.5 %fusion.19 = f32[1408,512]{1,0:T(8,128)S(1)} fusion(bf16[320,512]{1,0:T(8,128)(2,1)S(1)} %collective-permute-done.7, bf16[320,512]{1,0:T(8,128)(2,1)S(1)} %get-tuple-element.7, bf16[320,1408]{1,0:T(8,128)(2,1)} %collective-permute-done.2, bf16[320,1408]{1,0:T(8,128)(2,1)S(1)} %bitcast.50), kind=kOutput, calls=%fused_computation.37 | convolution fusion | flops 927662080 | bytes 5341184 | tf_op jit(solution)/shard_map/dot_general | solution.py:57
  79.8 3.0 %collective-permute-done.4 = bf16[320,512]{1,0:T(8,128)(2,1)S(1)} collective-permute-done((bf16[320,512]{1,0:T(8,128)(2,1)S(1)}, bf16[320,512]{1,0:T(8,128)(2,1)S(1)}, u32[]{:S(2)}, u32[]{:S(2)}) %collective-permute-start.4) | collective-permute-done | bytes 327712 | tf_op jit(solution)/shard_map/ppermute | solution.py:55
  82.9 2.5 %fusion.15 = f32[1408,512]{1,0:T(8,128)S(1)} fusion(bf16[320,512]{1,0:T(8,128)(2,1)S(1)} %collective-permute-done.4, bf16[320,512]{1,0:T(8,128)(2,1)S(1)} %get-tuple-element.6, bf16[320,1408]{1,0:T(8,128)(2,1)} %collective-permute-done.2, bf16[320,1408]{1,0:T(8,128)(2,1)S(1)} %bitcast.51), kind=kOutput, calls=%fused_computation.33 | convolution fusion | flops 927662080 | bytes 5341184 | tf_op jit(solution)/shard_map/dot_general | solution.py:57
  86.2 3.2 %fusion.5 = bf16[1,1,1,320,1408]{4,3,2,1,0:T(8,128)(2,1)} fusion(bf16[320,2048]{1,0:T(8,128)(2,1)S(1)} %pad_maximum_fusion.1, bf16[1,1,1408,2048]{3,2,1,0:T(8,128)(2,1)S(1)} %bitcast.55), kind=kOutput, calls=%fused_computation.4 | convolution fusion | flops 1845944320 | bytes 7979008 | tf_op jit(solution)/shard_map/sd,hd->sh/dot_general | solution.py:105
  95.1 10.1 %collective-permute-done.14 = bf16[352,512]{1,0:T(8,128)(2,1)S(1)} collective-permute-done((bf16[352,512]{1,0:T(8,128)(2,1)S(1)}, bf16[352,512]{1,0:T(8,128)(2,1)S(1)}, u32[]{:S(2)}, u32[]{:S(2)}) %collective-permute-start.14) | collective-permute-done | bytes 360480 | tf_op jit(solution)/shard_map/ppermute | solution.py:66
  105.4 6.2 %collective-permute-done.12 = bf16[352,512]{1,0:T(8,128)(2,1)S(1)} collective-permute-done((bf16[352,512]{1,0:T(8,128)(2,1)S(1)}, bf16[352,512]{1,0:T(8,128)(2,1)S(1)}, u32[]{:S(2)}, u32[]{:S(2)}) %collective-permute-start.12) | collective-permute-done | bytes 360480 | tf_op jit(solution)/shard_map/ppermute | solution.py:66
  111.8 14.5 %collective-permute-done.9 = bf16[352,512]{1,0:T(8,128)(2,1)S(1)} collective-permute-done((bf16[352,512]{1,0:T(8,128)(2,1)S(1)}, bf16[352,512]{1,0:T(8,128)(2,1)S(1)}, u32[]{:S(2)}, u32[]{:S(2)}) %collective-permute-start.9) | collective-permute-done | bytes 360480 | tf_op jit(solution)/shard_map/ppermute | solution.py:66
  126.4 14.8 %collective-permute-done.6 = bf16[352,512]{1,0:T(8,128)(2,1)S(1)} collective-permute-done((bf16[352,512]{1,0:T(8,128)(2,1)S(1)}, bf16[352,512]{1,0:T(8,128)(2,1)S(1)}, u32[]{:S(2)}, u32[]{:S(2)}) %collective-permute-start.6) | collective-permute-done | bytes 360480 | tf_op jit(solution)/shard_map/ppermute | solution.py:66
  141.4 1.8 %maximum_bitcast_fusion = f32[1,1,352,2048]{3,2,1,0:T(8,128)} fusion(f32[352,512]{1,0:T(8,128)S(1)} %convert_add_fusion, f32[352,512]{1,0:T(8,128)S(1)} %convert_add_fusion.1, f32[352,512]{1,0:T(8,128)S(1)} %convert_add_fusion.2, f32[352,512]{1,0:T(8,128)S(1)} %convert_add_fusion.3), kind=kLoop, calls=%fused_computation.2 | loop fusion | flops 2162688 | bytes 5767168 | tf_op jit(solution)/shard_map/reshape | solution.py:109
  (62 shorter events, 21.6 us)
Async XLA Ops:
  1.7 10.2 %collective-permute-start.1 = (bf16[128,1024]{1,0:T(8,128)(2,1)S(1)}, bf16[128,1024]{1,0:T(8,128)(2,1)S(1)}, u32[]{:S(2)}, u32[]{:S(2)}) collective-permute-start(bf16[128,1024]{1,0:T(8,128)(2,1)S(1)} %get-tuple-element.11), channel_id=1, source_target_pairs={{0,16},{16,0},{1,17},{17,1},{2,18},{18,2},{3,19},{19,3},{4,20},{20... | collective-permute-start | bytes 786440 | tf_op jit(solution)/shard_map/ppermute | solution.py:10
  4.7 12.3 %collective-permute-start = (bf16[128,1024]{1,0:T(8,128)(2,1)S(1)}, bf16[128,1024]{1,0:T(8,128)(2,1)S(1)}, u32[]{:S(2)}, u32[]{:S(2)}) collective-permute-start(bf16[128,1024]{1,0:T(8,128)(2,1)S(1)} %get-tuple-element.10), channel_id=1, source_target_pairs={{0,16},{16,0},{1,17},{17,1},{2,18},{18,2},{3,19},{19,3},{4,20},{20... | collective-permute-start | bytes 786440 | tf_op jit(solution)/shard_map/ppermute | solution.py:10
  13.5 13.7 %all-to-all-start.1 = ((bf16[4,80,1024]{2,1,0:T(8,128)(2,1)}), bf16[4,80,1024]{2,1,0:T(8,128)(2,1)S(1)}, u32[]{:S(2)}, u32[]{:S(2)}) async-start(bf16[4,80,1024]{2,1,0:T(8,128)(2,1)} %bitcast.10), calls=%async_computation.1 | async-start | bytes 1310720 | tf_op jit(solution)/shard_map/all_to_all | solution.py:91
  17.5 13.3 %copy-start = (bf16[1,1,1,320,1408]{4,3,2,1,0:T(8,128)(2,1)S(1)}, bf16[1,1,1,320,1408]{4,3,2,1,0:T(8,128)(2,1)}, u32[]{:S(2)}) copy-start(bf16[1,1,1,320,1408]{4,3,2,1,0:T(8,128)(2,1)} %param.8) | copy-start | bytes 2703364
  27.2 13.7 %all-to-all-start = ((bf16[4,80,1024]{2,1,0:T(8,128)(2,1)}), bf16[4,80,1024]{2,1,0:T(8,128)(2,1)S(1)}, u32[]{:S(2)}, u32[]{:S(2)}) async-start(bf16[4,80,1024]{2,1,0:T(8,128)(2,1)} %bitcast.7), calls=%async_computation | async-start | bytes 1310720 | tf_op jit(solution)/shard_map/all_to_all | solution.py:91
  30.9 24.4 %collective-permute-start.2 = (bf16[320,1408]{1,0:T(8,128)(2,1)S(1)}, bf16[320,1408]{1,0:T(8,128)(2,1)}, u32[]{:S(2)}, u32[]{:S(2)}) collective-permute-start(bf16[320,1408]{1,0:T(8,128)(2,1)S(1)} %fusion.8), channel_id=1, source_target_pairs={{0,4},{12,8},{1,5},{13,9},{2,6},{14,10},{3,7},{15,11},{16,20},{28,... | collective-permute-start | bytes 2703368 | tf_op jit(solution)/shard_map/ppermute | solution.py:36
  36.6 25.8 %collective-permute-start.3 = (bf16[320,512]{1,0:T(8,128)(2,1)}, bf16[320,512]{1,0:T(8,128)(2,1)}, u32[]{:S(2)}, u32[]{:S(2)}) collective-permute-start(bf16[320,512]{1,0:T(8,128)(2,1)} %get-tuple-element.9), channel_id=1, source_target_pairs={{0,4},{12,8},{1,5},{13,9},{2,6},{14,10},{3,7},{15,11},{16,20},{28,... | collective-permute-start | bytes 983048 | tf_op jit(solution)/shard_map/ppermute | solution.py:55
  41.0 28.3 %collective-permute-start.10 = (bf16[320,512]{1,0:T(8,128)(2,1)S(1)}, bf16[320,512]{1,0:T(8,128)(2,1)S(1)}, u32[]{:S(2)}, u32[]{:S(2)}) collective-permute-start(bf16[320,512]{1,0:T(8,128)(2,1)S(1)} %get-tuple-element.8), channel_id=1, source_target_pairs={{0,4},{12,8},{1,5},{13,9},{2,6},{14,10},{3,7},{15,11},{16,20},{28,... | collective-permute-start | bytes 983048 | tf_op jit(solution)/shard_map/ppermute | solution.py:55
  45.1 31.2 %collective-permute-start.7 = (bf16[320,512]{1,0:T(8,128)(2,1)S(1)}, bf16[320,512]{1,0:T(8,128)(2,1)S(1)}, u32[]{:S(2)}, u32[]{:S(2)}) collective-permute-start(bf16[320,512]{1,0:T(8,128)(2,1)S(1)} %get-tuple-element.7), channel_id=1, source_target_pairs={{0,4},{12,8},{1,5},{13,9},{2,6},{14,10},{3,7},{15,11},{16,20},{28,... | collective-permute-start | bytes 983048 | tf_op jit(solution)/shard_map/ppermute | solution.py:55
  46.4 36.4 %collective-permute-start.4 = (bf16[320,512]{1,0:T(8,128)(2,1)S(1)}, bf16[320,512]{1,0:T(8,128)(2,1)S(1)}, u32[]{:S(2)}, u32[]{:S(2)}) collective-permute-start(bf16[320,512]{1,0:T(8,128)(2,1)S(1)} %get-tuple-element.6), channel_id=1, source_target_pairs={{0,4},{12,8},{1,5},{13,9},{2,6},{14,10},{3,7},{15,11},{16,20},{28,... | collective-permute-start | bytes 983048 | tf_op jit(solution)/shard_map/ppermute | solution.py:55
  65.2 24.2 %collective-permute-start.13 = (bf16[704,512]{1,0:T(8,128)(2,1)S(1)}, bf16[704,512]{1,0:T(8,128)(2,1)S(1)}, u32[]{:S(2)}, u32[]{:S(2)}) collective-permute-start(bf16[704,512]{1,0:T(8,128)(2,1)S(1)} %dynamic-slice_convert_fusion.3), channel_id=1, source_target_pairs={{4,8},{8,4},{5,9},{9,5},{6,10},{10,6},{7,11},{11,7},{20,24},{24,20... | collective-permute-start | bytes 2162696 | tf_op jit(solution)/shard_map/ppermute | solution.py:61
  71.9 18.9 %collective-permute-start.11 = (bf16[704,512]{1,0:T(8,128)(2,1)S(1)}, bf16[704,512]{1,0:T(8,128)(2,1)S(1)}, u32[]{:S(2)}, u32[]{:S(2)}) collective-permute-start(bf16[704,512]{1,0:T(8,128)(2,1)S(1)} %dynamic-slice_convert_fusion), channel_id=1, source_target_pairs={{4,8},{8,4},{5,9},{9,5},{6,10},{10,6},{7,11},{11,7},{20,24},{24,20... | collective-permute-start | bytes 2162696 | tf_op jit(solution)/shard_map/ppermute | solution.py:61
  78.9 7.3 %slice-start = ((s8[5767168]{0:T(1024)(128)(4,1)}), s8[4194304]{0:T(1024)(128)(4,1)S(1)}, s32[]{:S(2)}) async-start(s8[5767168]{0:T(1024)(128)(4,1)} %bitcast.54), calls=%async_computation.2 | async-start | bytes 8388608
  79.0 7.2 %slice-start.1 = ((s8[5767168]{0:T(1024)(128)(4,1)}), s8[1572864]{0:T(1024)(128)(4,1)S(1)}, s32[]{:S(2)}) async-start(s8[5767168]{0:T(1024)(128)(4,1)} %bitcast.54), calls=%async_computation.3 | async-start | bytes 3145728
  79.0 13.3 %collective-permute-start.8 = (bf16[704,512]{1,0:T(8,128)(2,1)S(1)}, bf16[704,512]{1,0:T(8,128)(2,1)S(1)}, u32[]{:S(2)}, u32[]{:S(2)}) collective-permute-start(bf16[704,512]{1,0:T(8,128)(2,1)S(1)} %dynamic-slice_convert_fusion.1), channel_id=1, source_target_pairs={{4,8},{8,4},{5,9},{9,5},{6,10},{10,6},{7,11},{11,7},{20,24},{24,20... | collective-permute-start | bytes 2162696 | tf_op jit(solution)/shard_map/ppermute | solution.py:61
  85.5 8.2 %collective-permute-start.5 = (bf16[704,512]{1,0:T(8,128)(2,1)S(1)}, bf16[704,512]{1,0:T(8,128)(2,1)S(1)}, u32[]{:S(2)}, u32[]{:S(2)}) collective-permute-start(bf16[704,512]{1,0:T(8,128)(2,1)S(1)} %dynamic-slice_convert_fusion.2), channel_id=1, source_target_pairs={{4,8},{8,4},{5,9},{9,5},{6,10},{10,6},{7,11},{11,7},{20,24},{24,20... | collective-permute-start | bytes 2162696 | tf_op jit(solution)/shard_map/ppermute | solution.py:61
  89.5 15.8 %collective-permute-start.14 = (bf16[352,512]{1,0:T(8,128)(2,1)S(1)}, bf16[352,512]{1,0:T(8,128)(2,1)S(1)}, u32[]{:S(2)}, u32[]{:S(2)}) collective-permute-start(bf16[352,512]{1,0:T(8,128)(2,1)S(1)} %add_convert_fusion), channel_id=1, source_target_pairs={{4,0},{8,12},{5,1},{9,13},{6,2},{10,14},{7,3},{11,15},{20,16},{24,... | collective-permute-start | bytes 1081352 | tf_op jit(solution)/shard_map/ppermute | solution.py:66
  90.9 20.7 %collective-permute-start.12 = (bf16[352,512]{1,0:T(8,128)(2,1)S(1)}, bf16[352,512]{1,0:T(8,128)(2,1)S(1)}, u32[]{:S(2)}, u32[]{:S(2)}) collective-permute-start(bf16[352,512]{1,0:T(8,128)(2,1)S(1)} %add_convert_fusion.1), channel_id=1, source_target_pairs={{4,0},{8,12},{5,1},{9,13},{6,2},{10,14},{7,3},{11,15},{20,16},{24,... | collective-permute-start | bytes 1081352 | tf_op jit(solution)/shard_map/ppermute | solution.py:66
  92.4 33.9 %collective-permute-start.9 = (bf16[352,512]{1,0:T(8,128)(2,1)S(1)}, bf16[352,512]{1,0:T(8,128)(2,1)S(1)}, u32[]{:S(2)}, u32[]{:S(2)}) collective-permute-start(bf16[352,512]{1,0:T(8,128)(2,1)S(1)} %add_convert_fusion.2), channel_id=1, source_target_pairs={{4,0},{8,12},{5,1},{9,13},{6,2},{10,14},{7,3},{11,15},{20,16},{24,... | collective-permute-start | bytes 1081352 | tf_op jit(solution)/shard_map/ppermute | solution.py:66
  93.8 47.4 %collective-permute-start.6 = (bf16[352,512]{1,0:T(8,128)(2,1)S(1)}, bf16[352,512]{1,0:T(8,128)(2,1)S(1)}, u32[]{:S(2)}, u32[]{:S(2)}) collective-permute-start(bf16[352,512]{1,0:T(8,128)(2,1)S(1)} %add_convert_fusion.3), channel_id=1, source_target_pairs={{4,0},{8,12},{5,1},{9,13},{6,2},{10,14},{7,3},{11,15},{20,16},{24,... | collective-permute-start | bytes 1081352 | tf_op jit(solution)/shard_map/ppermute | solution.py:66

commit v13 on v6

--- a/solution.py
+++ b/solution.py
@@ -49,7 +49,7 @@
     own = d * blk
     half = jnp.where(d == 1, blk, 0)
     edge = (d == 0) | (d == 3)
-    pieces = []
+    result = jnp.zeros((blk, scaled.shape[1]), jnp.float32)
     for c in range(chunks):
         sc = scaled[:, c * width:(c + 1) * width]
         srecv = lax.ppermute(sc, "dp", ends)
@@ -65,10 +65,11 @@
         ).astype(jnp.bfloat16)
         r3 = lax.ppermute(s3, "dp", [(1, 0), (2, 3)])
         extra = jnp.where(edge, r3, lax.dynamic_slice_in_dim(r2, half, blk, axis=0))
-        pieces.append(
-            lax.dynamic_slice_in_dim(acc, own, blk, axis=0) + extra.astype(jnp.float32)
+        result = lax.dynamic_update_slice_in_dim(
+            result, lax.dynamic_slice_in_dim(acc, own, blk, axis=0) + extra.astype(jnp.float32),
+            c * width, axis=1,
         )
-    return jnp.concatenate(pieces, axis=1), s2
+    return result, s2
 
 
 def shards(grad_out, routes, gates, hidden, w_down):

time: 135 us -> 149 us (1.10)
  waiting for transfers between devices: 80.4 us -> 94.8 us
  local copies, waits for them, and re-layouts: 3.81 us -> 5.71 us
  other arithmetic: 4.44 us -> 2.62 us
    ppermute x4, waiting for transfers between devices: 45.8 us -> 60 us  [line_weight_grad(): r3 = lax.ppermute(s3, 'dp', [(1, 0), (2, 3)])]
    reshape x1 -> x0, other arithmetic: 1.83 us -> none  [shards(): weight_grad.reshape(1, 1, weight_grad.shape[0], model_width)]
    unnamed x9 -> x11, local copies, waits for them, and re-layouts: 0.81 us -> 2.38 us
  transfers between devices with their start and end apart: 15 -> 15, of which waited for: 10 -> 10; matrix products, arithmetic and copies ran while one was open for 15% -> 14% of each run, Pallas kernels for 0% -> 0%
where the time goes in v13:
time: 149 us; the launch traced here: 148 us
  waiting for transfers between devices  94.8 us (64%)
  starting transfers between devices  28.5 us (19%)
  matrix products  15.8 us (11%)
  local copies, waits for them, and re-layouts  5.71 us (4%)
  other arithmetic  2.62 us (2%)
    ppermute x4, waiting for transfers between devices, line_weight_grad(): r3 = lax.ppermute(s3, 'dp', [(1, 0), (2, 3)])  60 us
    ppermute x4, waiting for transfers between devices, line_weight_grad(): srecv = lax.ppermute(sc, 'dp', ends)  14.1 us
    all_to_all x1, waiting for transfers between devices, shards(): lax.all_to_all(outgoing, 'expert', split_axis=0, concat_axis=0, tiled=True)  12.3 us
    dot_general x4, matrix products, line_weight_grad(): lax.dot_general(lhs, rhs, (((0,), (0,)), ((), ())), preferred_element_typ...  10.3 us
    ppermute x4, starting transfers between devices, line_weight_grad(): srecv = lax.ppermute(sc, 'dp', ends)  9.09 us
    ppermute x1, waiting for transfers between devices, shifted(): return lax.ppermute(value, axis, pairs)  8.3 us
    ppermute x4, starting transfers between devices, line_weight_grad(): r3 = lax.ppermute(s3, 'dp', [(1, 0), (2, 3)])  5.17 us
    ppermute x1, starting transfers between devices, send_hidden(): return lax.ppermute(hsend, 'dp', [(0, 1), (3, 2)])  4.66 us
  transfers between devices with their start and end apart: 15, of which 10 were waited for; matrix products, arithmetic and copies ran while one was open for 14% of the time, Pallas kernels for 0%

profile of v13, /device:TPU:0, one launch (start us, length us, event | category | flops | bytes accessed | tf_op | source)
XLA Modules:
  0.0 148.4 jit_solution(8501556240911927035)
XLA Ops:
  0.6 3.0 %collective-permute-start = (bf16[1,128,2048]{2,1,0:T(8,128)(2,1)}, bf16[1,128,2048]{2,1,0:T(8,128)(2,1)S(1)}, u32[]{:S(2)}, u32[]{:S(2)}) collective-permute-start(bf16[1,128,2048]{2,1,0:T(8,128)(2,1)} %param.5), channel_id=1, source_target_pairs={{0,16},{16,0},{1,17},{17,1},{2,18},{18,2},{3,19},{19,3},{4,20},{20... | collective-permute-start | bytes 1572872 | tf_op jit(solution)/shard_map/ppermute | solution.py:10
  7.5 8.3 %collective-permute-done = bf16[1,128,2048]{2,1,0:T(8,128)(2,1)S(1)} collective-permute-done((bf16[1,128,2048]{2,1,0:T(8,128)(2,1)}, bf16[1,128,2048]{2,1,0:T(8,128)(2,1)S(1)}, u32[]{:S(2)}, u32[]{:S(2)}) %collective-permute-start) | collective-permute-done | bytes 524320 | tf_op jit(solution)/shard_map/ppermute | solution.py:10
  16.4 1.7 %fusion.5 = bf16[320,2048]{1,0:T(8,128)(2,1)} fusion(f32[320,2048]{1,0:T(8,128)S(1)} %fusion.28, bf16[1,128,2048]{2,1,0:T(8,128)(2,1)S(1)} %collective-permute-done, f32[128]{0:T(128)S(1)} %get-tuple-element.10, s32[128]{0:T(128)S(1)} %get-tuple-element.4), kind=kOutput, calls=%fused_computation.5 | convolution fusion | flops 169910272 | bytes 4457472 | tf_op jit(solution)/shard_map/dot_general | solution.py:26
  18.0 3.5 %all-to-all-start = ((bf16[4,80,2048]{2,1,0:T(8,128)(2,1)}), bf16[4,80,2048]{2,1,0:T(8,128)(2,1)S(1)}, u32[]{:S(2)}, u32[]{:S(2)}) async-start(bf16[4,80,2048]{2,1,0:T(8,128)(2,1)} %bitcast.8), calls=%async_computation | async-start | bytes 2621440 | tf_op jit(solution)/shard_map/all_to_all | solution.py:88
  21.8 4.7 %collective-permute-start.1 = (bf16[320,1408]{1,0:T(8,128)(2,1)S(1)}, bf16[320,1408]{1,0:T(8,128)(2,1)}, u32[]{:S(2)}, u32[]{:S(2)}) collective-permute-start(bf16[320,1408]{1,0:T(8,128)(2,1)S(1)} %fusion.9), channel_id=1, source_target_pairs={{0,4},{12,8},{1,5},{13,9},{2,6},{14,10},{3,7},{15,11},{16,20},{28,... | collective-permute-start | bytes 2703368 | tf_op jit(solution)/shard_map/ppermute | solution.py:36
  26.5 12.3 %all-to-all-done = bf16[4,80,2048]{2,1,0:T(8,128)(2,1)S(1)} async-done(((bf16[4,80,2048]{2,1,0:T(8,128)(2,1)}), bf16[4,80,2048]{2,1,0:T(8,128)(2,1)S(1)}, u32[]{:S(2)}, u32[]{:S(2)}) %all-to-all-start) | async-done | bytes 1310752 | tf_op jit(solution)/shard_map/all_to_all | solution.py:88
  39.8 4.5 %collective-permute-start.2 = (bf16[320,512]{1,0:T(8,128)(2,1)}, bf16[320,512]{1,0:T(8,128)(2,1)}, u32[]{:S(2)}, u32[]{:S(2)}) collective-permute-start(bf16[320,512]{1,0:T(8,128)(2,1)} %get-tuple-element.9), channel_id=1, source_target_pairs={{0,4},{12,8},{1,5},{13,9},{2,6},{14,10},{3,7},{15,11},{16,20},{28,... | collective-permute-start | bytes 983048 | tf_op jit(solution)/shard_map/ppermute | solution.py:55
  44.2 2.0 %collective-permute-start.3 = (bf16[320,512]{1,0:T(8,128)(2,1)}, bf16[320,512]{1,0:T(8,128)(2,1)}, u32[]{:S(2)}, u32[]{:S(2)}) collective-permute-start(bf16[320,512]{1,0:T(8,128)(2,1)} %get-tuple-element.8), channel_id=1, source_target_pairs={{0,4},{12,8},{1,5},{13,9},{2,6},{14,10},{3,7},{15,11},{16,20},{28,... | collective-permute-start | bytes 983048 | tf_op jit(solution)/shard_map/ppermute | solution.py:55
  46.2 1.3 collective-permute-start.6
  47.5 1.3 collective-permute-start.9
  48.9 4.2 %collective-permute-done.2 = bf16[320,512]{1,0:T(8,128)(2,1)} collective-permute-done((bf16[320,512]{1,0:T(8,128)(2,1)}, bf16[320,512]{1,0:T(8,128)(2,1)}, u32[]{:S(2)}, u32[]{:S(2)}) %collective-permute-start.2) | collective-permute-done | bytes 327712 | tf_op jit(solution)/shard_map/ppermute | solution.py:55
  53.0 2.7 %fusion.12 = f32[1408,512]{1,0:T(8,128)S(1)} fusion(bf16[320,512]{1,0:T(8,128)(2,1)} %collective-permute-done.2, bf16[320,512]{1,0:T(8,128)(2,1)} %get-tuple-element.9, bf16[320,1408]{1,0:T(8,128)(2,1)} %collective-permute-done.1, bf16[320,1408]{1,0:T(8,128)(2,1)S(1)} %bitcast.56), kind=kOutput, calls=%fused_computation.26 | convolution fusion | flops 927662080 | bytes 5341184 | tf_op jit(solution)/shard_map/dot_general | solution.py:57
  55.8 4.2 %collective-permute-done.3 = bf16[320,512]{1,0:T(8,128)(2,1)} collective-permute-done((bf16[320,512]{1,0:T(8,128)(2,1)}, bf16[320,512]{1,0:T(8,128)(2,1)}, u32[]{:S(2)}, u32[]{:S(2)}) %collective-permute-start.3) | collective-permute-done | bytes 327712 | tf_op jit(solution)/shard_map/ppermute | solution.py:55
  60.1 2.7 %fusion.16 = f32[1408,512]{1,0:T(8,128)S(1)} fusion(bf16[320,512]{1,0:T(8,128)(2,1)} %collective-permute-done.3, bf16[320,512]{1,0:T(8,128)(2,1)} %get-tuple-element.8, bf16[320,1408]{1,0:T(8,128)(2,1)} %collective-permute-done.1, bf16[320,1408]{1,0:T(8,128)(2,1)S(1)} %bitcast.57), kind=kOutput, calls=%fused_computation.30 | convolution fusion | flops 927662080 | bytes 5341184 | tf_op jit(solution)/shard_map/dot_general | solution.py:57
  64.3 2.8 %collective-permute-done.6 = bf16[320,512]{1,0:T(8,128)(2,1)S(1)} collective-permute-done((bf16[320,512]{1,0:T(8,128)(2,1)}, bf16[320,512]{1,0:T(8,128)(2,1)S(1)}, u32[]{:S(2)}, u32[]{:S(2)}) %collective-permute-start.6) | collective-permute-done | bytes 327712 | tf_op jit(solution)/shard_map/ppermute | solution.py:55
  67.1 2.5 %fusion.20 = f32[1408,512]{1,0:T(8,128)S(1)} fusion(bf16[320,512]{1,0:T(8,128)(2,1)S(1)} %collective-permute-done.6, bf16[320,512]{1,0:T(8,128)(2,1)S(1)} %copy-done.2, bf16[320,1408]{1,0:T(8,128)(2,1)} %collective-permute-done.1, bf16[320,1408]{1,0:T(8,128)(2,1)S(1)} %bitcast.58), kind=kOutput, calls=%fused_computation.34 | convolution fusion | flops 927662080 | bytes 5341184 | tf_op jit(solution)/shard_map/dot_general | solution.py:57
  70.6 2.9 %collective-permute-done.9 = bf16[320,512]{1,0:T(8,128)(2,1)S(1)} collective-permute-done((bf16[320,512]{1,0:T(8,128)(2,1)S(1)}, bf16[320,512]{1,0:T(8,128)(2,1)S(1)}, u32[]{:S(2)}, u32[]{:S(2)}) %collective-permute-start.9) | collective-permute-done | bytes 327712 | tf_op jit(solution)/shard_map/ppermute | solution.py:55
  73.5 2.5 %fusion.24 = f32[1408,512]{1,0:T(8,128)S(1)} fusion(bf16[320,512]{1,0:T(8,128)(2,1)S(1)} %collective-permute-done.9, bf16[320,512]{1,0:T(8,128)(2,1)S(1)} %get-tuple-element.6, bf16[320,1408]{1,0:T(8,128)(2,1)} %collective-permute-done.1, bf16[320,1408]{1,0:T(8,128)(2,1)S(1)} %bitcast.59), kind=kOutput, calls=%fused_computation.38 | convolution fusion | flops 927662080 | bytes 5341184 | tf_op jit(solution)/shard_map/dot_general | solution.py:57
  76.9 3.2 %fusion.6 = bf16[1,1,1,320,1408]{4,3,2,1,0:T(8,128)(2,1)} fusion(bf16[320,2048]{1,0:T(8,128)(2,1)S(1)} %bitcast.55, bf16[1,1,1408,2048]{3,2,1,0:T(8,128)(2,1)S(1)} %bitcast.63), kind=kOutput, calls=%fused_computation.6 | convolution fusion | flops 1845944320 | bytes 7979008 | tf_op jit(solution)/shard_map/sd,hd->sh/dot_general | solution.py:101
  85.8 22.6 %collective-permute-done.5 = bf16[352,512]{1,0:T(8,128)(2,1)S(1)} collective-permute-done((bf16[352,512]{1,0:T(8,128)(2,1)S(1)}, bf16[352,512]{1,0:T(8,128)(2,1)S(1)}, u32[]{:S(2)}, u32[]{:S(2)}) %collective-permute-start.5) | collective-permute-done | bytes 360480 | tf_op jit(solution)/shard_map/ppermute | solution.py:66
  109.0 14.9 %collective-permute-done.8 = bf16[352,512]{1,0:T(8,128)(2,1)S(1)} collective-permute-done((bf16[352,512]{1,0:T(8,128)(2,1)S(1)}, bf16[352,512]{1,0:T(8,128)(2,1)S(1)}, u32[]{:S(2)}, u32[]{:S(2)}) %collective-permute-start.8) | collective-permute-done | bytes 360480 | tf_op jit(solution)/shard_map/ppermute | solution.py:66
  124.1 17.3 %collective-permute-done.11 = bf16[352,512]{1,0:T(8,128)(2,1)S(1)} collective-permute-done((bf16[352,512]{1,0:T(8,128)(2,1)S(1)}, bf16[352,512]{1,0:T(8,128)(2,1)S(1)}, u32[]{:S(2)}, u32[]{:S(2)}) %collective-permute-start.11) | collective-permute-done | bytes 360480 | tf_op jit(solution)/shard_map/ppermute | solution.py:66
  141.5 5.1 %collective-permute-done.13 = bf16[352,512]{1,0:T(8,128)(2,1)S(1)} collective-permute-done((bf16[352,512]{1,0:T(8,128)(2,1)S(1)}, bf16[352,512]{1,0:T(8,128)(2,1)S(1)}, u32[]{:S(2)}, u32[]{:S(2)}) %collective-permute-start.13) | collective-permute-done | bytes 360480 | tf_op jit(solution)/shard_map/ppermute | solution.py:66
  146.8 1.6 %copy-done = f32[1,1,352,2048]{3,2,1,0:T(8,128)} copy-done((f32[1,1,352,2048]{3,2,1,0:T(8,128)}, f32[1,1,352,2048]{3,2,1,0:T(8,128)S(1)}, u32[]{:S(2)}) %copy-start) | copy-done | bytes 2883608
  (57 shorter events, 15.5 us)
Async XLA Ops:
  0.6 15.2 %collective-permute-start = (bf16[1,128,2048]{2,1,0:T(8,128)(2,1)}, bf16[1,128,2048]{2,1,0:T(8,128)(2,1)S(1)}, u32[]{:S(2)}, u32[]{:S(2)}) collective-permute-start(bf16[1,128,2048]{2,1,0:T(8,128)(2,1)} %param.5), channel_id=1, source_target_pairs={{0,16},{16,0},{1,17},{17,1},{2,18},{18,2},{3,19},{19,3},{4,20},{20... | collective-permute-start | bytes 1572872 | tf_op jit(solution)/shard_map/ppermute | solution.py:10
  16.4 5.3 %copy-start.1 = (bf16[1,1,1,320,1408]{4,3,2,1,0:T(8,128)(2,1)S(1)}, bf16[1,1,1,320,1408]{4,3,2,1,0:T(8,128)(2,1)}, u32[]{:S(2)}) copy-start(bf16[1,1,1,320,1408]{4,3,2,1,0:T(8,128)(2,1)} %param.8) | copy-start | bytes 2703364
  18.0 20.8 %all-to-all-start = ((bf16[4,80,2048]{2,1,0:T(8,128)(2,1)}), bf16[4,80,2048]{2,1,0:T(8,128)(2,1)S(1)}, u32[]{:S(2)}, u32[]{:S(2)}) async-start(bf16[4,80,2048]{2,1,0:T(8,128)(2,1)} %bitcast.8), calls=%async_computation | async-start | bytes 2621440 | tf_op jit(solution)/shard_map/all_to_all | solution.py:88
  21.8 27.1 %collective-permute-start.1 = (bf16[320,1408]{1,0:T(8,128)(2,1)S(1)}, bf16[320,1408]{1,0:T(8,128)(2,1)}, u32[]{:S(2)}, u32[]{:S(2)}) collective-permute-start(bf16[320,1408]{1,0:T(8,128)(2,1)S(1)} %fusion.9), channel_id=1, source_target_pairs={{0,4},{12,8},{1,5},{13,9},{2,6},{14,10},{3,7},{15,11},{16,20},{28,... | collective-permute-start | bytes 2703368 | tf_op jit(solution)/shard_map/ppermute | solution.py:36
  39.8 13.3 %collective-permute-start.2 = (bf16[320,512]{1,0:T(8,128)(2,1)}, bf16[320,512]{1,0:T(8,128)(2,1)}, u32[]{:S(2)}, u32[]{:S(2)}) collective-permute-start(bf16[320,512]{1,0:T(8,128)(2,1)} %get-tuple-element.9), channel_id=1, source_target_pairs={{0,4},{12,8},{1,5},{13,9},{2,6},{14,10},{3,7},{15,11},{16,20},{28,... | collective-permute-start | bytes 983048 | tf_op jit(solution)/shard_map/ppermute | solution.py:55
  44.2 15.8 %collective-permute-start.3 = (bf16[320,512]{1,0:T(8,128)(2,1)}, bf16[320,512]{1,0:T(8,128)(2,1)}, u32[]{:S(2)}, u32[]{:S(2)}) collective-permute-start(bf16[320,512]{1,0:T(8,128)(2,1)} %get-tuple-element.8), channel_id=1, source_target_pairs={{0,4},{12,8},{1,5},{13,9},{2,6},{14,10},{3,7},{15,11},{16,20},{28,... | collective-permute-start | bytes 983048 | tf_op jit(solution)/shard_map/ppermute | solution.py:55
  46.2 20.8 %collective-permute-start.6 = (bf16[320,512]{1,0:T(8,128)(2,1)}, bf16[320,512]{1,0:T(8,128)(2,1)S(1)}, u32[]{:S(2)}, u32[]{:S(2)}) collective-permute-start(bf16[320,512]{1,0:T(8,128)(2,1)} %get-tuple-element.7), channel_id=1, source_target_pairs={{0,4},{12,8},{1,5},{13,9},{2,6},{14,10},{3,7},{15,11},{16,20},{28,... | collective-permute-start | bytes 983048 | tf_op jit(solution)/shard_map/ppermute | solution.py:55
  47.5 26.0 %collective-permute-start.9 = (bf16[320,512]{1,0:T(8,128)(2,1)S(1)}, bf16[320,512]{1,0:T(8,128)(2,1)S(1)}, u32[]{:S(2)}, u32[]{:S(2)}) collective-permute-start(bf16[320,512]{1,0:T(8,128)(2,1)S(1)} %get-tuple-element.6), channel_id=1, source_target_pairs={{0,4},{12,8},{1,5},{13,9},{2,6},{14,10},{3,7},{15,11},{16,20},{28,... | collective-permute-start | bytes 983048 | tf_op jit(solution)/shard_map/ppermute | solution.py:55
  55.8 11.3 %copy-start.2 = (bf16[320,512]{1,0:T(8,128)(2,1)S(1)}, bf16[320,512]{1,0:T(8,128)(2,1)}, u32[]{:S(2)}) copy-start(bf16[320,512]{1,0:T(8,128)(2,1)} %get-tuple-element.7) | copy-start | bytes 983044
  62.8 21.5 %collective-permute-start.12 = (bf16[704,512]{1,0:T(8,128)(2,1)S(1)}, bf16[704,512]{1,0:T(8,128)(2,1)S(1)}, u32[]{:S(2)}, u32[]{:S(2)}) collective-permute-start(bf16[704,512]{1,0:T(8,128)(2,1)S(1)} %dynamic-slice_convert_fusion.3), channel_id=1, source_target_pairs={{4,8},{8,4},{5,9},{9,5},{6,10},{10,6},{7,11},{11,7},{20,24},{24,20... | collective-permute-start | bytes 2162696 | tf_op jit(solution)/shard_map/ppermute | solution.py:61
  63.6 16.5 %collective-permute-start.4 = (bf16[704,512]{1,0:T(8,128)(2,1)S(1)}, bf16[704,512]{1,0:T(8,128)(2,1)S(1)}, u32[]{:S(2)}, u32[]{:S(2)}) collective-permute-start(bf16[704,512]{1,0:T(8,128)(2,1)S(1)} %dynamic-slice_convert_fusion.2), channel_id=1, source_target_pairs={{4,8},{8,4},{5,9},{9,5},{6,10},{10,6},{7,11},{11,7},{20,24},{24,20... | collective-permute-start | bytes 2162696 | tf_op jit(solution)/shard_map/ppermute | solution.py:61
  69.6 7.2 %slice-start = ((s8[5767168]{0:T(1024)(128)(4,1)}), s8[4194304]{0:T(1024)(128)(4,1)S(1)}, s32[]{:S(2)}) async-start(s8[5767168]{0:T(1024)(128)(4,1)} %bitcast.62), calls=%async_computation.1 | async-start | bytes 8388608
  69.7 7.1 %slice-start.1 = ((s8[5767168]{0:T(1024)(128)(4,1)}), s8[1572864]{0:T(1024)(128)(4,1)S(1)}, s32[]{:S(2)}) async-start(s8[5767168]{0:T(1024)(128)(4,1)} %bitcast.62), calls=%async_computation.2 | async-start | bytes 3145728
  69.7 11.8 %collective-permute-start.7 = (bf16[704,512]{1,0:T(8,128)(2,1)S(1)}, bf16[704,512]{1,0:T(8,128)(2,1)S(1)}, u32[]{:S(2)}, u32[]{:S(2)}) collective-permute-start(bf16[704,512]{1,0:T(8,128)(2,1)S(1)} %dynamic-slice_convert_fusion.1), channel_id=1, source_target_pairs={{4,8},{8,4},{5,9},{9,5},{6,10},{10,6},{7,11},{11,7},{20,24},{24,20... | collective-permute-start | bytes 2162696 | tf_op jit(solution)/shard_map/ppermute | solution.py:61
  76.1 6.8 %collective-permute-start.10 = (bf16[704,512]{1,0:T(8,128)(2,1)S(1)}, bf16[704,512]{1,0:T(8,128)(2,1)S(1)}, u32[]{:S(2)}, u32[]{:S(2)}) collective-permute-start(bf16[704,512]{1,0:T(8,128)(2,1)S(1)} %dynamic-slice_convert_fusion), channel_id=1, source_target_pairs={{4,8},{8,4},{5,9},{9,5},{6,10},{10,6},{7,11},{11,7},{20,24},{24,20... | collective-permute-start | bytes 2162696 | tf_op jit(solution)/shard_map/ppermute | solution.py:61
  80.2 28.3 %collective-permute-start.5 = (bf16[352,512]{1,0:T(8,128)(2,1)S(1)}, bf16[352,512]{1,0:T(8,128)(2,1)S(1)}, u32[]{:S(2)}, u32[]{:S(2)}) collective-permute-start(bf16[352,512]{1,0:T(8,128)(2,1)S(1)} %add_convert_fusion.3), channel_id=1, source_target_pairs={{4,0},{8,12},{5,1},{9,13},{6,2},{10,14},{7,3},{11,15},{20,16},{24,... | collective-permute-start | bytes 1081352 | tf_op jit(solution)/shard_map/ppermute | solution.py:66
  81.7 42.3 %collective-permute-start.8 = (bf16[352,512]{1,0:T(8,128)(2,1)S(1)}, bf16[352,512]{1,0:T(8,128)(2,1)S(1)}, u32[]{:S(2)}, u32[]{:S(2)}) collective-permute-start(bf16[352,512]{1,0:T(8,128)(2,1)S(1)} %add_convert_fusion.2), channel_id=1, source_target_pairs={{4,0},{8,12},{5,1},{9,13},{6,2},{10,14},{7,3},{11,15},{20,16},{24,... | collective-permute-start | bytes 1081352 | tf_op jit(solution)/shard_map/ppermute | solution.py:66
  83.1 58.3 %collective-permute-start.11 = (bf16[352,512]{1,0:T(8,128)(2,1)S(1)}, bf16[352,512]{1,0:T(8,128)(2,1)S(1)}, u32[]{:S(2)}, u32[]{:S(2)}) collective-permute-start(bf16[352,512]{1,0:T(8,128)(2,1)S(1)} %add_convert_fusion.1), channel_id=1, source_target_pairs={{4,0},{8,12},{5,1},{9,13},{6,2},{10,14},{7,3},{11,15},{20,16},{24,... | collective-permute-start | bytes 1081352 | tf_op jit(solution)/shard_map/ppermute | solution.py:66
  84.5 62.1 %collective-permute-start.13 = (bf16[352,512]{1,0:T(8,128)(2,1)S(1)}, bf16[352,512]{1,0:T(8,128)(2,1)S(1)}, u32[]{:S(2)}, u32[]{:S(2)}) collective-permute-start(bf16[352,512]{1,0:T(8,128)(2,1)S(1)} %add_convert_fusion), channel_id=1, source_target_pairs={{4,0},{8,12},{5,1},{9,13},{6,2},{10,14},{7,3},{11,15},{20,16},{24,... | collective-permute-start | bytes 1081352 | tf_op jit(solution)/shard_map/ppermute | solution.py:66
  146.8 1.6 %copy-start = (f32[1,1,352,2048]{3,2,1,0:T(8,128)}, f32[1,1,352,2048]{3,2,1,0:T(8,128)S(1)}, u32[]{:S(2)}) copy-start(f32[1,1,352,2048]{3,2,1,0:T(8,128)S(1)} %bitcast_dynamic-update-slice_fusion) | copy-start | bytes 8650756

commit v14 on v6

--- a/solution.py
+++ b/solution.py
@@ -87,7 +87,7 @@
     piece = lax.all_to_all(outgoing, "expert", split_axis=0, concat_axis=0, tiled=True)
     scaled = piece.reshape(slot_count, model_width)
     if line:
-        weight_grad, anchor = line_weight_grad(saved, hfull, scaled, 4)
+        weight_grad, anchor = line_weight_grad(saved, hfull, scaled, 2)
         late, _ = lax.optimization_barrier((scaled, anchor))
     else:
         full = lax.dot_general(

time: 135 us -> 156 us (1.16)
  waiting for transfers between devices: 80.4 us -> 96.7 us
  other arithmetic: 4.44 us -> 10.4 us
  starting transfers between devices: 28.6 us -> 23.2 us
  local copies, waits for them, and re-layouts: 3.81 us -> 7.9 us
    ppermute x4 -> x2, waiting for transfers between devices: 45.8 us -> 55.3 us  [line_weight_grad(): r3 = lax.ppermute(s3, 'dp', [(1, 0), (2, 3)])]
    ppermute x4 -> x2, waiting for transfers between devices: 14 us -> 20.8 us  [line_weight_grad(): srecv = lax.ppermute(sc, 'dp', ends)]
    add x4 -> x2, other arithmetic: 0.57 us -> 3.55 us  [line_weight_grad(): lax.dynamic_slice_in_dim(acc, own, blk, axis=0) + extra.astype(jnp.float32)]
    convert_element_type x4 -> x2, other arithmetic: 0.48 us -> 3.35 us  [line_weight_grad(): s3 = (lax.dynamic_slice_in_dim(acc, row3a, blk, axis=0) + lax.dynamic_sli...]
    ppermute x4 -> x2, starting transfers between devices: 5.17 us -> 2.58 us  [line_weight_grad(): r3 = lax.ppermute(s3, 'dp', [(1, 0), (2, 3)])]
    dot_general x1, matrix products: 3.23 us -> 5.79 us  [shards(): jnp.einsum('sd,hd->sh', late, weight, preferred_element_type=jnp.float32)]
    convert_element_type x4 -> x2, local copies, waits for them, and re-layouts: 0.4 us -> 2.85 us  [line_weight_grad(): lax.dynamic_slice_in_dim(acc, row2, 2 * blk, axis=0).astype(jnp.bfloat16)]
    ppermute x4 -> x2, starting transfers between devices: 9.1 us -> 6.71 us  [line_weight_grad(): srecv = lax.ppermute(sc, 'dp', ends)]
  transfers between devices with their start and end apart: 15 -> 9, of which waited for: 10 -> 6; matrix products, arithmetic and copies ran while one was open for 15% -> 17% of each run, Pallas kernels for 0% -> 0%
where the time goes in v14:
time: 156 us; the launch traced here: 155 us
  waiting for transfers between devices  96.7 us (62%)
  starting transfers between devices  23.2 us (15%)
  matrix products  16 us (10%)
  other arithmetic  10.4 us (7%)
  local copies, waits for them, and re-layouts  7.9 us (5%)
    ppermute x2, waiting for transfers between devices, line_weight_grad(): r3 = lax.ppermute(s3, 'dp', [(1, 0), (2, 3)])  55.3 us
    ppermute x2, waiting for transfers between devices, line_weight_grad(): srecv = lax.ppermute(sc, 'dp', ends)  20.8 us
    all_to_all x1, waiting for transfers between devices, shards(): lax.all_to_all(outgoing, 'expert', split_axis=0, concat_axis=0, tiled=True)  12.3 us
    ppermute x1, waiting for transfers between devices, shifted(): return lax.ppermute(value, axis, pairs)  8.3 us
    dot_general x2, matrix products, line_weight_grad(): lax.dot_general(lhs, rhs, (((0,), (0,)), ((), ())), preferred_element_typ...  8.02 us
    ppermute x2, starting transfers between devices, line_weight_grad(): srecv = lax.ppermute(sc, 'dp', ends)  6.71 us
    dot_general x1, matrix products, shards(): jnp.einsum('sd,hd->sh', late, weight, preferred_element_type=jnp.float32)  5.79 us
    ppermute x1, starting transfers between devices, send_hidden(): return lax.ppermute(hsend, 'dp', [(0, 1), (3, 2)])  4.67 us
  transfers between devices with their start and end apart: 9, of which 6 were waited for; matrix products, arithmetic and copies ran while one was open for 17% of the time, Pallas kernels for 0%

profile of v14, /device:TPU:0, one launch (start us, length us, event | category | flops | bytes accessed | tf_op | source)
XLA Modules:
  0.0 155.1 jit_solution(16611211602506081207)
XLA Ops:
  0.6 3.0 %collective-permute-start = (bf16[1,128,2048]{2,1,0:T(8,128)(2,1)}, bf16[1,128,2048]{2,1,0:T(8,128)(2,1)S(1)}, u32[]{:S(2)}, u32[]{:S(2)}) collective-permute-start(bf16[1,128,2048]{2,1,0:T(8,128)(2,1)} %param.5), channel_id=1, source_target_pairs={{0,16},{16,0},{1,17},{17,1},{2,18},{18,2},{3,19},{19,3},{4,20},{20... | collective-permute-start | bytes 1572872 | tf_op jit(solution)/shard_map/ppermute | solution.py:10
  7.5 8.3 %collective-permute-done = bf16[1,128,2048]{2,1,0:T(8,128)(2,1)S(1)} collective-permute-done((bf16[1,128,2048]{2,1,0:T(8,128)(2,1)}, bf16[1,128,2048]{2,1,0:T(8,128)(2,1)S(1)}, u32[]{:S(2)}, u32[]{:S(2)}) %collective-permute-start) | collective-permute-done | bytes 524320 | tf_op jit(solution)/shard_map/ppermute | solution.py:10
  16.4 1.7 %fusion.5 = bf16[320,2048]{1,0:T(8,128)(2,1)} fusion(f32[320,2048]{1,0:T(8,128)S(1)} %fusion.20, bf16[1,128,2048]{2,1,0:T(8,128)(2,1)S(1)} %collective-permute-done, f32[128]{0:T(128)S(1)} %get-tuple-element.8, s32[128]{0:T(128)S(1)} %get-tuple-element.4), kind=kOutput, calls=%fused_computation.7 | convolution fusion | flops 169910272 | bytes 4457472 | tf_op jit(solution)/shard_map/dot_general | solution.py:26
  18.0 3.7 %all-to-all-start = ((bf16[4,80,2048]{2,1,0:T(8,128)(2,1)}), bf16[4,80,2048]{2,1,0:T(8,128)(2,1)S(1)}, u32[]{:S(2)}, u32[]{:S(2)}) async-start(bf16[4,80,2048]{2,1,0:T(8,128)(2,1)} %bitcast.8), calls=%async_computation | async-start | bytes 2621440 | tf_op jit(solution)/shard_map/all_to_all | solution.py:87
  21.9 4.7 %collective-permute-start.1 = (bf16[320,1408]{1,0:T(8,128)(2,1)S(1)}, bf16[320,1408]{1,0:T(8,128)(2,1)}, u32[]{:S(2)}, u32[]{:S(2)}) collective-permute-start(bf16[320,1408]{1,0:T(8,128)(2,1)S(1)} %fusion.9), channel_id=1, source_target_pairs={{0,4},{12,8},{1,5},{13,9},{2,6},{14,10},{3,7},{15,11},{16,20},{28,... | collective-permute-start | bytes 2703368 | tf_op jit(solution)/shard_map/ppermute | solution.py:36
  26.6 12.3 %all-to-all-done = bf16[4,80,2048]{2,1,0:T(8,128)(2,1)S(1)} async-done(((bf16[4,80,2048]{2,1,0:T(8,128)(2,1)}), bf16[4,80,2048]{2,1,0:T(8,128)(2,1)S(1)}, u32[]{:S(2)}, u32[]{:S(2)}) %all-to-all-start) | async-done | bytes 1310752 | tf_op jit(solution)/shard_map/all_to_all | solution.py:87
  40.1 4.6 %collective-permute-start.2 = (bf16[320,1024]{1,0:T(8,128)(2,1)}, bf16[320,1024]{1,0:T(8,128)(2,1)}, u32[]{:S(2)}, u32[]{:S(2)}) collective-permute-start(bf16[320,1024]{1,0:T(8,128)(2,1)} %get-tuple-element.7), channel_id=1, source_target_pairs={{0,4},{12,8},{1,5},{13,9},{2,6},{14,10},{3,7},{15,11},{16,20},{28,... | collective-permute-start | bytes 1966088 | tf_op jit(solution)/shard_map/ppermute | solution.py:55
  44.7 2.1 %collective-permute-start.3 = (bf16[320,1024]{1,0:T(8,128)(2,1)}, bf16[320,1024]{1,0:T(8,128)(2,1)}, u32[]{:S(2)}, u32[]{:S(2)}) collective-permute-start(bf16[320,1024]{1,0:T(8,128)(2,1)} %get-tuple-element.6), channel_id=1, source_target_pairs={{0,4},{12,8},{1,5},{13,9},{2,6},{14,10},{3,7},{15,11},{16,20},{28,... | collective-permute-start | bytes 1966088 | tf_op jit(solution)/shard_map/ppermute | solution.py:55
  46.8 13.4 %collective-permute-done.2 = bf16[320,1024]{1,0:T(8,128)(2,1)} collective-permute-done((bf16[320,1024]{1,0:T(8,128)(2,1)}, bf16[320,1024]{1,0:T(8,128)(2,1)}, u32[]{:S(2)}, u32[]{:S(2)}) %collective-permute-start.2) | collective-permute-done | bytes 655392 | tf_op jit(solution)/shard_map/ppermute | solution.py:55
  60.2 4.0 %fusion.10 = f32[1408,1024]{1,0:T(8,128)S(1)} fusion(bf16[320,1024]{1,0:T(8,128)(2,1)} %collective-permute-done.2, bf16[320,1024]{1,0:T(8,128)(2,1)} %get-tuple-element.7, bf16[320,1408]{1,0:T(8,128)(2,1)} %collective-permute-done.1, bf16[320,1408]{1,0:T(8,128)(2,1)S(1)} %bitcast.50), kind=kOutput, calls=%fused_computation.18 | convolution fusion | flops 1851719680 | bytes 8880128 | tf_op jit(solution)/shard_map/dot_general | solution.py:57
  64.2 1.3 dynamic-slice_convert_fusion.1
  66.3 7.4 %collective-permute-done.3 = bf16[320,1024]{1,0:T(8,128)(2,1)} collective-permute-done((bf16[320,1024]{1,0:T(8,128)(2,1)}, bf16[320,1024]{1,0:T(8,128)(2,1)}, u32[]{:S(2)}, u32[]{:S(2)}) %collective-permute-start.3) | collective-permute-done | bytes 655392 | tf_op jit(solution)/shard_map/ppermute | solution.py:55
  73.7 4.0 %fusion.14 = f32[1408,1024]{1,0:T(8,128)S(1)} fusion(bf16[320,1024]{1,0:T(8,128)(2,1)} %collective-permute-done.3, bf16[320,1024]{1,0:T(8,128)(2,1)} %get-tuple-element.6, bf16[320,1408]{1,0:T(8,128)(2,1)} %collective-permute-done.1, bf16[320,1408]{1,0:T(8,128)(2,1)S(1)} %bitcast.51), kind=kOutput, calls=%fused_computation.22 | convolution fusion | flops 1851719680 | bytes 8880128 | tf_op jit(solution)/shard_map/dot_general | solution.py:57
  77.8 1.5 dynamic-slice_convert_fusion
  79.3 1.4 copy-done.1
  80.8 1.8 %collective-permute-start.4 = (bf16[704,1024]{1,0:T(8,128)(2,1)}, bf16[704,1024]{1,0:T(8,128)(2,1)}, u32[]{:S(2)}, u32[]{:S(2)}) collective-permute-start(bf16[704,1024]{1,0:T(8,128)(2,1)} %dynamic-slice_convert_fusion), channel_id=1, source_target_pairs={{4,8},{8,4},{5,9},{9,5},{6,10},{10,6},{7,11},{11,7},{20,24},{24,20... | collective-permute-start | bytes 4325384 | tf_op jit(solution)/shard_map/ppermute | solution.py:61
  82.5 1.6 %add_convert_fusion = bf16[352,1024]{1,0:T(8,128)(2,1)S(1)} fusion(f32[1408,1024]{1,0:T(8,128)} %copy-done, s32[]{:T(128)S(6)} %select_n.51, bf16[704,1024]{1,0:T(8,128)(2,1)S(1)} %collective-permute-done.6, s32[]{:T(128)S(6)} %select_n.52), kind=kLoop, calls=%fused_computation.13 | loop fusion | flops 1081344 | bytes 2883592 | tf_op jit(solution)/shard_map/convert_element_type | solution.py:65
  85.4 1.8 %add_convert_fusion.1 = bf16[352,1024]{1,0:T(8,128)(2,1)S(1)} fusion(f32[1408,1024]{1,0:T(8,128)} %copy-done.1, s32[]{:T(128)S(6)} %select_n.51, bf16[704,1024]{1,0:T(8,128)(2,1)} %collective-permute-done.4, s32[]{:T(128)S(6)} %select_n.52), kind=kLoop, calls=%fused_computation.15 | loop fusion | flops 1081344 | bytes 2883592 | tf_op jit(solution)/shard_map/convert_element_type | solution.py:65
  88.5 5.8 %fusion.6 = bf16[1,1,1,320,1408]{4,3,2,1,0:T(8,128)(2,1)} fusion(bf16[320,2048]{1,0:T(8,128)(2,1)S(1)} %bitcast.49, bf16[1,1,1408,2048]{3,2,1,0:T(8,128)(2,1)} %param.9), kind=kOutput, calls=%fused_computation.8 | convolution fusion | flops 1845944320 | bytes 7979008 | tf_op jit(solution)/shard_map/sd,hd->sh/dot_general | solution.py:100
  94.3 25.8 %collective-permute-done.7 = bf16[352,1024]{1,0:T(8,128)(2,1)S(1)} collective-permute-done((bf16[352,1024]{1,0:T(8,128)(2,1)S(1)}, bf16[352,1024]{1,0:T(8,128)(2,1)S(1)}, u32[]{:S(2)}, u32[]{:S(2)}) %collective-permute-start.7) | collective-permute-done | bytes 720928 | tf_op jit(solution)/shard_map/ppermute | solution.py:66
  120.1 1.7 %convert_add_fusion = f32[352,1024]{1,0:T(8,128)S(1)} fusion(f32[1408,1024]{1,0:T(8,128)} %copy-done, s32[]{:T(128)S(6)} %select_n.49, bf16[352,1024]{1,0:T(8,128)(2,1)S(1)} %collective-permute-done.7, bf16[704,1024]{1,0:T(8,128)(2,1)S(1)} %collective-permute-done.6, s32[]{:T(128)S(6)} %select_n.53, pred[]{:T(512)S(6)} %or.3), kind=kLoop, calls=%fused_computation.12 | loop fusion | flops 1081344 | bytes 4325385 | tf_op jit(solution)/shard_map/add | solution.py:69
  121.8 29.5 %collective-permute-done.5 = bf16[352,1024]{1,0:T(8,128)(2,1)S(1)} collective-permute-done((bf16[352,1024]{1,0:T(8,128)(2,1)S(1)}, bf16[352,1024]{1,0:T(8,128)(2,1)S(1)}, u32[]{:S(2)}, u32[]{:S(2)}) %collective-permute-start.5) | collective-permute-done | bytes 720928 | tf_op jit(solution)/shard_map/ppermute | solution.py:66
  151.3 1.9 %convert_add_fusion.1 = f32[352,1024]{1,0:T(8,128)S(1)} fusion(f32[1408,1024]{1,0:T(8,128)} %copy-done.1, s32[]{:T(128)S(6)} %select_n.49, bf16[352,1024]{1,0:T(8,128)(2,1)S(1)} %collective-permute-done.5, bf16[704,1024]{1,0:T(8,128)(2,1)} %collective-permute-done.4, s32[]{:T(128)S(6)} %select_n.53, pred[]{:T(512)S(6)} %or.3), kind=kLoop, calls=%fused_computation.14 | loop fusion | flops 1081344 | bytes 4325385 | tf_op jit(solution)/shard_map/add | solution.py:69
  153.2 1.9 %maximum_bitcast_fusion = f32[1,1,352,2048]{3,2,1,0:T(8,128)} fusion(f32[352,1024]{1,0:T(8,128)S(1)} %convert_add_fusion, f32[352,1024]{1,0:T(8,128)S(1)} %convert_add_fusion.1), kind=kLoop, calls=%fused_computation.2 | loop fusion | flops 720896 | bytes 5767168 | tf_op jit(solution)/shard_map/reshape | solution.py:104
  (34 shorter events, 9.1 us)
Async XLA Ops:
  0.6 15.2 %collective-permute-start = (bf16[1,128,2048]{2,1,0:T(8,128)(2,1)}, bf16[1,128,2048]{2,1,0:T(8,128)(2,1)S(1)}, u32[]{:S(2)}, u32[]{:S(2)}) collective-permute-start(bf16[1,128,2048]{2,1,0:T(8,128)(2,1)} %param.5), channel_id=1, source_target_pairs={{0,16},{16,0},{1,17},{17,1},{2,18},{18,2},{3,19},{19,3},{4,20},{20... | collective-permute-start | bytes 1572872 | tf_op jit(solution)/shard_map/ppermute | solution.py:10
  18.0 3.7 %copy-start.2 = (bf16[1,1,1,320,1408]{4,3,2,1,0:T(8,128)(2,1)S(1)}, bf16[1,1,1,320,1408]{4,3,2,1,0:T(8,128)(2,1)}, u32[]{:S(2)}) copy-start(bf16[1,1,1,320,1408]{4,3,2,1,0:T(8,128)(2,1)} %param.8) | copy-start | bytes 2703364
  18.0 20.9 %all-to-all-start = ((bf16[4,80,2048]{2,1,0:T(8,128)(2,1)}), bf16[4,80,2048]{2,1,0:T(8,128)(2,1)S(1)}, u32[]{:S(2)}, u32[]{:S(2)}) async-start(bf16[4,80,2048]{2,1,0:T(8,128)(2,1)} %bitcast.8), calls=%async_computation | async-start | bytes 2621440 | tf_op jit(solution)/shard_map/all_to_all | solution.py:87
  21.9 24.9 %collective-permute-start.1 = (bf16[320,1408]{1,0:T(8,128)(2,1)S(1)}, bf16[320,1408]{1,0:T(8,128)(2,1)}, u32[]{:S(2)}, u32[]{:S(2)}) collective-permute-start(bf16[320,1408]{1,0:T(8,128)(2,1)S(1)} %fusion.9), channel_id=1, source_target_pairs={{0,4},{12,8},{1,5},{13,9},{2,6},{14,10},{3,7},{15,11},{16,20},{28,... | collective-permute-start | bytes 2703368 | tf_op jit(solution)/shard_map/ppermute | solution.py:36
  40.1 20.1 %collective-permute-start.2 = (bf16[320,1024]{1,0:T(8,128)(2,1)}, bf16[320,1024]{1,0:T(8,128)(2,1)}, u32[]{:S(2)}, u32[]{:S(2)}) collective-permute-start(bf16[320,1024]{1,0:T(8,128)(2,1)} %get-tuple-element.7), channel_id=1, source_target_pairs={{0,4},{12,8},{1,5},{13,9},{2,6},{14,10},{3,7},{15,11},{16,20},{28,... | collective-permute-start | bytes 1966088 | tf_op jit(solution)/shard_map/ppermute | solution.py:55
  44.7 29.1 %collective-permute-start.3 = (bf16[320,1024]{1,0:T(8,128)(2,1)}, bf16[320,1024]{1,0:T(8,128)(2,1)}, u32[]{:S(2)}, u32[]{:S(2)}) collective-permute-start(bf16[320,1024]{1,0:T(8,128)(2,1)} %get-tuple-element.6), channel_id=1, source_target_pairs={{0,4},{12,8},{1,5},{13,9},{2,6},{14,10},{3,7},{15,11},{16,20},{28,... | collective-permute-start | bytes 1966088 | tf_op jit(solution)/shard_map/ppermute | solution.py:55
  64.2 13.6 %copy-start = (f32[1408,1024]{1,0:T(8,128)}, f32[1408,1024]{1,0:T(8,128)S(1)}, u32[]{:S(2)}) copy-start(f32[1408,1024]{1,0:T(8,128)S(1)} %fusion.10) | copy-start | bytes 17301508
  64.2 9.5 %copy-start.3 = (bf16[1,1,1,320,1408]{4,3,2,1,0:T(8,128)(2,1)S(1)}, bf16[1,1,1,320,1408]{4,3,2,1,0:T(8,128)(2,1)}, u32[]{:S(2)}) copy-start(bf16[1,1,1,320,1408]{4,3,2,1,0:T(8,128)(2,1)} %param.8) | copy-start | bytes 2703364
  65.6 17.0 %collective-permute-start.6 = (bf16[704,1024]{1,0:T(8,128)(2,1)}, bf16[704,1024]{1,0:T(8,128)(2,1)S(1)}, u32[]{:S(2)}, u32[]{:S(2)}) collective-permute-start(bf16[704,1024]{1,0:T(8,128)(2,1)} %dynamic-slice_convert_fusion.1), channel_id=1, source_target_pairs={{4,8},{8,4},{5,9},{9,5},{6,10},{10,6},{7,11},{11,7},{20,24},{24,20... | collective-permute-start | bytes 4325384 | tf_op jit(solution)/shard_map/ppermute | solution.py:61
  77.8 3.0 %copy-start.1 = (f32[1408,1024]{1,0:T(8,128)}, f32[1408,1024]{1,0:T(8,128)S(1)}, u32[]{:S(2)}) copy-start(f32[1408,1024]{1,0:T(8,128)S(1)} %fusion.14) | copy-start | bytes 17301508
  80.8 4.7 %collective-permute-start.4 = (bf16[704,1024]{1,0:T(8,128)(2,1)}, bf16[704,1024]{1,0:T(8,128)(2,1)}, u32[]{:S(2)}, u32[]{:S(2)}) collective-permute-start(bf16[704,1024]{1,0:T(8,128)(2,1)} %dynamic-slice_convert_fusion), channel_id=1, source_target_pairs={{4,8},{8,4},{5,9},{9,5},{6,10},{10,6},{7,11},{11,7},{20,24},{24,20... | collective-permute-start | bytes 4325384 | tf_op jit(solution)/shard_map/ppermute | solution.py:61
  84.1 36.0 %collective-permute-start.7 = (bf16[352,1024]{1,0:T(8,128)(2,1)S(1)}, bf16[352,1024]{1,0:T(8,128)(2,1)S(1)}, u32[]{:S(2)}, u32[]{:S(2)}) collective-permute-start(bf16[352,1024]{1,0:T(8,128)(2,1)S(1)} %add_convert_fusion), channel_id=1, source_target_pairs={{4,0},{8,12},{5,1},{9,13},{6,2},{10,14},{7,3},{11,15},{20,16},{24,... | collective-permute-start | bytes 2162696 | tf_op jit(solution)/shard_map/ppermute | solution.py:66
  87.2 64.1 %collective-permute-start.5 = (bf16[352,1024]{1,0:T(8,128)(2,1)S(1)}, bf16[352,1024]{1,0:T(8,128)(2,1)S(1)}, u32[]{:S(2)}, u32[]{:S(2)}) collective-permute-start(bf16[352,1024]{1,0:T(8,128)(2,1)S(1)} %add_convert_fusion.1), channel_id=1, source_target_pairs={{4,0},{8,12},{5,1},{9,13},{6,2},{10,14},{7,3},{11,15},{20,16},{24,... | collective-permute-start | bytes 2162696 | tf_op jit(solution)/shard_map/ppermute | solution.py:66

commit v15 on v6

--- a/solution.py
+++ b/solution.py
@@ -88,7 +88,7 @@
     scaled = piece.reshape(slot_count, model_width)
     if line:
         weight_grad, anchor = line_weight_grad(saved, hfull, scaled, 4)
-        late, _ = lax.optimization_barrier((scaled, anchor))
+        late = scaled
     else:
         full = lax.dot_general(
             saved, scaled, (((0,), (0,)), ((), ())), preferred_element_type=jnp.float32

time: 135 us -> 135 us (level)
  no operation moved by 1% of the time
where the time goes in v15:
time: 135 us; the launch traced here: 134 us
  waiting for transfers between devices  80.4 us (60%)
  starting transfers between devices  28.6 us (21%)
  matrix products  15.8 us (12%)
  other arithmetic  4.44 us (3%)
  local copies, waits for them, and re-layouts  3.81 us (3%)
    ppermute x4, waiting for transfers between devices, line_weight_grad(): r3 = lax.ppermute(s3, 'dp', [(1, 0), (2, 3)])  45.8 us
    ppermute x4, waiting for transfers between devices, line_weight_grad(): srecv = lax.ppermute(sc, 'dp', ends)  14 us
    all_to_all x1, waiting for transfers between devices, shards(): lax.all_to_all(outgoing, 'expert', split_axis=0, concat_axis=0, tiled=True)  12.3 us
    dot_general x4, matrix products, line_weight_grad(): lax.dot_general(lhs, rhs, (((0,), (0,)), ((), ())), preferred_element_typ...  10.3 us
    ppermute x4, starting transfers between devices, line_weight_grad(): srecv = lax.ppermute(sc, 'dp', ends)  9.1 us
    ppermute x1, waiting for transfers between devices, shifted(): return lax.ppermute(value, axis, pairs)  8.3 us
    ppermute x4, starting transfers between devices, line_weight_grad(): r3 = lax.ppermute(s3, 'dp', [(1, 0), (2, 3)])  5.17 us
    ppermute x1, starting transfers between devices, send_hidden(): return lax.ppermute(hsend, 'dp', [(0, 1), (3, 2)])  4.67 us
  transfers between devices with their start and end apart: 15, of which 10 were waited for; matrix products, arithmetic and copies ran while one was open for 15% of the time, Pallas kernels for 0%

profile of v15, /device:TPU:0, one launch (start us, length us, event | category | flops | bytes accessed | tf_op | source)
XLA Modules:
  0.0 134.0 jit_solution(11930617188466390848)
XLA Ops:
  0.6 3.0 %collective-permute-start = (bf16[1,128,2048]{2,1,0:T(8,128)(2,1)}, bf16[1,128,2048]{2,1,0:T(8,128)(2,1)S(1)}, u32[]{:S(2)}, u32[]{:S(2)}) collective-permute-start(bf16[1,128,2048]{2,1,0:T(8,128)(2,1)} %param.5), channel_id=1, source_target_pairs={{0,16},{16,0},{1,17},{17,1},{2,18},{18,2},{3,19},{19,3},{4,20},{20... | collective-permute-start | bytes 1572872 | tf_op jit(solution)/shard_map/ppermute | solution.py:10
  7.5 8.3 %collective-permute-done = bf16[1,128,2048]{2,1,0:T(8,128)(2,1)S(1)} collective-permute-done((bf16[1,128,2048]{2,1,0:T(8,128)(2,1)}, bf16[1,128,2048]{2,1,0:T(8,128)(2,1)S(1)}, u32[]{:S(2)}, u32[]{:S(2)}) %collective-permute-start) | collective-permute-done | bytes 524320 | tf_op jit(solution)/shard_map/ppermute | solution.py:10
  16.4 1.7 %fusion.5 = bf16[320,2048]{1,0:T(8,128)(2,1)} fusion(f32[320,2048]{1,0:T(8,128)S(1)} %fusion.28, bf16[1,128,2048]{2,1,0:T(8,128)(2,1)S(1)} %collective-permute-done, f32[128]{0:T(128)S(1)} %get-tuple-element.8, s32[128]{0:T(128)S(1)} %get-tuple-element.2), kind=kOutput, calls=%fused_computation.5 | convolution fusion | flops 169910272 | bytes 4457472 | tf_op jit(solution)/shard_map/dot_general | solution.py:26
  18.0 3.5 %all-to-all-start = ((bf16[4,80,2048]{2,1,0:T(8,128)(2,1)}), bf16[4,80,2048]{2,1,0:T(8,128)(2,1)S(1)}, u32[]{:S(2)}, u32[]{:S(2)}) async-start(bf16[4,80,2048]{2,1,0:T(8,128)(2,1)} %bitcast.8), calls=%async_computation | async-start | bytes 2621440 | tf_op jit(solution)/shard_map/all_to_all | solution.py:87
  21.8 4.7 %collective-permute-start.1 = (bf16[320,1408]{1,0:T(8,128)(2,1)S(1)}, bf16[320,1408]{1,0:T(8,128)(2,1)}, u32[]{:S(2)}, u32[]{:S(2)}) collective-permute-start(bf16[320,1408]{1,0:T(8,128)(2,1)S(1)} %fusion.9), channel_id=1, source_target_pairs={{0,4},{12,8},{1,5},{13,9},{2,6},{14,10},{3,7},{15,11},{16,20},{28,... | collective-permute-start | bytes 2703368 | tf_op jit(solution)/shard_map/ppermute | solution.py:36
  26.5 12.3 %all-to-all-done = bf16[4,80,2048]{2,1,0:T(8,128)(2,1)S(1)} async-done(((bf16[4,80,2048]{2,1,0:T(8,128)(2,1)}), bf16[4,80,2048]{2,1,0:T(8,128)(2,1)S(1)}, u32[]{:S(2)}, u32[]{:S(2)}) %all-to-all-start) | async-done | bytes 1310752 | tf_op jit(solution)/shard_map/all_to_all | solution.py:87
  39.8 4.5 %collective-permute-start.11 = (bf16[320,512]{1,0:T(8,128)(2,1)}, bf16[320,512]{1,0:T(8,128)(2,1)}, u32[]{:S(2)}, u32[]{:S(2)}) collective-permute-start(bf16[320,512]{1,0:T(8,128)(2,1)} %get-tuple-element.5), channel_id=1, source_target_pairs={{0,4},{12,8},{1,5},{13,9},{2,6},{14,10},{3,7},{15,11},{16,20},{28,... | collective-permute-start | bytes 983048 | tf_op jit(solution)/shard_map/ppermute | solution.py:55
  44.2 2.0 %collective-permute-start.8 = (bf16[320,512]{1,0:T(8,128)(2,1)}, bf16[320,512]{1,0:T(8,128)(2,1)}, u32[]{:S(2)}, u32[]{:S(2)}) collective-permute-start(bf16[320,512]{1,0:T(8,128)(2,1)} %get-tuple-element.6), channel_id=1, source_target_pairs={{0,4},{12,8},{1,5},{13,9},{2,6},{14,10},{3,7},{15,11},{16,20},{28,... | collective-permute-start | bytes 983048 | tf_op jit(solution)/shard_map/ppermute | solution.py:55
  46.3 1.3 collective-permute-start.5
  47.6 1.3 collective-permute-start.2
  48.9 4.2 %collective-permute-done.11 = bf16[320,512]{1,0:T(8,128)(2,1)} collective-permute-done((bf16[320,512]{1,0:T(8,128)(2,1)}, bf16[320,512]{1,0:T(8,128)(2,1)}, u32[]{:S(2)}, u32[]{:S(2)}) %collective-permute-start.11) | collective-permute-done | bytes 327712 | tf_op jit(solution)/shard_map/ppermute | solution.py:55
  53.0 2.7 %fusion.24 = f32[1408,512]{1,0:T(8,128)S(1)} fusion(bf16[320,512]{1,0:T(8,128)(2,1)} %collective-permute-done.11, bf16[320,512]{1,0:T(8,128)(2,1)} %get-tuple-element.5, bf16[320,1408]{1,0:T(8,128)(2,1)} %collective-permute-done.1, bf16[320,1408]{1,0:T(8,128)(2,1)S(1)} %bitcast.50), kind=kOutput, calls=%fused_computation.38 | convolution fusion | flops 927662080 | bytes 5341184 | tf_op jit(solution)/shard_map/dot_general | solution.py:57
  56.7 3.4 %collective-permute-done.8 = bf16[320,512]{1,0:T(8,128)(2,1)} collective-permute-done((bf16[320,512]{1,0:T(8,128)(2,1)}, bf16[320,512]{1,0:T(8,128)(2,1)}, u32[]{:S(2)}, u32[]{:S(2)}) %collective-permute-start.8) | collective-permute-done | bytes 327712 | tf_op jit(solution)/shard_map/ppermute | solution.py:55
  60.1 2.7 %fusion.20 = f32[1408,512]{1,0:T(8,128)S(1)} fusion(bf16[320,512]{1,0:T(8,128)(2,1)} %collective-permute-done.8, bf16[320,512]{1,0:T(8,128)(2,1)} %get-tuple-element.6, bf16[320,1408]{1,0:T(8,128)(2,1)} %collective-permute-done.1, bf16[320,1408]{1,0:T(8,128)(2,1)S(1)} %bitcast.51), kind=kOutput, calls=%fused_computation.34 | convolution fusion | flops 927662080 | bytes 5341184 | tf_op jit(solution)/shard_map/dot_general | solution.py:57
  63.6 3.5 %collective-permute-done.5 = bf16[320,512]{1,0:T(8,128)(2,1)S(1)} collective-permute-done((bf16[320,512]{1,0:T(8,128)(2,1)}, bf16[320,512]{1,0:T(8,128)(2,1)S(1)}, u32[]{:S(2)}, u32[]{:S(2)}) %collective-permute-start.5) | collective-permute-done | bytes 327712 | tf_op jit(solution)/shard_map/ppermute | solution.py:55
  67.1 2.5 %fusion.16 = f32[1408,512]{1,0:T(8,128)S(1)} fusion(bf16[320,512]{1,0:T(8,128)(2,1)S(1)} %collective-permute-done.5, bf16[320,512]{1,0:T(8,128)(2,1)S(1)} %copy-done.1, bf16[320,1408]{1,0:T(8,128)(2,1)} %collective-permute-done.1, bf16[320,1408]{1,0:T(8,128)(2,1)S(1)} %bitcast.52), kind=kOutput, calls=%fused_computation.30 | convolution fusion | flops 927662080 | bytes 5341184 | tf_op jit(solution)/shard_map/dot_general | solution.py:57
  70.6 2.9 %collective-permute-done.2 = bf16[320,512]{1,0:T(8,128)(2,1)S(1)} collective-permute-done((bf16[320,512]{1,0:T(8,128)(2,1)S(1)}, bf16[320,512]{1,0:T(8,128)(2,1)S(1)}, u32[]{:S(2)}, u32[]{:S(2)}) %collective-permute-start.2) | collective-permute-done | bytes 327712 | tf_op jit(solution)/shard_map/ppermute | solution.py:55
  73.5 2.5 %fusion.12 = f32[1408,512]{1,0:T(8,128)S(1)} fusion(bf16[320,512]{1,0:T(8,128)(2,1)S(1)} %collective-permute-done.2, bf16[320,512]{1,0:T(8,128)(2,1)S(1)} %get-tuple-element.4, bf16[320,1408]{1,0:T(8,128)(2,1)} %collective-permute-done.1, bf16[320,1408]{1,0:T(8,128)(2,1)S(1)} %bitcast.53), kind=kOutput, calls=%fused_computation.26 | convolution fusion | flops 927662080 | bytes 5341184 | tf_op jit(solution)/shard_map/dot_general | solution.py:57
  76.9 3.2 %fusion.6 = bf16[1,1,1,320,1408]{4,3,2,1,0:T(8,128)(2,1)} fusion(bf16[320,2048]{1,0:T(8,128)(2,1)S(1)} %bitcast.49, bf16[1,1,1408,2048]{3,2,1,0:T(8,128)(2,1)S(1)} %bitcast.57), kind=kOutput, calls=%fused_computation.6 | convolution fusion | flops 1845944320 | bytes 7979008 | tf_op jit(solution)/shard_map/sd,hd->sh/dot_general | solution.py:100
  85.8 10.0 %collective-permute-done.13 = bf16[352,512]{1,0:T(8,128)(2,1)S(1)} collective-permute-done((bf16[352,512]{1,0:T(8,128)(2,1)S(1)}, bf16[352,512]{1,0:T(8,128)(2,1)S(1)}, u32[]{:S(2)}, u32[]{:S(2)}) %collective-permute-start.13) | collective-permute-done | bytes 360480 | tf_op jit(solution)/shard_map/ppermute | solution.py:66
  96.0 6.4 %collective-permute-done.10 = bf16[352,512]{1,0:T(8,128)(2,1)S(1)} collective-permute-done((bf16[352,512]{1,0:T(8,128)(2,1)S(1)}, bf16[352,512]{1,0:T(8,128)(2,1)S(1)}, u32[]{:S(2)}, u32[]{:S(2)}) %collective-permute-start.10) | collective-permute-done | bytes 360480 | tf_op jit(solution)/shard_map/ppermute | solution.py:66
  102.5 14.5 %collective-permute-done.7 = bf16[352,512]{1,0:T(8,128)(2,1)S(1)} collective-permute-done((bf16[352,512]{1,0:T(8,128)(2,1)S(1)}, bf16[352,512]{1,0:T(8,128)(2,1)S(1)}, u32[]{:S(2)}, u32[]{:S(2)}) %collective-permute-start.7) | collective-permute-done | bytes 360480 | tf_op jit(solution)/shard_map/ppermute | solution.py:66
  117.2 14.9 %collective-permute-done.4 = bf16[352,512]{1,0:T(8,128)(2,1)S(1)} collective-permute-done((bf16[352,512]{1,0:T(8,128)(2,1)S(1)}, bf16[352,512]{1,0:T(8,128)(2,1)S(1)}, u32[]{:S(2)}, u32[]{:S(2)}) %collective-permute-start.4) | collective-permute-done | bytes 360480 | tf_op jit(solution)/shard_map/ppermute | solution.py:66
  132.2 1.8 %maximum_bitcast_fusion = f32[1,1,352,2048]{3,2,1,0:T(8,128)} fusion(f32[352,512]{1,0:T(8,128)S(1)} %convert_add_fusion, f32[352,512]{1,0:T(8,128)S(1)} %convert_add_fusion.1, f32[352,512]{1,0:T(8,128)S(1)} %convert_add_fusion.2, f32[352,512]{1,0:T(8,128)S(1)} %convert_add_fusion.3), kind=kLoop, calls=%fused_computation.2 | loop fusion | flops 2162688 | bytes 5767168 | tf_op jit(solution)/shard_map/reshape | solution.py:104
  (55 shorter events, 15.3 us)
Async XLA Ops:
  0.6 15.2 %collective-permute-start = (bf16[1,128,2048]{2,1,0:T(8,128)(2,1)}, bf16[1,128,2048]{2,1,0:T(8,128)(2,1)S(1)}, u32[]{:S(2)}, u32[]{:S(2)}) collective-permute-start(bf16[1,128,2048]{2,1,0:T(8,128)(2,1)} %param.5), channel_id=1, source_target_pairs={{0,16},{16,0},{1,17},{17,1},{2,18},{18,2},{3,19},{19,3},{4,20},{20... | collective-permute-start | bytes 1572872 | tf_op jit(solution)/shard_map/ppermute | solution.py:10
  16.4 5.3 %copy-start = (bf16[1,1,1,320,1408]{4,3,2,1,0:T(8,128)(2,1)S(1)}, bf16[1,1,1,320,1408]{4,3,2,1,0:T(8,128)(2,1)}, u32[]{:S(2)}) copy-start(bf16[1,1,1,320,1408]{4,3,2,1,0:T(8,128)(2,1)} %param.8) | copy-start | bytes 2703364
  18.0 20.8 %all-to-all-start = ((bf16[4,80,2048]{2,1,0:T(8,128)(2,1)}), bf16[4,80,2048]{2,1,0:T(8,128)(2,1)S(1)}, u32[]{:S(2)}, u32[]{:S(2)}) async-start(bf16[4,80,2048]{2,1,0:T(8,128)(2,1)} %bitcast.8), calls=%async_computation | async-start | bytes 2621440 | tf_op jit(solution)/shard_map/all_to_all | solution.py:87
  21.8 27.1 %collective-permute-start.1 = (bf16[320,1408]{1,0:T(8,128)(2,1)S(1)}, bf16[320,1408]{1,0:T(8,128)(2,1)}, u32[]{:S(2)}, u32[]{:S(2)}) collective-permute-start(bf16[320,1408]{1,0:T(8,128)(2,1)S(1)} %fusion.9), channel_id=1, source_target_pairs={{0,4},{12,8},{1,5},{13,9},{2,6},{14,10},{3,7},{15,11},{16,20},{28,... | collective-permute-start | bytes 2703368 | tf_op jit(solution)/shard_map/ppermute | solution.py:36
  39.8 13.3 %collective-permute-start.11 = (bf16[320,512]{1,0:T(8,128)(2,1)}, bf16[320,512]{1,0:T(8,128)(2,1)}, u32[]{:S(2)}, u32[]{:S(2)}) collective-permute-start(bf16[320,512]{1,0:T(8,128)(2,1)} %get-tuple-element.5), channel_id=1, source_target_pairs={{0,4},{12,8},{1,5},{13,9},{2,6},{14,10},{3,7},{15,11},{16,20},{28,... | collective-permute-start | bytes 983048 | tf_op jit(solution)/shard_map/ppermute | solution.py:55
  44.2 15.8 %collective-permute-start.8 = (bf16[320,512]{1,0:T(8,128)(2,1)}, bf16[320,512]{1,0:T(8,128)(2,1)}, u32[]{:S(2)}, u32[]{:S(2)}) collective-permute-start(bf16[320,512]{1,0:T(8,128)(2,1)} %get-tuple-element.6), channel_id=1, source_target_pairs={{0,4},{12,8},{1,5},{13,9},{2,6},{14,10},{3,7},{15,11},{16,20},{28,... | collective-permute-start | bytes 983048 | tf_op jit(solution)/shard_map/ppermute | solution.py:55
  46.3 20.8 %collective-permute-start.5 = (bf16[320,512]{1,0:T(8,128)(2,1)}, bf16[320,512]{1,0:T(8,128)(2,1)S(1)}, u32[]{:S(2)}, u32[]{:S(2)}) collective-permute-start(bf16[320,512]{1,0:T(8,128)(2,1)} %get-tuple-element.7), channel_id=1, source_target_pairs={{0,4},{12,8},{1,5},{13,9},{2,6},{14,10},{3,7},{15,11},{16,20},{28,... | collective-permute-start | bytes 983048 | tf_op jit(solution)/shard_map/ppermute | solution.py:55
  47.6 25.9 %collective-permute-start.2 = (bf16[320,512]{1,0:T(8,128)(2,1)S(1)}, bf16[320,512]{1,0:T(8,128)(2,1)S(1)}, u32[]{:S(2)}, u32[]{:S(2)}) collective-permute-start(bf16[320,512]{1,0:T(8,128)(2,1)S(1)} %get-tuple-element.4), channel_id=1, source_target_pairs={{0,4},{12,8},{1,5},{13,9},{2,6},{14,10},{3,7},{15,11},{16,20},{28,... | collective-permute-start | bytes 983048 | tf_op jit(solution)/shard_map/ppermute | solution.py:55
  55.8 11.3 %copy-start.1 = (bf16[320,512]{1,0:T(8,128)(2,1)S(1)}, bf16[320,512]{1,0:T(8,128)(2,1)}, u32[]{:S(2)}) copy-start(bf16[320,512]{1,0:T(8,128)(2,1)} %get-tuple-element.7) | copy-start | bytes 983044
  55.8 24.3 %collective-permute-start.12 = (bf16[704,512]{1,0:T(8,128)(2,1)S(1)}, bf16[704,512]{1,0:T(8,128)(2,1)S(1)}, u32[]{:S(2)}, u32[]{:S(2)}) collective-permute-start(bf16[704,512]{1,0:T(8,128)(2,1)S(1)} %dynamic-slice_convert_fusion), channel_id=1, source_target_pairs={{4,8},{8,4},{5,9},{9,5},{6,10},{10,6},{7,11},{11,7},{20,24},{24,20... | collective-permute-start | bytes 2162696 | tf_op jit(solution)/shard_map/ppermute | solution.py:61
  62.8 18.7 %collective-permute-start.9 = (bf16[704,512]{1,0:T(8,128)(2,1)S(1)}, bf16[704,512]{1,0:T(8,128)(2,1)S(1)}, u32[]{:S(2)}, u32[]{:S(2)}) collective-permute-start(bf16[704,512]{1,0:T(8,128)(2,1)S(1)} %dynamic-slice_convert_fusion.1), channel_id=1, source_target_pairs={{4,8},{8,4},{5,9},{9,5},{6,10},{10,6},{7,11},{11,7},{20,24},{24,20... | collective-permute-start | bytes 2162696 | tf_op jit(solution)/shard_map/ppermute | solution.py:61
  69.6 7.2 %slice-start = ((s8[5767168]{0:T(1024)(128)(4,1)}), s8[4194304]{0:T(1024)(128)(4,1)S(1)}, s32[]{:S(2)}) async-start(s8[5767168]{0:T(1024)(128)(4,1)} %bitcast.56), calls=%async_computation.1 | async-start | bytes 8388608
  69.7 7.1 %slice-start.1 = ((s8[5767168]{0:T(1024)(128)(4,1)}), s8[1572864]{0:T(1024)(128)(4,1)S(1)}, s32[]{:S(2)}) async-start(s8[5767168]{0:T(1024)(128)(4,1)} %bitcast.56), calls=%async_computation.2 | async-start | bytes 3145728
  69.7 13.2 %collective-permute-start.6 = (bf16[704,512]{1,0:T(8,128)(2,1)S(1)}, bf16[704,512]{1,0:T(8,128)(2,1)S(1)}, u32[]{:S(2)}, u32[]{:S(2)}) collective-permute-start(bf16[704,512]{1,0:T(8,128)(2,1)S(1)} %dynamic-slice_convert_fusion.2), channel_id=1, source_target_pairs={{4,8},{8,4},{5,9},{9,5},{6,10},{10,6},{7,11},{11,7},{20,24},{24,20... | collective-permute-start | bytes 2162696 | tf_op jit(solution)/shard_map/ppermute | solution.py:61
  76.1 8.3 %collective-permute-start.3 = (bf16[704,512]{1,0:T(8,128)(2,1)S(1)}, bf16[704,512]{1,0:T(8,128)(2,1)S(1)}, u32[]{:S(2)}, u32[]{:S(2)}) collective-permute-start(bf16[704,512]{1,0:T(8,128)(2,1)S(1)} %dynamic-slice_convert_fusion.3), channel_id=1, source_target_pairs={{4,8},{8,4},{5,9},{9,5},{6,10},{10,6},{7,11},{11,7},{20,24},{24,20... | collective-permute-start | bytes 2162696 | tf_op jit(solution)/shard_map/ppermute | solution.py:61
  80.2 15.7 %collective-permute-start.13 = (bf16[352,512]{1,0:T(8,128)(2,1)S(1)}, bf16[352,512]{1,0:T(8,128)(2,1)S(1)}, u32[]{:S(2)}, u32[]{:S(2)}) collective-permute-start(bf16[352,512]{1,0:T(8,128)(2,1)S(1)} %add_convert_fusion), channel_id=1, source_target_pairs={{4,0},{8,12},{5,1},{9,13},{6,2},{10,14},{7,3},{11,15},{20,16},{24,... | collective-permute-start | bytes 1081352 | tf_op jit(solution)/shard_map/ppermute | solution.py:66
  81.7 20.7 %collective-permute-start.10 = (bf16[352,512]{1,0:T(8,128)(2,1)S(1)}, bf16[352,512]{1,0:T(8,128)(2,1)S(1)}, u32[]{:S(2)}, u32[]{:S(2)}) collective-permute-start(bf16[352,512]{1,0:T(8,128)(2,1)S(1)} %add_convert_fusion.1), channel_id=1, source_target_pairs={{4,0},{8,12},{5,1},{9,13},{6,2},{10,14},{7,3},{11,15},{20,16},{24,... | collective-permute-start | bytes 1081352 | tf_op jit(solution)/shard_map/ppermute | solution.py:66
  83.1 34.0 %collective-permute-start.7 = (bf16[352,512]{1,0:T(8,128)(2,1)S(1)}, bf16[352,512]{1,0:T(8,128)(2,1)S(1)}, u32[]{:S(2)}, u32[]{:S(2)}) collective-permute-start(bf16[352,512]{1,0:T(8,128)(2,1)S(1)} %add_convert_fusion.2), channel_id=1, source_target_pairs={{4,0},{8,12},{5,1},{9,13},{6,2},{10,14},{7,3},{11,15},{20,16},{24,... | collective-permute-start | bytes 1081352 | tf_op jit(solution)/shard_map/ppermute | solution.py:66
  84.5 47.5 %collective-permute-start.4 = (bf16[352,512]{1,0:T(8,128)(2,1)S(1)}, bf16[352,512]{1,0:T(8,128)(2,1)S(1)}, u32[]{:S(2)}, u32[]{:S(2)}) collective-permute-start(bf16[352,512]{1,0:T(8,128)(2,1)S(1)} %add_convert_fusion.3), channel_id=1, source_target_pairs={{4,0},{8,12},{5,1},{9,13},{6,2},{10,14},{7,3},{11,15},{20,16},{24,... | collective-permute-start | bytes 1081352 | tf_op jit(solution)/shard_map/ppermute | solution.py:66

commit v16 on v15

--- a/solution.py
+++ b/solution.py
@@ -29,11 +29,7 @@
 
 
 def send_hidden(saved):
-    d = lax.axis_index("dp")
-    blk = saved.shape[1] // 4
-    column_block = lax.broadcasted_iota(jnp.int32, saved.shape, 1) // blk
-    hsend = jnp.where(column_block == d, jnp.zeros_like(saved), saved)
-    return lax.ppermute(hsend, "dp", [(0, 1), (3, 2)])
+    return lax.ppermute(saved, "dp", [(0, 1), (3, 2)])
 
 
 def line_weight_grad(saved, hfull, scaled, chunks):
@@ -64,10 +60,10 @@
             + lax.dynamic_slice_in_dim(r2, row3b, blk, axis=0).astype(jnp.float32)
         ).astype(jnp.bfloat16)
         r3 = lax.ppermute(s3, "dp", [(1, 0), (2, 3)])
-        extra = jnp.where(edge, r3, lax.dynamic_slice_in_dim(r2, half, blk, axis=0))
-        pieces.append(
-            lax.dynamic_slice_in_dim(acc, own, blk, axis=0) + extra.astype(jnp.float32)
-        )
+        inside = lax.dynamic_slice_in_dim(acc, own, blk, axis=0) + lax.dynamic_slice_in_dim(
+            r2, half, blk, axis=0
+        ).astype(jnp.float32)
+        pieces.append(jnp.where(edge, r3.astype(jnp.float32), inside))
     return jnp.concatenate(pieces, axis=1), s2
 
 

time: 135 us -> 134 us (level)
  transfers between devices with their start and end apart: 15 -> 15, of which waited for: 10 -> 10; matrix products, arithmetic and copies ran while one was open for 15% -> 14% of each run, Pallas kernels for 0% -> 0%
where the time goes in v16:
time: 134 us
  waiting for transfers between devices  81.3 us (61%)
  starting transfers between devices  28.5 us (21%)
  matrix products  15.6 us (12%)
  other arithmetic  4.27 us (3%)
  local copies, waits for them, and re-layouts  2.96 us (2%)
    ppermute x4, waiting for transfers between devices, line_weight_grad(): r3 = lax.ppermute(s3, 'dp', [(1, 0), (2, 3)])  45.5 us
    ppermute x4, waiting for transfers between devices, line_weight_grad(): srecv = lax.ppermute(sc, 'dp', ends)  15 us
    all_to_all x1, waiting for transfers between devices, shards(): lax.all_to_all(outgoing, 'expert', split_axis=0, concat_axis=0, tiled=True)  12.5 us
    dot_general x4, matrix products, line_weight_grad(): lax.dot_general(lhs, rhs, (((0,), (0,)), ((), ())), preferred_element_typ...  10.1 us
    ppermute x4, starting transfers between devices, line_weight_grad(): srecv = lax.ppermute(sc, 'dp', ends)  9.1 us
    ppermute x1, waiting for transfers between devices, shifted(): return lax.ppermute(value, axis, pairs)  8.3 us
    ppermute x4, starting transfers between devices, line_weight_grad(): r3 = lax.ppermute(s3, 'dp', [(1, 0), (2, 3)])  5.17 us
    ppermute x1, starting transfers between devices, send_hidden(): return lax.ppermute(saved, 'dp', [(0, 1), (3, 2)])  4.68 us
  transfers between devices with their start and end apart: 15, of which 10 were waited for; matrix products, arithmetic and copies ran while one was open for 14% of the time, Pallas kernels for 0%

profile of v16, /device:TPU:0, one launch (start us, length us, event | category | flops | bytes accessed | tf_op | source)
XLA Modules:
  0.0 133.5 jit_solution(15363831146748444233)
XLA Ops:
  0.6 3.0 %collective-permute-start = (bf16[1,128,2048]{2,1,0:T(8,128)(2,1)}, bf16[1,128,2048]{2,1,0:T(8,128)(2,1)S(1)}, u32[]{:S(2)}, u32[]{:S(2)}) collective-permute-start(bf16[1,128,2048]{2,1,0:T(8,128)(2,1)} %param.5), channel_id=1, source_target_pairs={{0,16},{16,0},{1,17},{17,1},{2,18},{18,2},{3,19},{19,3},{4,20},{20... | collective-permute-start | bytes 1572872 | tf_op jit(solution)/shard_map/ppermute | solution.py:10
  7.5 8.3 %collective-permute-done = bf16[1,128,2048]{2,1,0:T(8,128)(2,1)S(1)} collective-permute-done((bf16[1,128,2048]{2,1,0:T(8,128)(2,1)}, bf16[1,128,2048]{2,1,0:T(8,128)(2,1)S(1)}, u32[]{:S(2)}, u32[]{:S(2)}) %collective-permute-start) | collective-permute-done | bytes 524320 | tf_op jit(solution)/shard_map/ppermute | solution.py:10
  16.4 1.7 %fusion.5 = bf16[320,2048]{1,0:T(8,128)(2,1)} fusion(f32[320,2048]{1,0:T(8,128)S(1)} %fusion.27, bf16[1,128,2048]{2,1,0:T(8,128)(2,1)S(1)} %collective-permute-done, f32[128]{0:T(128)S(1)} %get-tuple-element.8, s32[128]{0:T(128)S(1)} %get-tuple-element.2), kind=kOutput, calls=%fused_computation.5 | convolution fusion | flops 169910272 | bytes 4457472 | tf_op jit(solution)/shard_map/dot_general | solution.py:26
  18.0 3.5 %all-to-all-start = ((bf16[4,80,2048]{2,1,0:T(8,128)(2,1)}), bf16[4,80,2048]{2,1,0:T(8,128)(2,1)S(1)}, u32[]{:S(2)}, u32[]{:S(2)}) async-start(bf16[4,80,2048]{2,1,0:T(8,128)(2,1)} %bitcast.8), calls=%async_computation | async-start | bytes 2621440 | tf_op jit(solution)/shard_map/all_to_all | solution.py:83
  21.6 4.7 %collective-permute-start.1 = (bf16[320,1408]{1,0:T(8,128)(2,1)S(1)}, bf16[320,1408]{1,0:T(8,128)(2,1)}, u32[]{:S(2)}, u32[]{:S(2)}) collective-permute-start(bf16[320,1408]{1,0:T(8,128)(2,1)S(1)} %bitcast.53), channel_id=1, source_target_pairs={{0,4},{12,8},{1,5},{13,9},{2,6},{14,10},{3,7},{15,11},{16,20},{28,... | collective-permute-start | bytes 2703368 | tf_op jit(solution)/shard_map/ppermute | solution.py:32
  26.3 12.5 %all-to-all-done = bf16[4,80,2048]{2,1,0:T(8,128)(2,1)S(1)} async-done(((bf16[4,80,2048]{2,1,0:T(8,128)(2,1)}), bf16[4,80,2048]{2,1,0:T(8,128)(2,1)S(1)}, u32[]{:S(2)}, u32[]{:S(2)}) %all-to-all-start) | async-done | bytes 1310752 | tf_op jit(solution)/shard_map/all_to_all | solution.py:83
  38.9 4.5 %collective-permute-start.11 = (bf16[320,512]{1,0:T(8,128)(2,1)S(1)}, bf16[320,512]{1,0:T(8,128)(2,1)}, u32[]{:S(2)}, u32[]{:S(2)}) collective-permute-start(bf16[320,512]{1,0:T(8,128)(2,1)S(1)} %get-tuple-element.5), channel_id=1, source_target_pairs={{0,4},{12,8},{1,5},{13,9},{2,6},{14,10},{3,7},{15,11},{16,20},{28,... | collective-permute-start | bytes 983048 | tf_op jit(solution)/shard_map/ppermute | solution.py:51
  43.4 2.0 %collective-permute-start.8 = (bf16[320,512]{1,0:T(8,128)(2,1)S(1)}, bf16[320,512]{1,0:T(8,128)(2,1)}, u32[]{:S(2)}, u32[]{:S(2)}) collective-permute-start(bf16[320,512]{1,0:T(8,128)(2,1)S(1)} %get-tuple-element.6), channel_id=1, source_target_pairs={{0,4},{12,8},{1,5},{13,9},{2,6},{14,10},{3,7},{15,11},{16,20},{28,... | collective-permute-start | bytes 983048 | tf_op jit(solution)/shard_map/ppermute | solution.py:51
  45.4 1.3 collective-permute-start.5
  46.7 1.3 collective-permute-start.2
  48.0 4.7 %collective-permute-done.11 = bf16[320,512]{1,0:T(8,128)(2,1)} collective-permute-done((bf16[320,512]{1,0:T(8,128)(2,1)S(1)}, bf16[320,512]{1,0:T(8,128)(2,1)}, u32[]{:S(2)}, u32[]{:S(2)}) %collective-permute-start.11) | collective-permute-done | bytes 327712 | tf_op jit(solution)/shard_map/ppermute | solution.py:51
  52.7 2.6 %fusion.23 = f32[1408,512]{1,0:T(8,128)S(1)} fusion(bf16[320,512]{1,0:T(8,128)(2,1)} %collective-permute-done.11, bf16[320,512]{1,0:T(8,128)(2,1)S(1)} %get-tuple-element.5, bf16[320,1408]{1,0:T(8,128)(2,1)} %collective-permute-done.1, bf16[320,1408]{1,0:T(8,128)(2,1)S(1)} %bitcast.54), kind=kOutput, calls=%fused_computation.36 | convolution fusion | flops 927662080 | bytes 5341184 | tf_op jit(solution)/shard_map/dot_general | solution.py:53
  56.1 3.6 %collective-permute-done.8 = bf16[320,512]{1,0:T(8,128)(2,1)} collective-permute-done((bf16[320,512]{1,0:T(8,128)(2,1)S(1)}, bf16[320,512]{1,0:T(8,128)(2,1)}, u32[]{:S(2)}, u32[]{:S(2)}) %collective-permute-start.8) | collective-permute-done | bytes 327712 | tf_op jit(solution)/shard_map/ppermute | solution.py:51
  59.8 2.6 %fusion.19 = f32[1408,512]{1,0:T(8,128)S(1)} fusion(bf16[320,512]{1,0:T(8,128)(2,1)} %collective-permute-done.8, bf16[320,512]{1,0:T(8,128)(2,1)S(1)} %get-tuple-element.6, bf16[320,1408]{1,0:T(8,128)(2,1)} %collective-permute-done.1, bf16[320,1408]{1,0:T(8,128)(2,1)S(1)} %bitcast.55), kind=kOutput, calls=%fused_computation.32 | convolution fusion | flops 927662080 | bytes 5341184 | tf_op jit(solution)/shard_map/dot_general | solution.py:53
  63.2 3.6 %collective-permute-done.5 = bf16[320,512]{1,0:T(8,128)(2,1)S(1)} collective-permute-done((bf16[320,512]{1,0:T(8,128)(2,1)S(1)}, bf16[320,512]{1,0:T(8,128)(2,1)S(1)}, u32[]{:S(2)}, u32[]{:S(2)}) %collective-permute-start.5) | collective-permute-done | bytes 327712 | tf_op jit(solution)/shard_map/ppermute | solution.py:51
  66.8 2.5 %fusion.15 = f32[1408,512]{1,0:T(8,128)S(1)} fusion(bf16[320,512]{1,0:T(8,128)(2,1)S(1)} %collective-permute-done.5, bf16[320,512]{1,0:T(8,128)(2,1)S(1)} %get-tuple-element.7, bf16[320,1408]{1,0:T(8,128)(2,1)} %collective-permute-done.1, bf16[320,1408]{1,0:T(8,128)(2,1)S(1)} %bitcast.56), kind=kOutput, calls=%fused_computation.28 | convolution fusion | flops 927662080 | bytes 5341184 | tf_op jit(solution)/shard_map/dot_general | solution.py:53
  70.3 3.0 %collective-permute-done.2 = bf16[320,512]{1,0:T(8,128)(2,1)S(1)} collective-permute-done((bf16[320,512]{1,0:T(8,128)(2,1)S(1)}, bf16[320,512]{1,0:T(8,128)(2,1)S(1)}, u32[]{:S(2)}, u32[]{:S(2)}) %collective-permute-start.2) | collective-permute-done | bytes 327712 | tf_op jit(solution)/shard_map/ppermute | solution.py:51
  73.3 2.5 %fusion.11 = f32[1408,512]{1,0:T(8,128)S(1)} fusion(bf16[320,512]{1,0:T(8,128)(2,1)S(1)} %collective-permute-done.2, bf16[320,512]{1,0:T(8,128)(2,1)S(1)} %get-tuple-element.4, bf16[320,1408]{1,0:T(8,128)(2,1)} %collective-permute-done.1, bf16[320,1408]{1,0:T(8,128)(2,1)S(1)} %bitcast.57), kind=kOutput, calls=%fused_computation.24 | convolution fusion | flops 927662080 | bytes 5341184 | tf_op jit(solution)/shard_map/dot_general | solution.py:53
  76.6 3.2 %fusion.6 = bf16[1,1,1,320,1408]{4,3,2,1,0:T(8,128)(2,1)} fusion(bf16[320,2048]{1,0:T(8,128)(2,1)S(1)} %bitcast.48, bf16[1,1,1408,2048]{3,2,1,0:T(8,128)(2,1)S(1)} %bitcast.52), kind=kOutput, calls=%fused_computation.6 | convolution fusion | flops 1845944320 | bytes 7979008 | tf_op jit(solution)/shard_map/sd,hd->sh/dot_general | solution.py:96
  85.6 10.2 %collective-permute-done.13 = bf16[352,512]{1,0:T(8,128)(2,1)S(1)} collective-permute-done((bf16[352,512]{1,0:T(8,128)(2,1)S(1)}, bf16[352,512]{1,0:T(8,128)(2,1)S(1)}, u32[]{:S(2)}, u32[]{:S(2)}) %collective-permute-start.13) | collective-permute-done | bytes 360480 | tf_op jit(solution)/shard_map/ppermute | solution.py:62
  95.9 6.2 %collective-permute-done.10 = bf16[352,512]{1,0:T(8,128)(2,1)S(1)} collective-permute-done((bf16[352,512]{1,0:T(8,128)(2,1)S(1)}, bf16[352,512]{1,0:T(8,128)(2,1)S(1)}, u32[]{:S(2)}, u32[]{:S(2)}) %collective-permute-start.10) | collective-permute-done | bytes 360480 | tf_op jit(solution)/shard_map/ppermute | solution.py:62
  102.3 14.3 %collective-permute-done.7 = bf16[352,512]{1,0:T(8,128)(2,1)S(1)} collective-permute-done((bf16[352,512]{1,0:T(8,128)(2,1)S(1)}, bf16[352,512]{1,0:T(8,128)(2,1)S(1)}, u32[]{:S(2)}, u32[]{:S(2)}) %collective-permute-start.7) | collective-permute-done | bytes 360480 | tf_op jit(solution)/shard_map/ppermute | solution.py:62
  116.7 14.8 %collective-permute-done.4 = bf16[352,512]{1,0:T(8,128)(2,1)S(1)} collective-permute-done((bf16[352,512]{1,0:T(8,128)(2,1)S(1)}, bf16[352,512]{1,0:T(8,128)(2,1)S(1)}, u32[]{:S(2)}, u32[]{:S(2)}) %collective-permute-start.4) | collective-permute-done | bytes 360480 | tf_op jit(solution)/shard_map/ppermute | solution.py:62
  131.7 1.8 %maximum_bitcast_fusion = f32[1,1,352,2048]{3,2,1,0:T(8,128)} fusion(f32[352,512]{1,0:T(8,128)S(1)} %add_select_fusion, f32[352,512]{1,0:T(8,128)S(1)} %add_select_fusion.1, f32[352,512]{1,0:T(8,128)S(1)} %add_select_fusion.2, f32[352,512]{1,0:T(8,128)S(1)} %add_select_fusion.3), kind=kLoop, calls=%fused_computation.2 | loop fusion | flops 2162688 | bytes 5767168 | tf_op jit(solution)/shard_map/reshape | solution.py:100
  (50 shorter events, 14.1 us)
Async XLA Ops:
  0.6 15.2 %collective-permute-start = (bf16[1,128,2048]{2,1,0:T(8,128)(2,1)}, bf16[1,128,2048]{2,1,0:T(8,128)(2,1)S(1)}, u32[]{:S(2)}, u32[]{:S(2)}) collective-permute-start(bf16[1,128,2048]{2,1,0:T(8,128)(2,1)} %param.5), channel_id=1, source_target_pairs={{0,16},{16,0},{1,17},{17,1},{2,18},{18,2},{3,19},{19,3},{4,20},{20... | collective-permute-start | bytes 1572872 | tf_op jit(solution)/shard_map/ppermute | solution.py:10
  16.4 5.2 %copy-start = (bf16[1,1,1,320,1408]{4,3,2,1,0:T(8,128)(2,1)S(1)}, bf16[1,1,1,320,1408]{4,3,2,1,0:T(8,128)(2,1)}, u32[]{:S(2)}) copy-start(bf16[1,1,1,320,1408]{4,3,2,1,0:T(8,128)(2,1)} %param.8) | copy-start | bytes 2703364
  18.0 20.8 %all-to-all-start = ((bf16[4,80,2048]{2,1,0:T(8,128)(2,1)}), bf16[4,80,2048]{2,1,0:T(8,128)(2,1)S(1)}, u32[]{:S(2)}, u32[]{:S(2)}) async-start(bf16[4,80,2048]{2,1,0:T(8,128)(2,1)} %bitcast.8), calls=%async_computation | async-start | bytes 2621440 | tf_op jit(solution)/shard_map/all_to_all | solution.py:83
  21.6 26.4 %collective-permute-start.1 = (bf16[320,1408]{1,0:T(8,128)(2,1)S(1)}, bf16[320,1408]{1,0:T(8,128)(2,1)}, u32[]{:S(2)}, u32[]{:S(2)}) collective-permute-start(bf16[320,1408]{1,0:T(8,128)(2,1)S(1)} %bitcast.53), channel_id=1, source_target_pairs={{0,4},{12,8},{1,5},{13,9},{2,6},{14,10},{3,7},{15,11},{16,20},{28,... | collective-permute-start | bytes 2703368 | tf_op jit(solution)/shard_map/ppermute | solution.py:32
  38.9 13.8 %collective-permute-start.11 = (bf16[320,512]{1,0:T(8,128)(2,1)S(1)}, bf16[320,512]{1,0:T(8,128)(2,1)}, u32[]{:S(2)}, u32[]{:S(2)}) collective-permute-start(bf16[320,512]{1,0:T(8,128)(2,1)S(1)} %get-tuple-element.5), channel_id=1, source_target_pairs={{0,4},{12,8},{1,5},{13,9},{2,6},{14,10},{3,7},{15,11},{16,20},{28,... | collective-permute-start | bytes 983048 | tf_op jit(solution)/shard_map/ppermute | solution.py:51
  43.4 16.4 %collective-permute-start.8 = (bf16[320,512]{1,0:T(8,128)(2,1)S(1)}, bf16[320,512]{1,0:T(8,128)(2,1)}, u32[]{:S(2)}, u32[]{:S(2)}) collective-permute-start(bf16[320,512]{1,0:T(8,128)(2,1)S(1)} %get-tuple-element.6), channel_id=1, source_target_pairs={{0,4},{12,8},{1,5},{13,9},{2,6},{14,10},{3,7},{15,11},{16,20},{28,... | collective-permute-start | bytes 983048 | tf_op jit(solution)/shard_map/ppermute | solution.py:51
  45.4 21.4 %collective-permute-start.5 = (bf16[320,512]{1,0:T(8,128)(2,1)S(1)}, bf16[320,512]{1,0:T(8,128)(2,1)S(1)}, u32[]{:S(2)}, u32[]{:S(2)}) collective-permute-start(bf16[320,512]{1,0:T(8,128)(2,1)S(1)} %get-tuple-element.7), channel_id=1, source_target_pairs={{0,4},{12,8},{1,5},{13,9},{2,6},{14,10},{3,7},{15,11},{16,20},{28,... | collective-permute-start | bytes 983048 | tf_op jit(solution)/shard_map/ppermute | solution.py:51
  46.7 26.6 %collective-permute-start.2 = (bf16[320,512]{1,0:T(8,128)(2,1)S(1)}, bf16[320,512]{1,0:T(8,128)(2,1)S(1)}, u32[]{:S(2)}, u32[]{:S(2)}) collective-permute-start(bf16[320,512]{1,0:T(8,128)(2,1)S(1)} %get-tuple-element.4), channel_id=1, source_target_pairs={{0,4},{12,8},{1,5},{13,9},{2,6},{14,10},{3,7},{15,11},{16,20},{28,... | collective-permute-start | bytes 983048 | tf_op jit(solution)/shard_map/ppermute | solution.py:51
  55.4 24.5 %collective-permute-start.12 = (bf16[704,512]{1,0:T(8,128)(2,1)S(1)}, bf16[704,512]{1,0:T(8,128)(2,1)S(1)}, u32[]{:S(2)}, u32[]{:S(2)}) collective-permute-start(bf16[704,512]{1,0:T(8,128)(2,1)S(1)} %dynamic-slice_convert_fusion), channel_id=1, source_target_pairs={{4,8},{8,4},{5,9},{9,5},{6,10},{10,6},{7,11},{11,7},{20,24},{24,20... | collective-permute-start | bytes 2162696 | tf_op jit(solution)/shard_map/ppermute | solution.py:57
  62.4 18.9 %collective-permute-start.9 = (bf16[704,512]{1,0:T(8,128)(2,1)S(1)}, bf16[704,512]{1,0:T(8,128)(2,1)S(1)}, u32[]{:S(2)}, u32[]{:S(2)}) collective-permute-start(bf16[704,512]{1,0:T(8,128)(2,1)S(1)} %dynamic-slice_convert_fusion.1), channel_id=1, source_target_pairs={{4,8},{8,4},{5,9},{9,5},{6,10},{10,6},{7,11},{11,7},{20,24},{24,20... | collective-permute-start | bytes 2162696 | tf_op jit(solution)/shard_map/ppermute | solution.py:57
  69.3 7.3 %slice-start = ((s8[5767168]{0:T(1024)(128)(4,1)}), s8[4194304]{0:T(1024)(128)(4,1)S(1)}, s32[]{:S(2)}) async-start(s8[5767168]{0:T(1024)(128)(4,1)} %bitcast.51), calls=%async_computation.1 | async-start | bytes 8388608
  69.4 7.2 %slice-start.1 = ((s8[5767168]{0:T(1024)(128)(4,1)}), s8[1572864]{0:T(1024)(128)(4,1)S(1)}, s32[]{:S(2)}) async-start(s8[5767168]{0:T(1024)(128)(4,1)} %bitcast.51), calls=%async_computation.2 | async-start | bytes 3145728
  69.4 13.3 %collective-permute-start.6 = (bf16[704,512]{1,0:T(8,128)(2,1)S(1)}, bf16[704,512]{1,0:T(8,128)(2,1)S(1)}, u32[]{:S(2)}, u32[]{:S(2)}) collective-permute-start(bf16[704,512]{1,0:T(8,128)(2,1)S(1)} %dynamic-slice_convert_fusion.2), channel_id=1, source_target_pairs={{4,8},{8,4},{5,9},{9,5},{6,10},{10,6},{7,11},{11,7},{20,24},{24,20... | collective-permute-start | bytes 2162696 | tf_op jit(solution)/shard_map/ppermute | solution.py:57
  75.9 8.3 %collective-permute-start.3 = (bf16[704,512]{1,0:T(8,128)(2,1)S(1)}, bf16[704,512]{1,0:T(8,128)(2,1)S(1)}, u32[]{:S(2)}, u32[]{:S(2)}) collective-permute-start(bf16[704,512]{1,0:T(8,128)(2,1)S(1)} %dynamic-slice_convert_fusion.3), channel_id=1, source_target_pairs={{4,8},{8,4},{5,9},{9,5},{6,10},{10,6},{7,11},{11,7},{20,24},{24,20... | collective-permute-start | bytes 2162696 | tf_op jit(solution)/shard_map/ppermute | solution.py:57
  80.0 15.8 %collective-permute-start.13 = (bf16[352,512]{1,0:T(8,128)(2,1)S(1)}, bf16[352,512]{1,0:T(8,128)(2,1)S(1)}, u32[]{:S(2)}, u32[]{:S(2)}) collective-permute-start(bf16[352,512]{1,0:T(8,128)(2,1)S(1)} %add_convert_fusion), channel_id=1, source_target_pairs={{4,0},{8,12},{5,1},{9,13},{6,2},{10,14},{7,3},{11,15},{20,16},{24,... | collective-permute-start | bytes 1081352 | tf_op jit(solution)/shard_map/ppermute | solution.py:62
  81.4 20.7 %collective-permute-start.10 = (bf16[352,512]{1,0:T(8,128)(2,1)S(1)}, bf16[352,512]{1,0:T(8,128)(2,1)S(1)}, u32[]{:S(2)}, u32[]{:S(2)}) collective-permute-start(bf16[352,512]{1,0:T(8,128)(2,1)S(1)} %add_convert_fusion.1), channel_id=1, source_target_pairs={{4,0},{8,12},{5,1},{9,13},{6,2},{10,14},{7,3},{11,15},{20,16},{24,... | collective-permute-start | bytes 1081352 | tf_op jit(solution)/shard_map/ppermute | solution.py:62
  82.9 33.7 %collective-permute-start.7 = (bf16[352,512]{1,0:T(8,128)(2,1)S(1)}, bf16[352,512]{1,0:T(8,128)(2,1)S(1)}, u32[]{:S(2)}, u32[]{:S(2)}) collective-permute-start(bf16[352,512]{1,0:T(8,128)(2,1)S(1)} %add_convert_fusion.2), channel_id=1, source_target_pairs={{4,0},{8,12},{5,1},{9,13},{6,2},{10,14},{7,3},{11,15},{20,16},{24,... | collective-permute-start | bytes 1081352 | tf_op jit(solution)/shard_map/ppermute | solution.py:62
  84.3 47.2 %collective-permute-start.4 = (bf16[352,512]{1,0:T(8,128)(2,1)S(1)}, bf16[352,512]{1,0:T(8,128)(2,1)S(1)}, u32[]{:S(2)}, u32[]{:S(2)}) collective-permute-start(bf16[352,512]{1,0:T(8,128)(2,1)S(1)} %add_convert_fusion.3), channel_id=1, source_target_pairs={{4,0},{8,12},{5,1},{9,13},{6,2},{10,14},{7,3},{11,15},{20,16},{24,... | collective-permute-start | bytes 1081352 | tf_op jit(solution)/shard_map/ppermute | solution.py:62

commit v17 on v15

--- a/solution.py
+++ b/solution.py
@@ -44,6 +44,7 @@
     ends = [(0, 1), (3, 2)]
     lhs = jnp.concatenate([saved, hfull], axis=0)
     row2 = jnp.where(d == 1, 2 * blk, 0)
+    lhs2 = lax.dynamic_slice_in_dim(lhs, row2, 2 * blk, axis=1)
     row3a = jnp.where(d == 1, 0, 3 * blk)
     row3b = jnp.where(d == 1, 0, blk)
     own = d * blk
@@ -57,7 +58,9 @@
         acc = lax.dot_general(
             lhs, rhs, (((0,), (0,)), ((), ())), preferred_element_type=jnp.float32
         )
-        s2 = lax.dynamic_slice_in_dim(acc, row2, 2 * blk, axis=0).astype(jnp.bfloat16)
+        s2 = lax.dot_general(
+            lhs2, rhs, (((0,), (0,)), ((), ())), preferred_element_type=jnp.float32
+        ).astype(jnp.bfloat16)
         r2 = lax.ppermute(s2, "dp", [(1, 2), (2, 1)])
         s3 = (
             lax.dynamic_slice_in_dim(acc, row3a, blk, axis=0)

time: 135 us -> 128 us (0.948)
  waiting for transfers between devices: 80.4 us -> 73.8 us
  other arithmetic: 4.44 us -> 8.15 us
  starting transfers between devices: 28.6 us -> 26.2 us
  local copies, waits for them, and re-layouts: 3.81 us -> 2.03 us
    ppermute x1, waiting for transfers between devices: 0.01 us -> 6.95 us  [send_hidden(): return lax.ppermute(hsend, 'dp', [(0, 1), (3, 2)])]
    dot_general x4, matrix products: 10.3 us -> 5.32 us  [line_weight_grad(): lax.dot_general(lhs, rhs, (((0,), (0,)), ((), ())), preferred_element_typ...]
    all_to_all x1, waiting for transfers between devices: 12.3 us -> 7.67 us  [shards(): lax.all_to_all(outgoing, 'expert', split_axis=0, concat_axis=0, tiled=True)]
    ppermute x1, waiting for transfers between devices: 8.3 us -> 3.9 us  [shifted(): return lax.ppermute(value, axis, pairs)]
    ppermute x4, waiting for transfers between devices: 45.8 us -> 41.9 us  [line_weight_grad(): r3 = lax.ppermute(s3, 'dp', [(1, 0), (2, 3)])]
    dot_general x0 -> x4, matrix products: none -> 3.01 us  [line_weight_grad(): lax.dot_general(lhs2, rhs, (((0,), (0,)), ((), ())), preferred_element_ty...]
    dot_general x1, matrix products: 3.23 us -> 5.79 us  [shards(): jnp.einsum('sd,hd->sh', late, weight, preferred_element_type=jnp.float32)]
    select_n x1, other arithmetic: 0.16 us -> 2.25 us  [send_hidden(): hsend = jnp.where(column_block == d, jnp.zeros_like(saved), saved)]
  transfers between devices with their start and end apart: 15 -> 15, of which waited for: 10 -> 10; matrix products, arithmetic and copies ran while one was open for 15% -> 18% of each run, Pallas kernels for 0% -> 0%
where the time goes in v17:
time: 128 us
  waiting for transfers between devices  73.8 us (58%)
  starting transfers between devices  26.2 us (20%)
  matrix products  16.3 us (13%)
  other arithmetic  8.15 us (6%)
  local copies, waits for them, and re-layouts  2.03 us (2%)
    ppermute x4, waiting for transfers between devices, line_weight_grad(): r3 = lax.ppermute(s3, 'dp', [(1, 0), (2, 3)])  41.9 us
    ppermute x4, waiting for transfers between devices, line_weight_grad(): srecv = lax.ppermute(sc, 'dp', ends)  13.4 us
    all_to_all x1, waiting for transfers between devices, shards(): lax.all_to_all(outgoing, 'expert', split_axis=0, concat_axis=0, tiled=True)  7.67 us
    ppermute x4, starting transfers between devices, line_weight_grad(): srecv = lax.ppermute(sc, 'dp', ends)  7.66 us
    ppermute x1, waiting for transfers between devices, send_hidden(): return lax.ppermute(hsend, 'dp', [(0, 1), (3, 2)])  6.95 us
    dot_general x1, matrix products, shards(): jnp.einsum('sd,hd->sh', late, weight, preferred_element_type=jnp.float32)  5.79 us
    dot_general x4, matrix products, line_weight_grad(): lax.dot_general(lhs, rhs, (((0,), (0,)), ((), ())), preferred_element_typ...  5.32 us
    ppermute x4, starting transfers between devices, line_weight_grad(): r3 = lax.ppermute(s3, 'dp', [(1, 0), (2, 3)])  5.17 us
  transfers between devices with their start and end apart: 15, of which 10 were waited for; matrix products, arithmetic and copies ran while one was open for 18% of the time, Pallas kernels for 0%

profile of v17, /device:TPU:0, one launch (start us, length us, event | category | flops | bytes accessed | tf_op | source)
XLA Modules:
  0.0 127.6 jit_solution(5793500794188049980)
XLA Ops:
  0.6 3.0 %collective-permute-start = (bf16[1,128,2048]{2,1,0:T(8,128)(2,1)}, bf16[1,128,2048]{2,1,0:T(8,128)(2,1)S(1)}, u32[]{:S(2)}, u32[]{:S(2)}) collective-permute-start(bf16[1,128,2048]{2,1,0:T(8,128)(2,1)} %param.5), channel_id=1, source_target_pairs={{0,16},{16,0},{1,17},{17,1},{2,18},{18,2},{3,19},{19,3},{4,20},{20... | collective-permute-start | bytes 1572872 | tf_op jit(solution)/shard_map/ppermute | solution.py:10
  3.7 2.2 %fusion.9 = bf16[320,1408]{1,0:T(8,128)(2,1)} fusion(s32[]{:T(128)S(6)} %axis_index.19, s32[1408]{0:T(1024)S(1)} %get-tuple-element.10, s32[1408]{0:T(1024)S(1)} %get-tuple-element.11, pred[1408]{0:T(1024)(128)(4,1)S(1)} %fusion.28, bf16[1,1,1,320,1408]{4,3,2,1,0:T(8,128)(2,1)} %param.8), kind=kLoop, calls=%fused_computation.11 | loop fusion | flops 1351680 | bytes 1814916 | tf_op jit(solution)/shard_map/jit(_where)/select_n | solution.py:35
  6.0 3.5 %collective-permute-start.1 = (bf16[320,1408]{1,0:T(8,128)(2,1)}, bf16[320,1408]{1,0:T(8,128)(2,1)S(1)}, u32[]{:S(2)}, u32[]{:S(2)}) collective-permute-start(bf16[320,1408]{1,0:T(8,128)(2,1)} %fusion.9), channel_id=1, source_target_pairs={{0,4},{12,8},{1,5},{13,9},{2,6},{14,10},{3,7},{15,11},{16,20},{28,... | collective-permute-start | bytes 2703368 | tf_op jit(solution)/shard_map/ppermute | solution.py:36
  11.9 3.9 %collective-permute-done = bf16[1,128,2048]{2,1,0:T(8,128)(2,1)S(1)} collective-permute-done((bf16[1,128,2048]{2,1,0:T(8,128)(2,1)}, bf16[1,128,2048]{2,1,0:T(8,128)(2,1)S(1)}, u32[]{:S(2)}, u32[]{:S(2)}) %collective-permute-start) | collective-permute-done | bytes 524320 | tf_op jit(solution)/shard_map/ppermute | solution.py:10
  16.4 1.7 %fusion.5 = bf16[320,2048]{1,0:T(8,128)(2,1)} fusion(f32[320,2048]{1,0:T(8,128)S(1)} %fusion.13, bf16[1,128,2048]{2,1,0:T(8,128)(2,1)S(1)} %collective-permute-done, f32[128]{0:T(128)S(1)} %get-tuple-element.8, s32[128]{0:T(128)S(1)} %get-tuple-element.2), kind=kOutput, calls=%fused_computation.5 | convolution fusion | flops 169910272 | bytes 4457472 | tf_op jit(solution)/shard_map/dot_general | solution.py:26
  18.1 3.7 %all-to-all-start = ((bf16[4,80,2048]{2,1,0:T(8,128)(2,1)}), bf16[4,80,2048]{2,1,0:T(8,128)(2,1)S(1)}, u32[]{:S(2)}, u32[]{:S(2)}) async-start(bf16[4,80,2048]{2,1,0:T(8,128)(2,1)} %bitcast.8), calls=%async_computation | async-start | bytes 2621440 | tf_op jit(solution)/shard_map/all_to_all | solution.py:90
  21.8 6.9 %collective-permute-done.1 = bf16[320,1408]{1,0:T(8,128)(2,1)S(1)} collective-permute-done((bf16[320,1408]{1,0:T(8,128)(2,1)}, bf16[320,1408]{1,0:T(8,128)(2,1)S(1)}, u32[]{:S(2)}, u32[]{:S(2)}) %collective-permute-start.1) | collective-permute-done | bytes 901152 | tf_op jit(solution)/shard_map/ppermute | solution.py:36
  29.6 1.6 %fusion.12 = bf16[640,704]{1,0:T(8,128)(2,1)S(1)} fusion(s32[]{:T(128)S(6)} %select_n.66, bf16[320,1408]{1,0:T(8,128)(2,1)S(1)} %bitcast.54, bf16[320,1408]{1,0:T(8,128)(2,1)} %copy-done.1), kind=kLoop, calls=%fused_computation.20 | loop fusion | flops 1802240 | bytes 2703364 | tf_op jit(solution)/shard_map/concatenate | solution.py:45
  31.3 7.7 %all-to-all-done = bf16[4,80,2048]{2,1,0:T(8,128)(2,1)S(1)} async-done(((bf16[4,80,2048]{2,1,0:T(8,128)(2,1)}), bf16[4,80,2048]{2,1,0:T(8,128)(2,1)S(1)}, u32[]{:S(2)}, u32[]{:S(2)}) %all-to-all-start) | async-done | bytes 1310752 | tf_op jit(solution)/shard_map/all_to_all | solution.py:90
  39.0 3.7 %collective-permute-start.11 = (bf16[320,512]{1,0:T(8,128)(2,1)S(1)}, bf16[320,512]{1,0:T(8,128)(2,1)S(1)}, u32[]{:S(2)}, u32[]{:S(2)}) collective-permute-start(bf16[320,512]{1,0:T(8,128)(2,1)S(1)} %get-tuple-element.5), channel_id=1, source_target_pairs={{0,4},{12,8},{1,5},{13,9},{2,6},{14,10},{3,7},{15,11},{16,20},{28,... | collective-permute-start | bytes 983048 | tf_op jit(solution)/shard_map/ppermute | solution.py:56
  42.8 1.3 %collective-permute-start.8 = (bf16[320,512]{1,0:T(8,128)(2,1)S(1)}, bf16[320,512]{1,0:T(8,128)(2,1)S(1)}, u32[]{:S(2)}, u32[]{:S(2)}) collective-permute-start(bf16[320,512]{1,0:T(8,128)(2,1)S(1)} %get-tuple-element.6), channel_id=1, source_target_pairs={{0,4},{12,8},{1,5},{13,9},{2,6},{14,10},{3,7},{15,11},{16,20},{28,... | collective-permute-start | bytes 983048 | tf_op jit(solution)/shard_map/ppermute | solution.py:56
  44.1 5.8 %fusion.6 = bf16[1,1,1,320,1408]{4,3,2,1,0:T(8,128)(2,1)} fusion(bf16[320,2048]{1,0:T(8,128)(2,1)S(1)} %bitcast.53, bf16[1,1,1408,2048]{3,2,1,0:T(8,128)(2,1)} %param.9), kind=kOutput, calls=%fused_computation.6 | convolution fusion | flops 1845944320 | bytes 7979008 | tf_op jit(solution)/shard_map/sd,hd->sh/dot_general | solution.py:103
  54.0 3.9 %collective-permute-done.8 = bf16[320,512]{1,0:T(8,128)(2,1)S(1)} collective-permute-done((bf16[320,512]{1,0:T(8,128)(2,1)S(1)}, bf16[320,512]{1,0:T(8,128)(2,1)S(1)}, u32[]{:S(2)}, u32[]{:S(2)}) %collective-permute-start.8) | collective-permute-done | bytes 327712 | tf_op jit(solution)/shard_map/ppermute | solution.py:56
  59.4 5.6 %collective-permute-done.5 = bf16[320,512]{1,0:T(8,128)(2,1)S(1)} collective-permute-done((bf16[320,512]{1,0:T(8,128)(2,1)S(1)}, bf16[320,512]{1,0:T(8,128)(2,1)S(1)}, u32[]{:S(2)}, u32[]{:S(2)}) %collective-permute-start.5) | collective-permute-done | bytes 327712 | tf_op jit(solution)/shard_map/ppermute | solution.py:56
  66.5 4.0 %collective-permute-done.2 = bf16[320,512]{1,0:T(8,128)(2,1)S(1)} collective-permute-done((bf16[320,512]{1,0:T(8,128)(2,1)S(1)}, bf16[320,512]{1,0:T(8,128)(2,1)S(1)}, u32[]{:S(2)}, u32[]{:S(2)}) %collective-permute-start.2) | collective-permute-done | bytes 327712 | tf_op jit(solution)/shard_map/ppermute | solution.py:56
  72.2 1.3 %fusion.20 = f32[1408,512]{1,0:T(8,128)S(1)} fusion(bf16[320,512]{1,0:T(8,128)(2,1)S(1)} %collective-permute-done.11, bf16[320,512]{1,0:T(8,128)(2,1)S(1)} %get-tuple-element.5, bf16[320,1408]{1,0:T(8,128)(2,1)S(1)} %copy-done.2, bf16[320,1408]{1,0:T(8,128)(2,1)S(1)} %bitcast.55), kind=kOutput, calls=%fused_computation.38 | convolution fusion | flops 927662080 | bytes 5341184 | tf_op jit(solution)/shard_map/dot_general | solution.py:58
  73.5 1.3 %fusion.21 = f32[1408,512]{1,0:T(8,128)S(1)} fusion(bf16[320,512]{1,0:T(8,128)(2,1)S(1)} %collective-permute-done.8, bf16[320,512]{1,0:T(8,128)(2,1)S(1)} %get-tuple-element.6, bf16[320,1408]{1,0:T(8,128)(2,1)S(1)} %copy-done.2, bf16[320,1408]{1,0:T(8,128)(2,1)S(1)} %bitcast.56), kind=kOutput, calls=%fused_computation.39 | convolution fusion | flops 927662080 | bytes 5341184 | tf_op jit(solution)/shard_map/dot_general | solution.py:58
  74.8 1.3 %fusion.22 = f32[1408,512]{1,0:T(8,128)S(1)} fusion(bf16[320,512]{1,0:T(8,128)(2,1)S(1)} %collective-permute-done.5, bf16[320,512]{1,0:T(8,128)(2,1)S(1)} %get-tuple-element.7, bf16[320,1408]{1,0:T(8,128)(2,1)S(1)} %copy-done.2, bf16[320,1408]{1,0:T(8,128)(2,1)S(1)} %bitcast.57), kind=kOutput, calls=%fused_computation.40 | convolution fusion | flops 927662080 | bytes 5341184 | tf_op jit(solution)/shard_map/dot_general | solution.py:58
  76.2 1.3 %fusion.23 = f32[1408,512]{1,0:T(8,128)S(1)} fusion(bf16[320,512]{1,0:T(8,128)(2,1)S(1)} %collective-permute-done.2, bf16[320,512]{1,0:T(8,128)(2,1)S(1)} %get-tuple-element.4, bf16[320,1408]{1,0:T(8,128)(2,1)S(1)} %copy-done.2, bf16[320,1408]{1,0:T(8,128)(2,1)S(1)} %bitcast.58), kind=kOutput, calls=%fused_computation.41 | convolution fusion | flops 927662080 | bytes 5341184 | tf_op jit(solution)/shard_map/dot_general | solution.py:58
  83.3 10.2 %collective-permute-done.13 = bf16[352,512]{1,0:T(8,128)(2,1)S(1)} collective-permute-done((bf16[352,512]{1,0:T(8,128)(2,1)S(1)}, bf16[352,512]{1,0:T(8,128)(2,1)S(1)}, u32[]{:S(2)}, u32[]{:S(2)}) %collective-permute-start.13) | collective-permute-done | bytes 360480 | tf_op jit(solution)/shard_map/ppermute | solution.py:69
  93.6 5.3 %collective-permute-done.10 = bf16[352,512]{1,0:T(8,128)(2,1)S(1)} collective-permute-done((bf16[352,512]{1,0:T(8,128)(2,1)S(1)}, bf16[352,512]{1,0:T(8,128)(2,1)S(1)}, u32[]{:S(2)}, u32[]{:S(2)}) %collective-permute-start.10) | collective-permute-done | bytes 360480 | tf_op jit(solution)/shard_map/ppermute | solution.py:69
  99.0 13.7 %collective-permute-done.7 = bf16[352,512]{1,0:T(8,128)(2,1)S(1)} collective-permute-done((bf16[352,512]{1,0:T(8,128)(2,1)S(1)}, bf16[352,512]{1,0:T(8,128)(2,1)S(1)}, u32[]{:S(2)}, u32[]{:S(2)}) %collective-permute-start.7) | collective-permute-done | bytes 360480 | tf_op jit(solution)/shard_map/ppermute | solution.py:69
  112.8 12.7 %collective-permute-done.4 = bf16[352,512]{1,0:T(8,128)(2,1)S(1)} collective-permute-done((bf16[352,512]{1,0:T(8,128)(2,1)S(1)}, bf16[352,512]{1,0:T(8,128)(2,1)S(1)}, u32[]{:S(2)}, u32[]{:S(2)}) %collective-permute-start.4) | collective-permute-done | bytes 360480 | tf_op jit(solution)/shard_map/ppermute | solution.py:69
  125.7 1.8 %maximum_bitcast_fusion = f32[1,1,352,2048]{3,2,1,0:T(8,128)} fusion(f32[352,512]{1,0:T(8,128)S(1)} %convert_add_fusion, f32[352,512]{1,0:T(8,128)S(1)} %convert_add_fusion.1, f32[352,512]{1,0:T(8,128)S(1)} %convert_add_fusion.2, f32[352,512]{1,0:T(8,128)S(1)} %convert_add_fusion.3), kind=kLoop, calls=%fused_computation.2 | loop fusion | flops 2162688 | bytes 5767168 | tf_op jit(solution)/shard_map/reshape | solution.py:107
  (57 shorter events, 19.0 us)
Async XLA Ops:
  0.6 8.9 %copy-start.3 = (s32[1,128,2]{1,2,0:T(2,128)S(1)}, s32[1,128,2]{1,2,0:T(2,128)}, u32[]{:S(2)}) copy-start(s32[1,128,2]{1,2,0:T(2,128)} %param.6) | copy-start | bytes 3076
  0.6 11.3 %copy-start.4 = (f32[1,128,2]{1,2,0:T(2,128)S(1)}, f32[1,128,2]{1,2,0:T(2,128)}, u32[]{:S(2)}) copy-start(f32[1,128,2]{1,2,0:T(2,128)} %param.7) | copy-start | bytes 3076
  0.6 15.2 %collective-permute-start = (bf16[1,128,2048]{2,1,0:T(8,128)(2,1)}, bf16[1,128,2048]{2,1,0:T(8,128)(2,1)S(1)}, u32[]{:S(2)}, u32[]{:S(2)}) collective-permute-start(bf16[1,128,2048]{2,1,0:T(8,128)(2,1)} %param.5), channel_id=1, source_target_pairs={{0,16},{16,0},{1,17},{17,1},{2,18},{18,2},{3,19},{19,3},{4,20},{20... | collective-permute-start | bytes 1572872 | tf_op jit(solution)/shard_map/ppermute | solution.py:10
  6.0 22.8 %collective-permute-start.1 = (bf16[320,1408]{1,0:T(8,128)(2,1)}, bf16[320,1408]{1,0:T(8,128)(2,1)S(1)}, u32[]{:S(2)}, u32[]{:S(2)}) collective-permute-start(bf16[320,1408]{1,0:T(8,128)(2,1)} %fusion.9), channel_id=1, source_target_pairs={{0,4},{12,8},{1,5},{13,9},{2,6},{14,10},{3,7},{15,11},{16,20},{28,... | collective-permute-start | bytes 2703368 | tf_op jit(solution)/shard_map/ppermute | solution.py:36
  18.1 11.6 %copy-start = (bf16[1,1,1,320,1408]{4,3,2,1,0:T(8,128)(2,1)S(1)}, bf16[1,1,1,320,1408]{4,3,2,1,0:T(8,128)(2,1)}, u32[]{:S(2)}) copy-start(bf16[1,1,1,320,1408]{4,3,2,1,0:T(8,128)(2,1)} %param.8) | copy-start | bytes 2703364
  18.1 20.9 %all-to-all-start = ((bf16[4,80,2048]{2,1,0:T(8,128)(2,1)}), bf16[4,80,2048]{2,1,0:T(8,128)(2,1)S(1)}, u32[]{:S(2)}, u32[]{:S(2)}) async-start(bf16[4,80,2048]{2,1,0:T(8,128)(2,1)} %bitcast.8), calls=%async_computation | async-start | bytes 2621440 | tf_op jit(solution)/shard_map/all_to_all | solution.py:90
  28.7 0.9 copy-start.1
  39.0 13.5 %collective-permute-start.11 = (bf16[320,512]{1,0:T(8,128)(2,1)S(1)}, bf16[320,512]{1,0:T(8,128)(2,1)S(1)}, u32[]{:S(2)}, u32[]{:S(2)}) collective-permute-start(bf16[320,512]{1,0:T(8,128)(2,1)S(1)} %get-tuple-element.5), channel_id=1, source_target_pairs={{0,4},{12,8},{1,5},{13,9},{2,6},{14,10},{3,7},{15,11},{16,20},{28,... | collective-permute-start | bytes 983048 | tf_op jit(solution)/shard_map/ppermute | solution.py:56
  42.8 15.1 %collective-permute-start.8 = (bf16[320,512]{1,0:T(8,128)(2,1)S(1)}, bf16[320,512]{1,0:T(8,128)(2,1)S(1)}, u32[]{:S(2)}, u32[]{:S(2)}) collective-permute-start(bf16[320,512]{1,0:T(8,128)(2,1)S(1)} %get-tuple-element.6), channel_id=1, source_target_pairs={{0,4},{12,8},{1,5},{13,9},{2,6},{14,10},{3,7},{15,11},{16,20},{28,... | collective-permute-start | bytes 983048 | tf_op jit(solution)/shard_map/ppermute | solution.py:56
  49.9 15.0 %collective-permute-start.5 = (bf16[320,512]{1,0:T(8,128)(2,1)S(1)}, bf16[320,512]{1,0:T(8,128)(2,1)S(1)}, u32[]{:S(2)}, u32[]{:S(2)}) collective-permute-start(bf16[320,512]{1,0:T(8,128)(2,1)S(1)} %get-tuple-element.7), channel_id=1, source_target_pairs={{0,4},{12,8},{1,5},{13,9},{2,6},{14,10},{3,7},{15,11},{16,20},{28,... | collective-permute-start | bytes 983048 | tf_op jit(solution)/shard_map/ppermute | solution.py:56
  51.2 19.3 %collective-permute-start.2 = (bf16[320,512]{1,0:T(8,128)(2,1)S(1)}, bf16[320,512]{1,0:T(8,128)(2,1)S(1)}, u32[]{:S(2)}, u32[]{:S(2)}) collective-permute-start(bf16[320,512]{1,0:T(8,128)(2,1)S(1)} %get-tuple-element.4), channel_id=1, source_target_pairs={{0,4},{12,8},{1,5},{13,9},{2,6},{14,10},{3,7},{15,11},{16,20},{28,... | collective-permute-start | bytes 983048 | tf_op jit(solution)/shard_map/ppermute | solution.py:56
  53.3 24.2 %collective-permute-start.12 = (bf16[704,512]{1,0:T(8,128)(2,1)S(1)}, bf16[704,512]{1,0:T(8,128)(2,1)S(1)}, u32[]{:S(2)}, u32[]{:S(2)}) collective-permute-start(bf16[704,512]{1,0:T(8,128)(2,1)S(1)} %convolution_convert_fusion), channel_id=1, source_target_pairs={{4,8},{8,4},{5,9},{9,5},{6,10},{10,6},{7,11},{11,7},{20,24},{24,20... | collective-permute-start | bytes 2162696 | tf_op jit(solution)/shard_map/ppermute | solution.py:64
  58.6 20.3 %collective-permute-start.9 = (bf16[704,512]{1,0:T(8,128)(2,1)S(1)}, bf16[704,512]{1,0:T(8,128)(2,1)S(1)}, u32[]{:S(2)}, u32[]{:S(2)}) collective-permute-start(bf16[704,512]{1,0:T(8,128)(2,1)S(1)} %convolution_convert_fusion.1), channel_id=1, source_target_pairs={{4,8},{8,4},{5,9},{9,5},{6,10},{10,6},{7,11},{11,7},{20,24},{24,20... | collective-permute-start | bytes 2162696 | tf_op jit(solution)/shard_map/ppermute | solution.py:64
  65.7 6.5 %copy-start.2 = (bf16[320,1408]{1,0:T(8,128)(2,1)S(1)}, bf16[320,1408]{1,0:T(8,128)(2,1)}, u32[]{:S(2)}) copy-start(bf16[320,1408]{1,0:T(8,128)(2,1)} %copy-done.1) | copy-start | bytes 2703364
  65.7 14.7 %collective-permute-start.6 = (bf16[704,512]{1,0:T(8,128)(2,1)S(1)}, bf16[704,512]{1,0:T(8,128)(2,1)S(1)}, u32[]{:S(2)}, u32[]{:S(2)}) collective-permute-start(bf16[704,512]{1,0:T(8,128)(2,1)S(1)} %convolution_convert_fusion.2), channel_id=1, source_target_pairs={{4,8},{8,4},{5,9},{9,5},{6,10},{10,6},{7,11},{11,7},{20,24},{24,20... | collective-permute-start | bytes 2162696 | tf_op jit(solution)/shard_map/ppermute | solution.py:64
  71.3 10.6 %collective-permute-start.3 = (bf16[704,512]{1,0:T(8,128)(2,1)S(1)}, bf16[704,512]{1,0:T(8,128)(2,1)S(1)}, u32[]{:S(2)}, u32[]{:S(2)}) collective-permute-start(bf16[704,512]{1,0:T(8,128)(2,1)S(1)} %convolution_convert_fusion.3), channel_id=1, source_target_pairs={{4,8},{8,4},{5,9},{9,5},{6,10},{10,6},{7,11},{11,7},{20,24},{24,20... | collective-permute-start | bytes 2162696 | tf_op jit(solution)/shard_map/ppermute | solution.py:64
  77.6 15.8 %collective-permute-start.13 = (bf16[352,512]{1,0:T(8,128)(2,1)S(1)}, bf16[352,512]{1,0:T(8,128)(2,1)S(1)}, u32[]{:S(2)}, u32[]{:S(2)}) collective-permute-start(bf16[352,512]{1,0:T(8,128)(2,1)S(1)} %add_convert_fusion), channel_id=1, source_target_pairs={{4,0},{8,12},{5,1},{9,13},{6,2},{10,14},{7,3},{11,15},{20,16},{24,... | collective-permute-start | bytes 1081352 | tf_op jit(solution)/shard_map/ppermute | solution.py:69
  79.1 19.8 %collective-permute-start.10 = (bf16[352,512]{1,0:T(8,128)(2,1)S(1)}, bf16[352,512]{1,0:T(8,128)(2,1)S(1)}, u32[]{:S(2)}, u32[]{:S(2)}) collective-permute-start(bf16[352,512]{1,0:T(8,128)(2,1)S(1)} %add_convert_fusion.1), channel_id=1, source_target_pairs={{4,0},{8,12},{5,1},{9,13},{6,2},{10,14},{7,3},{11,15},{20,16},{24,... | collective-permute-start | bytes 1081352 | tf_op jit(solution)/shard_map/ppermute | solution.py:69
  80.5 32.2 %collective-permute-start.7 = (bf16[352,512]{1,0:T(8,128)(2,1)S(1)}, bf16[352,512]{1,0:T(8,128)(2,1)S(1)}, u32[]{:S(2)}, u32[]{:S(2)}) collective-permute-start(bf16[352,512]{1,0:T(8,128)(2,1)S(1)} %add_convert_fusion.2), channel_id=1, source_target_pairs={{4,0},{8,12},{5,1},{9,13},{6,2},{10,14},{7,3},{11,15},{20,16},{24,... | collective-permute-start | bytes 1081352 | tf_op jit(solution)/shard_map/ppermute | solution.py:69
  82.0 43.6 %collective-permute-start.4 = (bf16[352,512]{1,0:T(8,128)(2,1)S(1)}, bf16[352,512]{1,0:T(8,128)(2,1)S(1)}, u32[]{:S(2)}, u32[]{:S(2)}) collective-permute-start(bf16[352,512]{1,0:T(8,128)(2,1)S(1)} %add_convert_fusion.3), channel_id=1, source_target_pairs={{4,0},{8,12},{5,1},{9,13},{6,2},{10,14},{7,3},{11,15},{20,16},{24,... | collective-permute-start | bytes 1081352 | tf_op jit(solution)/shard_map/ppermute | solution.py:69

commit v18 on v17

--- a/solution.py
+++ b/solution.py
@@ -45,6 +45,7 @@
     lhs = jnp.concatenate([saved, hfull], axis=0)
     row2 = jnp.where(d == 1, 2 * blk, 0)
     lhs2 = lax.dynamic_slice_in_dim(lhs, row2, 2 * blk, axis=1)
+    rows = saved.shape[0]
     row3a = jnp.where(d == 1, 0, 3 * blk)
     row3b = jnp.where(d == 1, 0, blk)
     own = d * blk
@@ -58,8 +59,9 @@
         acc = lax.dot_general(
             lhs, rhs, (((0,), (0,)), ((), ())), preferred_element_type=jnp.float32
         )
-        s2 = lax.dot_general(
-            lhs2, rhs, (((0,), (0,)), ((), ())), preferred_element_type=jnp.float32
+        s2 = (
+            lax.dot_general(lhs2[:rows], sc, (((0,), (0,)), ((), ())), preferred_element_type=jnp.float32)
+            + lax.dot_general(lhs2[rows:], srecv, (((0,), (0,)), ((), ())), preferred_element_type=jnp.float32)
         ).astype(jnp.bfloat16)
         r2 = lax.ppermute(s2, "dp", [(1, 2), (2, 1)])
         s3 = (

time: 128 us -> 129 us (level)
  matrix products: 16.3 us -> 17.9 us
    dot_general x4 -> x8, matrix products: 3.01 us -> 4.52 us  [the longest x4 2.27 us: line_weight_grad(): lax.dot_general(lhs2[:rows], sc, (((0,), (0,)), ((), ())), preferred_elem...]
  transfers between devices with their start and end apart: 15 -> 15, of which waited for: 10 -> 10; matrix products, arithmetic and copies ran while one was open for 18% -> 20% of each run, Pallas kernels for 0% -> 0%
where the time goes in v18:
time: 129 us; the launch traced here: 128 us
  waiting for transfers between devices  72.8 us (56%)
  starting transfers between devices  26.1 us (20%)
  matrix products  17.9 us (14%)
  other arithmetic  8.16 us (6%)
  local copies, waits for them, and re-layouts  2.03 us (2%)
    ppermute x4, waiting for transfers between devices, line_weight_grad(): r3 = lax.ppermute(s3, 'dp', [(1, 0), (2, 3)])  41.9 us
    ppermute x4, waiting for transfers between devices, line_weight_grad(): srecv = lax.ppermute(sc, 'dp', ends)  12.4 us
    ppermute x4, starting transfers between devices, line_weight_grad(): srecv = lax.ppermute(sc, 'dp', ends)  7.68 us
    all_to_all x1, waiting for transfers between devices, shards(): lax.all_to_all(outgoing, 'expert', split_axis=0, concat_axis=0, tiled=True)  7.67 us
    ppermute x1, waiting for transfers between devices, send_hidden(): return lax.ppermute(hsend, 'dp', [(0, 1), (3, 2)])  6.95 us
    dot_general x1, matrix products, shards(): jnp.einsum('sd,hd->sh', late, weight, preferred_element_type=jnp.float32)  5.79 us
    dot_general x4, matrix products, line_weight_grad(): lax.dot_general(lhs, rhs, (((0,), (0,)), ((), ())), preferred_element_typ...  5.31 us
    ppermute x4, starting transfers between devices, line_weight_grad(): r3 = lax.ppermute(s3, 'dp', [(1, 0), (2, 3)])  5.17 us
  transfers between devices with their start and end apart: 15, of which 10 were waited for; matrix products, arithmetic and copies ran while one was open for 20% of the time, Pallas kernels for 0%

profile of v18, /device:TPU:0, one launch (start us, length us, event | category | flops | bytes accessed | tf_op | source)
XLA Modules:
  0.0 128.0 jit_solution(11674853885672556374)
XLA Ops:
  0.6 3.0 %collective-permute-start = (bf16[1,128,2048]{2,1,0:T(8,128)(2,1)}, bf16[1,128,2048]{2,1,0:T(8,128)(2,1)S(1)}, u32[]{:S(2)}, u32[]{:S(2)}) collective-permute-start(bf16[1,128,2048]{2,1,0:T(8,128)(2,1)} %param.5), channel_id=1, source_target_pairs={{0,16},{16,0},{1,17},{17,1},{2,18},{18,2},{3,19},{19,3},{4,20},{20... | collective-permute-start | bytes 1572872 | tf_op jit(solution)/shard_map/ppermute | solution.py:10
  3.7 2.2 %fusion.9 = bf16[320,1408]{1,0:T(8,128)(2,1)} fusion(s32[]{:T(128)S(6)} %axis_index.19, s32[1408]{0:T(1024)S(1)} %get-tuple-element.10, s32[1408]{0:T(1024)S(1)} %get-tuple-element.11, pred[1408]{0:T(1024)(128)(4,1)S(1)} %fusion.56, bf16[1,1,1,320,1408]{4,3,2,1,0:T(8,128)(2,1)} %param.8), kind=kLoop, calls=%fused_computation.11 | loop fusion | flops 1351680 | bytes 1814916 | tf_op jit(solution)/shard_map/jit(_where)/select_n | solution.py:35
  6.0 3.5 %collective-permute-start.1 = (bf16[320,1408]{1,0:T(8,128)(2,1)}, bf16[320,1408]{1,0:T(8,128)(2,1)S(1)}, u32[]{:S(2)}, u32[]{:S(2)}) collective-permute-start(bf16[320,1408]{1,0:T(8,128)(2,1)} %fusion.9), channel_id=1, source_target_pairs={{0,4},{12,8},{1,5},{13,9},{2,6},{14,10},{3,7},{15,11},{16,20},{28,... | collective-permute-start | bytes 2703368 | tf_op jit(solution)/shard_map/ppermute | solution.py:36
  11.9 3.9 %collective-permute-done = bf16[1,128,2048]{2,1,0:T(8,128)(2,1)S(1)} collective-permute-done((bf16[1,128,2048]{2,1,0:T(8,128)(2,1)}, bf16[1,128,2048]{2,1,0:T(8,128)(2,1)S(1)}, u32[]{:S(2)}, u32[]{:S(2)}) %collective-permute-start) | collective-permute-done | bytes 524320 | tf_op jit(solution)/shard_map/ppermute | solution.py:10
  16.4 1.7 %fusion.5 = bf16[320,2048]{1,0:T(8,128)(2,1)} fusion(f32[320,2048]{1,0:T(8,128)S(1)} %fusion.33, bf16[1,128,2048]{2,1,0:T(8,128)(2,1)S(1)} %collective-permute-done, f32[128]{0:T(128)S(1)} %get-tuple-element.8, s32[128]{0:T(128)S(1)} %get-tuple-element.2), kind=kOutput, calls=%fused_computation.5 | convolution fusion | flops 169910272 | bytes 4457472 | tf_op jit(solution)/shard_map/dot_general | solution.py:26
  18.1 3.7 %all-to-all-start = ((bf16[4,80,2048]{2,1,0:T(8,128)(2,1)}), bf16[4,80,2048]{2,1,0:T(8,128)(2,1)S(1)}, u32[]{:S(2)}, u32[]{:S(2)}) async-start(bf16[4,80,2048]{2,1,0:T(8,128)(2,1)} %bitcast.8), calls=%async_computation | async-start | bytes 2621440 | tf_op jit(solution)/shard_map/all_to_all | solution.py:92
  21.8 6.9 %collective-permute-done.1 = bf16[320,1408]{1,0:T(8,128)(2,1)S(1)} collective-permute-done((bf16[320,1408]{1,0:T(8,128)(2,1)}, bf16[320,1408]{1,0:T(8,128)(2,1)S(1)}, u32[]{:S(2)}, u32[]{:S(2)}) %collective-permute-start.1) | collective-permute-done | bytes 901152 | tf_op jit(solution)/shard_map/ppermute | solution.py:36
  29.6 1.6 %fusion.16 = bf16[640,704]{1,0:T(8,128)(2,1)S(1)} fusion(s32[]{:T(128)S(6)} %select_n.66, bf16[320,1408]{1,0:T(8,128)(2,1)S(1)} %bitcast.58, bf16[320,1408]{1,0:T(8,128)(2,1)} %copy-done.1), kind=kLoop, calls=%fused_computation.24 | loop fusion | flops 1802240 | bytes 2703364 | tf_op jit(solution)/shard_map/concatenate | solution.py:45
  31.3 7.7 %all-to-all-done = bf16[4,80,2048]{2,1,0:T(8,128)(2,1)S(1)} async-done(((bf16[4,80,2048]{2,1,0:T(8,128)(2,1)}), bf16[4,80,2048]{2,1,0:T(8,128)(2,1)S(1)}, u32[]{:S(2)}, u32[]{:S(2)}) %all-to-all-start) | async-done | bytes 1310752 | tf_op jit(solution)/shard_map/all_to_all | solution.py:92
  39.0 3.7 %collective-permute-start.2 = (bf16[320,512]{1,0:T(8,128)(2,1)S(1)}, bf16[320,512]{1,0:T(8,128)(2,1)S(1)}, u32[]{:S(2)}, u32[]{:S(2)}) collective-permute-start(bf16[320,512]{1,0:T(8,128)(2,1)S(1)} %get-tuple-element.4), channel_id=1, source_target_pairs={{0,4},{12,8},{1,5},{13,9},{2,6},{14,10},{3,7},{15,11},{16,20},{28,... | collective-permute-start | bytes 983048 | tf_op jit(solution)/shard_map/ppermute | solution.py:57
  42.8 1.3 %collective-permute-start.5 = (bf16[320,512]{1,0:T(8,128)(2,1)S(1)}, bf16[320,512]{1,0:T(8,128)(2,1)S(1)}, u32[]{:S(2)}, u32[]{:S(2)}) collective-permute-start(bf16[320,512]{1,0:T(8,128)(2,1)S(1)} %get-tuple-element.7), channel_id=1, source_target_pairs={{0,4},{12,8},{1,5},{13,9},{2,6},{14,10},{3,7},{15,11},{16,20},{28,... | collective-permute-start | bytes 983048 | tf_op jit(solution)/shard_map/ppermute | solution.py:57
  46.8 5.8 %fusion.6 = bf16[1,1,1,320,1408]{4,3,2,1,0:T(8,128)(2,1)} fusion(bf16[320,2048]{1,0:T(8,128)(2,1)S(1)} %bitcast.53, bf16[1,1,1408,2048]{3,2,1,0:T(8,128)(2,1)} %param.9), kind=kOutput, calls=%fused_computation.6 | convolution fusion | flops 1845944320 | bytes 7979008 | tf_op jit(solution)/shard_map/sd,hd->sh/dot_general | solution.py:105
  54.4 3.5 %collective-permute-done.5 = bf16[320,512]{1,0:T(8,128)(2,1)S(1)} collective-permute-done((bf16[320,512]{1,0:T(8,128)(2,1)S(1)}, bf16[320,512]{1,0:T(8,128)(2,1)S(1)}, u32[]{:S(2)}, u32[]{:S(2)}) %collective-permute-start.5) | collective-permute-done | bytes 327712 | tf_op jit(solution)/shard_map/ppermute | solution.py:57
  59.7 5.2 %collective-permute-done.8 = bf16[320,512]{1,0:T(8,128)(2,1)S(1)} collective-permute-done((bf16[320,512]{1,0:T(8,128)(2,1)S(1)}, bf16[320,512]{1,0:T(8,128)(2,1)S(1)}, u32[]{:S(2)}, u32[]{:S(2)}) %collective-permute-start.8) | collective-permute-done | bytes 327712 | tf_op jit(solution)/shard_map/ppermute | solution.py:57
  66.8 3.7 %collective-permute-done.11 = bf16[320,512]{1,0:T(8,128)(2,1)S(1)} collective-permute-done((bf16[320,512]{1,0:T(8,128)(2,1)S(1)}, bf16[320,512]{1,0:T(8,128)(2,1)S(1)}, u32[]{:S(2)}, u32[]{:S(2)}) %collective-permute-start.11) | collective-permute-done | bytes 327712 | tf_op jit(solution)/shard_map/ppermute | solution.py:57
  72.6 1.3 %fusion.17 = f32[1408,512]{1,0:T(8,128)S(1)} fusion(bf16[320,512]{1,0:T(8,128)(2,1)S(1)} %collective-permute-done.2, bf16[320,512]{1,0:T(8,128)(2,1)S(1)} %get-tuple-element.4, bf16[320,1408]{1,0:T(8,128)(2,1)S(1)} %copy-done.2, bf16[320,1408]{1,0:T(8,128)(2,1)S(1)} %bitcast.59), kind=kOutput, calls=%fused_computation.33 | convolution fusion | flops 927662080 | bytes 5341184 | tf_op jit(solution)/shard_map/dot_general | solution.py:59
  73.9 1.3 %fusion.21 = f32[1408,512]{1,0:T(8,128)S(1)} fusion(bf16[320,512]{1,0:T(8,128)(2,1)S(1)} %collective-permute-done.5, bf16[320,512]{1,0:T(8,128)(2,1)S(1)} %get-tuple-element.7, bf16[320,1408]{1,0:T(8,128)(2,1)S(1)} %copy-done.2, bf16[320,1408]{1,0:T(8,128)(2,1)S(1)} %bitcast.60), kind=kOutput, calls=%fused_computation.37 | convolution fusion | flops 927662080 | bytes 5341184 | tf_op jit(solution)/shard_map/dot_general | solution.py:59
  75.2 1.3 %fusion.25 = f32[1408,512]{1,0:T(8,128)S(1)} fusion(bf16[320,512]{1,0:T(8,128)(2,1)S(1)} %collective-permute-done.8, bf16[320,512]{1,0:T(8,128)(2,1)S(1)} %get-tuple-element.6, bf16[320,1408]{1,0:T(8,128)(2,1)S(1)} %copy-done.2, bf16[320,1408]{1,0:T(8,128)(2,1)S(1)} %bitcast.61), kind=kOutput, calls=%fused_computation.41 | convolution fusion | flops 927662080 | bytes 5341184 | tf_op jit(solution)/shard_map/dot_general | solution.py:59
  76.6 1.3 %fusion.29 = f32[1408,512]{1,0:T(8,128)S(1)} fusion(bf16[320,512]{1,0:T(8,128)(2,1)S(1)} %collective-permute-done.11, bf16[320,512]{1,0:T(8,128)(2,1)S(1)} %get-tuple-element.5, bf16[320,1408]{1,0:T(8,128)(2,1)S(1)} %copy-done.2, bf16[320,1408]{1,0:T(8,128)(2,1)S(1)} %bitcast.62), kind=kOutput, calls=%fused_computation.45 | convolution fusion | flops 927662080 | bytes 5341184 | tf_op jit(solution)/shard_map/dot_general | solution.py:59
  83.6 10.2 %collective-permute-done.4 = bf16[352,512]{1,0:T(8,128)(2,1)S(1)} collective-permute-done((bf16[352,512]{1,0:T(8,128)(2,1)S(1)}, bf16[352,512]{1,0:T(8,128)(2,1)S(1)}, u32[]{:S(2)}, u32[]{:S(2)}) %collective-permute-start.4) | collective-permute-done | bytes 360480 | tf_op jit(solution)/shard_map/ppermute | solution.py:71
  94.0 5.3 %collective-permute-done.7 = bf16[352,512]{1,0:T(8,128)(2,1)S(1)} collective-permute-done((bf16[352,512]{1,0:T(8,128)(2,1)S(1)}, bf16[352,512]{1,0:T(8,128)(2,1)S(1)}, u32[]{:S(2)}, u32[]{:S(2)}) %collective-permute-start.7) | collective-permute-done | bytes 360480 | tf_op jit(solution)/shard_map/ppermute | solution.py:71
  99.4 13.7 %collective-permute-done.10 = bf16[352,512]{1,0:T(8,128)(2,1)S(1)} collective-permute-done((bf16[352,512]{1,0:T(8,128)(2,1)S(1)}, bf16[352,512]{1,0:T(8,128)(2,1)S(1)}, u32[]{:S(2)}, u32[]{:S(2)}) %collective-permute-start.10) | collective-permute-done | bytes 360480 | tf_op jit(solution)/shard_map/ppermute | solution.py:71
  113.2 12.8 %collective-permute-done.13 = bf16[352,512]{1,0:T(8,128)(2,1)S(1)} collective-permute-done((bf16[352,512]{1,0:T(8,128)(2,1)S(1)}, bf16[352,512]{1,0:T(8,128)(2,1)S(1)}, u32[]{:S(2)}, u32[]{:S(2)}) %collective-permute-start.13) | collective-permute-done | bytes 360480 | tf_op jit(solution)/shard_map/ppermute | solution.py:71
  126.1 1.8 %maximum_bitcast_fusion = f32[1,1,352,2048]{3,2,1,0:T(8,128)} fusion(f32[352,512]{1,0:T(8,128)S(1)} %convert_add_fusion, f32[352,512]{1,0:T(8,128)S(1)} %convert_add_fusion.1, f32[352,512]{1,0:T(8,128)S(1)} %convert_add_fusion.2, f32[352,512]{1,0:T(8,128)S(1)} %convert_add_fusion.3), kind=kLoop, calls=%fused_computation.2 | loop fusion | flops 2162688 | bytes 5767168 | tf_op jit(solution)/shard_map/reshape | solution.py:109
  (61 shorter events, 20.4 us)
Async XLA Ops:
  0.6 8.9 %copy-start.3 = (s32[1,128,2]{1,2,0:T(2,128)S(1)}, s32[1,128,2]{1,2,0:T(2,128)}, u32[]{:S(2)}) copy-start(s32[1,128,2]{1,2,0:T(2,128)} %param.6) | copy-start | bytes 3076
  0.6 11.3 %copy-start.4 = (f32[1,128,2]{1,2,0:T(2,128)S(1)}, f32[1,128,2]{1,2,0:T(2,128)}, u32[]{:S(2)}) copy-start(f32[1,128,2]{1,2,0:T(2,128)} %param.7) | copy-start | bytes 3076
  0.6 15.2 %collective-permute-start = (bf16[1,128,2048]{2,1,0:T(8,128)(2,1)}, bf16[1,128,2048]{2,1,0:T(8,128)(2,1)S(1)}, u32[]{:S(2)}, u32[]{:S(2)}) collective-permute-start(bf16[1,128,2048]{2,1,0:T(8,128)(2,1)} %param.5), channel_id=1, source_target_pairs={{0,16},{16,0},{1,17},{17,1},{2,18},{18,2},{3,19},{19,3},{4,20},{20... | collective-permute-start | bytes 1572872 | tf_op jit(solution)/shard_map/ppermute | solution.py:10
  6.0 22.8 %collective-permute-start.1 = (bf16[320,1408]{1,0:T(8,128)(2,1)}, bf16[320,1408]{1,0:T(8,128)(2,1)S(1)}, u32[]{:S(2)}, u32[]{:S(2)}) collective-permute-start(bf16[320,1408]{1,0:T(8,128)(2,1)} %fusion.9), channel_id=1, source_target_pairs={{0,4},{12,8},{1,5},{13,9},{2,6},{14,10},{3,7},{15,11},{16,20},{28,... | collective-permute-start | bytes 2703368 | tf_op jit(solution)/shard_map/ppermute | solution.py:36
  18.1 11.6 %copy-start = (bf16[1,1,1,320,1408]{4,3,2,1,0:T(8,128)(2,1)S(1)}, bf16[1,1,1,320,1408]{4,3,2,1,0:T(8,128)(2,1)}, u32[]{:S(2)}) copy-start(bf16[1,1,1,320,1408]{4,3,2,1,0:T(8,128)(2,1)} %param.8) | copy-start | bytes 2703364
  18.1 20.9 %all-to-all-start = ((bf16[4,80,2048]{2,1,0:T(8,128)(2,1)}), bf16[4,80,2048]{2,1,0:T(8,128)(2,1)S(1)}, u32[]{:S(2)}, u32[]{:S(2)}) async-start(bf16[4,80,2048]{2,1,0:T(8,128)(2,1)} %bitcast.8), calls=%async_computation | async-start | bytes 2621440 | tf_op jit(solution)/shard_map/all_to_all | solution.py:92
  28.7 0.9 copy-start.1
  39.0 13.5 %collective-permute-start.2 = (bf16[320,512]{1,0:T(8,128)(2,1)S(1)}, bf16[320,512]{1,0:T(8,128)(2,1)S(1)}, u32[]{:S(2)}, u32[]{:S(2)}) collective-permute-start(bf16[320,512]{1,0:T(8,128)(2,1)S(1)} %get-tuple-element.4), channel_id=1, source_target_pairs={{0,4},{12,8},{1,5},{13,9},{2,6},{14,10},{3,7},{15,11},{16,20},{28,... | collective-permute-start | bytes 983048 | tf_op jit(solution)/shard_map/ppermute | solution.py:57
  42.8 15.1 %collective-permute-start.5 = (bf16[320,512]{1,0:T(8,128)(2,1)S(1)}, bf16[320,512]{1,0:T(8,128)(2,1)S(1)}, u32[]{:S(2)}, u32[]{:S(2)}) collective-permute-start(bf16[320,512]{1,0:T(8,128)(2,1)S(1)} %get-tuple-element.7), channel_id=1, source_target_pairs={{0,4},{12,8},{1,5},{13,9},{2,6},{14,10},{3,7},{15,11},{16,20},{28,... | collective-permute-start | bytes 983048 | tf_op jit(solution)/shard_map/ppermute | solution.py:57
  44.1 20.8 %collective-permute-start.8 = (bf16[320,512]{1,0:T(8,128)(2,1)S(1)}, bf16[320,512]{1,0:T(8,128)(2,1)S(1)}, u32[]{:S(2)}, u32[]{:S(2)}) collective-permute-start(bf16[320,512]{1,0:T(8,128)(2,1)S(1)} %get-tuple-element.6), channel_id=1, source_target_pairs={{0,4},{12,8},{1,5},{13,9},{2,6},{14,10},{3,7},{15,11},{16,20},{28,... | collective-permute-start | bytes 983048 | tf_op jit(solution)/shard_map/ppermute | solution.py:57
  45.4 25.1 %collective-permute-start.11 = (bf16[320,512]{1,0:T(8,128)(2,1)S(1)}, bf16[320,512]{1,0:T(8,128)(2,1)S(1)}, u32[]{:S(2)}, u32[]{:S(2)}) collective-permute-start(bf16[320,512]{1,0:T(8,128)(2,1)S(1)} %get-tuple-element.5), channel_id=1, source_target_pairs={{0,4},{12,8},{1,5},{13,9},{2,6},{14,10},{3,7},{15,11},{16,20},{28,... | collective-permute-start | bytes 983048 | tf_op jit(solution)/shard_map/ppermute | solution.py:57
  53.7 24.2 %collective-permute-start.3 = (bf16[704,512]{1,0:T(8,128)(2,1)S(1)}, bf16[704,512]{1,0:T(8,128)(2,1)S(1)}, u32[]{:S(2)}, u32[]{:S(2)}) collective-permute-start(bf16[704,512]{1,0:T(8,128)(2,1)S(1)} %fusion.10), channel_id=1, source_target_pairs={{4,8},{8,4},{5,9},{9,5},{6,10},{10,6},{7,11},{11,7},{20,24},{24,20... | collective-permute-start | bytes 2162696 | tf_op jit(solution)/shard_map/ppermute | solution.py:66
  59.0 20.3 %collective-permute-start.6 = (bf16[704,512]{1,0:T(8,128)(2,1)S(1)}, bf16[704,512]{1,0:T(8,128)(2,1)S(1)}, u32[]{:S(2)}, u32[]{:S(2)}) collective-permute-start(bf16[704,512]{1,0:T(8,128)(2,1)S(1)} %fusion.11), channel_id=1, source_target_pairs={{4,8},{8,4},{5,9},{9,5},{6,10},{10,6},{7,11},{11,7},{20,24},{24,20... | collective-permute-start | bytes 2162696 | tf_op jit(solution)/shard_map/ppermute | solution.py:66
  66.0 14.7 %collective-permute-start.9 = (bf16[704,512]{1,0:T(8,128)(2,1)S(1)}, bf16[704,512]{1,0:T(8,128)(2,1)S(1)}, u32[]{:S(2)}, u32[]{:S(2)}) collective-permute-start(bf16[704,512]{1,0:T(8,128)(2,1)S(1)} %fusion.12), channel_id=1, source_target_pairs={{4,8},{8,4},{5,9},{9,5},{6,10},{10,6},{7,11},{11,7},{20,24},{24,20... | collective-permute-start | bytes 2162696 | tf_op jit(solution)/shard_map/ppermute | solution.py:66
  71.1 1.5 %copy-start.2 = (bf16[320,1408]{1,0:T(8,128)(2,1)S(1)}, bf16[320,1408]{1,0:T(8,128)(2,1)}, u32[]{:S(2)}) copy-start(bf16[320,1408]{1,0:T(8,128)(2,1)} %copy-done.1) | copy-start | bytes 2703364
  71.6 10.6 %collective-permute-start.12 = (bf16[704,512]{1,0:T(8,128)(2,1)S(1)}, bf16[704,512]{1,0:T(8,128)(2,1)S(1)}, u32[]{:S(2)}, u32[]{:S(2)}) collective-permute-start(bf16[704,512]{1,0:T(8,128)(2,1)S(1)} %fusion.13), channel_id=1, source_target_pairs={{4,8},{8,4},{5,9},{9,5},{6,10},{10,6},{7,11},{11,7},{20,24},{24,20... | collective-permute-start | bytes 2162696 | tf_op jit(solution)/shard_map/ppermute | solution.py:66
  78.0 15.8 %collective-permute-start.4 = (bf16[352,512]{1,0:T(8,128)(2,1)S(1)}, bf16[352,512]{1,0:T(8,128)(2,1)S(1)}, u32[]{:S(2)}, u32[]{:S(2)}) collective-permute-start(bf16[352,512]{1,0:T(8,128)(2,1)S(1)} %add_convert_fusion.3), channel_id=1, source_target_pairs={{4,0},{8,12},{5,1},{9,13},{6,2},{10,14},{7,3},{11,15},{20,16},{24,... | collective-permute-start | bytes 1081352 | tf_op jit(solution)/shard_map/ppermute | solution.py:71
  79.5 19.8 %collective-permute-start.7 = (bf16[352,512]{1,0:T(8,128)(2,1)S(1)}, bf16[352,512]{1,0:T(8,128)(2,1)S(1)}, u32[]{:S(2)}, u32[]{:S(2)}) collective-permute-start(bf16[352,512]{1,0:T(8,128)(2,1)S(1)} %add_convert_fusion.2), channel_id=1, source_target_pairs={{4,0},{8,12},{5,1},{9,13},{6,2},{10,14},{7,3},{11,15},{20,16},{24,... | collective-permute-start | bytes 1081352 | tf_op jit(solution)/shard_map/ppermute | solution.py:71
  80.9 32.2 %collective-permute-start.10 = (bf16[352,512]{1,0:T(8,128)(2,1)S(1)}, bf16[352,512]{1,0:T(8,128)(2,1)S(1)}, u32[]{:S(2)}, u32[]{:S(2)}) collective-permute-start(bf16[352,512]{1,0:T(8,128)(2,1)S(1)} %add_convert_fusion.1), channel_id=1, source_target_pairs={{4,0},{8,12},{5,1},{9,13},{6,2},{10,14},{7,3},{11,15},{20,16},{24,... | collective-permute-start | bytes 1081352 | tf_op jit(solution)/shard_map/ppermute | solution.py:71
  82.3 43.6 %collective-permute-start.13 = (bf16[352,512]{1,0:T(8,128)(2,1)S(1)}, bf16[352,512]{1,0:T(8,128)(2,1)S(1)}, u32[]{:S(2)}, u32[]{:S(2)}) collective-permute-start(bf16[352,512]{1,0:T(8,128)(2,1)S(1)} %add_convert_fusion), channel_id=1, source_target_pairs={{4,0},{8,12},{5,1},{9,13},{6,2},{10,14},{7,3},{11,15},{20,16},{24,... | collective-permute-start | bytes 1081352 | tf_op jit(solution)/shard_map/ppermute | solution.py:71

commit v19 on v17

--- a/solution.py
+++ b/solution.py
@@ -45,9 +45,11 @@
     lhs = jnp.concatenate([saved, hfull], axis=0)
     row2 = jnp.where(d == 1, 2 * blk, 0)
     lhs2 = lax.dynamic_slice_in_dim(lhs, row2, 2 * blk, axis=1)
-    row3a = jnp.where(d == 1, 0, 3 * blk)
+    base = jnp.where(d <= 1, 0, 2 * blk)
+    lhs_rest = lax.dynamic_slice_in_dim(lhs, base, 2 * blk, axis=1)
+    row3a = jnp.where(d == 1, 0, 3 * blk) - base
     row3b = jnp.where(d == 1, 0, blk)
-    own = d * blk
+    own = d * blk - base
     half = jnp.where(d == 1, blk, 0)
     edge = (d == 0) | (d == 3)
     pieces = []
@@ -56,7 +58,7 @@
         srecv = lax.ppermute(sc, "dp", ends)
         rhs = jnp.concatenate([sc, srecv], axis=0)
         acc = lax.dot_general(
-            lhs, rhs, (((0,), (0,)), ((), ())), preferred_element_type=jnp.float32
+            lhs_rest, rhs, (((0,), (0,)), ((), ())), preferred_element_type=jnp.float32
         )
         s2 = lax.dot_general(
             lhs2, rhs, (((0,), (0,)), ((), ())), preferred_element_type=jnp.float32

time: 128 us -> 128 us (level)
  matrix products: 16.3 us -> 14 us
  other arithmetic: 8.15 us -> 9.93 us
    ppermute x4, waiting for transfers between devices: 41.9 us -> 44.7 us  [line_weight_grad(): r3 = lax.ppermute(s3, 'dp', [(1, 0), (2, 3)])]
    dot_general x4, matrix products: 5.32 us -> 3.02 us  [line_weight_grad(): lax.dot_general(lhs_rest, rhs, (((0,), (0,)), ((), ())), preferred_elemen...]
    concatenate x1, other arithmetic: 1.63 us -> 3.42 us  [line_weight_grad(): lhs = jnp.concatenate([saved, hfull], axis=0)]
    all_to_all x1, waiting for transfers between devices: 7.67 us -> 5.89 us  [shards(): lax.all_to_all(outgoing, 'expert', split_axis=0, concat_axis=0, tiled=True)]
where the time goes in v19:
time: 128 us
  waiting for transfers between devices  74.8 us (58%)
  starting transfers between devices  26 us (20%)
  matrix products  14 us (11%)
  other arithmetic  9.93 us (8%)
  local copies, waits for them, and re-layouts  2.01 us (2%)
    ppermute x4, waiting for transfers between devices, line_weight_grad(): r3 = lax.ppermute(s3, 'dp', [(1, 0), (2, 3)])  44.7 us
    ppermute x4, waiting for transfers between devices, line_weight_grad(): srecv = lax.ppermute(sc, 'dp', ends)  13.4 us
    ppermute x4, starting transfers between devices, line_weight_grad(): srecv = lax.ppermute(sc, 'dp', ends)  7.8 us
    ppermute x1, waiting for transfers between devices, send_hidden(): return lax.ppermute(hsend, 'dp', [(0, 1), (3, 2)])  6.94 us
    all_to_all x1, waiting for transfers between devices, shards(): lax.all_to_all(outgoing, 'expert', split_axis=0, concat_axis=0, tiled=True)  5.89 us
    dot_general x1, matrix products, shards(): jnp.einsum('sd,hd->sh', late, weight, preferred_element_type=jnp.float32)  5.78 us
    ppermute x4, starting transfers between devices, line_weight_grad(): r3 = lax.ppermute(s3, 'dp', [(1, 0), (2, 3)])  5.17 us
    ppermute x1, waiting for transfers between devices, shifted(): return lax.ppermute(value, axis, pairs)  3.9 us
  transfers between devices with their start and end apart: 15, of which 10 were waited for; matrix products, arithmetic and copies ran while one was open for 18% of the time, Pallas kernels for 0%

profile of v19, /device:TPU:0, one launch (start us, length us, event | category | flops | bytes accessed | tf_op | source)
XLA Modules:
  0.0 127.9 jit_solution(9847615657246057304)
XLA Ops:
  0.6 3.0 %collective-permute-start = (bf16[1,128,2048]{2,1,0:T(8,128)(2,1)}, bf16[1,128,2048]{2,1,0:T(8,128)(2,1)S(1)}, u32[]{:S(2)}, u32[]{:S(2)}) collective-permute-start(bf16[1,128,2048]{2,1,0:T(8,128)(2,1)} %param.5), channel_id=1, source_target_pairs={{0,16},{16,0},{1,17},{17,1},{2,18},{18,2},{3,19},{19,3},{4,20},{20... | collective-permute-start | bytes 1572872 | tf_op jit(solution)/shard_map/ppermute | solution.py:10
  3.7 2.2 %fusion.9 = bf16[320,1408]{1,0:T(8,128)(2,1)} fusion(s32[]{:T(128)S(6)} %axis_index.19, s32[1408]{0:T(1024)S(1)} %get-tuple-element.12, s32[1408]{0:T(1024)S(1)} %get-tuple-element.13, pred[1408]{0:T(1024)(128)(4,1)S(1)} %fusion.29, bf16[1,1,1,320,1408]{4,3,2,1,0:T(8,128)(2,1)} %param.8), kind=kLoop, calls=%fused_computation.12 | loop fusion | flops 1351680 | bytes 1814916 | tf_op jit(solution)/shard_map/jit(_where)/select_n | solution.py:35
  6.0 3.5 %collective-permute-start.1 = (bf16[320,1408]{1,0:T(8,128)(2,1)}, bf16[320,1408]{1,0:T(8,128)(2,1)S(1)}, u32[]{:S(2)}, u32[]{:S(2)}) collective-permute-start(bf16[320,1408]{1,0:T(8,128)(2,1)} %fusion.9), channel_id=1, source_target_pairs={{0,4},{12,8},{1,5},{13,9},{2,6},{14,10},{3,7},{15,11},{16,20},{28,... | collective-permute-start | bytes 2703368 | tf_op jit(solution)/shard_map/ppermute | solution.py:36
  11.9 3.9 %collective-permute-done = bf16[1,128,2048]{2,1,0:T(8,128)(2,1)S(1)} collective-permute-done((bf16[1,128,2048]{2,1,0:T(8,128)(2,1)}, bf16[1,128,2048]{2,1,0:T(8,128)(2,1)S(1)}, u32[]{:S(2)}, u32[]{:S(2)}) %collective-permute-start) | collective-permute-done | bytes 524320 | tf_op jit(solution)/shard_map/ppermute | solution.py:10
  16.4 1.7 %fusion.5 = bf16[320,2048]{1,0:T(8,128)(2,1)} fusion(f32[320,2048]{1,0:T(8,128)S(1)} %fusion.14, bf16[1,128,2048]{2,1,0:T(8,128)(2,1)S(1)} %collective-permute-done, f32[128]{0:T(128)S(1)} %get-tuple-element.10, s32[128]{0:T(128)S(1)} %get-tuple-element.2), kind=kOutput, calls=%fused_computation.5 | convolution fusion | flops 169910272 | bytes 4457472 | tf_op jit(solution)/shard_map/dot_general | solution.py:26
  18.1 3.7 %all-to-all-start = ((bf16[4,80,2048]{2,1,0:T(8,128)(2,1)}), bf16[4,80,2048]{2,1,0:T(8,128)(2,1)S(1)}, u32[]{:S(2)}, u32[]{:S(2)}) async-start(bf16[4,80,2048]{2,1,0:T(8,128)(2,1)} %bitcast.8), calls=%async_computation | async-start | bytes 2621440 | tf_op jit(solution)/shard_map/all_to_all | solution.py:92
  21.8 6.9 %collective-permute-done.1 = bf16[320,1408]{1,0:T(8,128)(2,1)S(1)} collective-permute-done((bf16[320,1408]{1,0:T(8,128)(2,1)}, bf16[320,1408]{1,0:T(8,128)(2,1)S(1)}, u32[]{:S(2)}, u32[]{:S(2)}) %collective-permute-start.1) | collective-permute-done | bytes 901152 | tf_op jit(solution)/shard_map/ppermute | solution.py:36
  29.6 3.4 %fusion.12 = (bf16[640,704]{1,0:T(8,128)(2,1)}, bf16[640,704]{1,0:T(8,128)(2,1)S(1)}) fusion(s32[]{:T(128)S(6)} %select_n.74, bf16[320,1408]{1,0:T(8,128)(2,1)S(1)} %bitcast.58, bf16[320,1408]{1,0:T(8,128)(2,1)} %copy-done.2, s32[]{:T(128)S(6)} %select_n.69), kind=kLoop, calls=%fused_computation.21 | loop fusion | flops 3604480 | bytes 3604488 | tf_op jit(solution)/shard_map/concatenate | solution.py:45
  33.0 5.9 %all-to-all-done = bf16[4,80,2048]{2,1,0:T(8,128)(2,1)S(1)} async-done(((bf16[4,80,2048]{2,1,0:T(8,128)(2,1)}), bf16[4,80,2048]{2,1,0:T(8,128)(2,1)S(1)}, u32[]{:S(2)}, u32[]{:S(2)}) %all-to-all-start) | async-done | bytes 1310752 | tf_op jit(solution)/shard_map/all_to_all | solution.py:92
  39.0 3.7 %collective-permute-start.11 = (bf16[320,512]{1,0:T(8,128)(2,1)S(1)}, bf16[320,512]{1,0:T(8,128)(2,1)S(1)}, u32[]{:S(2)}, u32[]{:S(2)}) collective-permute-start(bf16[320,512]{1,0:T(8,128)(2,1)S(1)} %get-tuple-element.7), channel_id=1, source_target_pairs={{0,4},{12,8},{1,5},{13,9},{2,6},{14,10},{3,7},{15,11},{16,20},{28,... | collective-permute-start | bytes 983048 | tf_op jit(solution)/shard_map/ppermute | solution.py:58
  42.8 1.4 %collective-permute-start.8 = (bf16[320,512]{1,0:T(8,128)(2,1)S(1)}, bf16[320,512]{1,0:T(8,128)(2,1)S(1)}, u32[]{:S(2)}, u32[]{:S(2)}) collective-permute-start(bf16[320,512]{1,0:T(8,128)(2,1)S(1)} %get-tuple-element.8), channel_id=1, source_target_pairs={{0,4},{12,8},{1,5},{13,9},{2,6},{14,10},{3,7},{15,11},{16,20},{28,... | collective-permute-start | bytes 983048 | tf_op jit(solution)/shard_map/ppermute | solution.py:58
  44.3 5.8 %fusion.6 = bf16[1,1,1,320,1408]{4,3,2,1,0:T(8,128)(2,1)} fusion(bf16[320,2048]{1,0:T(8,128)(2,1)S(1)} %bitcast.57, bf16[1,1,1408,2048]{3,2,1,0:T(8,128)(2,1)} %param.9), kind=kOutput, calls=%fused_computation.6 | convolution fusion | flops 1845944320 | bytes 7979008 | tf_op jit(solution)/shard_map/sd,hd->sh/dot_general | solution.py:105
  50.0 1.3 %collective-permute-start.5 = (bf16[320,512]{1,0:T(8,128)(2,1)S(1)}, bf16[320,512]{1,0:T(8,128)(2,1)S(1)}, u32[]{:S(2)}, u32[]{:S(2)}) collective-permute-start(bf16[320,512]{1,0:T(8,128)(2,1)S(1)} %get-tuple-element.9), channel_id=1, source_target_pairs={{0,4},{12,8},{1,5},{13,9},{2,6},{14,10},{3,7},{15,11},{16,20},{28,... | collective-permute-start | bytes 983048 | tf_op jit(solution)/shard_map/ppermute | solution.py:58
  51.3 1.3 %collective-permute-start.2 = (bf16[320,512]{1,0:T(8,128)(2,1)S(1)}, bf16[320,512]{1,0:T(8,128)(2,1)S(1)}, u32[]{:S(2)}, u32[]{:S(2)}) collective-permute-start(bf16[320,512]{1,0:T(8,128)(2,1)S(1)} %get-tuple-element.6), channel_id=1, source_target_pairs={{0,4},{12,8},{1,5},{13,9},{2,6},{14,10},{3,7},{15,11},{16,20},{28,... | collective-permute-start | bytes 983048 | tf_op jit(solution)/shard_map/ppermute | solution.py:58
  54.2 3.7 %collective-permute-done.8 = bf16[320,512]{1,0:T(8,128)(2,1)S(1)} collective-permute-done((bf16[320,512]{1,0:T(8,128)(2,1)S(1)}, bf16[320,512]{1,0:T(8,128)(2,1)S(1)}, u32[]{:S(2)}, u32[]{:S(2)}) %collective-permute-start.8) | collective-permute-done | bytes 327712 | tf_op jit(solution)/shard_map/ppermute | solution.py:58
  59.4 5.6 %collective-permute-done.5 = bf16[320,512]{1,0:T(8,128)(2,1)S(1)} collective-permute-done((bf16[320,512]{1,0:T(8,128)(2,1)S(1)}, bf16[320,512]{1,0:T(8,128)(2,1)S(1)}, u32[]{:S(2)}, u32[]{:S(2)}) %collective-permute-start.5) | collective-permute-done | bytes 327712 | tf_op jit(solution)/shard_map/ppermute | solution.py:58
  66.4 4.1 %collective-permute-done.2 = bf16[320,512]{1,0:T(8,128)(2,1)S(1)} collective-permute-done((bf16[320,512]{1,0:T(8,128)(2,1)S(1)}, bf16[320,512]{1,0:T(8,128)(2,1)S(1)}, u32[]{:S(2)}, u32[]{:S(2)}) %collective-permute-start.2) | collective-permute-done | bytes 327712 | tf_op jit(solution)/shard_map/ppermute | solution.py:58
  75.1 1.3 %collective-permute-start.13 = (bf16[352,512]{1,0:T(8,128)(2,1)S(1)}, bf16[352,512]{1,0:T(8,128)(2,1)S(1)}, u32[]{:S(2)}, u32[]{:S(2)}) collective-permute-start(bf16[352,512]{1,0:T(8,128)(2,1)S(1)} %add_convert_fusion), channel_id=1, source_target_pairs={{4,0},{8,12},{5,1},{9,13},{6,2},{10,14},{7,3},{11,15},{20,16},{24,... | collective-permute-start | bytes 1081352 | tf_op jit(solution)/shard_map/ppermute | solution.py:71
  76.6 1.3 %collective-permute-start.10 = (bf16[352,512]{1,0:T(8,128)(2,1)S(1)}, bf16[352,512]{1,0:T(8,128)(2,1)S(1)}, u32[]{:S(2)}, u32[]{:S(2)}) collective-permute-start(bf16[352,512]{1,0:T(8,128)(2,1)S(1)} %add_convert_fusion.1), channel_id=1, source_target_pairs={{4,0},{8,12},{5,1},{9,13},{6,2},{10,14},{7,3},{11,15},{20,16},{24,... | collective-permute-start | bytes 1081352 | tf_op jit(solution)/shard_map/ppermute | solution.py:71
  80.7 9.3 %collective-permute-done.13 = bf16[352,512]{1,0:T(8,128)(2,1)S(1)} collective-permute-done((bf16[352,512]{1,0:T(8,128)(2,1)S(1)}, bf16[352,512]{1,0:T(8,128)(2,1)S(1)}, u32[]{:S(2)}, u32[]{:S(2)}) %collective-permute-start.13) | collective-permute-done | bytes 360480 | tf_op jit(solution)/shard_map/ppermute | solution.py:71
  90.2 7.0 %collective-permute-done.10 = bf16[352,512]{1,0:T(8,128)(2,1)S(1)} collective-permute-done((bf16[352,512]{1,0:T(8,128)(2,1)S(1)}, bf16[352,512]{1,0:T(8,128)(2,1)S(1)}, u32[]{:S(2)}, u32[]{:S(2)}) %collective-permute-start.10) | collective-permute-done | bytes 360480 | tf_op jit(solution)/shard_map/ppermute | solution.py:71
  97.4 15.3 %collective-permute-done.7 = bf16[352,512]{1,0:T(8,128)(2,1)S(1)} collective-permute-done((bf16[352,512]{1,0:T(8,128)(2,1)S(1)}, bf16[352,512]{1,0:T(8,128)(2,1)S(1)}, u32[]{:S(2)}, u32[]{:S(2)}) %collective-permute-start.7) | collective-permute-done | bytes 360480 | tf_op jit(solution)/shard_map/ppermute | solution.py:71
  112.8 13.1 %collective-permute-done.4 = bf16[352,512]{1,0:T(8,128)(2,1)S(1)} collective-permute-done((bf16[352,512]{1,0:T(8,128)(2,1)S(1)}, bf16[352,512]{1,0:T(8,128)(2,1)S(1)}, u32[]{:S(2)}, u32[]{:S(2)}) %collective-permute-start.4) | collective-permute-done | bytes 360480 | tf_op jit(solution)/shard_map/ppermute | solution.py:71
  126.0 1.8 %maximum_bitcast_fusion = f32[1,1,352,2048]{3,2,1,0:T(8,128)} fusion(f32[352,512]{1,0:T(8,128)S(1)} %convert_add_fusion, f32[352,512]{1,0:T(8,128)S(1)} %convert_add_fusion.1, f32[352,512]{1,0:T(8,128)S(1)} %convert_add_fusion.2, f32[352,512]{1,0:T(8,128)S(1)} %convert_add_fusion.3), kind=kLoop, calls=%fused_computation.2 | loop fusion | flops 2162688 | bytes 5767168 | tf_op jit(solution)/shard_map/reshape | solution.py:109
  (57 shorter events, 16.5 us)
Async XLA Ops:
  0.6 8.9 %copy-start.3 = (s32[1,128,2]{1,2,0:T(2,128)S(1)}, s32[1,128,2]{1,2,0:T(2,128)}, u32[]{:S(2)}) copy-start(s32[1,128,2]{1,2,0:T(2,128)} %param.6) | copy-start | bytes 3076
  0.6 11.3 %copy-start.4 = (f32[1,128,2]{1,2,0:T(2,128)S(1)}, f32[1,128,2]{1,2,0:T(2,128)}, u32[]{:S(2)}) copy-start(f32[1,128,2]{1,2,0:T(2,128)} %param.7) | copy-start | bytes 3076
  0.6 15.2 %collective-permute-start = (bf16[1,128,2048]{2,1,0:T(8,128)(2,1)}, bf16[1,128,2048]{2,1,0:T(8,128)(2,1)S(1)}, u32[]{:S(2)}, u32[]{:S(2)}) collective-permute-start(bf16[1,128,2048]{2,1,0:T(8,128)(2,1)} %param.5), channel_id=1, source_target_pairs={{0,16},{16,0},{1,17},{17,1},{2,18},{18,2},{3,19},{19,3},{4,20},{20... | collective-permute-start | bytes 1572872 | tf_op jit(solution)/shard_map/ppermute | solution.py:10
  6.0 22.8 %collective-permute-start.1 = (bf16[320,1408]{1,0:T(8,128)(2,1)}, bf16[320,1408]{1,0:T(8,128)(2,1)S(1)}, u32[]{:S(2)}, u32[]{:S(2)}) collective-permute-start(bf16[320,1408]{1,0:T(8,128)(2,1)} %fusion.9), channel_id=1, source_target_pairs={{0,4},{12,8},{1,5},{13,9},{2,6},{14,10},{3,7},{15,11},{16,20},{28,... | collective-permute-start | bytes 2703368 | tf_op jit(solution)/shard_map/ppermute | solution.py:36
  18.1 11.6 %copy-start = (bf16[1,1,1,320,1408]{4,3,2,1,0:T(8,128)(2,1)S(1)}, bf16[1,1,1,320,1408]{4,3,2,1,0:T(8,128)(2,1)}, u32[]{:S(2)}) copy-start(bf16[1,1,1,320,1408]{4,3,2,1,0:T(8,128)(2,1)} %param.8) | copy-start | bytes 2703364
  18.1 20.9 %all-to-all-start = ((bf16[4,80,2048]{2,1,0:T(8,128)(2,1)}), bf16[4,80,2048]{2,1,0:T(8,128)(2,1)S(1)}, u32[]{:S(2)}, u32[]{:S(2)}) async-start(bf16[4,80,2048]{2,1,0:T(8,128)(2,1)} %bitcast.8), calls=%async_computation | async-start | bytes 2621440 | tf_op jit(solution)/shard_map/all_to_all | solution.py:92
  28.7 0.9 copy-start.2
  39.0 13.6 %collective-permute-start.11 = (bf16[320,512]{1,0:T(8,128)(2,1)S(1)}, bf16[320,512]{1,0:T(8,128)(2,1)S(1)}, u32[]{:S(2)}, u32[]{:S(2)}) collective-permute-start(bf16[320,512]{1,0:T(8,128)(2,1)S(1)} %get-tuple-element.7), channel_id=1, source_target_pairs={{0,4},{12,8},{1,5},{13,9},{2,6},{14,10},{3,7},{15,11},{16,20},{28,... | collective-permute-start | bytes 983048 | tf_op jit(solution)/shard_map/ppermute | solution.py:58
  42.8 9.9 %copy-start.1 = (bf16[640,704]{1,0:T(8,128)(2,1)S(1)}, bf16[640,704]{1,0:T(8,128)(2,1)}, u32[]{:S(2)}) copy-start(bf16[640,704]{1,0:T(8,128)(2,1)} %get-tuple-element.4) | copy-start | bytes 2703364
  42.8 15.1 %collective-permute-start.8 = (bf16[320,512]{1,0:T(8,128)(2,1)S(1)}, bf16[320,512]{1,0:T(8,128)(2,1)S(1)}, u32[]{:S(2)}, u32[]{:S(2)}) collective-permute-start(bf16[320,512]{1,0:T(8,128)(2,1)S(1)} %get-tuple-element.8), channel_id=1, source_target_pairs={{0,4},{12,8},{1,5},{13,9},{2,6},{14,10},{3,7},{15,11},{16,20},{28,... | collective-permute-start | bytes 983048 | tf_op jit(solution)/shard_map/ppermute | solution.py:58
  50.0 14.9 %collective-permute-start.5 = (bf16[320,512]{1,0:T(8,128)(2,1)S(1)}, bf16[320,512]{1,0:T(8,128)(2,1)S(1)}, u32[]{:S(2)}, u32[]{:S(2)}) collective-permute-start(bf16[320,512]{1,0:T(8,128)(2,1)S(1)} %get-tuple-element.9), channel_id=1, source_target_pairs={{0,4},{12,8},{1,5},{13,9},{2,6},{14,10},{3,7},{15,11},{16,20},{28,... | collective-permute-start | bytes 983048 | tf_op jit(solution)/shard_map/ppermute | solution.py:58
  51.3 19.2 %collective-permute-start.2 = (bf16[320,512]{1,0:T(8,128)(2,1)S(1)}, bf16[320,512]{1,0:T(8,128)(2,1)S(1)}, u32[]{:S(2)}, u32[]{:S(2)}) collective-permute-start(bf16[320,512]{1,0:T(8,128)(2,1)S(1)} %get-tuple-element.6), channel_id=1, source_target_pairs={{0,4},{12,8},{1,5},{13,9},{2,6},{14,10},{3,7},{15,11},{16,20},{28,... | collective-permute-start | bytes 983048 | tf_op jit(solution)/shard_map/ppermute | solution.py:58
  53.4 21.6 %collective-permute-start.12 = (bf16[704,512]{1,0:T(8,128)(2,1)S(1)}, bf16[704,512]{1,0:T(8,128)(2,1)S(1)}, u32[]{:S(2)}, u32[]{:S(2)}) collective-permute-start(bf16[704,512]{1,0:T(8,128)(2,1)S(1)} %convolution_convert_fusion), channel_id=1, source_target_pairs={{4,8},{8,4},{5,9},{9,5},{6,10},{10,6},{7,11},{11,7},{20,24},{24,20... | collective-permute-start | bytes 2162696 | tf_op jit(solution)/shard_map/ppermute | solution.py:66
  58.6 17.8 %collective-permute-start.9 = (bf16[704,512]{1,0:T(8,128)(2,1)S(1)}, bf16[704,512]{1,0:T(8,128)(2,1)S(1)}, u32[]{:S(2)}, u32[]{:S(2)}) collective-permute-start(bf16[704,512]{1,0:T(8,128)(2,1)S(1)} %convolution_convert_fusion.1), channel_id=1, source_target_pairs={{4,8},{8,4},{5,9},{9,5},{6,10},{10,6},{7,11},{11,7},{20,24},{24,20... | collective-permute-start | bytes 2162696 | tf_op jit(solution)/shard_map/ppermute | solution.py:66
  65.7 12.2 %collective-permute-start.6 = (bf16[704,512]{1,0:T(8,128)(2,1)S(1)}, bf16[704,512]{1,0:T(8,128)(2,1)S(1)}, u32[]{:S(2)}, u32[]{:S(2)}) collective-permute-start(bf16[704,512]{1,0:T(8,128)(2,1)S(1)} %convolution_convert_fusion.2), channel_id=1, source_target_pairs={{4,8},{8,4},{5,9},{9,5},{6,10},{10,6},{7,11},{11,7},{20,24},{24,20... | collective-permute-start | bytes 2162696 | tf_op jit(solution)/shard_map/ppermute | solution.py:66
  71.3 8.0 %collective-permute-start.3 = (bf16[704,512]{1,0:T(8,128)(2,1)S(1)}, bf16[704,512]{1,0:T(8,128)(2,1)S(1)}, u32[]{:S(2)}, u32[]{:S(2)}) collective-permute-start(bf16[704,512]{1,0:T(8,128)(2,1)S(1)} %convolution_convert_fusion.3), channel_id=1, source_target_pairs={{4,8},{8,4},{5,9},{9,5},{6,10},{10,6},{7,11},{11,7},{20,24},{24,20... | collective-permute-start | bytes 2162696 | tf_op jit(solution)/shard_map/ppermute | solution.py:66
  75.1 14.9 %collective-permute-start.13 = (bf16[352,512]{1,0:T(8,128)(2,1)S(1)}, bf16[352,512]{1,0:T(8,128)(2,1)S(1)}, u32[]{:S(2)}, u32[]{:S(2)}) collective-permute-start(bf16[352,512]{1,0:T(8,128)(2,1)S(1)} %add_convert_fusion), channel_id=1, source_target_pairs={{4,0},{8,12},{5,1},{9,13},{6,2},{10,14},{7,3},{11,15},{20,16},{24,... | collective-permute-start | bytes 1081352 | tf_op jit(solution)/shard_map/ppermute | solution.py:71
  76.6 20.7 %collective-permute-start.10 = (bf16[352,512]{1,0:T(8,128)(2,1)S(1)}, bf16[352,512]{1,0:T(8,128)(2,1)S(1)}, u32[]{:S(2)}, u32[]{:S(2)}) collective-permute-start(bf16[352,512]{1,0:T(8,128)(2,1)S(1)} %add_convert_fusion.1), channel_id=1, source_target_pairs={{4,0},{8,12},{5,1},{9,13},{6,2},{10,14},{7,3},{11,15},{20,16},{24,... | collective-permute-start | bytes 1081352 | tf_op jit(solution)/shard_map/ppermute | solution.py:71
  78.0 34.7 %collective-permute-start.7 = (bf16[352,512]{1,0:T(8,128)(2,1)S(1)}, bf16[352,512]{1,0:T(8,128)(2,1)S(1)}, u32[]{:S(2)}, u32[]{:S(2)}) collective-permute-start(bf16[352,512]{1,0:T(8,128)(2,1)S(1)} %add_convert_fusion.2), channel_id=1, source_target_pairs={{4,0},{8,12},{5,1},{9,13},{6,2},{10,14},{7,3},{11,15},{20,16},{24,... | collective-permute-start | bytes 1081352 | tf_op jit(solution)/shard_map/ppermute | solution.py:71
  79.4 46.5 %collective-permute-start.4 = (bf16[352,512]{1,0:T(8,128)(2,1)S(1)}, bf16[352,512]{1,0:T(8,128)(2,1)S(1)}, u32[]{:S(2)}, u32[]{:S(2)}) collective-permute-start(bf16[352,512]{1,0:T(8,128)(2,1)S(1)} %add_convert_fusion.3), channel_id=1, source_target_pairs={{4,0},{8,12},{5,1},{9,13},{6,2},{10,14},{7,3},{11,15},{20,16},{24,... | collective-permute-start | bytes 1081352 | tf_op jit(solution)/shard_map/ppermute | solution.py:71
